TPU v7x, 256 devices: a whole 4x4x8 slice. The times are simulated.
256 devices in a mesh: row: 4 (over z_lo), col: 16 (over z_hi, y, core), layer: 4 (over x).
Axes of the slice: x: 4, y: 4, z: 8 (z_hi: 2, z_lo: 4; z = z_hi * 4 + z_lo), core: 2. Of those that a mesh axis runs over, the one named last changes fastest.
Arguments:
- left_blocks: bfloat16 [4096, 131072], P('row', ('layer', 'col')), may hold values from -6 to 6
- left_pattern: int32 [64, 2048], P('row', ('layer', 'col')), may hold values 0 or 1
- right_blocks: bfloat16 [131072, 2048], P(('layer', 'col'), 'row'), may hold values from -0.09375 to 0.09375
- right_pattern: int32 [2048, 32], P(('layer', 'col'), 'row'), may hold values 0 or 1
Outputs:
- product: bfloat16 [4096, 2048], P('row', ('col', 'layer'))
All inputs are finite; a program needn't handle non-finite values. No bound on the sum of `left_pattern` or of `right_pattern` on one device may be relied on, other than what follows from the above.
Results may differ from a plain program's by a relative error of at most 0.001.
Values may be sent and summed in bfloat16 or wider, within the bound.
No kernel may reach another device: no remote copies, remote signals or barrier semaphores. Data moves between devices by JAX's collectives and lax.ppermute only.
A program may use at most 64 MiB of HBM per device.

v0:
```python
import jax
import jax.numpy as jnp
from jax import lax
from jax.sharding import PartitionSpec as P


def from_behind(x, axis, by):
    size = lax.axis_size(axis)
    return lax.ppermute(x, axis, [(i, (i + by) % size) for i in range(size)])


def apply_pattern(values, pattern):
    rows, cols = values.shape
    block = rows // pattern.shape[0]
    shaped = values.reshape(pattern.shape[0], block, pattern.shape[1], block)
    masked = shaped * pattern[:, None, :, None].astype(jnp.bfloat16)
    return masked.reshape(rows, cols)


def local(left_blocks, left_pattern, right_blocks, right_pattern):
    left = apply_pattern(left_blocks, left_pattern)
    right = apply_pattern(right_blocks, right_pattern)
    left_rows = left.shape[0]
    range_cols = right.shape[1]
    cycle_size = lax.axis_size("row")
    position = lax.axis_index("row")
    partial_value = jnp.zeros((left_rows, range_cols * cycle_size), jnp.float32)
    current = right
    for step in range(cycle_size):
        if step > 0:
            current = from_behind(current, "row", 1)
        owner = (position - step) % cycle_size
        piece = jnp.dot(left, current, preferred_element_type=jnp.float32)
        partial_value = lax.dynamic_update_slice_in_dim(partial_value, piece, owner * range_cols, 1)
    reduced = lax.psum_scatter(partial_value, ("col", "layer"), scatter_dimension=1, tiled=True)
    return reduced.astype(jnp.bfloat16)


def solution(mesh):
    placed = (
        P("row", ("layer", "col")),
        P("row", ("layer", "col")),
        P(("layer", "col"), "row"),
        P(("layer", "col"), "row"),
    )
    return jax.shard_map(
        local, mesh=mesh, in_specs=placed, out_specs=P("row", ("col", "layer")), check_vma=False
    )
```

profile of v0, /device:TPU:2, one launch (start us, length us, event | category | flops | bytes accessed | tf_op | source)
XLA Modules:
  0.0 602.0 jit_solution(13439718006550730843)
XLA Ops:
  6.5 0.0 reduce-scatter.2.cloned.1.call-start
  6.5 0.7 convert_element_type.12
  7.2 0.1 copy.5
  7.3 2.6 mul.37
  9.9 5.4 mul.38
  15.3 0.0 copy-start.3
  15.3 2.2 mul.39
  17.5 0.0 copy-start.1
  17.5 1.3 copy-done.1
  18.8 1.9 collective-permute-start
  20.7 48.3 %collective-permute-done = bf16[2048,512]{1,0:T(8,128)(2,1)S(1)} collective-permute-done((bf16[2048,512]{1,0:T(8,128)(2,1)S(1)}, bf16[2048,512]{1,0:T(8,128)(2,1)S(1)}, u32[]{:S(2)}, u32[]{:S(2)}) %collective-permute-start) | collective-permute-done | bytes 2097184 | tf_op jit(solution)/shard_map/ppermute | solution.py:9
  69.1 0.0 collective-permute-start.1
  69.1 48.7 %collective-permute-done.1 = bf16[2048,512]{1,0:T(8,128)(2,1)} collective-permute-done((bf16[2048,512]{1,0:T(8,128)(2,1)S(1)}, bf16[2048,512]{1,0:T(8,128)(2,1)}, u32[]{:S(2)}, u32[]{:S(2)}) %collective-permute-start.1) | collective-permute-done | bytes 2097184 | tf_op jit(solution)/shard_map/ppermute | solution.py:9
  117.8 0.0 collective-permute-start.2
  117.8 0.0 copy-done.3
  117.8 4.4 mul.34
  122.2 12.3 %mul.35 = bf16[1024,2048]{1,0:T(8,128)(2,1)} reshape(bf16[16,64,32,64]{3,2,1,0:T(8,128)(2,1)} %mul.34) | data formatting | bytes 8388608 | tf_op jit(solution)/shard_map/mul | solution.py:16
  134.5 7.7 %mul.36 = bf16[1024,2048]{1,0:T(8,128)(2,1)} multiply(bf16[1024,2048]{1,0:T(8,128)(2,1)} %param.4, bf16[1024,2048]{1,0:T(8,128)(2,1)} %mul.35) | non-fusion elementwise | flops 2097152 | bytes 12582912 | tf_op jit(solution)/shard_map/mul | solution.py:16
  142.2 0.0 copy-start
  142.2 0.0 copy-start.2
  142.2 4.8 broadcast_in_dim.2
  147.0 0.0 copy-done
  147.0 0.0 copy-done.2
  147.0 3.8 convolution_dynamic-update-slice_fusion.3
  150.8 3.8 convolution_dynamic-update-slice_fusion.2
  154.6 5.4 convolution_dynamic-update-slice_fusion.1
  160.0 5.8 collective-permute-done.2
  165.8 5.3 convolution_dynamic-update-slice_fusion
  171.1 0.0 reduce-scatter.2.cloned.1.call-update
  171.1 422.5 %reduce-scatter.2.cloned.1.call-done = f32[1024,32]{0,1:T(8,128)} async-done(((f32[1024,2048]{0,1:T(8,128)}), f32[1024,32]{0,1:T(8,128)}) %reduce-scatter.2.cloned.1.call-update) | async-done | bytes 131088 | tf_op jit(solution)/shard_map/reduce_scatter | solution.py:35
  593.6 1.5 convert_element_type.13
  (1 shorter events, 0.0 us)
Async XLA Ops:
  6.5 587.1 %reduce-scatter.2.cloned.1.call-start = ((), (), s32[]{:S(2)}) async-start(), calls=%async_computation.1 | async-start | bytes 8519680 | tf_op jit(solution)/shard_map/reduce_scatter | solution.py:35
  15.3 102.5 %copy-start.3 = (s32[16,32]{1,0:T(8,128)S(1)}, s32[16,32]{1,0:T(8,128)}, u32[]{:S(2)}) copy-start(s32[16,32]{1,0:T(8,128)} %param.5) | copy-start | bytes 6148
  17.5 1.3 copy-start.1
  18.8 50.3 %collective-permute-start = (bf16[2048,512]{1,0:T(8,128)(2,1)S(1)}, bf16[2048,512]{1,0:T(8,128)(2,1)S(1)}, u32[]{:S(2)}, u32[]{:S(2)}) collective-permute-start(bf16[2048,512]{1,0:T(8,128)(2,1)S(1)} %mul.39), channel_id=1, source_target_pairs={{0,64},{64,128},{128,192},{192,0},{1,65},{65,129},{129,193},{193,1... | collective-permute-start | bytes 6291464 | tf_op jit(solution)/shard_map/ppermute | solution.py:9
  69.1 48.7 %collective-permute-start.1 = (bf16[2048,512]{1,0:T(8,128)(2,1)S(1)}, bf16[2048,512]{1,0:T(8,128)(2,1)}, u32[]{:S(2)}, u32[]{:S(2)}) collective-permute-start(bf16[2048,512]{1,0:T(8,128)(2,1)S(1)} %collective-permute-done), channel_id=1, source_target_pairs={{0,64},{64,128},{128,192},{192,0},{1,65},{65,129},{129,193},{193,1... | collective-permute-start | bytes 6291464 | tf_op jit(solution)/shard_map/ppermute | solution.py:9
  117.8 48.0 %collective-permute-start.2 = (bf16[2048,512]{1,0:T(8,128)(2,1)}, bf16[2048,512]{1,0:T(8,128)(2,1)}, u32[]{:S(2)}, u32[]{:S(2)}) collective-permute-start(bf16[2048,512]{1,0:T(8,128)(2,1)} %collective-permute-done.1), channel_id=1, source_target_pairs={{0,64},{64,128},{128,192},{192,0},{1,65},{65,129},{129,193},{193,1... | collective-permute-start | bytes 6291464 | tf_op jit(solution)/shard_map/ppermute | solution.py:9
  142.2 4.8 copy-start
  142.2 4.8 copy-start.2
Sparse Core Ops, SparseCore 0:
  171.3 422.3 reduce-scatter.1
where the time goes:
time: 609 us; the launch traced here: 602 us
  waiting for transfers between devices  525 us (86%)
  local copies, waits for them, and re-layouts  30.9 us (5%)
  matrix products  18.3 us (3%)
  between operations  13.4 us (2%)
  other arithmetic  12.1 us (2%)
    reduce_scatter x1, waiting for transfers between devices, local(): lax.psum_scatter(partial_value, ('col', 'layer'), scatter_dimension=1, ti...  422 us
    ppermute x3, waiting for transfers between devices, from_behind(): return lax.ppermute(x, axis, [(i, (i + by) % size) for i in range(size)])  103 us
    mul x4, local copies, waits for them, and re-layouts, apply_pattern(): masked = shaped * pattern[:, None, :, None].astype(jnp.bfloat16)  24.7 us
    dot_general x4, matrix products, local(): piece = jnp.dot(left, current, preferred_element_type=jnp.float32)  18.3 us
  transfers between devices with their start and end apart: 4, of which 4 were waited for; matrix products, arithmetic and copies ran while one was open for 7% of the time, Pallas kernels for 0%

commit v1 on v0

v1 whole, which is shorter than its diff:
```python
import jax
import jax.numpy as jnp
from jax import lax
from jax.sharding import Mesh
from jax.sharding import PartitionSpec as P

COL_PARTS = ("zhi", "y", "core")


def from_behind(x, axis, by):
    size = lax.axis_size(axis)
    return lax.ppermute(x, axis, [(i, (i + by) % size) for i in range(size)])


def apply_pattern(values, pattern):
    rows, cols = values.shape
    block = rows // pattern.shape[0]
    shaped = values.reshape(pattern.shape[0], block, pattern.shape[1], block)
    masked = shaped * pattern[:, None, :, None].astype(jnp.bfloat16)
    return masked.reshape(rows, cols)


def local(left_blocks, left_pattern, right_blocks, right_pattern):
    left = apply_pattern(left_blocks, left_pattern)
    right = apply_pattern(right_blocks, right_pattern)
    left_rows = left.shape[0]
    range_cols = right.shape[1]
    cycle_size = lax.axis_size("row")
    position = lax.axis_index("row")
    partial_t = jnp.zeros((range_cols * cycle_size, left_rows), jnp.float32)
    current = right
    for step in range(cycle_size):
        if step > 0:
            current = from_behind(current, "row", 1)
        owner = (position - step) % cycle_size
        piece = lax.dot_general(current, left, (((0,), (1,)), ((), ())), preferred_element_type=jnp.float32)
        partial_t = lax.dynamic_update_slice_in_dim(partial_t, piece, owner * range_cols, 0)
    zhi, ys, cores, layers = (lax.axis_size(a) for a in COL_PARTS + ("layer",))
    block = partial_t.shape[0] // (zhi * ys * cores * layers)
    ordered = partial_t.reshape(zhi, ys, cores, layers, block, left_rows)
    ordered = ordered.transpose(2, 3, 1, 0, 4, 5).reshape(-1, left_rows)
    for axis in ("core", "layer", "y", "zhi"):
        ordered = lax.psum_scatter(ordered, axis, scatter_dimension=0, tiled=True)
    return ordered.T.astype(jnp.bfloat16)


def solution(mesh):
    cols = mesh.shape["col"]
    fine = Mesh(
        mesh.devices.reshape(mesh.shape["row"], 2, cols // 4, 2, mesh.shape["layer"]),
        ("row",) + COL_PARTS + ("layer",),
    )
    inner = ("layer",) + COL_PARTS
    placed = (
        P("row", inner),
        P("row", inner),
        P(inner, "row"),
        P(inner, "row"),
    )
    return jax.shard_map(
        local, mesh=fine, in_specs=placed, out_specs=P("row", COL_PARTS + ("layer",)), check_vma=False
    )
```

time: 609 us -> 315 us (0.52)
  waiting for transfers between devices: 525 us -> 240 us
    reduce_scatter x1 -> x4, waiting for transfers between devices: 422 us -> 131 us  [local(): ordered = lax.psum_scatter(ordered, axis, scatter_dimension=0, tiled=True)]
    ppermute x3, waiting for transfers between devices: 103 us -> 109 us  [from_behind(): return lax.ppermute(x, axis, [(i, (i + by) % size) for i in range(size)])]
  transfers between devices with their start and end apart: 4 -> 7, of which waited for: 4 -> 7; matrix products, arithmetic and copies ran while one was open for 7% -> 11% of each run, Pallas kernels for 0% -> 0%
where the time goes in v1:
time: 315 us; the launch traced here: 313 us
  waiting for transfers between devices  240 us (76%)
  local copies, waits for them, and re-layouts  33 us (10%)
  between operations  13.2 us (4%)
  matrix products  12.7 us (4%)
  other arithmetic  12.1 us (4%)
    reduce_scatter x4, waiting for transfers between devices, local(): ordered = lax.psum_scatter(ordered, axis, scatter_dimension=0, tiled=True)  131 us
    ppermute x3, waiting for transfers between devices, from_behind(): return lax.ppermute(x, axis, [(i, (i + by) % size) for i in range(size)])  109 us
    mul x4, local copies, waits for them, and re-layouts, apply_pattern(): masked = shaped * pattern[:, None, :, None].astype(jnp.bfloat16)  24.7 us
    dot_general x4, matrix products, local(): lax.dot_general(current, left, (((0,), (1,)), ((), ())), preferred_elemen...  12.7 us
    mul x2, other arithmetic, apply_pattern(): masked = shaped * pattern[:, None, :, None].astype(jnp.bfloat16)  9.9 us
  transfers between devices with their start and end apart: 7, of which 7 were waited for; matrix products, arithmetic and copies ran while one was open for 11% of the time, Pallas kernels for 0%

profile of v1, /device:TPU:2, one launch (start us, length us, event | category | flops | bytes accessed | tf_op | source)
XLA Modules:
  0.0 313.4 jit_solution(16482765259417406555)
XLA Ops:
  6.5 0.7 convert_element_type.14
  7.2 0.1 copy.7
  7.3 2.6 mul.34
  9.9 5.4 %mul.35 = bf16[2048,512]{1,0:T(8,128)(2,1)S(1)} reshape(bf16[32,64,8,64]{3,2,1,0:T(8,128)(2,1)} %mul.34) | data formatting | bytes 4194304 | tf_op jit(solution)/shard_map/mul | solution.py:19
  15.3 2.2 mul.36
  17.5 1.3 copy-done.1
  18.8 1.9 collective-permute-start
  20.7 48.3 %collective-permute-done = bf16[2048,512]{1,0:T(8,128)(2,1)S(1)} collective-permute-done((bf16[2048,512]{1,0:T(8,128)(2,1)S(1)}, bf16[2048,512]{1,0:T(8,128)(2,1)S(1)}, u32[]{:S(2)}, u32[]{:S(2)}) %collective-permute-start) | collective-permute-done | bytes 2097184 | tf_op jit(solution)/shard_map/ppermute | solution.py:12
  69.0 48.7 %collective-permute-done.1 = bf16[2048,512]{1,0:T(8,128)(2,1)} collective-permute-done((bf16[2048,512]{1,0:T(8,128)(2,1)S(1)}, bf16[2048,512]{1,0:T(8,128)(2,1)}, u32[]{:S(2)}, u32[]{:S(2)}) %collective-permute-start.1) | collective-permute-done | bytes 2097184 | tf_op jit(solution)/shard_map/ppermute | solution.py:12
  117.8 4.4 %mul.37 = bf16[16,64,32,64]{3,2,1,0:T(8,128)(2,1)} broadcast(bf16[16,32]{1,0:T(8,128)(2,1)S(1)} %convert_element_type.15), dimensions={0,2} | broadcast | bytes 4195328 | tf_op jit(solution)/shard_map/mul | solution.py:19
  122.2 12.3 %mul.38 = bf16[1024,2048]{1,0:T(8,128)(2,1)} reshape(bf16[16,64,32,64]{3,2,1,0:T(8,128)(2,1)} %mul.37) | data formatting | bytes 8388608 | tf_op jit(solution)/shard_map/mul | solution.py:19
  134.5 7.7 %mul.39 = bf16[1024,2048]{1,0:T(8,128)(2,1)} multiply(bf16[1024,2048]{1,0:T(8,128)(2,1)} %param.4, bf16[1024,2048]{1,0:T(8,128)(2,1)} %mul.38) | non-fusion elementwise | flops 2097152 | bytes 12582912 | tf_op jit(solution)/shard_map/mul | solution.py:19
  142.2 1.1 broadcast_in_dim.2
  143.3 1.1 copy-done
  144.4 0.7 copy-done.2
  145.1 2.4 convolution_dynamic-update-slice_fusion.3
  147.5 2.4 convolution_dynamic-update-slice_fusion.2
  149.8 4.0 %convolution_dynamic-update-slice_fusion.1 = f32[2048,1024]{1,0:T(8,128)S(1)} fusion(f32[2048,1024]{1,0:T(8,128)S(1)} %convolution_dynamic-update-slice_fusion.2, s32[]{:T(128)S(6)} %select_n.36, bf16[2048,512]{1,0:T(8,128)(2,1)} %collective-permute-done.1, bf16[1024,2048]{1,0:T(8,128)(2,1)S(1)} %copy-done), kind=kOutput, calls=%fused_computation.1 | convolution fusion | flops 2147483648 | bytes 8388612 | tf_op jit(solution)/shard_map/dot_general | solution.py:36
  153.8 11.9 %collective-permute-done.2 = bf16[2048,512]{1,0:T(8,128)(2,1)} collective-permute-done((bf16[2048,512]{1,0:T(8,128)(2,1)}, bf16[2048,512]{1,0:T(8,128)(2,1)}, u32[]{:S(2)}, u32[]{:S(2)}) %collective-permute-start.2) | collective-permute-done | bytes 2097184 | tf_op jit(solution)/shard_map/ppermute | solution.py:12
  165.8 4.0 %convolution_dynamic-update-slice_fusion = f32[2048,1024]{1,0:T(8,128)S(1)} fusion(f32[2048,1024]{1,0:T(8,128)S(1)} %convolution_dynamic-update-slice_fusion.1, s32[]{:T(128)S(6)} %select_n.38, bf16[2048,512]{1,0:T(8,128)(2,1)} %collective-permute-done.2, bf16[1024,2048]{1,0:T(8,128)(2,1)S(1)} %copy-done), kind=kOutput, calls=%fused_computation | convolution fusion | flops 2147483648 | bytes 8388612 | tf_op jit(solution)/shard_map/dot_general | solution.py:36
  169.7 4.1 %copy.8 = f32[2,4,4,2,32,1024]{5,4,3,2,1,0:T(8,128)} copy(f32[2,4,4,2,32,1024]{5,4,1,0,2,3:T(8,128)S(1)} %bitcast.19) | data formatting | bytes 16777216 | tf_op jit(solution)/shard_map/transpose | solution.py:41
  173.8 0.0 reduce-scatter.7.cloned.1.call-start
  173.9 23.6 %reduce-scatter.5.cloned.1.call-done = f32[1024,1024]{1,0:T(8,128)} async-done(((f32[2048,1024]{1,0:T(8,128)}), f32[1024,1024]{1,0:T(8,128)}) %reduce-scatter.5.cloned.1.call-update) | async-done | bytes 4194320 | tf_op jit(solution)/shard_map/reduce_scatter | solution.py:43
  197.4 0.0 reduce-scatter.7.cloned.1.call-update
  197.5 0.0 reduce-scatter.9.cloned.1.call-start
  197.5 52.1 %reduce-scatter.7.cloned.1.call-done = f32[256,1024]{1,0:T(8,128)} async-done(((f32[1024,1024]{1,0:T(8,128)}), f32[256,1024]{1,0:T(8,128)}) %reduce-scatter.7.cloned.1.call-update) | async-done | bytes 1048592 | tf_op jit(solution)/shard_map/reduce_scatter | solution.py:43
  249.6 0.0 reduce-scatter.9.cloned.1.call-update
  249.7 0.0 reduce-scatter.11.cloned.1.call-start
  249.7 29.6 %reduce-scatter.9.cloned.1.call-done = f32[64,1024]{1,0:T(8,128)} async-done(((f32[256,1024]{1,0:T(8,128)}), f32[64,1024]{1,0:T(8,128)}) %reduce-scatter.9.cloned.1.call-update) | async-done | bytes 262160 | tf_op jit(solution)/shard_map/reduce_scatter | solution.py:43
  279.3 0.0 reduce-scatter.11.cloned.1.call-update
  279.4 25.9 %reduce-scatter.11.cloned.1.call-done = f32[32,1024]{1,0:T(8,128)} async-done(((f32[64,1024]{1,0:T(8,128)}), f32[32,1024]{1,0:T(8,128)}) %reduce-scatter.11.cloned.1.call-update) | async-done | bytes 131088 | tf_op jit(solution)/shard_map/reduce_scatter | solution.py:43
  305.3 1.5 convert_bitcast_fusion
  (10 shorter events, 0.0 us)
Async XLA Ops:
  6.5 190.9 %reduce-scatter.5.cloned.1.call-start = ((), (), s32[]{:S(2)}) async-start(), calls=%async_computation.4 | async-start | bytes 12582912 | tf_op jit(solution)/shard_map/reduce_scatter | solution.py:43
  15.3 102.5 %copy-start.3 = (s32[16,32]{1,0:T(8,128)S(1)}, s32[16,32]{1,0:T(8,128)}, u32[]{:S(2)}) copy-start(s32[16,32]{1,0:T(8,128)} %param.5) | copy-start | bytes 6148
  17.5 1.3 copy-start.1
  18.8 50.3 %collective-permute-start = (bf16[2048,512]{1,0:T(8,128)(2,1)S(1)}, bf16[2048,512]{1,0:T(8,128)(2,1)S(1)}, u32[]{:S(2)}, u32[]{:S(2)}) collective-permute-start(bf16[2048,512]{1,0:T(8,128)(2,1)S(1)} %mul.36), channel_id=1, source_target_pairs={{0,64},{64,128},{128,192},{192,0},{1,65},{65,129},{129,193},{193,1... | collective-permute-start | bytes 6291464 | tf_op jit(solution)/shard_map/ppermute | solution.py:12
  69.0 48.7 %collective-permute-start.1 = (bf16[2048,512]{1,0:T(8,128)(2,1)S(1)}, bf16[2048,512]{1,0:T(8,128)(2,1)}, u32[]{:S(2)}, u32[]{:S(2)}) collective-permute-start(bf16[2048,512]{1,0:T(8,128)(2,1)S(1)} %collective-permute-done), channel_id=1, source_target_pairs={{0,64},{64,128},{128,192},{192,0},{1,65},{65,129},{129,193},{193,1... | collective-permute-start | bytes 6291464 | tf_op jit(solution)/shard_map/ppermute | solution.py:12
  117.8 48.0 %collective-permute-start.2 = (bf16[2048,512]{1,0:T(8,128)(2,1)}, bf16[2048,512]{1,0:T(8,128)(2,1)}, u32[]{:S(2)}, u32[]{:S(2)}) collective-permute-start(bf16[2048,512]{1,0:T(8,128)(2,1)} %collective-permute-done.1), channel_id=1, source_target_pairs={{0,64},{64,128},{128,192},{192,0},{1,65},{65,129},{129,193},{193,1... | collective-permute-start | bytes 6291464 | tf_op jit(solution)/shard_map/ppermute | solution.py:12
  142.2 2.2 copy-start
  142.2 2.9 copy-start.2
  173.8 75.8 %reduce-scatter.7.cloned.1.call-start = ((), (), s32[]{:S(2)}) async-start(), calls=%async_computation.5 | async-start | bytes 5242880 | tf_op jit(solution)/shard_map/reduce_scatter | solution.py:43
  197.5 81.9 %reduce-scatter.9.cloned.1.call-start = ((), (), s32[]{:S(2)}) async-start(), calls=%async_computation.6 | async-start | bytes 1310720 | tf_op jit(solution)/shard_map/reduce_scatter | solution.py:43
  249.7 55.6 %reduce-scatter.11.cloned.1.call-start = ((), (), s32[]{:S(2)}) async-start(), calls=%async_computation.7 | async-start | bytes 393216 | tf_op jit(solution)/shard_map/reduce_scatter | solution.py:43
Sparse Core Ops, SparseCore 0:
  174.0 23.4 reduce-scatter.4
  200.2 49.4 reduce-scatter.6
  252.2 27.1 reduce-scatter.8
  281.8 23.4 reduce-scatter.10

commit v2 on v1

v2 whole, which is shorter than its diff:
```python
import jax
import jax.numpy as jnp
from jax import lax
from jax.sharding import Mesh
from jax.sharding import PartitionSpec as P

COL_PARTS = ("zhi", "y", "core")


def from_behind(x, axis, by):
    size = lax.axis_size(axis)
    return lax.ppermute(x, axis, [(i, (i + by) % size) for i in range(size)])


def apply_pattern(values, pattern):
    rows, cols = values.shape
    block = rows // pattern.shape[0]
    widened = jnp.repeat(pattern.astype(jnp.bfloat16), cols // pattern.shape[1], axis=1)
    masked = values.reshape(pattern.shape[0], block, cols) * widened[:, None, :]
    return masked.reshape(rows, cols)


def halve_over(x, axis):
    half = x.shape[0] // 2
    first = lax.axis_index(axis) == 0
    keep = jnp.where(first, x[:half], x[half:])
    send = jnp.where(first, x[half:], x[:half])
    return keep + lax.ppermute(send, axis, [(0, 1), (1, 0)])


def spread_over(x, axis):
    n = lax.axis_size(axis)
    x = x.reshape(n, x.shape[0] // n, *x.shape[1:])
    return lax.all_to_all(x, axis, 0, 0, tiled=False).sum(0)


def local(left_blocks, left_pattern, right_blocks, right_pattern):
    left = apply_pattern(left_blocks, left_pattern)
    right = apply_pattern(right_blocks, right_pattern)
    left_rows = left.shape[0]
    cycle_size = lax.axis_size("row")
    position = lax.axis_index("row")
    zhi, ys, cores, layers = (lax.axis_size(a) for a in COL_PARTS + ("layer",))
    halves = ys // 2
    block = right.shape[1] // (halves * cores * layers)
    gathered = jnp.zeros((cycle_size, halves, block, left_rows), jnp.float32)
    current = right
    for step in range(cycle_size):
        if step > 0:
            current = from_behind(current, "row", 1)
        owner = (position - step) % cycle_size
        piece = lax.dot_general(current, left, (((0,), (1,)), ((), ())), preferred_element_type=jnp.float32)
        piece = piece.reshape(halves, cores, layers, block, left_rows).transpose(1, 2, 0, 3, 4)
        piece = halve_over(piece.reshape(cores * layers, halves, block, left_rows), "core")
        piece = spread_over(piece, "layer")
        gathered = lax.dynamic_update_slice_in_dim(gathered, piece, owner, 0)
    ordered = gathered.reshape(zhi, ys, block, left_rows).transpose(1, 0, 2, 3)
    ordered = spread_over(ordered, "y")[0]
    ordered = halve_over(ordered, "zhi")
    return ordered.reshape(block, left_rows).T.astype(jnp.bfloat16)


def solution(mesh):
    cols = mesh.shape["col"]
    fine = Mesh(
        mesh.devices.reshape(mesh.shape["row"], 2, cols // 4, 2, mesh.shape["layer"]),
        ("row",) + COL_PARTS + ("layer",),
    )
    inner = ("layer",) + COL_PARTS
    placed = (
        P("row", inner),
        P("row", inner),
        P(inner, "row"),
        P(inner, "row"),
    )
    return jax.shard_map(
        local, mesh=fine, in_specs=placed, out_specs=P("row", COL_PARTS + ("layer",)), check_vma=False
    )
```

time: 315 us -> 235 us (0.75)
  waiting for transfers between devices: 240 us -> 142 us
  starting transfers between devices: 2.04 us -> 32.7 us
  between operations: 13.2 us -> 0.24 us
  local copies, waits for them, and re-layouts: 33 us -> 23.1 us
  other arithmetic: 12.1 us -> 18.2 us
  matrix products: 12.7 us -> 17.3 us
    reduce_scatter x4 -> x0, waiting for transfers between devices: 131 us -> none  [local(): ordered = lax.psum_scatter(ordered, axis, scatter_dimension=0, tiled=True)]
    all_to_all x0 -> x5, waiting for transfers between devices: none -> 31.8 us  [spread_over(): return lax.all_to_all(x, axis, 0, 0, tiled=False).sum(0)]
    all_to_all x0 -> x5, starting transfers between devices: none -> 25.2 us  [spread_over(): return lax.all_to_all(x, axis, 0, 0, tiled=False).sum(0)]
    mul x4 -> x2, local copies, waits for them, and re-layouts: 24.7 us -> 0.29 us  [apply_pattern(): masked = values.reshape(pattern.shape[0], block, cols) * widened[:, None, :]]
    dot_general x0 -> x4, local copies, waits for them, and re-layouts: none -> 13.4 us  [local(): lax.dot_general(current, left, (((0,), (1,)), ((), ())), preferred_elemen...]
    reshape x0 -> x4, other arithmetic: none -> 6.08 us  [spread_over(): x = x.reshape(n, x.shape[0] // n, *x.shape[1:])]
    mul x2, other arithmetic: 9.9 us -> 4.37 us  [apply_pattern(): masked = values.reshape(pattern.shape[0], block, cols) * widened[:, None, :]]
    ppermute x0 -> x5, starting transfers between devices: none -> 5.5 us  [halve_over(): return keep + lax.ppermute(send, axis, [(0, 1), (1, 0)])]
  transfers between devices with their start and end apart: 7 -> 13, of which waited for: 7 -> 8; matrix products, arithmetic and copies ran while one was open for 11% -> 22% of each run, Pallas kernels for 0% -> 0%
where the time goes in v2:
time: 235 us; the launch traced here: 234 us
  waiting for transfers between devices  142 us (60%)
  starting transfers between devices  32.7 us (14%)
  local copies, waits for them, and re-layouts  23.1 us (10%)
  other arithmetic  18.2 us (8%)
  matrix products  17.3 us (7%)
    ppermute x3, waiting for transfers between devices, from_behind(): return lax.ppermute(x, axis, [(i, (i + by) % size) for i in range(size)])  105 us
    all_to_all x5, waiting for transfers between devices, spread_over(): return lax.all_to_all(x, axis, 0, 0, tiled=False).sum(0)  31.8 us
    all_to_all x5, starting transfers between devices, spread_over(): return lax.all_to_all(x, axis, 0, 0, tiled=False).sum(0)  25.2 us
    dot_general x4, matrix products, local(): lax.dot_general(current, left, (((0,), (1,)), ((), ())), preferred_elemen...  17.3 us
    dot_general x4, local copies, waits for them, and re-layouts, local(): lax.dot_general(current, left, (((0,), (1,)), ((), ())), preferred_elemen...  13.4 us
    reshape x4, other arithmetic, spread_over(): x = x.reshape(n, x.shape[0] // n, *x.shape[1:])  6.08 us
    ppermute x5, starting transfers between devices, halve_over(): return keep + lax.ppermute(send, axis, [(0, 1), (1, 0)])  5.5 us
    reshape x5, local copies, waits for them, and re-layouts, spread_over(): x = x.reshape(n, x.shape[0] // n, *x.shape[1:])  5.34 us
  transfers between devices with their start and end apart: 13, of which 8 were waited for; matrix products, arithmetic and copies ran while one was open for 22% of the time, Pallas kernels for 0%

profile of v2, /device:TPU:2, one launch (start us, length us, event | category | flops | bytes accessed | tf_op | source)
XLA Modules:
  0.0 233.6 jit_solution(6812805521626777782)
XLA Ops:
  1.0 1.7 bitcast_multiply_fusion.1
  2.8 2.0 collective-permute-start.1
  5.1 2.5 %copy.54 = bf16[512,2048]{1,0:T(8,128)(2,1)} copy(bf16[512,2048]{0,1:T(8,128)(2,1)S(1)} %bitcast.116) | data formatting | bytes 4194304 | tf_op jit(solution)/shard_map/dot_general | solution.py:52
  7.6 2.6 %bitcast_multiply_fusion = bf16[1024,2048]{1,0:T(8,128)(2,1)S(1)} fusion(bf16[1024,2048]{1,0:T(8,128)(2,1)} %param.4, bf16[16,2048]{1,0:T(8,128)(2,1)S(1)} %mul.30), kind=kLoop, calls=%fused_computation.8 | loop fusion | flops 2097152 | bytes 8454144 | tf_op jit(solution)/shard_map/mul | solution.py:19
  10.2 43.0 %collective-permute-done.1 = bf16[2048,512]{1,0:T(8,128)(2,1)} collective-permute-done((bf16[2048,512]{1,0:T(8,128)(2,1)S(1)}, bf16[2048,512]{1,0:T(8,128)(2,1)}, u32[]{:S(2)}, u32[]{:S(2)}) %collective-permute-start.1) | collective-permute-done | bytes 2097184 | tf_op jit(solution)/shard_map/ppermute | solution.py:12
  53.2 2.4 %fusion.26 = f32[2,4,2,32,1024]{4,3,1,0,2:T(8,128)S(1)} fusion(bf16[2,2,4,32,2048]{4,3,2,1,0:T(8,128)(2,1)S(1)} %bitcast.120, bf16[1024,2048]{1,0:T(8,128)(2,1)S(1)} %bitcast_multiply_fusion), kind=kOutput, calls=%fused_computation.16 | convolution fusion | flops 2147483648 | bytes 8388608 | tf_op jit(solution)/shard_map/dot_general | solution.py:52
  55.6 1.3 copy-done.2
  57.2 4.0 %copy.60 = bf16[512,2048]{1,0:T(8,128)(2,1)} copy(bf16[512,2048]{0,1:T(8,128)(2,1)} %bitcast.14) | data formatting | bytes 4194304 | tf_op jit(solution)/shard_map/dot_general | solution.py:52
  61.1 5.2 %fusion.11 = f32[2,4,2,32,1024]{4,3,1,2,0:T(8,128)S(1)} fusion(bf16[1024,2048]{1,0:T(8,128)(2,1)} %copy-done.4, bf16[2,2,4,32,2048]{4,3,2,1,0:T(8,128)(2,1)} %bitcast.122), kind=kOutput, calls=%fused_computation.13 | convolution fusion | flops 2147483648 | bytes 8388608 | tf_op jit(solution)/shard_map/dot_general | solution.py:52
  68.0 34.2 %collective-permute-done.3 = bf16[2048,512]{1,0:T(8,128)(2,1)} collective-permute-done((bf16[2048,512]{1,0:T(8,128)(2,1)}, bf16[2048,512]{1,0:T(8,128)(2,1)}, u32[]{:S(2)}, u32[]{:S(2)}) %collective-permute-start.3) | collective-permute-done | bytes 2097184 | tf_op jit(solution)/shard_map/ppermute | solution.py:12
  102.1 1.5 fusion.31
  104.8 4.8 %all-to-all-start = ((f32[4,1,2,32,1024]{4,3,2,1,0:T(8,128)}), f32[4,1,2,32,1024]{4,3,2,1,0:T(8,128)S(1)}, u32[]{:S(2)}, u32[]{:S(2)}) async-start(f32[4,1,2,32,1024]{4,3,2,1,0:T(8,128)} %copy.59), calls=%async_computation | async-start | bytes 2097152 | tf_op jit(solution)/shard_map/all_to_all | solution.py:34
  109.6 1.5 fusion.34
  112.2 2.9 %copy.63 = bf16[512,2048]{1,0:T(8,128)(2,1)S(1)} copy(bf16[512,2048]{0,1:T(8,128)(2,1)} %bitcast.22) | data formatting | bytes 4194304 | tf_op jit(solution)/shard_map/dot_general | solution.py:52
  115.1 4.5 %fusion.16 = f32[2,4,2,32,1024]{4,3,1,2,0:T(8,128)S(1)} fusion(bf16[1024,2048]{1,0:T(8,128)(2,1)} %copy-done.4, bf16[2,2,4,32,2048]{4,3,2,1,0:T(8,128)(2,1)S(1)} %bitcast.123), kind=kOutput, calls=%fused_computation.14 | convolution fusion | flops 2147483648 | bytes 8388608 | tf_op jit(solution)/shard_map/dot_general | solution.py:52
  119.7 1.3 copy-done
  122.2 27.9 %collective-permute-done.5 = bf16[2048,512]{1,0:T(8,128)(2,1)} collective-permute-done((bf16[2048,512]{1,0:T(8,128)(2,1)}, bf16[2048,512]{1,0:T(8,128)(2,1)}, u32[]{:S(2)}, u32[]{:S(2)}) %collective-permute-start.5) | collective-permute-done | bytes 2097184 | tf_op jit(solution)/shard_map/ppermute | solution.py:12
  150.1 4.0 %copy.66 = bf16[512,2048]{1,0:T(8,128)(2,1)} copy(bf16[512,2048]{0,1:T(8,128)(2,1)} %bitcast.30) | data formatting | bytes 4194304 | tf_op jit(solution)/shard_map/dot_general | solution.py:52
  154.1 5.2 %fusion.21 = f32[2,4,2,32,1024]{4,3,1,2,0:T(8,128)S(1)} fusion(bf16[1024,2048]{1,0:T(8,128)(2,1)} %copy-done.4, bf16[2,2,4,32,2048]{4,3,2,1,0:T(8,128)(2,1)} %bitcast.121), kind=kOutput, calls=%fused_computation.15 | convolution fusion | flops 2147483648 | bytes 8388608 | tf_op jit(solution)/shard_map/dot_general | solution.py:52
  159.3 4.8 %all-to-all-start.1 = ((f32[4,1,2,32,1024]{4,3,2,1,0:T(8,128)}), f32[4,1,2,32,1024]{4,3,2,1,0:T(8,128)}, u32[]{:S(2)}, u32[]{:S(2)}) async-start(f32[4,1,2,32,1024]{4,3,2,1,0:T(8,128)} %copy.62), calls=%async_computation.1 | async-start | bytes 2097152 | tf_op jit(solution)/shard_map/all_to_all | solution.py:34
  166.1 1.5 fusion.33
  168.7 6.8 %all-to-all-done.1 = f32[4,1,2,32,1024]{4,3,2,1,0:T(8,128)} async-done(((f32[4,1,2,32,1024]{4,3,2,1,0:T(8,128)}), f32[4,1,2,32,1024]{4,3,2,1,0:T(8,128)}, u32[]{:S(2)}, u32[]{:S(2)}) %all-to-all-start.1) | async-done | bytes 1048608 | tf_op jit(solution)/shard_map/all_to_all | solution.py:34
  175.5 5.6 %all-to-all-start.2 = ((f32[4,1,2,32,1024]{4,3,2,1,0:T(8,128)}), f32[4,1,2,32,1024]{4,3,2,1,0:T(8,128)}, u32[]{:S(2)}, u32[]{:S(2)}) async-start(f32[4,1,2,32,1024]{4,3,2,1,0:T(8,128)} %copy.65), calls=%async_computation.2 | async-start | bytes 2097152 | tf_op jit(solution)/shard_map/all_to_all | solution.py:34
  181.2 1.5 fusion.32
  183.7 7.6 %all-to-all-done.2 = f32[4,1,2,32,1024]{4,3,2,1,0:T(8,128)} async-done(((f32[4,1,2,32,1024]{4,3,2,1,0:T(8,128)}), f32[4,1,2,32,1024]{4,3,2,1,0:T(8,128)}, u32[]{:S(2)}, u32[]{:S(2)}) %all-to-all-start.2) | async-done | bytes 1048608 | tf_op jit(solution)/shard_map/all_to_all | solution.py:34
  191.3 4.9 %all-to-all-start.3 = ((f32[4,1,2,32,1024]{4,3,2,1,0:T(8,128)}), f32[4,1,2,32,1024]{4,3,2,1,0:T(8,128)S(1)}, u32[]{:S(2)}, u32[]{:S(2)}) async-start(f32[4,1,2,32,1024]{4,3,2,1,0:T(8,128)} %copy.68), calls=%async_computation.3 | async-start | bytes 2097152 | tf_op jit(solution)/shard_map/all_to_all | solution.py:34
  197.8 1.3 reduce_sum.59
  199.2 6.5 %all-to-all-done.3 = f32[4,1,2,32,1024]{4,3,2,1,0:T(8,128)S(1)} async-done(((f32[4,1,2,32,1024]{4,3,2,1,0:T(8,128)}), f32[4,1,2,32,1024]{4,3,2,1,0:T(8,128)S(1)}, u32[]{:S(2)}, u32[]{:S(2)}) %all-to-all-start.3) | async-done | bytes 1048608 | tf_op jit(solution)/shard_map/all_to_all | solution.py:34
  206.9 5.0 %all-to-all-start.4 = ((f32[4,1,2,32,1024]{4,3,2,1,0:T(8,128)}), f32[4,1,2,32,1024]{4,3,2,1,0:T(8,128)S(1)}, u32[]{:S(2)}, u32[]{:S(2)}) async-start(f32[4,1,2,32,1024]{4,3,2,1,0:T(8,128)} %copy.69), calls=%async_computation.4 | async-start | bytes 2097152 | tf_op jit(solution)/shard_map/all_to_all | solution.py:34
  211.8 10.9 %all-to-all-done.4 = f32[4,1,2,32,1024]{4,3,2,1,0:T(8,128)S(1)} async-done(((f32[4,1,2,32,1024]{4,3,2,1,0:T(8,128)}), f32[4,1,2,32,1024]{4,3,2,1,0:T(8,128)S(1)}, u32[]{:S(2)}, u32[]{:S(2)}) %all-to-all-start.4) | async-done | bytes 1048608 | tf_op jit(solution)/shard_map/all_to_all | solution.py:34
  222.8 4.9 %collective-permute-start.7 = (f32[1,32,1024]{2,1,0:T(8,128)S(1)}, f32[1,32,1024]{2,1,0:T(8,128)S(1)}, u32[]{:S(2)}, u32[]{:S(2)}) collective-permute-start(f32[1,32,1024]{2,1,0:T(8,128)S(1)} %select_bitcast_fusion.4), channel_id=1, source_target_pairs={{0,32},{32,0},{1,33},{33,1},{2,34},{34,2},{3,35},{35,3},{4,36},{36... | collective-permute-start | bytes 393224 | tf_op jit(solution)/shard_map/ppermute | solution.py:28
  227.8 5.2 %collective-permute-done.7 = f32[1,32,1024]{2,1,0:T(8,128)S(1)} collective-permute-done((f32[1,32,1024]{2,1,0:T(8,128)S(1)}, f32[1,32,1024]{2,1,0:T(8,128)S(1)}, u32[]{:S(2)}, u32[]{:S(2)}) %collective-permute-start.7) | collective-permute-done | bytes 131104 | tf_op jit(solution)/shard_map/ppermute | solution.py:28
  (50 shorter events, 14.1 us)
Async XLA Ops:
  1.0 3.8 %copy-start.6 = (s32[16,32]{1,0:T(8,128)S(1)}, s32[16,32]{1,0:T(8,128)}, u32[]{:S(2)}) copy-start(s32[16,32]{1,0:T(8,128)} %param.5) | copy-start | bytes 6148
  2.8 50.4 %collective-permute-start.1 = (bf16[2048,512]{1,0:T(8,128)(2,1)S(1)}, bf16[2048,512]{1,0:T(8,128)(2,1)}, u32[]{:S(2)}, u32[]{:S(2)}) collective-permute-start(bf16[2048,512]{1,0:T(8,128)(2,1)S(1)} %bitcast_multiply_fusion.1), channel_id=1, source_target_pairs={{0,64},{64,128},{128,192},{192,0},{1,65},{65,129},{129,193},{193,1... | collective-permute-start | bytes 6291464 | tf_op jit(solution)/shard_map/ppermute | solution.py:12
  7.6 45.6 %copy-start.5 = (bf16[512,2048]{1,0:T(8,128)(2,1)S(1)}, bf16[512,2048]{1,0:T(8,128)(2,1)}, u32[]{:S(2)}) copy-start(bf16[512,2048]{1,0:T(8,128)(2,1)} %copy.54) | copy-start | bytes 6291460
  10.2 45.4 %copy-start.4 = (bf16[1024,2048]{1,0:T(8,128)(2,1)}, bf16[1024,2048]{1,0:T(8,128)(2,1)S(1)}, u32[]{:S(2)}) copy-start(bf16[1024,2048]{1,0:T(8,128)(2,1)S(1)} %bitcast_multiply_fusion) | copy-start | bytes 12582916
  53.2 48.9 %collective-permute-start.3 = (bf16[2048,512]{1,0:T(8,128)(2,1)}, bf16[2048,512]{1,0:T(8,128)(2,1)}, u32[]{:S(2)}, u32[]{:S(2)}) collective-permute-start(bf16[2048,512]{1,0:T(8,128)(2,1)} %collective-permute-done.1), channel_id=1, source_target_pairs={{0,64},{64,128},{128,192},{192,0},{1,65},{65,129},{129,193},{193,1... | collective-permute-start | bytes 6291464 | tf_op jit(solution)/shard_map/ppermute | solution.py:12
  55.6 1.3 copy-start.2
  57.1 45.1 %collective-permute-start = (f32[4,2,32,1024]{3,2,0,1:T(8,128)S(1)}, f32[4,2,32,1024]{3,2,0,1:T(8,128)}, u32[]{:S(2)}, u32[]{:S(2)}) collective-permute-start(f32[4,2,32,1024]{3,2,0,1:T(8,128)S(1)} %select_bitcast_fusion.3), channel_id=1, source_target_pairs={{0,4},{4,0},{1,5},{5,1},{2,6},{6,2},{3,7},{7,3},{8,12},{12,8},{9,1... | collective-permute-start | bytes 3145736 | tf_op jit(solution)/shard_map/ppermute | solution.py:28
  66.3 35.8 %copy-start.3 = (f32[2,4,2,32,1024]{4,3,1,0,2:T(8,128)S(1)}, f32[2,4,2,32,1024]{4,3,1,0,2:T(8,128)}, u32[]{:S(2)}) copy-start(f32[2,4,2,32,1024]{4,3,1,0,2:T(8,128)} %copy-done.2) | copy-start | bytes 6291460
  67.5 42.2 %collective-permute-start.2 = (f32[4,2,32,1024]{3,2,0,1:T(8,128)}, f32[4,2,32,1024]{3,2,0,1:T(8,128)}, u32[]{:S(2)}, u32[]{:S(2)}) collective-permute-start(f32[4,2,32,1024]{3,2,0,1:T(8,128)} %select_bitcast_fusion.2), channel_id=1, source_target_pairs={{0,4},{4,0},{1,5},{5,1},{2,6},{6,2},{3,7},{7,3},{8,12},{12,8},{9,1... | collective-permute-start | bytes 3145736 | tf_op jit(solution)/shard_map/ppermute | solution.py:28
  102.1 48.0 %collective-permute-start.5 = (bf16[2048,512]{1,0:T(8,128)(2,1)}, bf16[2048,512]{1,0:T(8,128)(2,1)}, u32[]{:S(2)}, u32[]{:S(2)}) collective-permute-start(bf16[2048,512]{1,0:T(8,128)(2,1)} %collective-permute-done.3), channel_id=1, source_target_pairs={{0,64},{64,128},{128,192},{192,0},{1,65},{65,129},{129,193},{193,1... | collective-permute-start | bytes 6291464 | tf_op jit(solution)/shard_map/ppermute | solution.py:12
  104.8 54.5 %all-to-all-start = ((f32[4,1,2,32,1024]{4,3,2,1,0:T(8,128)}), f32[4,1,2,32,1024]{4,3,2,1,0:T(8,128)S(1)}, u32[]{:S(2)}, u32[]{:S(2)}) async-start(f32[4,1,2,32,1024]{4,3,2,1,0:T(8,128)} %copy.59), calls=%async_computation | async-start | bytes 2097152 | tf_op jit(solution)/shard_map/all_to_all | solution.py:34
  119.7 1.3 copy-start
  122.2 43.1 %collective-permute-start.4 = (f32[4,2,32,1024]{3,2,0,1:T(8,128)}, f32[4,2,32,1024]{3,2,0,1:T(8,128)}, u32[]{:S(2)}, u32[]{:S(2)}) collective-permute-start(f32[4,2,32,1024]{3,2,0,1:T(8,128)} %select_bitcast_fusion.1), channel_id=1, source_target_pairs={{0,4},{4,0},{1,5},{5,1},{2,6},{6,2},{3,7},{7,3},{8,12},{12,8},{9,1... | collective-permute-start | bytes 3145736 | tf_op jit(solution)/shard_map/ppermute | solution.py:28
  159.3 16.2 %all-to-all-start.1 = ((f32[4,1,2,32,1024]{4,3,2,1,0:T(8,128)}), f32[4,1,2,32,1024]{4,3,2,1,0:T(8,128)}, u32[]{:S(2)}, u32[]{:S(2)}) async-start(f32[4,1,2,32,1024]{4,3,2,1,0:T(8,128)} %copy.62), calls=%async_computation.1 | async-start | bytes 2097152 | tf_op jit(solution)/shard_map/all_to_all | solution.py:34
  164.2 2.0 copy-start.1
  165.3 15.9 %collective-permute-start.6 = (f32[4,2,32,1024]{3,2,0,1:T(8,128)}, f32[4,2,32,1024]{3,2,0,1:T(8,128)}, u32[]{:S(2)}, u32[]{:S(2)}) collective-permute-start(f32[4,2,32,1024]{3,2,0,1:T(8,128)} %select_bitcast_fusion), channel_id=1, source_target_pairs={{0,4},{4,0},{1,5},{5,1},{2,6},{6,2},{3,7},{7,3},{8,12},{12,8},{9,1... | collective-permute-start | bytes 3145736 | tf_op jit(solution)/shard_map/ppermute | solution.py:28
  175.5 15.8 %all-to-all-start.2 = ((f32[4,1,2,32,1024]{4,3,2,1,0:T(8,128)}), f32[4,1,2,32,1024]{4,3,2,1,0:T(8,128)}, u32[]{:S(2)}, u32[]{:S(2)}) async-start(f32[4,1,2,32,1024]{4,3,2,1,0:T(8,128)} %copy.65), calls=%async_computation.2 | async-start | bytes 2097152 | tf_op jit(solution)/shard_map/all_to_all | solution.py:34
  191.3 14.4 %all-to-all-start.3 = ((f32[4,1,2,32,1024]{4,3,2,1,0:T(8,128)}), f32[4,1,2,32,1024]{4,3,2,1,0:T(8,128)S(1)}, u32[]{:S(2)}, u32[]{:S(2)}) async-start(f32[4,1,2,32,1024]{4,3,2,1,0:T(8,128)} %copy.68), calls=%async_computation.3 | async-start | bytes 2097152 | tf_op jit(solution)/shard_map/all_to_all | solution.py:34
  206.9 15.8 %all-to-all-start.4 = ((f32[4,1,2,32,1024]{4,3,2,1,0:T(8,128)}), f32[4,1,2,32,1024]{4,3,2,1,0:T(8,128)S(1)}, u32[]{:S(2)}, u32[]{:S(2)}) async-start(f32[4,1,2,32,1024]{4,3,2,1,0:T(8,128)} %copy.69), calls=%async_computation.4 | async-start | bytes 2097152 | tf_op jit(solution)/shard_map/all_to_all | solution.py:34
  222.8 10.1 %collective-permute-start.7 = (f32[1,32,1024]{2,1,0:T(8,128)S(1)}, f32[1,32,1024]{2,1,0:T(8,128)S(1)}, u32[]{:S(2)}, u32[]{:S(2)}) collective-permute-start(f32[1,32,1024]{2,1,0:T(8,128)S(1)} %select_bitcast_fusion.4), channel_id=1, source_target_pairs={{0,32},{32,0},{1,33},{33,1},{2,34},{34,2},{3,35},{35,3},{4,36},{36... | collective-permute-start | bytes 393224 | tf_op jit(solution)/shard_map/ppermute | solution.py:28

commit v3 on v2

--- a/solution.py
+++ b/solution.py
@@ -22,9 +22,9 @@
 
 def halve_over(x, axis):
     half = x.shape[0] // 2
-    first = lax.axis_index(axis) == 0
-    keep = jnp.where(first, x[:half], x[half:])
-    send = jnp.where(first, x[half:], x[:half])
+    index = lax.axis_index(axis)
+    keep = lax.dynamic_slice_in_dim(x, index * half, half, 0)
+    send = lax.dynamic_slice_in_dim(x, (1 - index) * half, half, 0)
     return keep + lax.ppermute(send, axis, [(0, 1), (1, 0)])
 
 
@@ -43,17 +43,19 @@
     zhi, ys, cores, layers = (lax.axis_size(a) for a in COL_PARTS + ("layer",))
     halves = ys // 2
     block = right.shape[1] // (halves * cores * layers)
+    right = right.reshape(-1, halves, cores, layers, block).transpose(0, 2, 3, 1, 4).reshape(right.shape)
     gathered = jnp.zeros((cycle_size, halves, block, left_rows), jnp.float32)
     current = right
+    reduced = None
     for step in range(cycle_size):
         if step > 0:
             current = from_behind(current, "row", 1)
-        owner = (position - step) % cycle_size
+            current, reduced = lax.optimization_barrier((current, reduced))
+            gathered = lax.dynamic_update_slice_in_dim(gathered, reduced, (position - step + 1) % cycle_size, 0)
         piece = lax.dot_general(current, left, (((0,), (1,)), ((), ())), preferred_element_type=jnp.float32)
-        piece = piece.reshape(halves, cores, layers, block, left_rows).transpose(1, 2, 0, 3, 4)
         piece = halve_over(piece.reshape(cores * layers, halves, block, left_rows), "core")
-        piece = spread_over(piece, "layer")
-        gathered = lax.dynamic_update_slice_in_dim(gathered, piece, owner, 0)
+        reduced = spread_over(piece, "layer")
+    gathered = lax.dynamic_update_slice_in_dim(gathered, reduced, (position + 1) % cycle_size, 0)
     ordered = gathered.reshape(zhi, ys, block, left_rows).transpose(1, 0, 2, 3)
     ordered = spread_over(ordered, "y")[0]
     ordered = halve_over(ordered, "zhi")

time: 235 us -> 248 us (1.055)
  blocking collectives: 0 us -> 56 us
  waiting for transfers between devices: 142 us -> 126 us
  starting transfers between devices: 32.7 us -> 17.9 us
  other arithmetic: 18.2 us -> 9.52 us
  local copies, waits for them, and re-layouts: 23.1 us -> 17 us
  matrix products: 17.3 us -> 21 us
    all_to_all x0 -> x3, blocking collectives: none -> 56 us  [spread_over(): return lax.all_to_all(x, axis, 0, 0, tiled=False).sum(0)]
    ppermute x3, waiting for transfers between devices: 105 us -> 85.5 us  [from_behind(): return lax.ppermute(x, axis, [(i, (i + by) % size) for i in range(size)])]
    all_to_all x5 -> x2, starting transfers between devices: 25.2 us -> 9.14 us  [spread_over(): return lax.all_to_all(x, axis, 0, 0, tiled=False).sum(0)]
    dot_general x4 -> x0, local copies, waits for them, and re-layouts: 13.4 us -> none  [local(): lax.dot_general(current, left, (((0,), (1,)), ((), ())), preferred_elemen...]
    mul x2 -> x3, local copies, waits for them, and re-layouts: 0.29 us -> 9.8 us  [apply_pattern(): masked = values.reshape(pattern.shape[0], block, cols) * widened[:, None, :]]
    ppermute x5, waiting for transfers between devices: 5.16 us -> 12.3 us  [halve_over(): return keep + lax.ppermute(send, axis, [(0, 1), (1, 0)])]
    reshape x5 -> x1, local copies, waits for them, and re-layouts: 5.34 us -> 1.06 us  [spread_over(): x = x.reshape(n, x.shape[0] // n, *x.shape[1:])]
    dot_general x4, matrix products: 17.3 us -> 21 us  [local(): lax.dot_general(current, left, (((0,), (1,)), ((), ())), preferred_elemen...]
  transfers between devices with their start and end apart: 13 -> 10, of which waited for: 8 -> 10; matrix products, arithmetic and copies ran while one was open for 22% -> 1% of each run, Pallas kernels for 0% -> 0%
where the time goes in v3:
time: 248 us
  waiting for transfers between devices  126 us (51%)
  blocking collectives  56 us (23%)
  matrix products  21 us (8%)
  starting transfers between devices  17.9 us (7%)
  local copies, waits for them, and re-layouts  17 us (7%)
  other arithmetic  9.52 us (4%)
    ppermute x3, waiting for transfers between devices, from_behind(): return lax.ppermute(x, axis, [(i, (i + by) % size) for i in range(size)])  85.5 us
    all_to_all x3, blocking collectives, spread_over(): return lax.all_to_all(x, axis, 0, 0, tiled=False).sum(0)  56 us
    all_to_all x2, waiting for transfers between devices, spread_over(): return lax.all_to_all(x, axis, 0, 0, tiled=False).sum(0)  28.1 us
    dot_general x4, matrix products, local(): lax.dot_general(current, left, (((0,), (1,)), ((), ())), preferred_elemen...  21 us
    ppermute x5, waiting for transfers between devices, halve_over(): return keep + lax.ppermute(send, axis, [(0, 1), (1, 0)])  12.3 us
    mul x3, local copies, waits for them, and re-layouts, apply_pattern(): masked = values.reshape(pattern.shape[0], block, cols) * widened[:, None, :]  9.8 us
    all_to_all x2, starting transfers between devices, spread_over(): return lax.all_to_all(x, axis, 0, 0, tiled=False).sum(0)  9.14 us
    ppermute x5, starting transfers between devices, halve_over(): return keep + lax.ppermute(send, axis, [(0, 1), (1, 0)])  6.58 us
  transfers between devices with their start and end apart: 10, of which 10 were waited for; matrix products, arithmetic and copies ran while one was open for 1% of the time, Pallas kernels for 0%

profile of v3, /device:TPU:2, one launch (start us, length us, event | category | flops | bytes accessed | tf_op | source)
XLA Modules:
  0.0 247.6 jit_solution(7705561368386548844)
XLA Ops:
  0.0 0.7 convert_element_type.16
  1.0 0.7 convert_element_type.15
  1.7 3.9 %mul.39 = bf16[32,64,512]{1,0,2:T(8,128)(2,1)} broadcast(bf16[32,512]{0,1:T(8,128)(2,1)S(1)} %bitcast.72), dimensions={0,2} | broadcast | bytes 2129920 | tf_op jit(solution)/shard_map/mul | solution.py:19
  5.6 5.8 %mul.40 = bf16[2048,2,2,4,32]{0,4,3,2,1:T(8,128)(2,1)S(1)} reshape(bf16[32,64,512]{1,0,2:T(8,128)(2,1)} %mul.39) | data formatting | bytes 4194304 | tf_op jit(solution)/shard_map/mul | solution.py:19
  11.4 4.0 %copy.14 = bf16[2048,512]{0,1:T(8,128)(2,1)} copy(bf16[2048,512]{1,0:T(8,128)(2,1)} %param.6) | data formatting | bytes 4194304 | tf_op args[2]
  15.4 1.8 multiply_bitcast_fusion
  17.2 1.5 copy.15
  18.6 2.5 %bitcast_multiply_fusion = bf16[1024,2048]{1,0:T(8,128)(2,1)S(1)} fusion(bf16[1024,2048]{1,0:T(8,128)(2,1)} %param.4, bf16[16,2048]{1,0:T(8,128)(2,1)S(1)} %mul.42), kind=kLoop, calls=%fused_computation.8 | loop fusion | flops 2097152 | bytes 8454144 | tf_op jit(solution)/shard_map/mul | solution.py:19
  21.1 5.5 %fusion.6 = f32[8,2,32,1024]{3,2,1,0:T(8,128)S(1)} fusion(bf16[8,2,32,2048]{3,2,1,0:T(8,128)(2,1)} %bitcast.5, bf16[1024,2048]{1,0:T(8,128)(2,1)S(1)} %bitcast_multiply_fusion), kind=kOutput, calls=%fused_computation.6 | convolution fusion | flops 2147483648 | bytes 8388608 | tf_op jit(solution)/shard_map/dot_general | solution.py:55
  26.8 2.0 collective-permute-start
  28.8 0.8 collective-permute-done.1
  29.6 1.4 add_bitcast_fusion.3
  31.0 18.9 %all_to_all.25 = f32[4,1,2,32,1024]{4,3,2,1,0:T(8,128)S(1)} all-to-all(f32[4,1,2,32,1024]{4,3,2,1,0:T(8,128)S(1)} %add_bitcast_fusion.3), channel_id=1, replica_groups=mesh['row'=4,'zhi'=2,'y'=4,'core'=2,'layer'=4] {'layer'}, dimensions={0} | all-to-all | bytes 2097152 | tf_op jit(solution)/shard_map/all_to_all | solution.py:34
  50.0 28.1 %collective-permute-done = bf16[2048,512]{0,1:T(8,128)(2,1)} collective-permute-done((bf16[2048,512]{0,1:T(8,128)(2,1)}, bf16[2048,512]{0,1:T(8,128)(2,1)}, u32[]{:S(2)}, u32[]{:S(2)}) %collective-permute-start) | collective-permute-done | bytes 2097184 | tf_op jit(solution)/shard_map/ppermute | solution.py:12
  78.1 5.2 %fusion.4 = f32[8,2,32,1024]{3,2,1,0:T(8,128)S(1)} fusion(bf16[8,2,32,2048]{3,2,1,0:T(8,128)(2,1)} %bitcast.13, bf16[1024,2048]{1,0:T(8,128)(2,1)} %copy-done), kind=kOutput, calls=%fused_computation.4 | convolution fusion | flops 2147483648 | bytes 8388608 | tf_op jit(solution)/shard_map/dot_general | solution.py:55
  83.5 2.6 %collective-permute-done.3 = f32[4,2,32,1024]{3,2,1,0:T(8,128)S(1)} collective-permute-done((f32[4,2,32,1024]{3,2,1,0:T(8,128)S(1)}, f32[4,2,32,1024]{3,2,1,0:T(8,128)S(1)}, u32[]{:S(2)}, u32[]{:S(2)}) %collective-permute-start.3) | collective-permute-done | bytes 1048608 | tf_op jit(solution)/shard_map/ppermute | solution.py:28
  86.3 18.6 %all_to_all.26 = f32[4,1,2,32,1024]{4,3,2,1,0:T(8,128)S(1)} all-to-all(f32[4,1,2,32,1024]{4,3,2,1,0:T(8,128)S(1)} %add_bitcast_fusion.2), channel_id=1, replica_groups=mesh['row'=4,'zhi'=2,'y'=4,'core'=2,'layer'=4] {'layer'}, dimensions={0} | all-to-all | bytes 2097152 | tf_op jit(solution)/shard_map/all_to_all | solution.py:34
  104.9 28.7 %collective-permute-done.2 = bf16[2048,512]{0,1:T(8,128)(2,1)} collective-permute-done((bf16[2048,512]{0,1:T(8,128)(2,1)}, bf16[2048,512]{0,1:T(8,128)(2,1)}, u32[]{:S(2)}, u32[]{:S(2)}) %collective-permute-start.2) | collective-permute-done | bytes 2097184 | tf_op jit(solution)/shard_map/ppermute | solution.py:12
  133.6 5.2 %fusion.2 = f32[8,2,32,1024]{3,2,1,0:T(8,128)S(1)} fusion(bf16[8,2,32,2048]{3,2,1,0:T(8,128)(2,1)} %bitcast.19, bf16[1024,2048]{1,0:T(8,128)(2,1)} %copy-done), kind=kOutput, calls=%fused_computation.2 | convolution fusion | flops 2147483648 | bytes 8388608 | tf_op jit(solution)/shard_map/dot_general | solution.py:55
  139.1 2.6 %collective-permute-done.5 = f32[4,2,32,1024]{3,2,1,0:T(8,128)S(1)} collective-permute-done((f32[4,2,32,1024]{3,2,1,0:T(8,128)S(1)}, f32[4,2,32,1024]{3,2,1,0:T(8,128)S(1)}, u32[]{:S(2)}, u32[]{:S(2)}) %collective-permute-start.5) | collective-permute-done | bytes 1048608 | tf_op jit(solution)/shard_map/ppermute | solution.py:28
  141.8 18.6 %all_to_all.27 = f32[4,1,2,32,1024]{4,3,2,1,0:T(8,128)S(1)} all-to-all(f32[4,1,2,32,1024]{4,3,2,1,0:T(8,128)S(1)} %add_bitcast_fusion.1), channel_id=1, replica_groups=mesh['row'=4,'zhi'=2,'y'=4,'core'=2,'layer'=4] {'layer'}, dimensions={0} | all-to-all | bytes 2097152 | tf_op jit(solution)/shard_map/all_to_all | solution.py:34
  160.5 28.7 %collective-permute-done.4 = bf16[2048,512]{0,1:T(8,128)(2,1)} collective-permute-done((bf16[2048,512]{0,1:T(8,128)(2,1)}, bf16[2048,512]{0,1:T(8,128)(2,1)}, u32[]{:S(2)}, u32[]{:S(2)}) %collective-permute-start.4) | collective-permute-done | bytes 2097184 | tf_op jit(solution)/shard_map/ppermute | solution.py:12
  189.1 5.2 %fusion = f32[8,2,32,1024]{3,2,1,0:T(8,128)S(1)} fusion(bf16[8,2,32,2048]{3,2,1,0:T(8,128)(2,1)} %bitcast.24, bf16[1024,2048]{1,0:T(8,128)(2,1)} %copy-done), kind=kOutput, calls=%fused_computation | convolution fusion | flops 2147483648 | bytes 8388608 | tf_op jit(solution)/shard_map/dot_general | solution.py:55
  194.5 2.6 %collective-permute-done.6 = f32[4,2,32,1024]{3,2,1,0:T(8,128)S(1)} collective-permute-done((f32[4,2,32,1024]{3,2,1,0:T(8,128)S(1)}, f32[4,2,32,1024]{3,2,1,0:T(8,128)S(1)}, u32[]{:S(2)}, u32[]{:S(2)}) %collective-permute-start.6) | collective-permute-done | bytes 1048608 | tf_op jit(solution)/shard_map/ppermute | solution.py:28
  197.2 1.1 add_bitcast_fusion
  198.3 4.8 %all-to-all-start.3 = ((f32[4,1,2,32,1024]{4,3,2,1,0:T(8,128)}), f32[4,1,2,32,1024]{4,3,2,1,0:T(8,128)S(1)}, u32[]{:S(2)}, u32[]{:S(2)}) async-start(f32[4,1,2,32,1024]{4,3,2,1,0:T(8,128)} %add_bitcast_fusion), calls=%async_computation.3 | async-start | bytes 2097152 | tf_op jit(solution)/shard_map/all_to_all | solution.py:34
  203.3 13.9 %all-to-all-done.3 = f32[4,1,2,32,1024]{4,3,2,1,0:T(8,128)S(1)} async-done(((f32[4,1,2,32,1024]{4,3,2,1,0:T(8,128)}), f32[4,1,2,32,1024]{4,3,2,1,0:T(8,128)S(1)}, u32[]{:S(2)}, u32[]{:S(2)}) %all-to-all-start.3) | async-done | bytes 1048608 | tf_op jit(solution)/shard_map/all_to_all | solution.py:34
  217.3 1.1 copy.20
  218.4 4.3 %all-to-all-start.4 = ((f32[4,1,2,32,1024]{4,3,2,1,0:T(8,128)}), f32[4,1,2,32,1024]{4,3,2,1,0:T(8,128)S(1)}, u32[]{:S(2)}, u32[]{:S(2)}) async-start(f32[4,1,2,32,1024]{4,3,2,1,0:T(8,128)} %copy.20), calls=%async_computation.4 | async-start | bytes 2097152 | tf_op jit(solution)/shard_map/all_to_all | solution.py:34
  222.7 14.2 %all-to-all-done.4 = f32[4,1,2,32,1024]{4,3,2,1,0:T(8,128)S(1)} async-done(((f32[4,1,2,32,1024]{4,3,2,1,0:T(8,128)}), f32[4,1,2,32,1024]{4,3,2,1,0:T(8,128)S(1)}, u32[]{:S(2)}, u32[]{:S(2)}) %all-to-all-start.4) | async-done | bytes 1048608 | tf_op jit(solution)/shard_map/all_to_all | solution.py:34
  237.0 6.2 %collective-permute-start.7 = (f32[1,32,1024]{2,1,0:T(8,128)S(1)}, f32[1,32,1024]{2,1,0:T(8,128)S(1)}, u32[]{:S(2)}, u32[]{:S(2)}) collective-permute-start(f32[1,32,1024]{2,1,0:T(8,128)S(1)} %constant_dynamic-slice_fusion), channel_id=1, source_target_pairs={{0,32},{32,0},{1,33},{33,1},{2,34},{34,2},{3,35},{35,3},{4,36},{36... | collective-permute-start | bytes 393224 | tf_op jit(solution)/shard_map/ppermute | solution.py:28
  243.2 3.7 %collective-permute-done.7 = f32[1,32,1024]{2,1,0:T(8,128)S(1)} collective-permute-done((f32[1,32,1024]{2,1,0:T(8,128)S(1)}, f32[1,32,1024]{2,1,0:T(8,128)S(1)}, u32[]{:S(2)}, u32[]{:S(2)}) %collective-permute-start.7) | collective-permute-done | bytes 131104 | tf_op jit(solution)/shard_map/ppermute | solution.py:28
  (29 shorter events, 2.8 us)
Async XLA Ops:
  21.1 5.5 %copy-start = (bf16[1024,2048]{1,0:T(8,128)(2,1)}, bf16[1024,2048]{1,0:T(8,128)(2,1)S(1)}, u32[]{:S(2)}) copy-start(bf16[1024,2048]{1,0:T(8,128)(2,1)S(1)} %bitcast_multiply_fusion) | copy-start | bytes 12582916
  26.7 2.9 %collective-permute-start.1 = (f32[4,2,32,1024]{3,2,1,0:T(8,128)S(1)}, f32[4,2,32,1024]{3,2,1,0:T(8,128)}, u32[]{:S(2)}, u32[]{:S(2)}) collective-permute-start(f32[4,2,32,1024]{3,2,1,0:T(8,128)S(1)} %constant_dynamic-slice_fusion.4), channel_id=1, source_target_pairs={{0,4},{4,0},{1,5},{5,1},{2,6},{6,2},{3,7},{7,3},{8,12},{12,8},{9,1... | collective-permute-start | bytes 3145736 | tf_op jit(solution)/shard_map/ppermute | solution.py:28
  26.8 51.2 %collective-permute-start = (bf16[2048,512]{0,1:T(8,128)(2,1)}, bf16[2048,512]{0,1:T(8,128)(2,1)}, u32[]{:S(2)}, u32[]{:S(2)}) collective-permute-start(bf16[2048,512]{0,1:T(8,128)(2,1)} %bitcast.3), channel_id=1, source_target_pairs={{0,64},{64,128},{128,192},{192,0},{1,65},{65,129},{129,193},{193,1... | collective-permute-start | bytes 6291464 | tf_op jit(solution)/shard_map/ppermute | solution.py:12
  83.3 2.7 %collective-permute-start.3 = (f32[4,2,32,1024]{3,2,1,0:T(8,128)S(1)}, f32[4,2,32,1024]{3,2,1,0:T(8,128)S(1)}, u32[]{:S(2)}, u32[]{:S(2)}) collective-permute-start(f32[4,2,32,1024]{3,2,1,0:T(8,128)S(1)} %constant_dynamic-slice_fusion.3), channel_id=1, source_target_pairs={{0,4},{4,0},{1,5},{5,1},{2,6},{6,2},{3,7},{7,3},{8,12},{12,8},{9,1... | collective-permute-start | bytes 3145736 | tf_op jit(solution)/shard_map/ppermute | solution.py:28
  83.4 50.2 %collective-permute-start.2 = (bf16[2048,512]{0,1:T(8,128)(2,1)}, bf16[2048,512]{0,1:T(8,128)(2,1)}, u32[]{:S(2)}, u32[]{:S(2)}) collective-permute-start(bf16[2048,512]{0,1:T(8,128)(2,1)} %collective-permute-done), channel_id=1, source_target_pairs={{0,64},{64,128},{128,192},{192,0},{1,65},{65,129},{129,193},{193,1... | collective-permute-start | bytes 6291464 | tf_op jit(solution)/shard_map/ppermute | solution.py:12
  138.9 2.7 %collective-permute-start.5 = (f32[4,2,32,1024]{3,2,1,0:T(8,128)S(1)}, f32[4,2,32,1024]{3,2,1,0:T(8,128)S(1)}, u32[]{:S(2)}, u32[]{:S(2)}) collective-permute-start(f32[4,2,32,1024]{3,2,1,0:T(8,128)S(1)} %constant_dynamic-slice_fusion.2), channel_id=1, source_target_pairs={{0,4},{4,0},{1,5},{5,1},{2,6},{6,2},{3,7},{7,3},{8,12},{12,8},{9,1... | collective-permute-start | bytes 3145736 | tf_op jit(solution)/shard_map/ppermute | solution.py:28
  139.0 50.2 %collective-permute-start.4 = (bf16[2048,512]{0,1:T(8,128)(2,1)}, bf16[2048,512]{0,1:T(8,128)(2,1)}, u32[]{:S(2)}, u32[]{:S(2)}) collective-permute-start(bf16[2048,512]{0,1:T(8,128)(2,1)} %collective-permute-done.2), channel_id=1, source_target_pairs={{0,64},{64,128},{128,192},{192,0},{1,65},{65,129},{129,193},{193,1... | collective-permute-start | bytes 6291464 | tf_op jit(solution)/shard_map/ppermute | solution.py:12
  194.4 2.7 %collective-permute-start.6 = (f32[4,2,32,1024]{3,2,1,0:T(8,128)S(1)}, f32[4,2,32,1024]{3,2,1,0:T(8,128)S(1)}, u32[]{:S(2)}, u32[]{:S(2)}) collective-permute-start(f32[4,2,32,1024]{3,2,1,0:T(8,128)S(1)} %constant_dynamic-slice_fusion.1), channel_id=1, source_target_pairs={{0,4},{4,0},{1,5},{5,1},{2,6},{6,2},{3,7},{7,3},{8,12},{12,8},{9,1... | collective-permute-start | bytes 3145736 | tf_op jit(solution)/shard_map/ppermute | solution.py:28
  198.3 18.9 %all-to-all-start.3 = ((f32[4,1,2,32,1024]{4,3,2,1,0:T(8,128)}), f32[4,1,2,32,1024]{4,3,2,1,0:T(8,128)S(1)}, u32[]{:S(2)}, u32[]{:S(2)}) async-start(f32[4,1,2,32,1024]{4,3,2,1,0:T(8,128)} %add_bitcast_fusion), calls=%async_computation.3 | async-start | bytes 2097152 | tf_op jit(solution)/shard_map/all_to_all | solution.py:34
  218.4 18.6 %all-to-all-start.4 = ((f32[4,1,2,32,1024]{4,3,2,1,0:T(8,128)}), f32[4,1,2,32,1024]{4,3,2,1,0:T(8,128)S(1)}, u32[]{:S(2)}, u32[]{:S(2)}) async-start(f32[4,1,2,32,1024]{4,3,2,1,0:T(8,128)} %copy.20), calls=%async_computation.4 | async-start | bytes 2097152 | tf_op jit(solution)/shard_map/all_to_all | solution.py:34
  237.0 9.9 %collective-permute-start.7 = (f32[1,32,1024]{2,1,0:T(8,128)S(1)}, f32[1,32,1024]{2,1,0:T(8,128)S(1)}, u32[]{:S(2)}, u32[]{:S(2)}) collective-permute-start(f32[1,32,1024]{2,1,0:T(8,128)S(1)} %constant_dynamic-slice_fusion), channel_id=1, source_target_pairs={{0,32},{32,0},{1,33},{33,1},{2,34},{34,2},{3,35},{35,3},{4,36},{36... | collective-permute-start | bytes 393224 | tf_op jit(solution)/shard_map/ppermute | solution.py:28

commit v4 on v3

--- a/solution.py
+++ b/solution.py
@@ -30,8 +30,12 @@
 
 def spread_over(x, axis):
     n = lax.axis_size(axis)
-    x = x.reshape(n, x.shape[0] // n, *x.shape[1:])
-    return lax.all_to_all(x, axis, 0, 0, tiled=False).sum(0)
+    index = lax.axis_index(axis)
+    total = lax.dynamic_index_in_dim(x, index, 0, keepdims=False)
+    for shift in range(1, n):
+        send = lax.dynamic_index_in_dim(x, (index + shift) % n, 0, keepdims=False)
+        total = total + lax.ppermute(send, axis, [(i, (i + shift) % n) for i in range(n)])
+    return total
 
 
 def local(left_blocks, left_pattern, right_blocks, right_pattern):
@@ -43,21 +47,23 @@
     zhi, ys, cores, layers = (lax.axis_size(a) for a in COL_PARTS + ("layer",))
     halves = ys // 2
     block = right.shape[1] // (halves * cores * layers)
-    right = right.reshape(-1, halves, cores, layers, block).transpose(0, 2, 3, 1, 4).reshape(right.shape)
     gathered = jnp.zeros((cycle_size, halves, block, left_rows), jnp.float32)
-    current = right
+    arrived = right
     reduced = None
     for step in range(cycle_size):
+        current = arrived
         if step > 0:
-            current = from_behind(current, "row", 1)
             current, reduced = lax.optimization_barrier((current, reduced))
-            gathered = lax.dynamic_update_slice_in_dim(gathered, reduced, (position - step + 1) % cycle_size, 0)
+            gathered = lax.dynamic_update_slice_in_dim(gathered, reduced[None], (position - step + 1) % cycle_size, 0)
+        if step + 1 < cycle_size:
+            arrived = from_behind(arrived, "row", 1)
+        current = current.reshape(-1, halves, cores, layers, block).transpose(0, 2, 3, 1, 4)
         piece = lax.dot_general(current, left, (((0,), (1,)), ((), ())), preferred_element_type=jnp.float32)
         piece = halve_over(piece.reshape(cores * layers, halves, block, left_rows), "core")
         reduced = spread_over(piece, "layer")
-    gathered = lax.dynamic_update_slice_in_dim(gathered, reduced, (position + 1) % cycle_size, 0)
+    gathered = lax.dynamic_update_slice_in_dim(gathered, reduced[None], (position + 1) % cycle_size, 0)
     ordered = gathered.reshape(zhi, ys, block, left_rows).transpose(1, 0, 2, 3)
-    ordered = spread_over(ordered, "y")[0]
+    ordered = spread_over(ordered, "y")
     ordered = halve_over(ordered, "zhi")
     return ordered.reshape(block, left_rows).T.astype(jnp.bfloat16)
 

time: 248 us -> 226 us (0.911)
  blocking collectives: 56 us -> 0 us
  starting transfers between devices: 17.9 us -> 33.4 us
  waiting for transfers between devices: 126 us -> 135 us
  local copies, waits for them, and re-layouts: 17 us -> 25.2 us
  matrix products: 21 us -> 17.3 us
  other arithmetic: 9.52 us -> 12.8 us
    all_to_all x3 -> x0, blocking collectives: 56 us -> none  [spread_over(): return lax.all_to_all(x, axis, 0, 0, tiled=False).sum(0)]
    ppermute x0 -> x15, waiting for transfers between devices: none -> 54.5 us  [spread_over(): lax.ppermute(send, axis, [(i, (i + shift) % n) for i in range(n)])]
    all_to_all x2 -> x0, waiting for transfers between devices: 28.1 us -> none  [spread_over(): return lax.all_to_all(x, axis, 0, 0, tiled=False).sum(0)]
    ppermute x0 -> x15, starting transfers between devices: none -> 25.3 us  [spread_over(): lax.ppermute(send, axis, [(i, (i + shift) % n) for i in range(n)])]
    ppermute x3, waiting for transfers between devices: 85.5 us -> 65.4 us  [from_behind(): return lax.ppermute(x, axis, [(i, (i + by) % size) for i in range(size)])]
    optimization_barrier x0 -> x3, local copies, waits for them, and re-layouts: none -> 9.36 us  [local(): current, reduced = lax.optimization_barrier((current, reduced))]
    all_to_all x2 -> x0, starting transfers between devices: 9.14 us -> none  [spread_over(): return lax.all_to_all(x, axis, 0, 0, tiled=False).sum(0)]
    add x0 -> x8, other arithmetic: none -> 4.71 us  [the longest x4 3.01 us: halve_over(): return keep + lax.ppermute(send, axis, [(0, 1), (1, 0)])]
  transfers between devices with their start and end apart: 10 -> 23, of which waited for: 10 -> 22; matrix products, arithmetic and copies ran while one was open for 1% -> 10% of each run, Pallas kernels for 0% -> 0%
where the time goes in v4:
time: 226 us; the launch traced here: 224 us
  waiting for transfers between devices  135 us (60%)
  starting transfers between devices  33.4 us (15%)
  local copies, waits for them, and re-layouts  25.2 us (11%)
  matrix products  17.3 us (8%)
  other arithmetic  12.8 us (6%)
    ppermute x3, waiting for transfers between devices, from_behind(): return lax.ppermute(x, axis, [(i, (i + by) % size) for i in range(size)])  65.4 us
    ppermute x15, waiting for transfers between devices, spread_over(): lax.ppermute(send, axis, [(i, (i + shift) % n) for i in range(n)])  54.5 us
    ppermute x15, starting transfers between devices, spread_over(): lax.ppermute(send, axis, [(i, (i + shift) % n) for i in range(n)])  25.3 us
    dot_general x4, matrix products, local(): lax.dot_general(current, left, (((0,), (1,)), ((), ())), preferred_elemen...  17.3 us
    ppermute x5, waiting for transfers between devices, halve_over(): return keep + lax.ppermute(send, axis, [(0, 1), (1, 0)])  15.1 us
    mul x4, local copies, waits for them, and re-layouts, apply_pattern(): masked = values.reshape(pattern.shape[0], block, cols) * widened[:, None, :]  9.84 us
    optimization_barrier x3, local copies, waits for them, and re-layouts, local(): current, reduced = lax.optimization_barrier((current, reduced))  9.36 us
    mul x3, other arithmetic, apply_pattern(): masked = values.reshape(pattern.shape[0], block, cols) * widened[:, None, :]  6.69 us
  transfers between devices with their start and end apart: 23, of which 22 were waited for; matrix products, arithmetic and copies ran while one was open for 10% of the time, Pallas kernels for 0%

profile of v4, /device:TPU:2, one launch (start us, length us, event | category | flops | bytes accessed | tf_op | source)
XLA Modules:
  0.0 224.1 jit_solution(6731002101360962974)
XLA Ops:
  1.0 3.3 %bitcast_multiply_fusion.1 = bf16[2048,512]{1,0:T(8,128)(2,1)} fusion(bf16[2048,512]{1,0:T(8,128)(2,1)} %param.6, bf16[32,512]{1,0:T(8,128)(2,1)S(1)} %mul.43), kind=kLoop, calls=%fused_computation.9 | loop fusion | flops 1048576 | bytes 4227072 | tf_op jit(solution)/shard_map/mul | solution.py:19
  9.2 3.8 %mul.44.clone = bf16[32,64,512]{1,0,2:T(8,128)(2,1)} broadcast(bf16[32,512]{0,1:T(8,128)(2,1)S(1)} %copy.27), dimensions={0,2} | broadcast | bytes 2129920 | tf_op jit(solution)/shard_map/mul | solution.py:19
  13.0 5.8 %mul.47 = bf16[2048,2,2,4,32]{0,4,3,2,1:T(8,128)(2,1)S(1)} reshape(bf16[32,64,512]{1,0,2:T(8,128)(2,1)} %mul.44.clone) | data formatting | bytes 4194304 | tf_op jit(solution)/shard_map/mul | solution.py:19
  26.0 2.7 %collective-permute-done.1 = f32[4,2,32,1024]{3,2,1,0:T(8,128)} collective-permute-done((f32[4,2,32,1024]{3,2,1,0:T(8,128)S(1)}, f32[4,2,32,1024]{3,2,1,0:T(8,128)}, u32[]{:S(2)}, u32[]{:S(2)}) %collective-permute-start.1) | collective-permute-done | bytes 1048608 | tf_op jit(solution)/shard_map/ppermute | solution.py:28
  35.0 4.4 %collective-permute-done.2 = f32[2,32,1024]{2,1,0:T(8,128)S(1)} collective-permute-done((f32[2,32,1024]{2,1,0:T(8,128)S(1)}, f32[2,32,1024]{2,1,0:T(8,128)S(1)}, u32[]{:S(2)}, u32[]{:S(2)}) %collective-permute-start.2) | collective-permute-done | bytes 262176 | tf_op jit(solution)/shard_map/ppermute | solution.py:37
  39.4 3.0 %collective-permute-done.3 = f32[2,32,1024]{2,1,0:T(8,128)S(1)} collective-permute-done((f32[2,32,1024]{2,1,0:T(8,128)S(1)}, f32[2,32,1024]{2,1,0:T(8,128)S(1)}, u32[]{:S(2)}, u32[]{:S(2)}) %collective-permute-start.3) | collective-permute-done | bytes 262176 | tf_op jit(solution)/shard_map/ppermute | solution.py:37
  42.4 3.8 %collective-permute-done.4 = f32[2,32,1024]{2,1,0:T(8,128)S(1)} collective-permute-done((f32[2,32,1024]{2,1,0:T(8,128)S(1)}, f32[2,32,1024]{2,1,0:T(8,128)S(1)}, u32[]{:S(2)}, u32[]{:S(2)}) %collective-permute-start.4) | collective-permute-done | bytes 262176 | tf_op jit(solution)/shard_map/ppermute | solution.py:37
  46.3 8.6 %collective-permute-done = bf16[2048,512]{1,0:T(8,128)(2,1)} collective-permute-done((bf16[2048,512]{1,0:T(8,128)(2,1)}, bf16[2048,512]{1,0:T(8,128)(2,1)}, u32[]{:S(2)}, u32[]{:S(2)}) %collective-permute-start) | collective-permute-done | bytes 2097184 | tf_op jit(solution)/shard_map/ppermute | solution.py:12
  54.9 2.9 %copy.20 = bf16[2048,512]{0,1:T(8,128)(2,1)S(1)} copy(bf16[2048,512]{1,0:T(8,128)(2,1)} %collective-permute-done) | data formatting | bytes 4194304 | tf_op jit(solution)/shard_map/optimization_barrier | solution.py:56
  57.8 4.5 %fusion.4 = f32[8,2,32,1024]{3,2,1,0:T(8,128)S(1)} fusion(bf16[1024,2048]{1,0:T(8,128)(2,1)} %copy-done.2, bf16[8,2,32,2048]{3,2,0,1:T(8,128)(2,1)S(1)} %bitcast.116), kind=kOutput, calls=%fused_computation.4 | convolution fusion | flops 2147483648 | bytes 8388608 | tf_op jit(solution)/shard_map/dot_general | solution.py:61
  62.8 2.6 %collective-permute-done.6 = f32[4,2,32,1024]{3,2,1,0:T(8,128)S(1)} collective-permute-done((f32[4,2,32,1024]{3,2,1,0:T(8,128)S(1)}, f32[4,2,32,1024]{3,2,1,0:T(8,128)S(1)}, u32[]{:S(2)}, u32[]{:S(2)}) %collective-permute-start.6) | collective-permute-done | bytes 1048608 | tf_op jit(solution)/shard_map/ppermute | solution.py:28
  70.5 4.4 %collective-permute-done.7 = f32[2,32,1024]{2,1,0:T(8,128)S(1)} collective-permute-done((f32[2,32,1024]{2,1,0:T(8,128)S(1)}, f32[2,32,1024]{2,1,0:T(8,128)S(1)}, u32[]{:S(2)}, u32[]{:S(2)}) %collective-permute-start.7) | collective-permute-done | bytes 262176 | tf_op jit(solution)/shard_map/ppermute | solution.py:37
  74.9 3.0 %collective-permute-done.8 = f32[2,32,1024]{2,1,0:T(8,128)S(1)} collective-permute-done((f32[2,32,1024]{2,1,0:T(8,128)S(1)}, f32[2,32,1024]{2,1,0:T(8,128)S(1)}, u32[]{:S(2)}, u32[]{:S(2)}) %collective-permute-start.8) | collective-permute-done | bytes 262176 | tf_op jit(solution)/shard_map/ppermute | solution.py:37
  78.0 3.8 %collective-permute-done.9 = f32[2,32,1024]{2,1,0:T(8,128)S(1)} collective-permute-done((f32[2,32,1024]{2,1,0:T(8,128)S(1)}, f32[2,32,1024]{2,1,0:T(8,128)S(1)}, u32[]{:S(2)}, u32[]{:S(2)}) %collective-permute-start.9) | collective-permute-done | bytes 262176 | tf_op jit(solution)/shard_map/ppermute | solution.py:37
  82.6 28.9 %collective-permute-done.5 = bf16[2048,512]{1,0:T(8,128)(2,1)S(1)} collective-permute-done((bf16[2048,512]{1,0:T(8,128)(2,1)}, bf16[2048,512]{1,0:T(8,128)(2,1)S(1)}, u32[]{:S(2)}, u32[]{:S(2)}) %collective-permute-start.5) | collective-permute-done | bytes 2097184 | tf_op jit(solution)/shard_map/ppermute | solution.py:12
  113.9 5.2 %fusion.2 = f32[8,2,32,1024]{3,2,1,0:T(8,128)S(1)} fusion(bf16[1024,2048]{1,0:T(8,128)(2,1)} %copy-done.2, bf16[8,2,32,2048]{3,2,0,1:T(8,128)(2,1)} %bitcast.117), kind=kOutput, calls=%fused_computation.2 | convolution fusion | flops 2147483648 | bytes 8388608 | tf_op jit(solution)/shard_map/dot_general | solution.py:61
  119.4 2.6 %collective-permute-done.11 = f32[4,2,32,1024]{3,2,1,0:T(8,128)S(1)} collective-permute-done((f32[4,2,32,1024]{3,2,1,0:T(8,128)S(1)}, f32[4,2,32,1024]{3,2,1,0:T(8,128)S(1)}, u32[]{:S(2)}, u32[]{:S(2)}) %collective-permute-start.11) | collective-permute-done | bytes 1048608 | tf_op jit(solution)/shard_map/ppermute | solution.py:28
  127.1 4.4 %collective-permute-done.12 = f32[2,32,1024]{2,1,0:T(8,128)S(1)} collective-permute-done((f32[2,32,1024]{2,1,0:T(8,128)S(1)}, f32[2,32,1024]{2,1,0:T(8,128)S(1)}, u32[]{:S(2)}, u32[]{:S(2)}) %collective-permute-start.12) | collective-permute-done | bytes 262176 | tf_op jit(solution)/shard_map/ppermute | solution.py:37
  131.5 3.0 %collective-permute-done.13 = f32[2,32,1024]{2,1,0:T(8,128)S(1)} collective-permute-done((f32[2,32,1024]{2,1,0:T(8,128)S(1)}, f32[2,32,1024]{2,1,0:T(8,128)S(1)}, u32[]{:S(2)}, u32[]{:S(2)}) %collective-permute-start.13) | collective-permute-done | bytes 262176 | tf_op jit(solution)/shard_map/ppermute | solution.py:37
  134.5 3.7 %collective-permute-done.14 = f32[2,32,1024]{2,1,0:T(8,128)S(1)} collective-permute-done((f32[2,32,1024]{2,1,0:T(8,128)S(1)}, f32[2,32,1024]{2,1,0:T(8,128)S(1)}, u32[]{:S(2)}, u32[]{:S(2)}) %collective-permute-start.14) | collective-permute-done | bytes 262176 | tf_op jit(solution)/shard_map/ppermute | solution.py:37
  139.1 27.9 %collective-permute-done.10 = bf16[2048,512]{1,0:T(8,128)(2,1)} collective-permute-done((bf16[2048,512]{1,0:T(8,128)(2,1)S(1)}, bf16[2048,512]{1,0:T(8,128)(2,1)}, u32[]{:S(2)}, u32[]{:S(2)}) %collective-permute-start.10) | collective-permute-done | bytes 2097184 | tf_op jit(solution)/shard_map/ppermute | solution.py:12
  167.0 4.0 %copy.24 = bf16[2048,512]{0,1:T(8,128)(2,1)} copy(bf16[2048,512]{1,0:T(8,128)(2,1)} %collective-permute-done.10) | data formatting | bytes 4194304 | tf_op jit(solution)/shard_map/optimization_barrier | solution.py:56
  171.0 5.2 %fusion = f32[8,2,32,1024]{3,2,1,0:T(8,128)S(1)} fusion(bf16[1024,2048]{1,0:T(8,128)(2,1)} %copy-done.2, bf16[8,2,32,2048]{3,2,0,1:T(8,128)(2,1)} %bitcast.115), kind=kOutput, calls=%fused_computation | convolution fusion | flops 2147483648 | bytes 8388608 | tf_op jit(solution)/shard_map/dot_general | solution.py:61
  177.4 2.8 %collective-permute-done.15 = f32[4,2,32,1024]{3,2,1,0:T(8,128)} collective-permute-done((f32[4,2,32,1024]{3,2,1,0:T(8,128)}, f32[4,2,32,1024]{3,2,1,0:T(8,128)}, u32[]{:S(2)}, u32[]{:S(2)}) %collective-permute-start.15) | collective-permute-done | bytes 1048608 | tf_op jit(solution)/shard_map/ppermute | solution.py:28
  186.5 4.3 %collective-permute-done.16 = f32[2,32,1024]{2,1,0:T(8,128)S(1)} collective-permute-done((f32[2,32,1024]{2,1,0:T(8,128)S(1)}, f32[2,32,1024]{2,1,0:T(8,128)S(1)}, u32[]{:S(2)}, u32[]{:S(2)}) %collective-permute-start.16) | collective-permute-done | bytes 262176 | tf_op jit(solution)/shard_map/ppermute | solution.py:37
  190.9 3.0 %collective-permute-done.17 = f32[2,32,1024]{2,1,0:T(8,128)S(1)} collective-permute-done((f32[2,32,1024]{2,1,0:T(8,128)S(1)}, f32[2,32,1024]{2,1,0:T(8,128)S(1)}, u32[]{:S(2)}, u32[]{:S(2)}) %collective-permute-start.17) | collective-permute-done | bytes 262176 | tf_op jit(solution)/shard_map/ppermute | solution.py:37
  193.9 3.7 %collective-permute-done.18 = f32[2,32,1024]{2,1,0:T(8,128)S(1)} collective-permute-done((f32[2,32,1024]{2,1,0:T(8,128)S(1)}, f32[2,32,1024]{2,1,0:T(8,128)S(1)}, u32[]{:S(2)}, u32[]{:S(2)}) %collective-permute-start.18) | collective-permute-done | bytes 262176 | tf_op jit(solution)/shard_map/ppermute | solution.py:37
  199.5 2.9 %collective-permute-start.20 = (f32[2,32,1024]{2,1,0:T(8,128)S(1)}, f32[2,32,1024]{2,1,0:T(8,128)S(1)}, u32[]{:S(2)}, u32[]{:S(2)}) collective-permute-start(f32[2,32,1024]{2,1,0:T(8,128)S(1)} %get-tuple-element.19), channel_id=1, source_target_pairs={{0,16},{8,24},{16,0},{24,8},{1,17},{9,25},{17,1},{25,9},{2,18},{10... | collective-permute-start | bytes 786440 | tf_op jit(solution)/shard_map/ppermute | solution.py:37
  203.8 3.5 %collective-permute-done.19 = f32[2,32,1024]{2,1,0:T(8,128)S(1)} collective-permute-done((f32[2,32,1024]{2,1,0:T(8,128)S(1)}, f32[2,32,1024]{2,1,0:T(8,128)S(1)}, u32[]{:S(2)}, u32[]{:S(2)}) %collective-permute-start.19) | collective-permute-done | bytes 262176 | tf_op jit(solution)/shard_map/ppermute | solution.py:37
  207.3 6.2 %collective-permute-done.20 = f32[2,32,1024]{2,1,0:T(8,128)S(1)} collective-permute-done((f32[2,32,1024]{2,1,0:T(8,128)S(1)}, f32[2,32,1024]{2,1,0:T(8,128)S(1)}, u32[]{:S(2)}, u32[]{:S(2)}) %collective-permute-start.20) | collective-permute-done | bytes 262176 | tf_op jit(solution)/shard_map/ppermute | solution.py:37
  213.6 5.5 %collective-permute-start.22 = (f32[1,32,1024]{2,1,0:T(8,128)S(1)}, f32[1,32,1024]{2,1,0:T(8,128)S(1)}, u32[]{:S(2)}, u32[]{:S(2)}) collective-permute-start(f32[1,32,1024]{2,1,0:T(8,128)S(1)} %constant_dynamic-slice_fusion), channel_id=1, source_target_pairs={{0,32},{32,0},{1,33},{33,1},{2,34},{34,2},{3,35},{35,3},{4,36},{36... | collective-permute-start | bytes 393224 | tf_op jit(solution)/shard_map/ppermute | solution.py:28
  219.2 4.3 %collective-permute-done.22 = f32[1,32,1024]{2,1,0:T(8,128)S(1)} collective-permute-done((f32[1,32,1024]{2,1,0:T(8,128)S(1)}, f32[1,32,1024]{2,1,0:T(8,128)S(1)}, u32[]{:S(2)}, u32[]{:S(2)}) %collective-permute-start.22) | collective-permute-done | bytes 131104 | tf_op jit(solution)/shard_map/ppermute | solution.py:28
  (71 shorter events, 45.7 us)
Async XLA Ops:
  1.0 5.3 %copy-start.1 = (bf16[2048,512]{1,0:T(8,128)(2,1)S(1)}, bf16[2048,512]{1,0:T(8,128)(2,1)}, u32[]{:S(2)}) copy-start(bf16[2048,512]{1,0:T(8,128)(2,1)} %param.6) | copy-start | bytes 6291460
  4.3 50.6 %collective-permute-start = (bf16[2048,512]{1,0:T(8,128)(2,1)}, bf16[2048,512]{1,0:T(8,128)(2,1)}, u32[]{:S(2)}, u32[]{:S(2)}) collective-permute-start(bf16[2048,512]{1,0:T(8,128)(2,1)} %bitcast_multiply_fusion.1), channel_id=1, source_target_pairs={{0,64},{64,128},{128,192},{192,0},{1,65},{65,129},{129,193},{193,1... | collective-permute-start | bytes 6291464 | tf_op jit(solution)/shard_map/ppermute | solution.py:12
  6.4 2.5 %copy-start.5 = (s32[16,32]{1,0:T(8,128)S(1)}, s32[16,32]{1,0:T(8,128)}, u32[]{:S(2)}) copy-start(s32[16,32]{1,0:T(8,128)} %param.5) | copy-start | bytes 6148
  18.7 2.9 %copy-start = (bf16[2048,512]{0,1:T(8,128)(2,1)S(1)}, bf16[2048,512]{0,1:T(8,128)(2,1)}, u32[]{:S(2)}) copy-start(bf16[2048,512]{0,1:T(8,128)(2,1)} %copy.17) | copy-start | bytes 6291460
  21.4 2.0 copy-start.2
  25.8 2.9 %collective-permute-start.1 = (f32[4,2,32,1024]{3,2,1,0:T(8,128)S(1)}, f32[4,2,32,1024]{3,2,1,0:T(8,128)}, u32[]{:S(2)}, u32[]{:S(2)}) collective-permute-start(f32[4,2,32,1024]{3,2,1,0:T(8,128)S(1)} %constant_dynamic-slice_fusion.4), channel_id=1, source_target_pairs={{0,4},{4,0},{1,5},{5,1},{2,6},{6,2},{3,7},{7,3},{8,12},{12,8},{9,1... | collective-permute-start | bytes 3145736 | tf_op jit(solution)/shard_map/ppermute | solution.py:28
  30.2 9.2 %collective-permute-start.2 = (f32[2,32,1024]{2,1,0:T(8,128)S(1)}, f32[2,32,1024]{2,1,0:T(8,128)S(1)}, u32[]{:S(2)}, u32[]{:S(2)}) collective-permute-start(f32[2,32,1024]{2,1,0:T(8,128)S(1)} %get-tuple-element.29), channel_id=1, source_target_pairs={{0,1},{1,2},{2,3},{3,0},{4,5},{5,6},{6,7},{7,4},{8,9},{9,10},{10,1... | collective-permute-start | bytes 786440 | tf_op jit(solution)/shard_map/ppermute | solution.py:37
  31.7 10.7 %collective-permute-start.3 = (f32[2,32,1024]{2,1,0:T(8,128)S(1)}, f32[2,32,1024]{2,1,0:T(8,128)S(1)}, u32[]{:S(2)}, u32[]{:S(2)}) collective-permute-start(f32[2,32,1024]{2,1,0:T(8,128)S(1)} %get-tuple-element.31), channel_id=1, source_target_pairs={{0,2},{1,3},{2,0},{3,1},{4,6},{5,7},{6,4},{7,5},{8,10},{9,11},{10,... | collective-permute-start | bytes 786440 | tf_op jit(solution)/shard_map/ppermute | solution.py:37
  32.9 13.4 %collective-permute-start.4 = (f32[2,32,1024]{2,1,0:T(8,128)S(1)}, f32[2,32,1024]{2,1,0:T(8,128)S(1)}, u32[]{:S(2)}, u32[]{:S(2)}) collective-permute-start(f32[2,32,1024]{2,1,0:T(8,128)S(1)} %get-tuple-element.30), channel_id=1, source_target_pairs={{0,3},{1,0},{2,1},{3,2},{4,7},{5,4},{6,5},{7,6},{8,11},{9,8},{10,9... | collective-permute-start | bytes 786440 | tf_op jit(solution)/shard_map/ppermute | solution.py:37
  62.4 49.1 %collective-permute-start.5 = (bf16[2048,512]{1,0:T(8,128)(2,1)}, bf16[2048,512]{1,0:T(8,128)(2,1)S(1)}, u32[]{:S(2)}, u32[]{:S(2)}) collective-permute-start(bf16[2048,512]{1,0:T(8,128)(2,1)} %collective-permute-done), channel_id=1, source_target_pairs={{0,64},{64,128},{128,192},{192,0},{1,65},{65,129},{129,193},{193,1... | collective-permute-start | bytes 6291464 | tf_op jit(solution)/shard_map/ppermute | solution.py:12
  62.7 2.7 %collective-permute-start.6 = (f32[4,2,32,1024]{3,2,1,0:T(8,128)S(1)}, f32[4,2,32,1024]{3,2,1,0:T(8,128)S(1)}, u32[]{:S(2)}, u32[]{:S(2)}) collective-permute-start(f32[4,2,32,1024]{3,2,1,0:T(8,128)S(1)} %constant_dynamic-slice_fusion.3), channel_id=1, source_target_pairs={{0,4},{4,0},{1,5},{5,1},{2,6},{6,2},{3,7},{7,3},{8,12},{12,8},{9,1... | collective-permute-start | bytes 3145736 | tf_op jit(solution)/shard_map/ppermute | solution.py:28
  65.7 9.2 %collective-permute-start.7 = (f32[2,32,1024]{2,1,0:T(8,128)S(1)}, f32[2,32,1024]{2,1,0:T(8,128)S(1)}, u32[]{:S(2)}, u32[]{:S(2)}) collective-permute-start(f32[2,32,1024]{2,1,0:T(8,128)S(1)} %get-tuple-element.26), channel_id=1, source_target_pairs={{0,1},{1,2},{2,3},{3,0},{4,5},{5,6},{6,7},{7,4},{8,9},{9,10},{10,1... | collective-permute-start | bytes 786440 | tf_op jit(solution)/shard_map/ppermute | solution.py:37
  67.3 10.7 %collective-permute-start.8 = (f32[2,32,1024]{2,1,0:T(8,128)S(1)}, f32[2,32,1024]{2,1,0:T(8,128)S(1)}, u32[]{:S(2)}, u32[]{:S(2)}) collective-permute-start(f32[2,32,1024]{2,1,0:T(8,128)S(1)} %get-tuple-element.28), channel_id=1, source_target_pairs={{0,2},{1,3},{2,0},{3,1},{4,6},{5,7},{6,4},{7,5},{8,10},{9,11},{10,... | collective-permute-start | bytes 786440 | tf_op jit(solution)/shard_map/ppermute | solution.py:37
  68.4 13.4 %collective-permute-start.9 = (f32[2,32,1024]{2,1,0:T(8,128)S(1)}, f32[2,32,1024]{2,1,0:T(8,128)S(1)}, u32[]{:S(2)}, u32[]{:S(2)}) collective-permute-start(f32[2,32,1024]{2,1,0:T(8,128)S(1)} %get-tuple-element.27), channel_id=1, source_target_pairs={{0,3},{1,0},{2,1},{3,2},{4,7},{5,4},{6,5},{7,6},{8,11},{9,8},{10,9... | collective-permute-start | bytes 786440 | tf_op jit(solution)/shard_map/ppermute | solution.py:37
  119.1 47.9 %collective-permute-start.10 = (bf16[2048,512]{1,0:T(8,128)(2,1)S(1)}, bf16[2048,512]{1,0:T(8,128)(2,1)}, u32[]{:S(2)}, u32[]{:S(2)}) collective-permute-start(bf16[2048,512]{1,0:T(8,128)(2,1)S(1)} %collective-permute-done.5), channel_id=1, source_target_pairs={{0,64},{64,128},{128,192},{192,0},{1,65},{65,129},{129,193},{193,1... | collective-permute-start | bytes 6291464 | tf_op jit(solution)/shard_map/ppermute | solution.py:12
  119.3 2.7 %collective-permute-start.11 = (f32[4,2,32,1024]{3,2,1,0:T(8,128)S(1)}, f32[4,2,32,1024]{3,2,1,0:T(8,128)S(1)}, u32[]{:S(2)}, u32[]{:S(2)}) collective-permute-start(f32[4,2,32,1024]{3,2,1,0:T(8,128)S(1)} %constant_dynamic-slice_fusion.2), channel_id=1, source_target_pairs={{0,4},{4,0},{1,5},{5,1},{2,6},{6,2},{3,7},{7,3},{8,12},{12,8},{9,1... | collective-permute-start | bytes 3145736 | tf_op jit(solution)/shard_map/ppermute | solution.py:28
  122.3 9.2 %collective-permute-start.12 = (f32[2,32,1024]{2,1,0:T(8,128)S(1)}, f32[2,32,1024]{2,1,0:T(8,128)S(1)}, u32[]{:S(2)}, u32[]{:S(2)}) collective-permute-start(f32[2,32,1024]{2,1,0:T(8,128)S(1)} %get-tuple-element.23), channel_id=1, source_target_pairs={{0,1},{1,2},{2,3},{3,0},{4,5},{5,6},{6,7},{7,4},{8,9},{9,10},{10,1... | collective-permute-start | bytes 786440 | tf_op jit(solution)/shard_map/ppermute | solution.py:37
  123.9 10.7 %collective-permute-start.13 = (f32[2,32,1024]{2,1,0:T(8,128)S(1)}, f32[2,32,1024]{2,1,0:T(8,128)S(1)}, u32[]{:S(2)}, u32[]{:S(2)}) collective-permute-start(f32[2,32,1024]{2,1,0:T(8,128)S(1)} %get-tuple-element.25), channel_id=1, source_target_pairs={{0,2},{1,3},{2,0},{3,1},{4,6},{5,7},{6,4},{7,5},{8,10},{9,11},{10,... | collective-permute-start | bytes 786440 | tf_op jit(solution)/shard_map/ppermute | solution.py:37
  124.6 13.7 %collective-permute-start.14 = (f32[2,32,1024]{2,1,0:T(8,128)S(1)}, f32[2,32,1024]{2,1,0:T(8,128)S(1)}, u32[]{:S(2)}, u32[]{:S(2)}) collective-permute-start(f32[2,32,1024]{2,1,0:T(8,128)S(1)} %get-tuple-element.24), channel_id=1, source_target_pairs={{0,3},{1,0},{2,1},{3,2},{4,7},{5,4},{6,5},{7,6},{8,11},{9,8},{10,9... | collective-permute-start | bytes 786440 | tf_op jit(solution)/shard_map/ppermute | solution.py:37
  177.2 3.0 %collective-permute-start.15 = (f32[4,2,32,1024]{3,2,1,0:T(8,128)}, f32[4,2,32,1024]{3,2,1,0:T(8,128)}, u32[]{:S(2)}, u32[]{:S(2)}) collective-permute-start(f32[4,2,32,1024]{3,2,1,0:T(8,128)} %constant_dynamic-slice_fusion.1), channel_id=1, source_target_pairs={{0,4},{4,0},{1,5},{5,1},{2,6},{6,2},{3,7},{7,3},{8,12},{12,8},{9,1... | collective-permute-start | bytes 3145736 | tf_op jit(solution)/shard_map/ppermute | solution.py:28
  177.3 9.1 %copy-start.3 = (f32[2,32,1024]{2,1,0:T(8,128)S(1)}, f32[2,32,1024]{2,1,0:T(8,128)}, u32[]{:S(2)}) copy-start(f32[2,32,1024]{2,1,0:T(8,128)} %fusion.19) | copy-start | bytes 786436
  177.4 9.2 %copy-start.4 = (f32[2,32,1024]{2,1,0:T(8,128)S(1)}, f32[2,32,1024]{2,1,0:T(8,128)}, u32[]{:S(2)}) copy-start(f32[2,32,1024]{2,1,0:T(8,128)} %fusion.17) | copy-start | bytes 786436
  181.6 9.2 %collective-permute-start.16 = (f32[2,32,1024]{2,1,0:T(8,128)S(1)}, f32[2,32,1024]{2,1,0:T(8,128)S(1)}, u32[]{:S(2)}, u32[]{:S(2)}) collective-permute-start(f32[2,32,1024]{2,1,0:T(8,128)S(1)} %get-tuple-element.20), channel_id=1, source_target_pairs={{0,1},{1,2},{2,3},{3,0},{4,5},{5,6},{6,7},{7,4},{8,9},{9,10},{10,1... | collective-permute-start | bytes 786440 | tf_op jit(solution)/shard_map/ppermute | solution.py:37
  183.2 10.7 %collective-permute-start.17 = (f32[2,32,1024]{2,1,0:T(8,128)S(1)}, f32[2,32,1024]{2,1,0:T(8,128)S(1)}, u32[]{:S(2)}, u32[]{:S(2)}) collective-permute-start(f32[2,32,1024]{2,1,0:T(8,128)S(1)} %get-tuple-element.22), channel_id=1, source_target_pairs={{0,2},{1,3},{2,0},{3,1},{4,6},{5,7},{6,4},{7,5},{8,10},{9,11},{10,... | collective-permute-start | bytes 786440 | tf_op jit(solution)/shard_map/ppermute | solution.py:37
  183.9 13.7 %collective-permute-start.18 = (f32[2,32,1024]{2,1,0:T(8,128)S(1)}, f32[2,32,1024]{2,1,0:T(8,128)S(1)}, u32[]{:S(2)}, u32[]{:S(2)}) collective-permute-start(f32[2,32,1024]{2,1,0:T(8,128)S(1)} %get-tuple-element.21), channel_id=1, source_target_pairs={{0,3},{1,0},{2,1},{3,2},{4,7},{5,4},{6,5},{7,6},{8,11},{9,8},{10,9... | collective-permute-start | bytes 786440 | tf_op jit(solution)/shard_map/ppermute | solution.py:37
  197.8 9.5 %collective-permute-start.19 = (f32[2,32,1024]{2,1,0:T(8,128)S(1)}, f32[2,32,1024]{2,1,0:T(8,128)S(1)}, u32[]{:S(2)}, u32[]{:S(2)}) collective-permute-start(f32[2,32,1024]{2,1,0:T(8,128)S(1)} %get-tuple-element.17), channel_id=1, source_target_pairs={{0,8},{8,16},{16,24},{24,0},{1,9},{9,17},{17,25},{25,1},{2,10},{10... | collective-permute-start | bytes 786440 | tf_op jit(solution)/shard_map/ppermute | solution.py:37
  199.5 14.0 %collective-permute-start.20 = (f32[2,32,1024]{2,1,0:T(8,128)S(1)}, f32[2,32,1024]{2,1,0:T(8,128)S(1)}, u32[]{:S(2)}, u32[]{:S(2)}) collective-permute-start(f32[2,32,1024]{2,1,0:T(8,128)S(1)} %get-tuple-element.19), channel_id=1, source_target_pairs={{0,16},{8,24},{16,0},{24,8},{1,17},{9,25},{17,1},{25,9},{2,18},{10... | collective-permute-start | bytes 786440 | tf_op jit(solution)/shard_map/ppermute | solution.py:37
  202.5 11.1 %collective-permute-start.21 = (f32[2,32,1024]{2,1,0:T(8,128)S(1)}, f32[2,32,1024]{2,1,0:T(8,128)S(1)}, u32[]{:S(2)}, u32[]{:S(2)}) collective-permute-start(f32[2,32,1024]{2,1,0:T(8,128)S(1)} %get-tuple-element.18), channel_id=1, source_target_pairs={{0,24},{8,0},{16,8},{24,16},{1,25},{9,1},{17,9},{25,17},{2,26},{10... | collective-permute-start | bytes 786440 | tf_op jit(solution)/shard_map/ppermute | solution.py:37
  213.6 9.8 %collective-permute-start.22 = (f32[1,32,1024]{2,1,0:T(8,128)S(1)}, f32[1,32,1024]{2,1,0:T(8,128)S(1)}, u32[]{:S(2)}, u32[]{:S(2)}) collective-permute-start(f32[1,32,1024]{2,1,0:T(8,128)S(1)} %constant_dynamic-slice_fusion), channel_id=1, source_target_pairs={{0,32},{32,0},{1,33},{33,1},{2,34},{34,2},{3,35},{35,3},{4,36},{36... | collective-permute-start | bytes 393224 | tf_op jit(solution)/shard_map/ppermute | solution.py:28

commit v5 on v4

--- a/solution.py
+++ b/solution.py
@@ -20,20 +20,19 @@
     return masked.reshape(rows, cols)
 
 
-def halve_over(x, axis):
-    half = x.shape[0] // 2
+def pair_over(x, axis, dim):
     index = lax.axis_index(axis)
-    keep = lax.dynamic_slice_in_dim(x, index * half, half, 0)
-    send = lax.dynamic_slice_in_dim(x, (1 - index) * half, half, 0)
+    keep = lax.dynamic_index_in_dim(x, index, dim, keepdims=False)
+    send = lax.dynamic_index_in_dim(x, 1 - index, dim, keepdims=False)
     return keep + lax.ppermute(send, axis, [(0, 1), (1, 0)])
 
 
-def spread_over(x, axis):
+def spread_over(x, axis, dim):
     n = lax.axis_size(axis)
     index = lax.axis_index(axis)
-    total = lax.dynamic_index_in_dim(x, index, 0, keepdims=False)
+    total = lax.dynamic_index_in_dim(x, index, dim, keepdims=False)
     for shift in range(1, n):
-        send = lax.dynamic_index_in_dim(x, (index + shift) % n, 0, keepdims=False)
+        send = lax.dynamic_index_in_dim(x, (index + shift) % n, dim, keepdims=False)
         total = total + lax.ppermute(send, axis, [(i, (i + shift) % n) for i in range(n)])
     return total
 
@@ -47,25 +46,29 @@
     zhi, ys, cores, layers = (lax.axis_size(a) for a in COL_PARTS + ("layer",))
     halves = ys // 2
     block = right.shape[1] // (halves * cores * layers)
-    gathered = jnp.zeros((cycle_size, halves, block, left_rows), jnp.float32)
+    mine = lax.axis_index("zhi") * 2 + lax.axis_index("y") // halves
+    result = jnp.zeros((block, left_rows), jnp.float32)
     arrived = right
     reduced = None
     for step in range(cycle_size):
         current = arrived
         if step > 0:
             current, reduced = lax.optimization_barrier((current, reduced))
-            gathered = lax.dynamic_update_slice_in_dim(gathered, reduced[None], (position - step + 1) % cycle_size, 0)
+            result = jnp.where(mine == (position - step + 1) % cycle_size, reduced, result)
         if step + 1 < cycle_size:
             arrived = from_behind(arrived, "row", 1)
-        current = current.reshape(-1, halves, cores, layers, block).transpose(0, 2, 3, 1, 4)
+        owner = (position - step) % cycle_size
         piece = lax.dot_general(current, left, (((0,), (1,)), ((), ())), preferred_element_type=jnp.float32)
-        piece = halve_over(piece.reshape(cores * layers, halves, block, left_rows), "core")
-        reduced = spread_over(piece, "layer")
-    gathered = lax.dynamic_update_slice_in_dim(gathered, reduced[None], (position + 1) % cycle_size, 0)
-    ordered = gathered.reshape(zhi, ys, block, left_rows).transpose(1, 0, 2, 3)
-    ordered = spread_over(ordered, "y")
-    ordered = halve_over(ordered, "zhi")
-    return ordered.reshape(block, left_rows).T.astype(jnp.bfloat16)
+        piece = piece.reshape(halves, cores, layers, block, left_rows)
+        piece = pair_over(piece, "core", 1)
+        piece = spread_over(piece, "layer", 1)
+        spread = lax.dynamic_update_slice_in_dim(
+            jnp.zeros((ys, block, left_rows), jnp.float32), piece, (owner % 2) * halves, 0
+        )
+        piece = spread_over(spread, "y", 0)
+        reduced = piece + lax.ppermute(piece, "zhi", [(0, 1), (1, 0)])
+    result = jnp.where(mine == (position + 1) % cycle_size, reduced, result)
+    return result.T.astype(jnp.bfloat16)
 
 
 def solution(mesh):

time: 226 us -> 251 us (1.11)
  starting transfers between devices: 33.4 us -> 60.9 us
  local copies, waits for them, and re-layouts: 25.2 us -> 17.1 us
  waiting for transfers between devices: 135 us -> 140 us
    ppermute x3, waiting for transfers between devices: 65.4 us -> 0.01 us  [from_behind(): return lax.ppermute(x, axis, [(i, (i + by) % size) for i in range(size)])]
    ppermute x5 -> x8, waiting for transfers between devices: 15.1 us -> 72 us  [the longest x4 67.2 us: local(): reduced = piece + lax.ppermute(piece, 'zhi', [(0, 1), (1, 0)])]
    ppermute x15 -> x24, starting transfers between devices: 25.3 us -> 39.7 us  [spread_over(): lax.ppermute(send, axis, [(i, (i + shift) % n) for i in range(n)])]
    ppermute x15 -> x24, waiting for transfers between devices: 54.5 us -> 67.7 us  [spread_over(): lax.ppermute(send, axis, [(i, (i + shift) % n) for i in range(n)])]
    dot_general x0 -> x4, local copies, waits for them, and re-layouts: none -> 10.9 us  [local(): lax.dot_general(current, left, (((0,), (1,)), ((), ())), preferred_elemen...]
    mul x4 -> x2, local copies, waits for them, and re-layouts: 9.84 us -> 0.29 us  [apply_pattern(): masked = values.reshape(pattern.shape[0], block, cols) * widened[:, None, :]]
    optimization_barrier x3 -> x0, local copies, waits for them, and re-layouts: 9.36 us -> none  [local(): current, reduced = lax.optimization_barrier((current, reduced))]
    ppermute x5 -> x8, starting transfers between devices: 5.82 us -> 13.3 us  [the longest x4 13 us: local(): reduced = piece + lax.ppermute(piece, 'zhi', [(0, 1), (1, 0)])]
  transfers between devices with their start and end apart: 23 -> 35, of which waited for: 22 -> 28; matrix products, arithmetic and copies ran while one was open for 10% -> 4% of each run, Pallas kernels for 0% -> 0%
where the time goes in v5:
time: 251 us; the launch traced here: 248 us
  waiting for transfers between devices  140 us (56%)
  starting transfers between devices  60.9 us (24%)
  local copies, waits for them, and re-layouts  17.1 us (7%)
  matrix products  16.7 us (7%)
  other arithmetic  13.3 us (5%)
    ppermute x24, waiting for transfers between devices, spread_over(): lax.ppermute(send, axis, [(i, (i + shift) % n) for i in range(n)])  67.7 us
    ppermute x4, waiting for transfers between devices, local(): reduced = piece + lax.ppermute(piece, 'zhi', [(0, 1), (1, 0)])  67.2 us
    ppermute x24, starting transfers between devices, spread_over(): lax.ppermute(send, axis, [(i, (i + shift) % n) for i in range(n)])  39.7 us
    dot_general x4, matrix products, local(): lax.dot_general(current, left, (((0,), (1,)), ((), ())), preferred_elemen...  16.7 us
    ppermute x4, starting transfers between devices, local(): reduced = piece + lax.ppermute(piece, 'zhi', [(0, 1), (1, 0)])  13 us
    dot_general x4, local copies, waits for them, and re-layouts, local(): lax.dot_general(current, left, (((0,), (1,)), ((), ())), preferred_elemen...  10.9 us
    ppermute x3, starting transfers between devices, from_behind(): return lax.ppermute(x, axis, [(i, (i + by) % size) for i in range(size)])  7.91 us
  transfers between devices with their start and end apart: 35, of which 28 were waited for; matrix products, arithmetic and copies ran while one was open for 4% of the time, Pallas kernels for 0%

profile of v5, /device:TPU:2, one launch (start us, length us, event | category | flops | bytes accessed | tf_op | source)
XLA Modules:
  0.0 248.1 jit_solution(5196803791538643372)
XLA Ops:
  19.8 2.8 %collective-permute-start.5 = (f32[2,32,1024]{2,1,0:T(8,128)}, f32[2,32,1024]{2,1,0:T(8,128)}, u32[]{:S(2)}, u32[]{:S(2)}) collective-permute-start(f32[2,32,1024]{2,1,0:T(8,128)} %get-tuple-element.28), channel_id=1, source_target_pairs={{0,2},{1,3},{2,0},{3,1},{4,6},{5,7},{6,4},{7,5},{8,10},{9,11},{10,... | collective-permute-start | bytes 786440 | tf_op jit(solution)/shard_map/ppermute | solution.py:36
  23.0 4.9 %collective-permute-done.4 = f32[2,32,1024]{2,1,0:T(8,128)} collective-permute-done((f32[2,32,1024]{2,1,0:T(8,128)}, f32[2,32,1024]{2,1,0:T(8,128)}, u32[]{:S(2)}, u32[]{:S(2)}) %collective-permute-start.4) | collective-permute-done | bytes 262176 | tf_op jit(solution)/shard_map/ppermute | solution.py:36
  27.9 2.9 %collective-permute-done.5 = f32[2,32,1024]{2,1,0:T(8,128)} collective-permute-done((f32[2,32,1024]{2,1,0:T(8,128)}, f32[2,32,1024]{2,1,0:T(8,128)}, u32[]{:S(2)}, u32[]{:S(2)}) %collective-permute-start.5) | collective-permute-done | bytes 262176 | tf_op jit(solution)/shard_map/ppermute | solution.py:36
  30.8 4.4 %collective-permute-done.6 = f32[2,32,1024]{2,1,0:T(8,128)} collective-permute-done((f32[2,32,1024]{2,1,0:T(8,128)S(1)}, f32[2,32,1024]{2,1,0:T(8,128)}, u32[]{:S(2)}, u32[]{:S(2)}) %collective-permute-start.6) | collective-permute-done | bytes 262176 | tf_op jit(solution)/shard_map/ppermute | solution.py:36
  38.1 2.9 %collective-permute-start.8 = (f32[32,1024]{1,0:T(8,128)S(1)}, f32[32,1024]{1,0:T(8,128)S(1)}, u32[]{:S(2)}, u32[]{:S(2)}) collective-permute-start(f32[32,1024]{1,0:T(8,128)S(1)} %get-tuple-element.40), channel_id=1, source_target_pairs={{0,16},{8,24},{16,0},{24,8},{1,17},{9,25},{17,1},{25,9},{2,18},{10... | collective-permute-start | bytes 393224 | tf_op jit(solution)/shard_map/ppermute | solution.py:36
  42.3 4.5 %collective-permute-done.7 = f32[32,1024]{1,0:T(8,128)S(1)} collective-permute-done((f32[32,1024]{1,0:T(8,128)S(1)}, f32[32,1024]{1,0:T(8,128)S(1)}, u32[]{:S(2)}, u32[]{:S(2)}) %collective-permute-start.7) | collective-permute-done | bytes 131104 | tf_op jit(solution)/shard_map/ppermute | solution.py:36
  48.3 6.4 %collective-permute-start.10 = (f32[32,1024]{1,0:T(8,128)S(1)}, f32[32,1024]{1,0:T(8,128)S(1)}, u32[]{:S(2)}, u32[]{:S(2)}) collective-permute-start(f32[32,1024]{1,0:T(8,128)S(1)} %fusion.27), channel_id=1, source_target_pairs={{0,32},{32,0},{1,33},{33,1},{2,34},{34,2},{3,35},{35,3},{4,36},{36... | collective-permute-start | bytes 393224 | tf_op jit(solution)/shard_map/ppermute | solution.py:69
  54.7 15.7 %collective-permute-done.10 = f32[32,1024]{1,0:T(8,128)S(1)} collective-permute-done((f32[32,1024]{1,0:T(8,128)S(1)}, f32[32,1024]{1,0:T(8,128)S(1)}, u32[]{:S(2)}, u32[]{:S(2)}) %collective-permute-start.10) | collective-permute-done | bytes 131104 | tf_op jit(solution)/shard_map/ppermute | solution.py:69
  70.4 2.9 %copy.13 = bf16[512,2048]{1,0:T(8,128)(2,1)S(1)} copy(bf16[512,2048]{0,1:T(8,128)(2,1)} %bitcast.16) | data formatting | bytes 4194304 | tf_op jit(solution)/shard_map/dot_general | solution.py:61
  73.4 4.5 %fusion.4 = f32[2,2,4,32,1024]{4,3,2,1,0:T(8,128)S(1)} fusion(bf16[2,2,4,32,2048]{4,3,2,1,0:T(8,128)(2,1)S(1)} %bitcast.153, bf16[1024,2048]{1,0:T(8,128)(2,1)} %copy-done), kind=kOutput, calls=%fused_computation.4 | convolution fusion | flops 2147483648 | bytes 8388608 | tf_op jit(solution)/shard_map/dot_general | solution.py:61
  78.1 4.6 %collective-permute-start.1 = (bf16[2048,512]{1,0:T(8,128)(2,1)}, bf16[2048,512]{1,0:T(8,128)(2,1)S(1)}, u32[]{:S(2)}, u32[]{:S(2)}) collective-permute-start(bf16[2048,512]{1,0:T(8,128)(2,1)} %collective-permute-done), channel_id=1, source_target_pairs={{0,64},{64,128},{128,192},{192,0},{1,65},{65,129},{129,193},{193,1... | collective-permute-start | bytes 6291464 | tf_op jit(solution)/shard_map/ppermute | solution.py:12
  88.6 4.7 %collective-permute-done.12 = f32[2,32,1024]{2,1,0:T(8,128)} collective-permute-done((f32[2,32,1024]{2,1,0:T(8,128)}, f32[2,32,1024]{2,1,0:T(8,128)}, u32[]{:S(2)}, u32[]{:S(2)}) %collective-permute-start.12) | collective-permute-done | bytes 262176 | tf_op jit(solution)/shard_map/ppermute | solution.py:36
  93.3 3.0 %collective-permute-done.13 = f32[2,32,1024]{2,1,0:T(8,128)} collective-permute-done((f32[2,32,1024]{2,1,0:T(8,128)}, f32[2,32,1024]{2,1,0:T(8,128)}, u32[]{:S(2)}, u32[]{:S(2)}) %collective-permute-start.13) | collective-permute-done | bytes 262176 | tf_op jit(solution)/shard_map/ppermute | solution.py:36
  96.3 4.2 %collective-permute-done.14 = f32[2,32,1024]{2,1,0:T(8,128)} collective-permute-done((f32[2,32,1024]{2,1,0:T(8,128)S(1)}, f32[2,32,1024]{2,1,0:T(8,128)}, u32[]{:S(2)}, u32[]{:S(2)}) %collective-permute-start.14) | collective-permute-done | bytes 262176 | tf_op jit(solution)/shard_map/ppermute | solution.py:36
  102.9 2.9 %collective-permute-start.16 = (f32[32,1024]{1,0:T(8,128)S(1)}, f32[32,1024]{1,0:T(8,128)S(1)}, u32[]{:S(2)}, u32[]{:S(2)}) collective-permute-start(f32[32,1024]{1,0:T(8,128)S(1)} %get-tuple-element.37), channel_id=1, source_target_pairs={{0,16},{8,24},{16,0},{24,8},{1,17},{9,25},{17,1},{25,9},{2,18},{10... | collective-permute-start | bytes 393224 | tf_op jit(solution)/shard_map/ppermute | solution.py:36
  112.3 21.7 %collective-permute-done.18 = f32[32,1024]{1,0:T(8,128)S(1)} collective-permute-done((f32[32,1024]{1,0:T(8,128)S(1)}, f32[32,1024]{1,0:T(8,128)S(1)}, u32[]{:S(2)}, u32[]{:S(2)}) %collective-permute-start.18) | collective-permute-done | bytes 131104 | tf_op jit(solution)/shard_map/ppermute | solution.py:69
  136.6 5.2 %fusion.2 = f32[2,2,4,32,1024]{4,3,2,1,0:T(8,128)S(1)} fusion(bf16[2,2,4,32,2048]{4,3,2,1,0:T(8,128)(2,1)} %bitcast.154, bf16[1024,2048]{1,0:T(8,128)(2,1)} %copy-done), kind=kOutput, calls=%fused_computation.2 | convolution fusion | flops 2147483648 | bytes 8388608 | tf_op jit(solution)/shard_map/dot_general | solution.py:61
  150.4 4.9 %collective-permute-done.20 = f32[2,32,1024]{2,1,0:T(8,128)} collective-permute-done((f32[2,32,1024]{2,1,0:T(8,128)}, f32[2,32,1024]{2,1,0:T(8,128)}, u32[]{:S(2)}, u32[]{:S(2)}) %collective-permute-start.20) | collective-permute-done | bytes 262176 | tf_op jit(solution)/shard_map/ppermute | solution.py:36
  155.3 2.9 %collective-permute-done.21 = f32[2,32,1024]{2,1,0:T(8,128)} collective-permute-done((f32[2,32,1024]{2,1,0:T(8,128)}, f32[2,32,1024]{2,1,0:T(8,128)}, u32[]{:S(2)}, u32[]{:S(2)}) %collective-permute-start.21) | collective-permute-done | bytes 262176 | tf_op jit(solution)/shard_map/ppermute | solution.py:36
  158.2 4.4 %collective-permute-done.22 = f32[2,32,1024]{2,1,0:T(8,128)} collective-permute-done((f32[2,32,1024]{2,1,0:T(8,128)S(1)}, f32[2,32,1024]{2,1,0:T(8,128)}, u32[]{:S(2)}, u32[]{:S(2)}) %collective-permute-start.22) | collective-permute-done | bytes 262176 | tf_op jit(solution)/shard_map/ppermute | solution.py:36
  164.7 2.9 %collective-permute-start.24 = (f32[32,1024]{1,0:T(8,128)S(1)}, f32[32,1024]{1,0:T(8,128)S(1)}, u32[]{:S(2)}, u32[]{:S(2)}) collective-permute-start(f32[32,1024]{1,0:T(8,128)S(1)} %get-tuple-element.34), channel_id=1, source_target_pairs={{0,16},{8,24},{16,0},{24,8},{1,17},{9,25},{17,1},{25,9},{2,18},{10... | collective-permute-start | bytes 393224 | tf_op jit(solution)/shard_map/ppermute | solution.py:36
  169.0 4.5 %collective-permute-done.23 = f32[32,1024]{1,0:T(8,128)S(1)} collective-permute-done((f32[32,1024]{1,0:T(8,128)S(1)}, f32[32,1024]{1,0:T(8,128)S(1)}, u32[]{:S(2)}, u32[]{:S(2)}) %collective-permute-start.23) | collective-permute-done | bytes 131104 | tf_op jit(solution)/shard_map/ppermute | solution.py:36
  174.1 5.9 %collective-permute-start.26 = (f32[32,1024]{1,0:T(8,128)S(1)}, f32[32,1024]{1,0:T(8,128)S(1)}, u32[]{:S(2)}, u32[]{:S(2)}) collective-permute-start(f32[32,1024]{1,0:T(8,128)S(1)} %fusion.23), channel_id=1, source_target_pairs={{0,32},{32,0},{1,33},{33,1},{2,34},{34,2},{3,35},{35,3},{4,36},{36... | collective-permute-start | bytes 393224 | tf_op jit(solution)/shard_map/ppermute | solution.py:69
  180.0 20.3 %collective-permute-done.26 = f32[32,1024]{1,0:T(8,128)S(1)} collective-permute-done((f32[32,1024]{1,0:T(8,128)S(1)}, f32[32,1024]{1,0:T(8,128)S(1)}, u32[]{:S(2)}, u32[]{:S(2)}) %collective-permute-start.26) | collective-permute-done | bytes 131104 | tf_op jit(solution)/shard_map/ppermute | solution.py:69
  200.3 2.9 %copy.15 = bf16[512,2048]{1,0:T(8,128)(2,1)S(1)} copy(bf16[512,2048]{0,1:T(8,128)(2,1)} %bitcast.40) | data formatting | bytes 4194304 | tf_op jit(solution)/shard_map/dot_general | solution.py:61
  203.2 4.6 %fusion = f32[2,2,4,32,1024]{4,3,2,1,0:T(8,128)S(1)} fusion(bf16[2,2,4,32,2048]{4,3,2,1,0:T(8,128)(2,1)S(1)} %bitcast.152, bf16[1024,2048]{1,0:T(8,128)(2,1)} %copy-done), kind=kOutput, calls=%fused_computation | convolution fusion | flops 2147483648 | bytes 8388608 | tf_op jit(solution)/shard_map/dot_general | solution.py:61
  215.7 4.4 %collective-permute-done.28 = f32[2,32,1024]{2,1,0:T(8,128)S(1)} collective-permute-done((f32[2,32,1024]{2,1,0:T(8,128)S(1)}, f32[2,32,1024]{2,1,0:T(8,128)S(1)}, u32[]{:S(2)}, u32[]{:S(2)}) %collective-permute-start.28) | collective-permute-done | bytes 262176 | tf_op jit(solution)/shard_map/ppermute | solution.py:36
  220.1 3.0 %collective-permute-done.29 = f32[2,32,1024]{2,1,0:T(8,128)S(1)} collective-permute-done((f32[2,32,1024]{2,1,0:T(8,128)S(1)}, f32[2,32,1024]{2,1,0:T(8,128)S(1)}, u32[]{:S(2)}, u32[]{:S(2)}) %collective-permute-start.29) | collective-permute-done | bytes 262176 | tf_op jit(solution)/shard_map/ppermute | solution.py:36
  223.2 4.4 %collective-permute-done.30 = f32[2,32,1024]{2,1,0:T(8,128)S(1)} collective-permute-done((f32[2,32,1024]{2,1,0:T(8,128)S(1)}, f32[2,32,1024]{2,1,0:T(8,128)S(1)}, u32[]{:S(2)}, u32[]{:S(2)}) %collective-permute-start.30) | collective-permute-done | bytes 262176 | tf_op jit(solution)/shard_map/ppermute | solution.py:36
  228.8 2.9 %collective-permute-start.32 = (f32[32,1024]{1,0:T(8,128)S(1)}, f32[32,1024]{1,0:T(8,128)S(1)}, u32[]{:S(2)}, u32[]{:S(2)}) collective-permute-start(f32[32,1024]{1,0:T(8,128)S(1)} %get-tuple-element.31), channel_id=1, source_target_pairs={{0,16},{8,24},{16,0},{24,8},{1,17},{9,25},{17,1},{25,9},{2,18},{10... | collective-permute-start | bytes 393224 | tf_op jit(solution)/shard_map/ppermute | solution.py:36
  233.0 4.2 %collective-permute-done.31 = f32[32,1024]{1,0:T(8,128)S(1)} collective-permute-done((f32[32,1024]{1,0:T(8,128)S(1)}, f32[32,1024]{1,0:T(8,128)S(1)}, u32[]{:S(2)}, u32[]{:S(2)}) %collective-permute-start.31) | collective-permute-done | bytes 131104 | tf_op jit(solution)/shard_map/ppermute | solution.py:36
  238.0 9.4 %collective-permute-done.34 = f32[32,1024]{1,0:T(8,128)S(1)} collective-permute-done((f32[32,1024]{1,0:T(8,128)S(1)}, f32[32,1024]{1,0:T(8,128)S(1)}, u32[]{:S(2)}, u32[]{:S(2)}) %collective-permute-start.34) | collective-permute-done | bytes 131104 | tf_op jit(solution)/shard_map/ppermute | solution.py:69
  (95 shorter events, 67.5 us)
Async XLA Ops:
  12.9 57.5 %collective-permute-start = (bf16[2048,512]{1,0:T(8,128)(2,1)S(1)}, bf16[2048,512]{1,0:T(8,128)(2,1)}, u32[]{:S(2)}, u32[]{:S(2)}) collective-permute-start(bf16[2048,512]{1,0:T(8,128)(2,1)S(1)} %bitcast_multiply_fusion.1), channel_id=1, source_target_pairs={{0,64},{64,128},{128,192},{192,0},{1,65},{65,129},{129,193},{193,1... | collective-permute-start | bytes 6291464 | tf_op jit(solution)/shard_map/ppermute | solution.py:12
  18.3 9.7 %collective-permute-start.4 = (f32[2,32,1024]{2,1,0:T(8,128)}, f32[2,32,1024]{2,1,0:T(8,128)}, u32[]{:S(2)}, u32[]{:S(2)}) collective-permute-start(f32[2,32,1024]{2,1,0:T(8,128)} %get-tuple-element.26), channel_id=1, source_target_pairs={{0,1},{1,2},{2,3},{3,0},{4,5},{5,6},{6,7},{7,4},{8,9},{9,10},{10,1... | collective-permute-start | bytes 786440 | tf_op jit(solution)/shard_map/ppermute | solution.py:36
  19.8 11.1 %collective-permute-start.5 = (f32[2,32,1024]{2,1,0:T(8,128)}, f32[2,32,1024]{2,1,0:T(8,128)}, u32[]{:S(2)}, u32[]{:S(2)}) collective-permute-start(f32[2,32,1024]{2,1,0:T(8,128)} %get-tuple-element.28), channel_id=1, source_target_pairs={{0,2},{1,3},{2,0},{3,1},{4,6},{5,7},{6,4},{7,5},{8,10},{9,11},{10,... | collective-permute-start | bytes 786440 | tf_op jit(solution)/shard_map/ppermute | solution.py:36
  22.6 12.7 %collective-permute-start.6 = (f32[2,32,1024]{2,1,0:T(8,128)S(1)}, f32[2,32,1024]{2,1,0:T(8,128)}, u32[]{:S(2)}, u32[]{:S(2)}) collective-permute-start(f32[2,32,1024]{2,1,0:T(8,128)S(1)} %get-tuple-element.27), channel_id=1, source_target_pairs={{0,3},{1,0},{2,1},{3,2},{4,7},{5,4},{6,5},{7,6},{8,11},{9,8},{10,9... | collective-permute-start | bytes 786440 | tf_op jit(solution)/shard_map/ppermute | solution.py:36
  37.3 9.5 %collective-permute-start.7 = (f32[32,1024]{1,0:T(8,128)S(1)}, f32[32,1024]{1,0:T(8,128)S(1)}, u32[]{:S(2)}, u32[]{:S(2)}) collective-permute-start(f32[32,1024]{1,0:T(8,128)S(1)} %get-tuple-element.38), channel_id=1, source_target_pairs={{0,8},{8,16},{16,24},{24,0},{1,9},{9,17},{17,25},{25,1},{2,10},{10... | collective-permute-start | bytes 393224 | tf_op jit(solution)/shard_map/ppermute | solution.py:36
  38.1 8.7 %collective-permute-start.8 = (f32[32,1024]{1,0:T(8,128)S(1)}, f32[32,1024]{1,0:T(8,128)S(1)}, u32[]{:S(2)}, u32[]{:S(2)}) collective-permute-start(f32[32,1024]{1,0:T(8,128)S(1)} %get-tuple-element.40), channel_id=1, source_target_pairs={{0,16},{8,24},{16,0},{24,8},{1,17},{9,25},{17,1},{25,9},{2,18},{10... | collective-permute-start | bytes 393224 | tf_op jit(solution)/shard_map/ppermute | solution.py:36
  41.0 6.4 %collective-permute-start.9 = (f32[32,1024]{1,0:T(8,128)S(1)}, f32[32,1024]{1,0:T(8,128)S(1)}, u32[]{:S(2)}, u32[]{:S(2)}) collective-permute-start(f32[32,1024]{1,0:T(8,128)S(1)} %get-tuple-element.39), channel_id=1, source_target_pairs={{0,24},{8,0},{16,8},{24,16},{1,25},{9,1},{17,9},{25,17},{2,26},{10... | collective-permute-start | bytes 393224 | tf_op jit(solution)/shard_map/ppermute | solution.py:36
  48.3 22.1 %collective-permute-start.10 = (f32[32,1024]{1,0:T(8,128)S(1)}, f32[32,1024]{1,0:T(8,128)S(1)}, u32[]{:S(2)}, u32[]{:S(2)}) collective-permute-start(f32[32,1024]{1,0:T(8,128)S(1)} %fusion.27), channel_id=1, source_target_pairs={{0,32},{32,0},{1,33},{33,1},{2,34},{34,2},{3,35},{35,3},{4,36},{36... | collective-permute-start | bytes 393224 | tf_op jit(solution)/shard_map/ppermute | solution.py:69
  78.0 4.7 %collective-permute-start.11 = (f32[2,4,32,1024]{3,2,1,0:T(8,128)S(1)}, f32[2,4,32,1024]{3,2,1,0:T(8,128)S(1)}, u32[]{:S(2)}, u32[]{:S(2)}) collective-permute-start(f32[2,4,32,1024]{3,2,1,0:T(8,128)S(1)} %dynamic-slice_bitcast_fusion.2), channel_id=1, source_target_pairs={{0,4},{4,0},{1,5},{5,1},{2,6},{6,2},{3,7},{7,3},{8,12},{12,8},{9,1... | collective-permute-start | bytes 3145736 | tf_op jit(solution)/shard_map/ppermute | solution.py:27
  78.1 56.0 %collective-permute-start.1 = (bf16[2048,512]{1,0:T(8,128)(2,1)}, bf16[2048,512]{1,0:T(8,128)(2,1)S(1)}, u32[]{:S(2)}, u32[]{:S(2)}) collective-permute-start(bf16[2048,512]{1,0:T(8,128)(2,1)} %collective-permute-done), channel_id=1, source_target_pairs={{0,64},{64,128},{128,192},{192,0},{1,65},{65,129},{129,193},{193,1... | collective-permute-start | bytes 6291464 | tf_op jit(solution)/shard_map/ppermute | solution.py:12
  83.8 9.5 %collective-permute-start.12 = (f32[2,32,1024]{2,1,0:T(8,128)}, f32[2,32,1024]{2,1,0:T(8,128)}, u32[]{:S(2)}, u32[]{:S(2)}) collective-permute-start(f32[2,32,1024]{2,1,0:T(8,128)} %get-tuple-element.23), channel_id=1, source_target_pairs={{0,1},{1,2},{2,3},{3,0},{4,5},{5,6},{6,7},{7,4},{8,9},{9,10},{10,1... | collective-permute-start | bytes 786440 | tf_op jit(solution)/shard_map/ppermute | solution.py:36
  85.3 11.0 %collective-permute-start.13 = (f32[2,32,1024]{2,1,0:T(8,128)}, f32[2,32,1024]{2,1,0:T(8,128)}, u32[]{:S(2)}, u32[]{:S(2)}) collective-permute-start(f32[2,32,1024]{2,1,0:T(8,128)} %get-tuple-element.25), channel_id=1, source_target_pairs={{0,2},{1,3},{2,0},{3,1},{4,6},{5,7},{6,4},{7,5},{8,10},{9,11},{10,... | collective-permute-start | bytes 786440 | tf_op jit(solution)/shard_map/ppermute | solution.py:36
  87.0 13.5 %collective-permute-start.14 = (f32[2,32,1024]{2,1,0:T(8,128)S(1)}, f32[2,32,1024]{2,1,0:T(8,128)}, u32[]{:S(2)}, u32[]{:S(2)}) collective-permute-start(f32[2,32,1024]{2,1,0:T(8,128)S(1)} %get-tuple-element.24), channel_id=1, source_target_pairs={{0,3},{1,0},{2,1},{3,2},{4,7},{5,4},{6,5},{7,6},{8,11},{9,8},{10,9... | collective-permute-start | bytes 786440 | tf_op jit(solution)/shard_map/ppermute | solution.py:36
  101.8 7.8 %collective-permute-start.15 = (f32[32,1024]{1,0:T(8,128)S(1)}, f32[32,1024]{1,0:T(8,128)S(1)}, u32[]{:S(2)}, u32[]{:S(2)}) collective-permute-start(f32[32,1024]{1,0:T(8,128)S(1)} %get-tuple-element.35), channel_id=1, source_target_pairs={{0,8},{8,16},{16,24},{24,0},{1,9},{9,17},{17,25},{25,1},{2,10},{10... | collective-permute-start | bytes 393224 | tf_op jit(solution)/shard_map/ppermute | solution.py:36
  102.9 8.2 %collective-permute-start.16 = (f32[32,1024]{1,0:T(8,128)S(1)}, f32[32,1024]{1,0:T(8,128)S(1)}, u32[]{:S(2)}, u32[]{:S(2)}) collective-permute-start(f32[32,1024]{1,0:T(8,128)S(1)} %get-tuple-element.37), channel_id=1, source_target_pairs={{0,16},{8,24},{16,0},{24,8},{1,17},{9,25},{17,1},{25,9},{2,18},{10... | collective-permute-start | bytes 393224 | tf_op jit(solution)/shard_map/ppermute | solution.py:36
  105.8 5.8 %collective-permute-start.17 = (f32[32,1024]{1,0:T(8,128)S(1)}, f32[32,1024]{1,0:T(8,128)S(1)}, u32[]{:S(2)}, u32[]{:S(2)}) collective-permute-start(f32[32,1024]{1,0:T(8,128)S(1)} %get-tuple-element.36), channel_id=1, source_target_pairs={{0,24},{8,0},{16,8},{24,16},{1,25},{9,1},{17,9},{25,17},{2,26},{10... | collective-permute-start | bytes 393224 | tf_op jit(solution)/shard_map/ppermute | solution.py:36
  111.6 22.4 %collective-permute-start.18 = (f32[32,1024]{1,0:T(8,128)S(1)}, f32[32,1024]{1,0:T(8,128)S(1)}, u32[]{:S(2)}, u32[]{:S(2)}) collective-permute-start(f32[32,1024]{1,0:T(8,128)S(1)} %fusion.25), channel_id=1, source_target_pairs={{0,32},{32,0},{1,33},{33,1},{2,34},{34,2},{3,35},{35,3},{4,36},{36... | collective-permute-start | bytes 393224 | tf_op jit(solution)/shard_map/ppermute | solution.py:69
  142.0 58.3 %collective-permute-start.2 = (bf16[2048,512]{1,0:T(8,128)(2,1)S(1)}, bf16[2048,512]{1,0:T(8,128)(2,1)}, u32[]{:S(2)}, u32[]{:S(2)}) collective-permute-start(bf16[2048,512]{1,0:T(8,128)(2,1)S(1)} %collective-permute-done.1), channel_id=1, source_target_pairs={{0,64},{64,128},{128,192},{192,0},{1,65},{65,129},{129,193},{193,1... | collective-permute-start | bytes 6291464 | tf_op jit(solution)/shard_map/ppermute | solution.py:12
  145.7 9.6 %collective-permute-start.20 = (f32[2,32,1024]{2,1,0:T(8,128)}, f32[2,32,1024]{2,1,0:T(8,128)}, u32[]{:S(2)}, u32[]{:S(2)}) collective-permute-start(f32[2,32,1024]{2,1,0:T(8,128)} %get-tuple-element.20), channel_id=1, source_target_pairs={{0,1},{1,2},{2,3},{3,0},{4,5},{5,6},{6,7},{7,4},{8,9},{9,10},{10,1... | collective-permute-start | bytes 786440 | tf_op jit(solution)/shard_map/ppermute | solution.py:36
  147.2 11.1 %collective-permute-start.21 = (f32[2,32,1024]{2,1,0:T(8,128)}, f32[2,32,1024]{2,1,0:T(8,128)}, u32[]{:S(2)}, u32[]{:S(2)}) collective-permute-start(f32[2,32,1024]{2,1,0:T(8,128)} %get-tuple-element.22), channel_id=1, source_target_pairs={{0,2},{1,3},{2,0},{3,1},{4,6},{5,7},{6,4},{7,5},{8,10},{9,11},{10,... | collective-permute-start | bytes 786440 | tf_op jit(solution)/shard_map/ppermute | solution.py:36
  150.0 12.7 %collective-permute-start.22 = (f32[2,32,1024]{2,1,0:T(8,128)S(1)}, f32[2,32,1024]{2,1,0:T(8,128)}, u32[]{:S(2)}, u32[]{:S(2)}) collective-permute-start(f32[2,32,1024]{2,1,0:T(8,128)S(1)} %get-tuple-element.21), channel_id=1, source_target_pairs={{0,3},{1,0},{2,1},{3,2},{4,7},{5,4},{6,5},{7,6},{8,11},{9,8},{10,9... | collective-permute-start | bytes 786440 | tf_op jit(solution)/shard_map/ppermute | solution.py:36
  163.9 9.5 %collective-permute-start.23 = (f32[32,1024]{1,0:T(8,128)S(1)}, f32[32,1024]{1,0:T(8,128)S(1)}, u32[]{:S(2)}, u32[]{:S(2)}) collective-permute-start(f32[32,1024]{1,0:T(8,128)S(1)} %get-tuple-element.32), channel_id=1, source_target_pairs={{0,8},{8,16},{16,24},{24,0},{1,9},{9,17},{17,25},{25,1},{2,10},{10... | collective-permute-start | bytes 393224 | tf_op jit(solution)/shard_map/ppermute | solution.py:36
  164.7 8.8 %collective-permute-start.24 = (f32[32,1024]{1,0:T(8,128)S(1)}, f32[32,1024]{1,0:T(8,128)S(1)}, u32[]{:S(2)}, u32[]{:S(2)}) collective-permute-start(f32[32,1024]{1,0:T(8,128)S(1)} %get-tuple-element.34), channel_id=1, source_target_pairs={{0,16},{8,24},{16,0},{24,8},{1,17},{9,25},{17,1},{25,9},{2,18},{10... | collective-permute-start | bytes 393224 | tf_op jit(solution)/shard_map/ppermute | solution.py:36
  167.6 6.4 %collective-permute-start.25 = (f32[32,1024]{1,0:T(8,128)S(1)}, f32[32,1024]{1,0:T(8,128)S(1)}, u32[]{:S(2)}, u32[]{:S(2)}) collective-permute-start(f32[32,1024]{1,0:T(8,128)S(1)} %get-tuple-element.33), channel_id=1, source_target_pairs={{0,24},{8,0},{16,8},{24,16},{1,25},{9,1},{17,9},{25,17},{2,26},{10... | collective-permute-start | bytes 393224 | tf_op jit(solution)/shard_map/ppermute | solution.py:36
  174.1 26.2 %collective-permute-start.26 = (f32[32,1024]{1,0:T(8,128)S(1)}, f32[32,1024]{1,0:T(8,128)S(1)}, u32[]{:S(2)}, u32[]{:S(2)}) collective-permute-start(f32[32,1024]{1,0:T(8,128)S(1)} %fusion.23), channel_id=1, source_target_pairs={{0,32},{32,0},{1,33},{33,1},{2,34},{34,2},{3,35},{35,3},{4,36},{36... | collective-permute-start | bytes 393224 | tf_op jit(solution)/shard_map/ppermute | solution.py:69
  210.9 9.2 %collective-permute-start.28 = (f32[2,32,1024]{2,1,0:T(8,128)S(1)}, f32[2,32,1024]{2,1,0:T(8,128)S(1)}, u32[]{:S(2)}, u32[]{:S(2)}) collective-permute-start(f32[2,32,1024]{2,1,0:T(8,128)S(1)} %get-tuple-element.17), channel_id=1, source_target_pairs={{0,1},{1,2},{2,3},{3,0},{4,5},{5,6},{6,7},{7,4},{8,9},{9,10},{10,1... | collective-permute-start | bytes 786440 | tf_op jit(solution)/shard_map/ppermute | solution.py:36
  212.5 10.7 %collective-permute-start.29 = (f32[2,32,1024]{2,1,0:T(8,128)S(1)}, f32[2,32,1024]{2,1,0:T(8,128)S(1)}, u32[]{:S(2)}, u32[]{:S(2)}) collective-permute-start(f32[2,32,1024]{2,1,0:T(8,128)S(1)} %get-tuple-element.19), channel_id=1, source_target_pairs={{0,2},{1,3},{2,0},{3,1},{4,6},{5,7},{6,4},{7,5},{8,10},{9,11},{10,... | collective-permute-start | bytes 786440 | tf_op jit(solution)/shard_map/ppermute | solution.py:36
  214.2 13.4 %collective-permute-start.30 = (f32[2,32,1024]{2,1,0:T(8,128)S(1)}, f32[2,32,1024]{2,1,0:T(8,128)S(1)}, u32[]{:S(2)}, u32[]{:S(2)}) collective-permute-start(f32[2,32,1024]{2,1,0:T(8,128)S(1)} %get-tuple-element.18), channel_id=1, source_target_pairs={{0,3},{1,0},{2,1},{3,2},{4,7},{5,4},{6,5},{7,6},{8,11},{9,8},{10,9... | collective-permute-start | bytes 786440 | tf_op jit(solution)/shard_map/ppermute | solution.py:36
  227.8 9.5 %collective-permute-start.31 = (f32[32,1024]{1,0:T(8,128)S(1)}, f32[32,1024]{1,0:T(8,128)S(1)}, u32[]{:S(2)}, u32[]{:S(2)}) collective-permute-start(f32[32,1024]{1,0:T(8,128)S(1)} %get-tuple-element.29), channel_id=1, source_target_pairs={{0,8},{8,16},{16,24},{24,0},{1,9},{9,17},{17,25},{25,1},{2,10},{10... | collective-permute-start | bytes 393224 | tf_op jit(solution)/shard_map/ppermute | solution.py:36
  228.8 8.4 %collective-permute-start.32 = (f32[32,1024]{1,0:T(8,128)S(1)}, f32[32,1024]{1,0:T(8,128)S(1)}, u32[]{:S(2)}, u32[]{:S(2)}) collective-permute-start(f32[32,1024]{1,0:T(8,128)S(1)} %get-tuple-element.31), channel_id=1, source_target_pairs={{0,16},{8,24},{16,0},{24,8},{1,17},{9,25},{17,1},{25,9},{2,18},{10... | collective-permute-start | bytes 393224 | tf_op jit(solution)/shard_map/ppermute | solution.py:36
  231.7 6.1 %collective-permute-start.33 = (f32[32,1024]{1,0:T(8,128)S(1)}, f32[32,1024]{1,0:T(8,128)S(1)}, u32[]{:S(2)}, u32[]{:S(2)}) collective-permute-start(f32[32,1024]{1,0:T(8,128)S(1)} %get-tuple-element.30), channel_id=1, source_target_pairs={{0,24},{8,0},{16,8},{24,16},{1,25},{9,1},{17,9},{25,17},{2,26},{10... | collective-permute-start | bytes 393224 | tf_op jit(solution)/shard_map/ppermute | solution.py:36
  237.8 9.6 %collective-permute-start.34 = (f32[32,1024]{1,0:T(8,128)S(1)}, f32[32,1024]{1,0:T(8,128)S(1)}, u32[]{:S(2)}, u32[]{:S(2)}) collective-permute-start(f32[32,1024]{1,0:T(8,128)S(1)} %fusion.21), channel_id=1, source_target_pairs={{0,32},{32,0},{1,33},{33,1},{2,34},{34,2},{3,35},{35,3},{4,36},{36... | collective-permute-start | bytes 393224 | tf_op jit(solution)/shard_map/ppermute | solution.py:69
  (7 other events, 15.9 us)

commit v6 on v5

--- a/solution.py
+++ b/solution.py
@@ -27,13 +27,13 @@
     return keep + lax.ppermute(send, axis, [(0, 1), (1, 0)])
 
 
-def spread_over(x, axis, dim):
-    n = lax.axis_size(axis)
-    index = lax.axis_index(axis)
+def spread_over(x, axes, dim):
+    n = x.shape[dim]
+    index = lax.axis_index(axes)
     total = lax.dynamic_index_in_dim(x, index, dim, keepdims=False)
     for shift in range(1, n):
         send = lax.dynamic_index_in_dim(x, (index + shift) % n, dim, keepdims=False)
-        total = total + lax.ppermute(send, axis, [(i, (i + shift) % n) for i in range(n)])
+        total = total + lax.ppermute(send, axes, [(i, (i + shift) % n) for i in range(n)])
     return total
 
 
@@ -46,29 +46,23 @@
     zhi, ys, cores, layers = (lax.axis_size(a) for a in COL_PARTS + ("layer",))
     halves = ys // 2
     block = right.shape[1] // (halves * cores * layers)
-    mine = lax.axis_index("zhi") * 2 + lax.axis_index("y") // halves
-    result = jnp.zeros((block, left_rows), jnp.float32)
+    gathered = jnp.zeros((cycle_size, halves, block, left_rows), jnp.float32)
     arrived = right
     reduced = None
     for step in range(cycle_size):
         current = arrived
         if step > 0:
             current, reduced = lax.optimization_barrier((current, reduced))
-            result = jnp.where(mine == (position - step + 1) % cycle_size, reduced, result)
+            gathered = lax.dynamic_update_slice_in_dim(gathered, reduced[None], (position - step + 1) % cycle_size, 0)
         if step + 1 < cycle_size:
             arrived = from_behind(arrived, "row", 1)
-        owner = (position - step) % cycle_size
         piece = lax.dot_general(current, left, (((0,), (1,)), ((), ())), preferred_element_type=jnp.float32)
         piece = piece.reshape(halves, cores, layers, block, left_rows)
         piece = pair_over(piece, "core", 1)
-        piece = spread_over(piece, "layer", 1)
-        spread = lax.dynamic_update_slice_in_dim(
-            jnp.zeros((ys, block, left_rows), jnp.float32), piece, (owner % 2) * halves, 0
-        )
-        piece = spread_over(spread, "y", 0)
-        reduced = piece + lax.ppermute(piece, "zhi", [(0, 1), (1, 0)])
-    result = jnp.where(mine == (position + 1) % cycle_size, reduced, result)
-    return result.T.astype(jnp.bfloat16)
+        reduced = spread_over(piece, "layer", 1)
+    gathered = lax.dynamic_update_slice_in_dim(gathered, reduced[None], (position + 1) % cycle_size, 0)
+    ordered = spread_over(gathered.reshape(zhi * ys, block, left_rows), ("zhi", "y"), 0)
+    return ordered.T.astype(jnp.bfloat16)
 
 
 def solution(mesh):

time: 251 us -> 234 us (0.932)
  starting transfers between devices: 60.9 us -> 40 us
  waiting for transfers between devices: 140 us -> 143 us
    ppermute x28 -> x19, waiting for transfers between devices: 135 us -> 59.9 us  [spread_over(): lax.ppermute(send, axes, [(i, (i + shift) % n) for i in range(n)])]
    ppermute x3, waiting for transfers between devices: 0.01 us -> 72.5 us  [from_behind(): return lax.ppermute(x, axis, [(i, (i + by) % size) for i in range(size)])]
    ppermute x28 -> x19, starting transfers between devices: 52.7 us -> 37.7 us  [spread_over(): lax.ppermute(send, axes, [(i, (i + shift) % n) for i in range(n)])]
    ppermute x4, waiting for transfers between devices: 4.81 us -> 10.9 us  [pair_over(): return keep + lax.ppermute(send, axis, [(0, 1), (1, 0)])]
    ppermute x3, starting transfers between devices: 7.91 us -> 2.16 us  [from_behind(): return lax.ppermute(x, axis, [(i, (i + by) % size) for i in range(size)])]
    dynamic_update_slice x4 -> x1, other arithmetic: 3.58 us -> 0.08 us  [local(): lax.dynamic_update_slice_in_dim(gathered, reduced[None], (position + 1) %...]
  transfers between devices with their start and end apart: 35 -> 26, of which waited for: 28 -> 25; matrix products, arithmetic and copies ran while one was open for 4% -> 6% of each run, Pallas kernels for 0% -> 0%
where the time goes in v6:
time: 234 us; the launch traced here: 231 us
  waiting for transfers between devices  143 us (61%)
  starting transfers between devices  40 us (17%)
  local copies, waits for them, and re-layouts  18.2 us (8%)
  matrix products  17.3 us (7%)
  other arithmetic  12 us (5%)
    ppermute x3, waiting for transfers between devices, from_behind(): return lax.ppermute(x, axis, [(i, (i + by) % size) for i in range(size)])  72.5 us
    ppermute x19, waiting for transfers between devices, spread_over(): lax.ppermute(send, axes, [(i, (i + shift) % n) for i in range(n)])  59.9 us
    ppermute x19, starting transfers between devices, spread_over(): lax.ppermute(send, axes, [(i, (i + shift) % n) for i in range(n)])  37.7 us
    dot_general x4, matrix products, local(): lax.dot_general(current, left, (((0,), (1,)), ((), ())), preferred_elemen...  17.3 us
    dot_general x4, local copies, waits for them, and re-layouts, local(): lax.dot_general(current, left, (((0,), (1,)), ((), ())), preferred_elemen...  11.9 us
    ppermute x4, waiting for transfers between devices, pair_over(): return keep + lax.ppermute(send, axis, [(0, 1), (1, 0)])  10.9 us
  transfers between devices with their start and end apart: 26, of which 25 were waited for; matrix products, arithmetic and copies ran while one was open for 6% of the time, Pallas kernels for 0%

profile of v6, /device:TPU:2, one launch (start us, length us, event | category | flops | bytes accessed | tf_op | source)
XLA Modules:
  0.0 231.1 jit_solution(17442111242029222575)
XLA Ops:
  5.1 2.6 %copy.12 = bf16[512,2048]{1,0:T(8,128)(2,1)} copy(bf16[512,2048]{0,1:T(8,128)(2,1)S(1)} %bitcast.136) | data formatting | bytes 4194304 | tf_op jit(solution)/shard_map/dot_general | solution.py:59
  7.7 2.6 %bitcast_multiply_fusion = bf16[1024,2048]{1,0:T(8,128)(2,1)S(1)} fusion(bf16[1024,2048]{1,0:T(8,128)(2,1)} %param.4, bf16[16,2048]{1,0:T(8,128)(2,1)S(1)} %mul.33), kind=kLoop, calls=%fused_computation.8 | loop fusion | flops 2097152 | bytes 8454144 | tf_op jit(solution)/shard_map/mul | solution.py:19
  14.3 2.8 %collective-permute-done.1 = f32[2,4,32,1024]{3,2,1,0:T(8,128)} collective-permute-done((f32[2,4,32,1024]{3,2,1,0:T(8,128)S(1)}, f32[2,4,32,1024]{3,2,1,0:T(8,128)}, u32[]{:S(2)}, u32[]{:S(2)}) %collective-permute-start.1) | collective-permute-done | bytes 1048608 | tf_op jit(solution)/shard_map/ppermute | solution.py:27
  24.5 4.6 %collective-permute-done.2 = f32[2,32,1024]{2,1,0:T(8,128)S(1)} collective-permute-done((f32[2,32,1024]{2,1,0:T(8,128)}, f32[2,32,1024]{2,1,0:T(8,128)S(1)}, u32[]{:S(2)}, u32[]{:S(2)}) %collective-permute-start.2) | collective-permute-done | bytes 262176 | tf_op jit(solution)/shard_map/ppermute | solution.py:36
  29.1 3.1 %collective-permute-done.3 = f32[2,32,1024]{2,1,0:T(8,128)} collective-permute-done((f32[2,32,1024]{2,1,0:T(8,128)}, f32[2,32,1024]{2,1,0:T(8,128)}, u32[]{:S(2)}, u32[]{:S(2)}) %collective-permute-start.3) | collective-permute-done | bytes 262176 | tf_op jit(solution)/shard_map/ppermute | solution.py:36
  32.2 3.8 %collective-permute-done.4 = f32[2,32,1024]{2,1,0:T(8,128)} collective-permute-done((f32[2,32,1024]{2,1,0:T(8,128)}, f32[2,32,1024]{2,1,0:T(8,128)}, u32[]{:S(2)}, u32[]{:S(2)}) %collective-permute-start.4) | collective-permute-done | bytes 262176 | tf_op jit(solution)/shard_map/ppermute | solution.py:36
  37.2 16.0 %collective-permute-done = bf16[2048,512]{1,0:T(8,128)(2,1)} collective-permute-done((bf16[2048,512]{1,0:T(8,128)(2,1)S(1)}, bf16[2048,512]{1,0:T(8,128)(2,1)}, u32[]{:S(2)}, u32[]{:S(2)}) %collective-permute-start) | collective-permute-done | bytes 2097184 | tf_op jit(solution)/shard_map/ppermute | solution.py:12
  53.2 2.9 %copy.13 = bf16[512,2048]{1,0:T(8,128)(2,1)S(1)} copy(bf16[512,2048]{0,1:T(8,128)(2,1)} %bitcast.13) | data formatting | bytes 4194304 | tf_op jit(solution)/shard_map/dot_general | solution.py:59
  56.1 4.5 %fusion.4 = f32[2,2,4,32,1024]{4,3,2,1,0:T(8,128)S(1)} fusion(bf16[2,2,4,32,2048]{4,3,2,1,0:T(8,128)(2,1)S(1)} %bitcast.143, bf16[1024,2048]{1,0:T(8,128)(2,1)} %copy-done), kind=kOutput, calls=%fused_computation.4 | convolution fusion | flops 2147483648 | bytes 8388608 | tf_op jit(solution)/shard_map/dot_general | solution.py:59
  61.0 2.6 %collective-permute-done.6 = f32[2,4,32,1024]{3,2,1,0:T(8,128)S(1)} collective-permute-done((f32[2,4,32,1024]{3,2,1,0:T(8,128)S(1)}, f32[2,4,32,1024]{3,2,1,0:T(8,128)S(1)}, u32[]{:S(2)}, u32[]{:S(2)}) %collective-permute-start.6) | collective-permute-done | bytes 1048608 | tf_op jit(solution)/shard_map/ppermute | solution.py:27
  68.8 4.4 %collective-permute-done.7 = f32[2,32,1024]{2,1,0:T(8,128)S(1)} collective-permute-done((f32[2,32,1024]{2,1,0:T(8,128)S(1)}, f32[2,32,1024]{2,1,0:T(8,128)S(1)}, u32[]{:S(2)}, u32[]{:S(2)}) %collective-permute-start.7) | collective-permute-done | bytes 262176 | tf_op jit(solution)/shard_map/ppermute | solution.py:36
  73.2 3.0 %collective-permute-done.8 = f32[2,32,1024]{2,1,0:T(8,128)S(1)} collective-permute-done((f32[2,32,1024]{2,1,0:T(8,128)S(1)}, f32[2,32,1024]{2,1,0:T(8,128)S(1)}, u32[]{:S(2)}, u32[]{:S(2)}) %collective-permute-start.8) | collective-permute-done | bytes 262176 | tf_op jit(solution)/shard_map/ppermute | solution.py:36
  76.2 3.9 %collective-permute-done.9 = f32[2,32,1024]{2,1,0:T(8,128)S(1)} collective-permute-done((f32[2,32,1024]{2,1,0:T(8,128)S(1)}, f32[2,32,1024]{2,1,0:T(8,128)S(1)}, u32[]{:S(2)}, u32[]{:S(2)}) %collective-permute-start.9) | collective-permute-done | bytes 262176 | tf_op jit(solution)/shard_map/ppermute | solution.py:36
  80.9 28.7 %collective-permute-done.5 = bf16[2048,512]{1,0:T(8,128)(2,1)S(1)} collective-permute-done((bf16[2048,512]{1,0:T(8,128)(2,1)}, bf16[2048,512]{1,0:T(8,128)(2,1)S(1)}, u32[]{:S(2)}, u32[]{:S(2)}) %collective-permute-start.5) | collective-permute-done | bytes 2097184 | tf_op jit(solution)/shard_map/ppermute | solution.py:12
  112.1 5.2 %fusion.2 = f32[2,2,4,32,1024]{4,3,2,1,0:T(8,128)S(1)} fusion(bf16[2,2,4,32,2048]{4,3,2,1,0:T(8,128)(2,1)} %bitcast.144, bf16[1024,2048]{1,0:T(8,128)(2,1)} %copy-done), kind=kOutput, calls=%fused_computation.2 | convolution fusion | flops 2147483648 | bytes 8388608 | tf_op jit(solution)/shard_map/dot_general | solution.py:59
  117.5 2.6 %collective-permute-done.11 = f32[2,4,32,1024]{3,2,1,0:T(8,128)S(1)} collective-permute-done((f32[2,4,32,1024]{3,2,1,0:T(8,128)S(1)}, f32[2,4,32,1024]{3,2,1,0:T(8,128)S(1)}, u32[]{:S(2)}, u32[]{:S(2)}) %collective-permute-start.11) | collective-permute-done | bytes 1048608 | tf_op jit(solution)/shard_map/ppermute | solution.py:27
  125.3 4.4 %collective-permute-done.12 = f32[2,32,1024]{2,1,0:T(8,128)S(1)} collective-permute-done((f32[2,32,1024]{2,1,0:T(8,128)S(1)}, f32[2,32,1024]{2,1,0:T(8,128)S(1)}, u32[]{:S(2)}, u32[]{:S(2)}) %collective-permute-start.12) | collective-permute-done | bytes 262176 | tf_op jit(solution)/shard_map/ppermute | solution.py:36
  129.7 3.0 %collective-permute-done.13 = f32[2,32,1024]{2,1,0:T(8,128)S(1)} collective-permute-done((f32[2,32,1024]{2,1,0:T(8,128)S(1)}, f32[2,32,1024]{2,1,0:T(8,128)S(1)}, u32[]{:S(2)}, u32[]{:S(2)}) %collective-permute-start.13) | collective-permute-done | bytes 262176 | tf_op jit(solution)/shard_map/ppermute | solution.py:36
  132.8 3.7 %collective-permute-done.14 = f32[2,32,1024]{2,1,0:T(8,128)S(1)} collective-permute-done((f32[2,32,1024]{2,1,0:T(8,128)S(1)}, f32[2,32,1024]{2,1,0:T(8,128)S(1)}, u32[]{:S(2)}, u32[]{:S(2)}) %collective-permute-start.14) | collective-permute-done | bytes 262176 | tf_op jit(solution)/shard_map/ppermute | solution.py:36
  137.3 27.7 %collective-permute-done.10 = bf16[2048,512]{1,0:T(8,128)(2,1)S(1)} collective-permute-done((bf16[2048,512]{1,0:T(8,128)(2,1)S(1)}, bf16[2048,512]{1,0:T(8,128)(2,1)S(1)}, u32[]{:S(2)}, u32[]{:S(2)}) %collective-permute-start.10) | collective-permute-done | bytes 2097184 | tf_op jit(solution)/shard_map/ppermute | solution.py:12
  166.4 3.9 %copy.15 = bf16[512,2048]{1,0:T(8,128)(2,1)} copy(bf16[512,2048]{0,1:T(8,128)(2,1)} %bitcast.140) | data formatting | bytes 4194304 | tf_op jit(solution)/shard_map/dot_general | solution.py:59
  170.4 5.2 %fusion = f32[2,2,4,32,1024]{4,3,2,1,0:T(8,128)S(1)} fusion(bf16[2,2,4,32,2048]{4,3,2,1,0:T(8,128)(2,1)} %bitcast.142, bf16[1024,2048]{1,0:T(8,128)(2,1)} %copy-done), kind=kOutput, calls=%fused_computation | convolution fusion | flops 2147483648 | bytes 8388608 | tf_op jit(solution)/shard_map/dot_general | solution.py:59
  176.8 2.8 %collective-permute-done.15 = f32[2,4,32,1024]{3,2,1,0:T(8,128)} collective-permute-done((f32[2,4,32,1024]{3,2,1,0:T(8,128)}, f32[2,4,32,1024]{3,2,1,0:T(8,128)}, u32[]{:S(2)}, u32[]{:S(2)}) %collective-permute-start.15) | collective-permute-done | bytes 1048608 | tf_op jit(solution)/shard_map/ppermute | solution.py:27
  186.0 4.3 %collective-permute-done.16 = f32[2,32,1024]{2,1,0:T(8,128)S(1)} collective-permute-done((f32[2,32,1024]{2,1,0:T(8,128)S(1)}, f32[2,32,1024]{2,1,0:T(8,128)S(1)}, u32[]{:S(2)}, u32[]{:S(2)}) %collective-permute-start.16) | collective-permute-done | bytes 262176 | tf_op jit(solution)/shard_map/ppermute | solution.py:36
  190.3 3.0 %collective-permute-done.17 = f32[2,32,1024]{2,1,0:T(8,128)S(1)} collective-permute-done((f32[2,32,1024]{2,1,0:T(8,128)S(1)}, f32[2,32,1024]{2,1,0:T(8,128)S(1)}, u32[]{:S(2)}, u32[]{:S(2)}) %collective-permute-start.17) | collective-permute-done | bytes 262176 | tf_op jit(solution)/shard_map/ppermute | solution.py:36
  193.3 3.7 %collective-permute-done.18 = f32[2,32,1024]{2,1,0:T(8,128)S(1)} collective-permute-done((f32[2,32,1024]{2,1,0:T(8,128)S(1)}, f32[2,32,1024]{2,1,0:T(8,128)S(1)}, u32[]{:S(2)}, u32[]{:S(2)}) %collective-permute-start.18) | collective-permute-done | bytes 262176 | tf_op jit(solution)/shard_map/ppermute | solution.py:36
  199.0 2.9 %collective-permute-start.20 = (f32[32,1024]{1,0:T(8,128)S(1)}, f32[32,1024]{1,0:T(8,128)S(1)}, u32[]{:S(2)}, u32[]{:S(2)}) collective-permute-start(f32[32,1024]{1,0:T(8,128)S(1)} %get-tuple-element.23), channel_id=1, source_target_pairs={{0,16},{8,24},{16,32},{24,40},{32,48},{40,56},{48,0},{56,8},{1,17}... | collective-permute-start | bytes 393224 | tf_op jit(solution)/shard_map/ppermute | solution.py:36
  201.9 6.2 %collective-permute-start.21 = (f32[32,1024]{1,0:T(8,128)S(1)}, f32[32,1024]{1,0:T(8,128)S(1)}, u32[]{:S(2)}, u32[]{:S(2)}) collective-permute-start(f32[32,1024]{1,0:T(8,128)S(1)} %get-tuple-element.22), channel_id=1, source_target_pairs={{0,24},{8,32},{16,40},{24,48},{32,56},{40,0},{48,8},{56,16},{1,25}... | collective-permute-start | bytes 393224 | tf_op jit(solution)/shard_map/ppermute | solution.py:36
  208.6 5.6 %collective-permute-start.23 = (f32[32,1024]{1,0:T(8,128)S(1)}, f32[32,1024]{1,0:T(8,128)S(1)}, u32[]{:S(2)}, u32[]{:S(2)}) collective-permute-start(f32[32,1024]{1,0:T(8,128)S(1)} %get-tuple-element.20), channel_id=1, source_target_pairs={{0,40},{8,48},{16,56},{24,0},{32,8},{40,16},{48,24},{56,32},{1,41}... | collective-permute-start | bytes 393224 | tf_op jit(solution)/shard_map/ppermute | solution.py:36
  214.2 4.7 %collective-permute-done.19 = f32[32,1024]{1,0:T(8,128)S(1)} collective-permute-done((f32[32,1024]{1,0:T(8,128)S(1)}, f32[32,1024]{1,0:T(8,128)S(1)}, u32[]{:S(2)}, u32[]{:S(2)}) %collective-permute-start.19) | collective-permute-done | bytes 131104 | tf_op jit(solution)/shard_map/ppermute | solution.py:36
  222.3 3.8 %collective-permute-done.24 = f32[32,1024]{1,0:T(8,128)S(1)} collective-permute-done((f32[32,1024]{1,0:T(8,128)S(1)}, f32[32,1024]{1,0:T(8,128)S(1)}, u32[]{:S(2)}, u32[]{:S(2)}) %collective-permute-start.24) | collective-permute-done | bytes 131104 | tf_op jit(solution)/shard_map/ppermute | solution.py:36
  226.1 4.3 %collective-permute-done.25 = f32[32,1024]{1,0:T(8,128)S(1)} collective-permute-done((f32[32,1024]{1,0:T(8,128)S(1)}, f32[32,1024]{1,0:T(8,128)S(1)}, u32[]{:S(2)}, u32[]{:S(2)}) %collective-permute-start.25) | collective-permute-done | bytes 131104 | tf_op jit(solution)/shard_map/ppermute | solution.py:36
  (75 shorter events, 47.8 us)
Async XLA Ops:
  1.0 3.8 %copy-start.7 = (s32[16,32]{1,0:T(8,128)S(1)}, s32[16,32]{1,0:T(8,128)}, u32[]{:S(2)}) copy-start(s32[16,32]{1,0:T(8,128)} %param.5) | copy-start | bytes 6148
  2.8 50.4 %collective-permute-start = (bf16[2048,512]{1,0:T(8,128)(2,1)S(1)}, bf16[2048,512]{1,0:T(8,128)(2,1)}, u32[]{:S(2)}, u32[]{:S(2)}) collective-permute-start(bf16[2048,512]{1,0:T(8,128)(2,1)S(1)} %bitcast_multiply_fusion.1), channel_id=1, source_target_pairs={{0,64},{64,128},{128,192},{192,0},{1,65},{65,129},{129,193},{193,1... | collective-permute-start | bytes 6291464 | tf_op jit(solution)/shard_map/ppermute | solution.py:12
  7.7 2.9 %copy-start.3 = (bf16[512,2048]{1,0:T(8,128)(2,1)S(1)}, bf16[512,2048]{1,0:T(8,128)(2,1)}, u32[]{:S(2)}) copy-start(bf16[512,2048]{1,0:T(8,128)(2,1)} %copy.12) | copy-start | bytes 6291460
  10.3 2.6 %copy-start = (bf16[1024,2048]{1,0:T(8,128)(2,1)}, bf16[1024,2048]{1,0:T(8,128)(2,1)S(1)}, u32[]{:S(2)}) copy-start(bf16[1024,2048]{1,0:T(8,128)(2,1)S(1)} %bitcast_multiply_fusion) | copy-start | bytes 12582916
  14.3 2.8 %collective-permute-start.1 = (f32[2,4,32,1024]{3,2,1,0:T(8,128)S(1)}, f32[2,4,32,1024]{3,2,1,0:T(8,128)}, u32[]{:S(2)}, u32[]{:S(2)}) collective-permute-start(f32[2,4,32,1024]{3,2,1,0:T(8,128)S(1)} %dynamic-slice_bitcast_fusion.3), channel_id=1, source_target_pairs={{0,4},{4,0},{1,5},{5,1},{2,6},{6,2},{3,7},{7,3},{8,12},{12,8},{9,1... | collective-permute-start | bytes 3145736 | tf_op jit(solution)/shard_map/ppermute | solution.py:27
  19.7 9.4 %collective-permute-start.2 = (f32[2,32,1024]{2,1,0:T(8,128)}, f32[2,32,1024]{2,1,0:T(8,128)S(1)}, u32[]{:S(2)}, u32[]{:S(2)}) collective-permute-start(f32[2,32,1024]{2,1,0:T(8,128)} %get-tuple-element.33), channel_id=1, source_target_pairs={{0,1},{1,2},{2,3},{3,0},{4,5},{5,6},{6,7},{7,4},{8,9},{9,10},{10,1... | collective-permute-start | bytes 786440 | tf_op jit(solution)/shard_map/ppermute | solution.py:36
  21.2 11.0 %collective-permute-start.3 = (f32[2,32,1024]{2,1,0:T(8,128)}, f32[2,32,1024]{2,1,0:T(8,128)}, u32[]{:S(2)}, u32[]{:S(2)}) collective-permute-start(f32[2,32,1024]{2,1,0:T(8,128)} %get-tuple-element.35), channel_id=1, source_target_pairs={{0,2},{1,3},{2,0},{3,1},{4,6},{5,7},{6,4},{7,5},{8,10},{9,11},{10,... | collective-permute-start | bytes 786440 | tf_op jit(solution)/shard_map/ppermute | solution.py:36
  22.3 13.7 %collective-permute-start.4 = (f32[2,32,1024]{2,1,0:T(8,128)}, f32[2,32,1024]{2,1,0:T(8,128)}, u32[]{:S(2)}, u32[]{:S(2)}) collective-permute-start(f32[2,32,1024]{2,1,0:T(8,128)} %get-tuple-element.34), channel_id=1, source_target_pairs={{0,3},{1,0},{2,1},{3,2},{4,7},{5,4},{6,5},{7,6},{8,11},{9,8},{10,9... | collective-permute-start | bytes 786440 | tf_op jit(solution)/shard_map/ppermute | solution.py:36
  29.1 3.1 %copy-start.6 = (f32[2,32,1024]{2,1,0:T(8,128)}, f32[2,32,1024]{2,1,0:T(8,128)S(1)}, u32[]{:S(2)}) copy-start(f32[2,32,1024]{2,1,0:T(8,128)S(1)} %collective-permute-done.2) | copy-start | bytes 786436
  60.7 48.9 %collective-permute-start.5 = (bf16[2048,512]{1,0:T(8,128)(2,1)}, bf16[2048,512]{1,0:T(8,128)(2,1)S(1)}, u32[]{:S(2)}, u32[]{:S(2)}) collective-permute-start(bf16[2048,512]{1,0:T(8,128)(2,1)} %collective-permute-done), channel_id=1, source_target_pairs={{0,64},{64,128},{128,192},{192,0},{1,65},{65,129},{129,193},{193,1... | collective-permute-start | bytes 6291464 | tf_op jit(solution)/shard_map/ppermute | solution.py:12
  60.9 2.7 %collective-permute-start.6 = (f32[2,4,32,1024]{3,2,1,0:T(8,128)S(1)}, f32[2,4,32,1024]{3,2,1,0:T(8,128)S(1)}, u32[]{:S(2)}, u32[]{:S(2)}) collective-permute-start(f32[2,4,32,1024]{3,2,1,0:T(8,128)S(1)} %dynamic-slice_bitcast_fusion.2), channel_id=1, source_target_pairs={{0,4},{4,0},{1,5},{5,1},{2,6},{6,2},{3,7},{7,3},{8,12},{12,8},{9,1... | collective-permute-start | bytes 3145736 | tf_op jit(solution)/shard_map/ppermute | solution.py:27
  63.9 9.2 %collective-permute-start.7 = (f32[2,32,1024]{2,1,0:T(8,128)S(1)}, f32[2,32,1024]{2,1,0:T(8,128)S(1)}, u32[]{:S(2)}, u32[]{:S(2)}) collective-permute-start(f32[2,32,1024]{2,1,0:T(8,128)S(1)} %get-tuple-element.30), channel_id=1, source_target_pairs={{0,1},{1,2},{2,3},{3,0},{4,5},{5,6},{6,7},{7,4},{8,9},{9,10},{10,1... | collective-permute-start | bytes 786440 | tf_op jit(solution)/shard_map/ppermute | solution.py:36
  65.5 10.7 %collective-permute-start.8 = (f32[2,32,1024]{2,1,0:T(8,128)S(1)}, f32[2,32,1024]{2,1,0:T(8,128)S(1)}, u32[]{:S(2)}, u32[]{:S(2)}) collective-permute-start(f32[2,32,1024]{2,1,0:T(8,128)S(1)} %get-tuple-element.32), channel_id=1, source_target_pairs={{0,2},{1,3},{2,0},{3,1},{4,6},{5,7},{6,4},{7,5},{8,10},{9,11},{10,... | collective-permute-start | bytes 786440 | tf_op jit(solution)/shard_map/ppermute | solution.py:36
  66.6 13.5 %collective-permute-start.9 = (f32[2,32,1024]{2,1,0:T(8,128)S(1)}, f32[2,32,1024]{2,1,0:T(8,128)S(1)}, u32[]{:S(2)}, u32[]{:S(2)}) collective-permute-start(f32[2,32,1024]{2,1,0:T(8,128)S(1)} %get-tuple-element.31), channel_id=1, source_target_pairs={{0,3},{1,0},{2,1},{3,2},{4,7},{5,4},{6,5},{7,6},{8,11},{9,8},{10,9... | collective-permute-start | bytes 786440 | tf_op jit(solution)/shard_map/ppermute | solution.py:36
  117.2 47.8 %collective-permute-start.10 = (bf16[2048,512]{1,0:T(8,128)(2,1)S(1)}, bf16[2048,512]{1,0:T(8,128)(2,1)S(1)}, u32[]{:S(2)}, u32[]{:S(2)}) collective-permute-start(bf16[2048,512]{1,0:T(8,128)(2,1)S(1)} %collective-permute-done.5), channel_id=1, source_target_pairs={{0,64},{64,128},{128,192},{192,0},{1,65},{65,129},{129,193},{193,1... | collective-permute-start | bytes 6291464 | tf_op jit(solution)/shard_map/ppermute | solution.py:12
  117.4 2.7 %collective-permute-start.11 = (f32[2,4,32,1024]{3,2,1,0:T(8,128)S(1)}, f32[2,4,32,1024]{3,2,1,0:T(8,128)S(1)}, u32[]{:S(2)}, u32[]{:S(2)}) collective-permute-start(f32[2,4,32,1024]{3,2,1,0:T(8,128)S(1)} %dynamic-slice_bitcast_fusion.1), channel_id=1, source_target_pairs={{0,4},{4,0},{1,5},{5,1},{2,6},{6,2},{3,7},{7,3},{8,12},{12,8},{9,1... | collective-permute-start | bytes 3145736 | tf_op jit(solution)/shard_map/ppermute | solution.py:27
  120.5 9.2 %collective-permute-start.12 = (f32[2,32,1024]{2,1,0:T(8,128)S(1)}, f32[2,32,1024]{2,1,0:T(8,128)S(1)}, u32[]{:S(2)}, u32[]{:S(2)}) collective-permute-start(f32[2,32,1024]{2,1,0:T(8,128)S(1)} %get-tuple-element.27), channel_id=1, source_target_pairs={{0,1},{1,2},{2,3},{3,0},{4,5},{5,6},{6,7},{7,4},{8,9},{9,10},{10,1... | collective-permute-start | bytes 786440 | tf_op jit(solution)/shard_map/ppermute | solution.py:36
  122.0 10.7 %collective-permute-start.13 = (f32[2,32,1024]{2,1,0:T(8,128)S(1)}, f32[2,32,1024]{2,1,0:T(8,128)S(1)}, u32[]{:S(2)}, u32[]{:S(2)}) collective-permute-start(f32[2,32,1024]{2,1,0:T(8,128)S(1)} %get-tuple-element.29), channel_id=1, source_target_pairs={{0,2},{1,3},{2,0},{3,1},{4,6},{5,7},{6,4},{7,5},{8,10},{9,11},{10,... | collective-permute-start | bytes 786440 | tf_op jit(solution)/shard_map/ppermute | solution.py:36
  122.8 13.7 %collective-permute-start.14 = (f32[2,32,1024]{2,1,0:T(8,128)S(1)}, f32[2,32,1024]{2,1,0:T(8,128)S(1)}, u32[]{:S(2)}, u32[]{:S(2)}) collective-permute-start(f32[2,32,1024]{2,1,0:T(8,128)S(1)} %get-tuple-element.28), channel_id=1, source_target_pairs={{0,3},{1,0},{2,1},{3,2},{4,7},{5,4},{6,5},{7,6},{8,11},{9,8},{10,9... | collective-permute-start | bytes 786440 | tf_op jit(solution)/shard_map/ppermute | solution.py:36
  176.6 3.0 %collective-permute-start.15 = (f32[2,4,32,1024]{3,2,1,0:T(8,128)}, f32[2,4,32,1024]{3,2,1,0:T(8,128)}, u32[]{:S(2)}, u32[]{:S(2)}) collective-permute-start(f32[2,4,32,1024]{3,2,1,0:T(8,128)} %dynamic-slice_bitcast_fusion), channel_id=1, source_target_pairs={{0,4},{4,0},{1,5},{5,1},{2,6},{6,2},{3,7},{7,3},{8,12},{12,8},{9,1... | collective-permute-start | bytes 3145736 | tf_op jit(solution)/shard_map/ppermute | solution.py:27
  176.7 9.1 %copy-start.4 = (f32[2,32,1024]{2,1,0:T(8,128)S(1)}, f32[2,32,1024]{2,1,0:T(8,128)}, u32[]{:S(2)}) copy-start(f32[2,32,1024]{2,1,0:T(8,128)} %fusion.13) | copy-start | bytes 786436
  176.7 9.2 %copy-start.5 = (f32[2,32,1024]{2,1,0:T(8,128)S(1)}, f32[2,32,1024]{2,1,0:T(8,128)}, u32[]{:S(2)}) copy-start(f32[2,32,1024]{2,1,0:T(8,128)} %fusion.11) | copy-start | bytes 786436
  181.0 9.2 %collective-permute-start.16 = (f32[2,32,1024]{2,1,0:T(8,128)S(1)}, f32[2,32,1024]{2,1,0:T(8,128)S(1)}, u32[]{:S(2)}, u32[]{:S(2)}) collective-permute-start(f32[2,32,1024]{2,1,0:T(8,128)S(1)} %get-tuple-element.24), channel_id=1, source_target_pairs={{0,1},{1,2},{2,3},{3,0},{4,5},{5,6},{6,7},{7,4},{8,9},{9,10},{10,1... | collective-permute-start | bytes 786440 | tf_op jit(solution)/shard_map/ppermute | solution.py:36
  182.6 10.7 %collective-permute-start.17 = (f32[2,32,1024]{2,1,0:T(8,128)S(1)}, f32[2,32,1024]{2,1,0:T(8,128)S(1)}, u32[]{:S(2)}, u32[]{:S(2)}) collective-permute-start(f32[2,32,1024]{2,1,0:T(8,128)S(1)} %get-tuple-element.26), channel_id=1, source_target_pairs={{0,2},{1,3},{2,0},{3,1},{4,6},{5,7},{6,4},{7,5},{8,10},{9,11},{10,... | collective-permute-start | bytes 786440 | tf_op jit(solution)/shard_map/ppermute | solution.py:36
  183.4 13.7 %collective-permute-start.18 = (f32[2,32,1024]{2,1,0:T(8,128)S(1)}, f32[2,32,1024]{2,1,0:T(8,128)S(1)}, u32[]{:S(2)}, u32[]{:S(2)}) collective-permute-start(f32[2,32,1024]{2,1,0:T(8,128)S(1)} %get-tuple-element.25), channel_id=1, source_target_pairs={{0,3},{1,0},{2,1},{3,2},{4,7},{5,4},{6,5},{7,6},{8,11},{9,8},{10,9... | collective-permute-start | bytes 786440 | tf_op jit(solution)/shard_map/ppermute | solution.py:36
  197.2 21.6 %collective-permute-start.19 = (f32[32,1024]{1,0:T(8,128)S(1)}, f32[32,1024]{1,0:T(8,128)S(1)}, u32[]{:S(2)}, u32[]{:S(2)}) collective-permute-start(f32[32,1024]{1,0:T(8,128)S(1)} %get-tuple-element.17), channel_id=1, source_target_pairs={{0,8},{8,16},{16,24},{24,32},{32,40},{40,48},{48,56},{56,0},{1,9},... | collective-permute-start | bytes 393224 | tf_op jit(solution)/shard_map/ppermute | solution.py:36
  199.0 21.6 %collective-permute-start.20 = (f32[32,1024]{1,0:T(8,128)S(1)}, f32[32,1024]{1,0:T(8,128)S(1)}, u32[]{:S(2)}, u32[]{:S(2)}) collective-permute-start(f32[32,1024]{1,0:T(8,128)S(1)} %get-tuple-element.23), channel_id=1, source_target_pairs={{0,16},{8,24},{16,32},{24,40},{32,48},{40,56},{48,0},{56,8},{1,17}... | collective-permute-start | bytes 393224 | tf_op jit(solution)/shard_map/ppermute | solution.py:36
  201.9 19.5 %collective-permute-start.21 = (f32[32,1024]{1,0:T(8,128)S(1)}, f32[32,1024]{1,0:T(8,128)S(1)}, u32[]{:S(2)}, u32[]{:S(2)}) collective-permute-start(f32[32,1024]{1,0:T(8,128)S(1)} %get-tuple-element.22), channel_id=1, source_target_pairs={{0,24},{8,32},{16,40},{24,48},{32,56},{40,0},{48,8},{56,16},{1,25}... | collective-permute-start | bytes 393224 | tf_op jit(solution)/shard_map/ppermute | solution.py:36
  208.1 14.2 %collective-permute-start.22 = (f32[32,1024]{1,0:T(8,128)S(1)}, f32[32,1024]{1,0:T(8,128)S(1)}, u32[]{:S(2)}, u32[]{:S(2)}) collective-permute-start(f32[32,1024]{1,0:T(8,128)S(1)} %get-tuple-element.21), channel_id=1, source_target_pairs={{0,32},{8,40},{16,48},{24,56},{32,0},{40,8},{48,16},{56,24},{1,33}... | collective-permute-start | bytes 393224 | tf_op jit(solution)/shard_map/ppermute | solution.py:36
  208.6 13.7 %collective-permute-start.23 = (f32[32,1024]{1,0:T(8,128)S(1)}, f32[32,1024]{1,0:T(8,128)S(1)}, u32[]{:S(2)}, u32[]{:S(2)}) collective-permute-start(f32[32,1024]{1,0:T(8,128)S(1)} %get-tuple-element.20), channel_id=1, source_target_pairs={{0,40},{8,48},{16,56},{24,0},{32,8},{40,16},{48,24},{56,32},{1,41}... | collective-permute-start | bytes 393224 | tf_op jit(solution)/shard_map/ppermute | solution.py:36
  218.9 7.3 %collective-permute-start.24 = (f32[32,1024]{1,0:T(8,128)S(1)}, f32[32,1024]{1,0:T(8,128)S(1)}, u32[]{:S(2)}, u32[]{:S(2)}) collective-permute-start(f32[32,1024]{1,0:T(8,128)S(1)} %get-tuple-element.19), channel_id=1, source_target_pairs={{0,48},{8,56},{16,0},{24,8},{32,16},{40,24},{48,32},{56,40},{1,49}... | collective-permute-start | bytes 393224 | tf_op jit(solution)/shard_map/ppermute | solution.py:36
  220.6 9.9 %collective-permute-start.25 = (f32[32,1024]{1,0:T(8,128)S(1)}, f32[32,1024]{1,0:T(8,128)S(1)}, u32[]{:S(2)}, u32[]{:S(2)}) collective-permute-start(f32[32,1024]{1,0:T(8,128)S(1)} %get-tuple-element.18), channel_id=1, source_target_pairs={{0,56},{8,0},{16,8},{24,16},{32,24},{40,32},{48,40},{56,48},{1,57}... | collective-permute-start | bytes 393224 | tf_op jit(solution)/shard_map/ppermute | solution.py:36
  (2 other events, 2.8 us)

commit v7 on v6

--- a/solution.py
+++ b/solution.py
@@ -39,13 +39,13 @@
 
 def local(left_blocks, left_pattern, right_blocks, right_pattern):
     left = apply_pattern(left_blocks, left_pattern)
-    right = apply_pattern(right_blocks, right_pattern)
+    right = apply_pattern(right_blocks, right_pattern).T
     left_rows = left.shape[0]
     cycle_size = lax.axis_size("row")
     position = lax.axis_index("row")
     zhi, ys, cores, layers = (lax.axis_size(a) for a in COL_PARTS + ("layer",))
     halves = ys // 2
-    block = right.shape[1] // (halves * cores * layers)
+    block = right.shape[0] // (halves * cores * layers)
     gathered = jnp.zeros((cycle_size, halves, block, left_rows), jnp.float32)
     arrived = right
     reduced = None
@@ -55,13 +55,15 @@
             current, reduced = lax.optimization_barrier((current, reduced))
             gathered = lax.dynamic_update_slice_in_dim(gathered, reduced[None], (position - step + 1) % cycle_size, 0)
         if step + 1 < cycle_size:
-            arrived = from_behind(arrived, "row", 1)
-        piece = lax.dot_general(current, left, (((0,), (1,)), ((), ())), preferred_element_type=jnp.float32)
+            arrived = from_behind(current, "row", 1)
+        piece = lax.dot_general(current, left, (((1,), (1,)), ((), ())), preferred_element_type=jnp.float32)
         piece = piece.reshape(halves, cores, layers, block, left_rows)
         piece = pair_over(piece, "core", 1)
         reduced = spread_over(piece, "layer", 1)
     gathered = lax.dynamic_update_slice_in_dim(gathered, reduced[None], (position + 1) % cycle_size, 0)
-    ordered = spread_over(gathered.reshape(zhi * ys, block, left_rows), ("zhi", "y"), 0)
+    ordered = gathered.reshape(zhi, ys, block, left_rows)
+    ordered = spread_over(ordered, "y", 1)
+    ordered = pair_over(ordered, "zhi", 0)
     return ordered.T.astype(jnp.bfloat16)
 
 

time: 234 us -> 215 us (0.919)
  waiting for transfers between devices: 143 us -> 132 us
  starting transfers between devices: 40 us -> 33 us
    ppermute x19 -> x15, starting transfers between devices: 37.7 us -> 25.2 us  [spread_over(): lax.ppermute(send, axes, [(i, (i + shift) % n) for i in range(n)])]
    dot_general x4 -> x0, local copies, waits for them, and re-layouts: 11.9 us -> none  [local(): lax.dot_general(current, left, (((0,), (1,)), ((), ())), preferred_elemen...]
    optimization_barrier x0 -> x3, local copies, waits for them, and re-layouts: none -> 10.6 us  [local(): current, reduced = lax.optimization_barrier((current, reduced))]
    ppermute x3, waiting for transfers between devices: 72.5 us -> 62.2 us  [from_behind(): return lax.ppermute(x, axis, [(i, (i + by) % size) for i in range(size)])]
    ppermute x4 -> x5, starting transfers between devices: 0.19 us -> 5.75 us  [pair_over(): return keep + lax.ppermute(send, axis, [(0, 1), (1, 0)])]
    ppermute x19 -> x15, waiting for transfers between devices: 59.9 us -> 54.9 us  [spread_over(): lax.ppermute(send, axes, [(i, (i + shift) % n) for i in range(n)])]
    ppermute x4 -> x5, waiting for transfers between devices: 10.9 us -> 15.2 us  [pair_over(): return keep + lax.ppermute(send, axis, [(0, 1), (1, 0)])]
    transpose x0 -> x1, local copies, waits for them, and re-layouts: none -> 2.56 us  [local(): right = apply_pattern(right_blocks, right_pattern).T]
  transfers between devices with their start and end apart: 26 -> 23, of which waited for: 25 -> 22; matrix products, arithmetic and copies ran while one was open for 6% -> 12% of each run, Pallas kernels for 0% -> 0%
where the time goes in v7:
time: 215 us; the launch traced here: 214 us
  waiting for transfers between devices  132 us (61%)
  starting transfers between devices  33 us (15%)
  local copies, waits for them, and re-layouts  18.1 us (8%)
  matrix products  17.9 us (8%)
  other arithmetic  12 us (6%)
    ppermute x3, waiting for transfers between devices, from_behind(): return lax.ppermute(x, axis, [(i, (i + by) % size) for i in range(size)])  62.2 us
    ppermute x15, waiting for transfers between devices, spread_over(): lax.ppermute(send, axes, [(i, (i + shift) % n) for i in range(n)])  54.9 us
    ppermute x15, starting transfers between devices, spread_over(): lax.ppermute(send, axes, [(i, (i + shift) % n) for i in range(n)])  25.2 us
    dot_general x4, matrix products, local(): lax.dot_general(current, left, (((1,), (1,)), ((), ())), preferred_elemen...  17.9 us
    ppermute x5, waiting for transfers between devices, pair_over(): return keep + lax.ppermute(send, axis, [(0, 1), (1, 0)])  15.2 us
    optimization_barrier x3, local copies, waits for them, and re-layouts, local(): current, reduced = lax.optimization_barrier((current, reduced))  10.6 us
    ppermute x5, starting transfers between devices, pair_over(): return keep + lax.ppermute(send, axis, [(0, 1), (1, 0)])  5.75 us
    mul x2, other arithmetic, apply_pattern(): masked = values.reshape(pattern.shape[0], block, cols) * widened[:, None, :]  4.37 us
  transfers between devices with their start and end apart: 23, of which 22 were waited for; matrix products, arithmetic and copies ran while one was open for 12% of the time, Pallas kernels for 0%

profile of v7, /device:TPU:2, one launch (start us, length us, event | category | flops | bytes accessed | tf_op | source)
XLA Modules:
  0.0 213.6 jit_solution(18182423053150399116)
XLA Ops:
  4.8 2.6 %copy.12 = bf16[512,2048]{1,0:T(8,128)(2,1)} copy(bf16[512,2048]{0,1:T(8,128)(2,1)S(1)} %bitcast.122) | data formatting | bytes 4194304 | tf_op jit(solution)/shard_map/transpose | solution.py:42
  7.7 2.6 %bitcast_multiply_fusion = bf16[1024,2048]{1,0:T(8,128)(2,1)S(1)} fusion(bf16[1024,2048]{1,0:T(8,128)(2,1)} %param.4, bf16[16,2048]{1,0:T(8,128)(2,1)S(1)} %mul.30), kind=kLoop, calls=%fused_computation.8 | loop fusion | flops 2097152 | bytes 8454144 | tf_op jit(solution)/shard_map/mul | solution.py:19
  14.3 2.8 %collective-permute-done.1 = f32[2,4,32,1024]{3,2,1,0:T(8,128)} collective-permute-done((f32[2,4,32,1024]{3,2,1,0:T(8,128)S(1)}, f32[2,4,32,1024]{3,2,1,0:T(8,128)}, u32[]{:S(2)}, u32[]{:S(2)}) %collective-permute-start.1) | collective-permute-done | bytes 1048608 | tf_op jit(solution)/shard_map/ppermute | solution.py:27
  24.5 4.6 %collective-permute-done.2 = f32[2,32,1024]{2,1,0:T(8,128)S(1)} collective-permute-done((f32[2,32,1024]{2,1,0:T(8,128)}, f32[2,32,1024]{2,1,0:T(8,128)S(1)}, u32[]{:S(2)}, u32[]{:S(2)}) %collective-permute-start.2) | collective-permute-done | bytes 262176 | tf_op jit(solution)/shard_map/ppermute | solution.py:36
  29.1 3.1 %collective-permute-done.3 = f32[2,32,1024]{2,1,0:T(8,128)} collective-permute-done((f32[2,32,1024]{2,1,0:T(8,128)}, f32[2,32,1024]{2,1,0:T(8,128)}, u32[]{:S(2)}, u32[]{:S(2)}) %collective-permute-start.3) | collective-permute-done | bytes 262176 | tf_op jit(solution)/shard_map/ppermute | solution.py:36
  32.2 3.8 %collective-permute-done.4 = f32[2,32,1024]{2,1,0:T(8,128)} collective-permute-done((f32[2,32,1024]{2,1,0:T(8,128)}, f32[2,32,1024]{2,1,0:T(8,128)}, u32[]{:S(2)}, u32[]{:S(2)}) %collective-permute-start.4) | collective-permute-done | bytes 262176 | tf_op jit(solution)/shard_map/ppermute | solution.py:36
  37.2 16.0 %collective-permute-done = bf16[512,2048]{0,1:T(8,128)(2,1)} collective-permute-done((bf16[512,2048]{0,1:T(8,128)(2,1)S(1)}, bf16[512,2048]{0,1:T(8,128)(2,1)}, u32[]{:S(2)}, u32[]{:S(2)}) %collective-permute-start) | collective-permute-done | bytes 2097184 | tf_op jit(solution)/shard_map/ppermute | solution.py:12
  53.2 4.0 %copy.13 = bf16[512,2048]{1,0:T(8,128)(2,1)} copy(bf16[512,2048]{0,1:T(8,128)(2,1)} %collective-permute-done) | data formatting | bytes 4194304 | tf_op jit(solution)/shard_map/optimization_barrier | solution.py:55
  57.2 5.2 %fusion.4 = f32[2,2,4,32,1024]{4,3,2,1,0:T(8,128)S(1)} fusion(bf16[2,2,4,32,2048]{4,3,2,1,0:T(8,128)(2,1)} %bitcast.126, bf16[1024,2048]{1,0:T(8,128)(2,1)} %copy-done), kind=kOutput, calls=%fused_computation.4 | convolution fusion | flops 2147483648 | bytes 8388608 | tf_op jit(solution)/shard_map/dot_general | solution.py:59
  62.6 2.6 %collective-permute-done.6 = f32[2,4,32,1024]{3,2,1,0:T(8,128)S(1)} collective-permute-done((f32[2,4,32,1024]{3,2,1,0:T(8,128)S(1)}, f32[2,4,32,1024]{3,2,1,0:T(8,128)S(1)}, u32[]{:S(2)}, u32[]{:S(2)}) %collective-permute-start.6) | collective-permute-done | bytes 1048608 | tf_op jit(solution)/shard_map/ppermute | solution.py:27
  70.4 4.4 %collective-permute-done.7 = f32[2,32,1024]{2,1,0:T(8,128)S(1)} collective-permute-done((f32[2,32,1024]{2,1,0:T(8,128)S(1)}, f32[2,32,1024]{2,1,0:T(8,128)S(1)}, u32[]{:S(2)}, u32[]{:S(2)}) %collective-permute-start.7) | collective-permute-done | bytes 262176 | tf_op jit(solution)/shard_map/ppermute | solution.py:36
  74.8 3.0 %collective-permute-done.8 = f32[2,32,1024]{2,1,0:T(8,128)S(1)} collective-permute-done((f32[2,32,1024]{2,1,0:T(8,128)S(1)}, f32[2,32,1024]{2,1,0:T(8,128)S(1)}, u32[]{:S(2)}, u32[]{:S(2)}) %collective-permute-start.8) | collective-permute-done | bytes 262176 | tf_op jit(solution)/shard_map/ppermute | solution.py:36
  77.8 3.9 %collective-permute-done.9 = f32[2,32,1024]{2,1,0:T(8,128)S(1)} collective-permute-done((f32[2,32,1024]{2,1,0:T(8,128)S(1)}, f32[2,32,1024]{2,1,0:T(8,128)S(1)}, u32[]{:S(2)}, u32[]{:S(2)}) %collective-permute-start.9) | collective-permute-done | bytes 262176 | tf_op jit(solution)/shard_map/ppermute | solution.py:36
  82.5 23.5 %collective-permute-done.5 = bf16[512,2048]{0,1:T(8,128)(2,1)S(1)} collective-permute-done((bf16[512,2048]{0,1:T(8,128)(2,1)}, bf16[512,2048]{0,1:T(8,128)(2,1)S(1)}, u32[]{:S(2)}, u32[]{:S(2)}) %collective-permute-start.5) | collective-permute-done | bytes 2097184 | tf_op jit(solution)/shard_map/ppermute | solution.py:12
  106.0 2.6 %copy.14 = bf16[512,2048]{1,0:T(8,128)(2,1)} copy(bf16[512,2048]{0,1:T(8,128)(2,1)S(1)} %collective-permute-done.5) | data formatting | bytes 4194304 | tf_op jit(solution)/shard_map/optimization_barrier | solution.py:55
  108.6 5.2 %fusion.2 = f32[2,2,4,32,1024]{4,3,2,1,0:T(8,128)S(1)} fusion(bf16[2,2,4,32,2048]{4,3,2,1,0:T(8,128)(2,1)} %bitcast.127, bf16[1024,2048]{1,0:T(8,128)(2,1)} %copy-done), kind=kOutput, calls=%fused_computation.2 | convolution fusion | flops 2147483648 | bytes 8388608 | tf_op jit(solution)/shard_map/dot_general | solution.py:59
  114.0 2.6 %collective-permute-done.11 = f32[2,4,32,1024]{3,2,1,0:T(8,128)S(1)} collective-permute-done((f32[2,4,32,1024]{3,2,1,0:T(8,128)S(1)}, f32[2,4,32,1024]{3,2,1,0:T(8,128)S(1)}, u32[]{:S(2)}, u32[]{:S(2)}) %collective-permute-start.11) | collective-permute-done | bytes 1048608 | tf_op jit(solution)/shard_map/ppermute | solution.py:27
  121.8 4.4 %collective-permute-done.12 = f32[2,32,1024]{2,1,0:T(8,128)S(1)} collective-permute-done((f32[2,32,1024]{2,1,0:T(8,128)S(1)}, f32[2,32,1024]{2,1,0:T(8,128)S(1)}, u32[]{:S(2)}, u32[]{:S(2)}) %collective-permute-start.12) | collective-permute-done | bytes 262176 | tf_op jit(solution)/shard_map/ppermute | solution.py:36
  126.2 3.0 %collective-permute-done.13 = f32[2,32,1024]{2,1,0:T(8,128)S(1)} collective-permute-done((f32[2,32,1024]{2,1,0:T(8,128)S(1)}, f32[2,32,1024]{2,1,0:T(8,128)S(1)}, u32[]{:S(2)}, u32[]{:S(2)}) %collective-permute-start.13) | collective-permute-done | bytes 262176 | tf_op jit(solution)/shard_map/ppermute | solution.py:36
  129.2 3.7 %collective-permute-done.14 = f32[2,32,1024]{2,1,0:T(8,128)S(1)} collective-permute-done((f32[2,32,1024]{2,1,0:T(8,128)S(1)}, f32[2,32,1024]{2,1,0:T(8,128)S(1)}, u32[]{:S(2)}, u32[]{:S(2)}) %collective-permute-start.14) | collective-permute-done | bytes 262176 | tf_op jit(solution)/shard_map/ppermute | solution.py:36
  133.7 22.7 %collective-permute-done.10 = bf16[512,2048]{0,1:T(8,128)(2,1)} collective-permute-done((bf16[512,2048]{0,1:T(8,128)(2,1)S(1)}, bf16[512,2048]{0,1:T(8,128)(2,1)}, u32[]{:S(2)}, u32[]{:S(2)}) %collective-permute-start.10) | collective-permute-done | bytes 2097184 | tf_op jit(solution)/shard_map/ppermute | solution.py:12
  156.4 4.0 %copy.15 = bf16[512,2048]{1,0:T(8,128)(2,1)} copy(bf16[512,2048]{0,1:T(8,128)(2,1)} %collective-permute-done.10) | data formatting | bytes 4194304 | tf_op jit(solution)/shard_map/optimization_barrier | solution.py:55
  160.4 5.2 %fusion = f32[2,2,4,32,1024]{4,3,2,1,0:T(8,128)S(1)} fusion(bf16[2,2,4,32,2048]{4,3,2,1,0:T(8,128)(2,1)} %bitcast.128, bf16[1024,2048]{1,0:T(8,128)(2,1)} %copy-done), kind=kOutput, calls=%fused_computation | convolution fusion | flops 2147483648 | bytes 8388608 | tf_op jit(solution)/shard_map/dot_general | solution.py:59
  166.8 2.8 %collective-permute-done.15 = f32[2,4,32,1024]{3,2,1,0:T(8,128)} collective-permute-done((f32[2,4,32,1024]{3,2,1,0:T(8,128)}, f32[2,4,32,1024]{3,2,1,0:T(8,128)}, u32[]{:S(2)}, u32[]{:S(2)}) %collective-permute-start.15) | collective-permute-done | bytes 1048608 | tf_op jit(solution)/shard_map/ppermute | solution.py:27
  176.0 4.3 %collective-permute-done.16 = f32[2,32,1024]{2,1,0:T(8,128)S(1)} collective-permute-done((f32[2,32,1024]{2,1,0:T(8,128)S(1)}, f32[2,32,1024]{2,1,0:T(8,128)S(1)}, u32[]{:S(2)}, u32[]{:S(2)}) %collective-permute-start.16) | collective-permute-done | bytes 262176 | tf_op jit(solution)/shard_map/ppermute | solution.py:36
  180.4 3.0 %collective-permute-done.17 = f32[2,32,1024]{2,1,0:T(8,128)S(1)} collective-permute-done((f32[2,32,1024]{2,1,0:T(8,128)S(1)}, f32[2,32,1024]{2,1,0:T(8,128)S(1)}, u32[]{:S(2)}, u32[]{:S(2)}) %collective-permute-start.17) | collective-permute-done | bytes 262176 | tf_op jit(solution)/shard_map/ppermute | solution.py:36
  183.4 3.7 %collective-permute-done.18 = f32[2,32,1024]{2,1,0:T(8,128)S(1)} collective-permute-done((f32[2,32,1024]{2,1,0:T(8,128)S(1)}, f32[2,32,1024]{2,1,0:T(8,128)S(1)}, u32[]{:S(2)}, u32[]{:S(2)}) %collective-permute-start.18) | collective-permute-done | bytes 262176 | tf_op jit(solution)/shard_map/ppermute | solution.py:36
  189.0 2.9 %collective-permute-start.20 = (f32[2,32,1024]{2,1,0:T(8,128)S(1)}, f32[2,32,1024]{2,1,0:T(8,128)S(1)}, u32[]{:S(2)}, u32[]{:S(2)}) collective-permute-start(f32[2,32,1024]{2,1,0:T(8,128)S(1)} %get-tuple-element.19), channel_id=1, source_target_pairs={{0,16},{8,24},{16,0},{24,8},{1,17},{9,25},{17,1},{25,9},{2,18},{10... | collective-permute-start | bytes 786440 | tf_op jit(solution)/shard_map/ppermute | solution.py:36
  193.3 3.5 %collective-permute-done.19 = f32[2,32,1024]{2,1,0:T(8,128)S(1)} collective-permute-done((f32[2,32,1024]{2,1,0:T(8,128)S(1)}, f32[2,32,1024]{2,1,0:T(8,128)S(1)}, u32[]{:S(2)}, u32[]{:S(2)}) %collective-permute-start.19) | collective-permute-done | bytes 262176 | tf_op jit(solution)/shard_map/ppermute | solution.py:36
  196.8 6.2 %collective-permute-done.20 = f32[2,32,1024]{2,1,0:T(8,128)S(1)} collective-permute-done((f32[2,32,1024]{2,1,0:T(8,128)S(1)}, f32[2,32,1024]{2,1,0:T(8,128)S(1)}, u32[]{:S(2)}, u32[]{:S(2)}) %collective-permute-start.20) | collective-permute-done | bytes 262176 | tf_op jit(solution)/shard_map/ppermute | solution.py:36
  203.1 5.6 %collective-permute-start.22 = (f32[32,1024]{1,0:T(8,128)S(1)}, f32[32,1024]{1,0:T(8,128)S(1)}, u32[]{:S(2)}, u32[]{:S(2)}) collective-permute-start(f32[32,1024]{1,0:T(8,128)S(1)} %dynamic-slice_bitcast_fusion.19), channel_id=1, source_target_pairs={{0,32},{32,0},{1,33},{33,1},{2,34},{34,2},{3,35},{35,3},{4,36},{36... | collective-permute-start | bytes 393224 | tf_op jit(solution)/shard_map/ppermute | solution.py:27
  208.7 4.3 %collective-permute-done.22 = f32[32,1024]{1,0:T(8,128)S(1)} collective-permute-done((f32[32,1024]{1,0:T(8,128)S(1)}, f32[32,1024]{1,0:T(8,128)S(1)}, u32[]{:S(2)}, u32[]{:S(2)}) %collective-permute-start.22) | collective-permute-done | bytes 131104 | tf_op jit(solution)/shard_map/ppermute | solution.py:27
  (69 shorter events, 41.2 us)
Async XLA Ops:
  2.8 50.4 %collective-permute-start = (bf16[512,2048]{0,1:T(8,128)(2,1)S(1)}, bf16[512,2048]{0,1:T(8,128)(2,1)}, u32[]{:S(2)}, u32[]{:S(2)}) collective-permute-start(bf16[512,2048]{0,1:T(8,128)(2,1)S(1)} %bitcast.121), channel_id=1, source_target_pairs={{0,64},{64,128},{128,192},{192,0},{1,65},{65,129},{129,193},{193,1... | collective-permute-start | bytes 6291464 | tf_op jit(solution)/shard_map/ppermute | solution.py:12
  4.7 2.6 %copy-start.6 = (s32[16,32]{1,0:T(8,128)S(1)}, s32[16,32]{1,0:T(8,128)}, u32[]{:S(2)}) copy-start(s32[16,32]{1,0:T(8,128)} %param.5) | copy-start | bytes 6148
  7.6 2.9 %copy-start.2 = (bf16[512,2048]{1,0:T(8,128)(2,1)S(1)}, bf16[512,2048]{1,0:T(8,128)(2,1)}, u32[]{:S(2)}) copy-start(bf16[512,2048]{1,0:T(8,128)(2,1)} %copy.12) | copy-start | bytes 6291460
  10.3 2.6 %copy-start = (bf16[1024,2048]{1,0:T(8,128)(2,1)}, bf16[1024,2048]{1,0:T(8,128)(2,1)S(1)}, u32[]{:S(2)}) copy-start(bf16[1024,2048]{1,0:T(8,128)(2,1)S(1)} %bitcast_multiply_fusion) | copy-start | bytes 12582916
  12.9 1.4 copy-start.1
  14.3 2.8 %collective-permute-start.1 = (f32[2,4,32,1024]{3,2,1,0:T(8,128)S(1)}, f32[2,4,32,1024]{3,2,1,0:T(8,128)}, u32[]{:S(2)}, u32[]{:S(2)}) collective-permute-start(f32[2,4,32,1024]{3,2,1,0:T(8,128)S(1)} %dynamic-slice_bitcast_fusion.3), channel_id=1, source_target_pairs={{0,4},{4,0},{1,5},{5,1},{2,6},{6,2},{3,7},{7,3},{8,12},{12,8},{9,1... | collective-permute-start | bytes 3145736 | tf_op jit(solution)/shard_map/ppermute | solution.py:27
  19.7 9.4 %collective-permute-start.2 = (f32[2,32,1024]{2,1,0:T(8,128)}, f32[2,32,1024]{2,1,0:T(8,128)S(1)}, u32[]{:S(2)}, u32[]{:S(2)}) collective-permute-start(f32[2,32,1024]{2,1,0:T(8,128)} %get-tuple-element.29), channel_id=1, source_target_pairs={{0,1},{1,2},{2,3},{3,0},{4,5},{5,6},{6,7},{7,4},{8,9},{9,10},{10,1... | collective-permute-start | bytes 786440 | tf_op jit(solution)/shard_map/ppermute | solution.py:36
  21.2 11.0 %collective-permute-start.3 = (f32[2,32,1024]{2,1,0:T(8,128)}, f32[2,32,1024]{2,1,0:T(8,128)}, u32[]{:S(2)}, u32[]{:S(2)}) collective-permute-start(f32[2,32,1024]{2,1,0:T(8,128)} %get-tuple-element.31), channel_id=1, source_target_pairs={{0,2},{1,3},{2,0},{3,1},{4,6},{5,7},{6,4},{7,5},{8,10},{9,11},{10,... | collective-permute-start | bytes 786440 | tf_op jit(solution)/shard_map/ppermute | solution.py:36
  22.3 13.7 %collective-permute-start.4 = (f32[2,32,1024]{2,1,0:T(8,128)}, f32[2,32,1024]{2,1,0:T(8,128)}, u32[]{:S(2)}, u32[]{:S(2)}) collective-permute-start(f32[2,32,1024]{2,1,0:T(8,128)} %get-tuple-element.30), channel_id=1, source_target_pairs={{0,3},{1,0},{2,1},{3,2},{4,7},{5,4},{6,5},{7,6},{8,11},{9,8},{10,9... | collective-permute-start | bytes 786440 | tf_op jit(solution)/shard_map/ppermute | solution.py:36
  29.1 3.1 %copy-start.5 = (f32[2,32,1024]{2,1,0:T(8,128)}, f32[2,32,1024]{2,1,0:T(8,128)S(1)}, u32[]{:S(2)}) copy-start(f32[2,32,1024]{2,1,0:T(8,128)S(1)} %collective-permute-done.2) | copy-start | bytes 786436
  57.2 48.8 %collective-permute-start.5 = (bf16[512,2048]{0,1:T(8,128)(2,1)}, bf16[512,2048]{0,1:T(8,128)(2,1)S(1)}, u32[]{:S(2)}, u32[]{:S(2)}) collective-permute-start(bf16[512,2048]{0,1:T(8,128)(2,1)} %collective-permute-done), channel_id=1, source_target_pairs={{0,64},{64,128},{128,192},{192,0},{1,65},{65,129},{129,193},{193,1... | collective-permute-start | bytes 6291464 | tf_op jit(solution)/shard_map/ppermute | solution.py:12
  62.5 2.7 %collective-permute-start.6 = (f32[2,4,32,1024]{3,2,1,0:T(8,128)S(1)}, f32[2,4,32,1024]{3,2,1,0:T(8,128)S(1)}, u32[]{:S(2)}, u32[]{:S(2)}) collective-permute-start(f32[2,4,32,1024]{3,2,1,0:T(8,128)S(1)} %dynamic-slice_bitcast_fusion.2), channel_id=1, source_target_pairs={{0,4},{4,0},{1,5},{5,1},{2,6},{6,2},{3,7},{7,3},{8,12},{12,8},{9,1... | collective-permute-start | bytes 3145736 | tf_op jit(solution)/shard_map/ppermute | solution.py:27
  65.5 9.2 %collective-permute-start.7 = (f32[2,32,1024]{2,1,0:T(8,128)S(1)}, f32[2,32,1024]{2,1,0:T(8,128)S(1)}, u32[]{:S(2)}, u32[]{:S(2)}) collective-permute-start(f32[2,32,1024]{2,1,0:T(8,128)S(1)} %get-tuple-element.26), channel_id=1, source_target_pairs={{0,1},{1,2},{2,3},{3,0},{4,5},{5,6},{6,7},{7,4},{8,9},{9,10},{10,1... | collective-permute-start | bytes 786440 | tf_op jit(solution)/shard_map/ppermute | solution.py:36
  67.1 10.7 %collective-permute-start.8 = (f32[2,32,1024]{2,1,0:T(8,128)S(1)}, f32[2,32,1024]{2,1,0:T(8,128)S(1)}, u32[]{:S(2)}, u32[]{:S(2)}) collective-permute-start(f32[2,32,1024]{2,1,0:T(8,128)S(1)} %get-tuple-element.28), channel_id=1, source_target_pairs={{0,2},{1,3},{2,0},{3,1},{4,6},{5,7},{6,4},{7,5},{8,10},{9,11},{10,... | collective-permute-start | bytes 786440 | tf_op jit(solution)/shard_map/ppermute | solution.py:36
  68.2 13.5 %collective-permute-start.9 = (f32[2,32,1024]{2,1,0:T(8,128)S(1)}, f32[2,32,1024]{2,1,0:T(8,128)S(1)}, u32[]{:S(2)}, u32[]{:S(2)}) collective-permute-start(f32[2,32,1024]{2,1,0:T(8,128)S(1)} %get-tuple-element.27), channel_id=1, source_target_pairs={{0,3},{1,0},{2,1},{3,2},{4,7},{5,4},{6,5},{7,6},{8,11},{9,8},{10,9... | collective-permute-start | bytes 786440 | tf_op jit(solution)/shard_map/ppermute | solution.py:36
  108.6 47.8 %collective-permute-start.10 = (bf16[512,2048]{0,1:T(8,128)(2,1)S(1)}, bf16[512,2048]{0,1:T(8,128)(2,1)}, u32[]{:S(2)}, u32[]{:S(2)}) collective-permute-start(bf16[512,2048]{0,1:T(8,128)(2,1)S(1)} %collective-permute-done.5), channel_id=1, source_target_pairs={{0,64},{64,128},{128,192},{192,0},{1,65},{65,129},{129,193},{193,1... | collective-permute-start | bytes 6291464 | tf_op jit(solution)/shard_map/ppermute | solution.py:12
  113.9 2.7 %collective-permute-start.11 = (f32[2,4,32,1024]{3,2,1,0:T(8,128)S(1)}, f32[2,4,32,1024]{3,2,1,0:T(8,128)S(1)}, u32[]{:S(2)}, u32[]{:S(2)}) collective-permute-start(f32[2,4,32,1024]{3,2,1,0:T(8,128)S(1)} %dynamic-slice_bitcast_fusion.1), channel_id=1, source_target_pairs={{0,4},{4,0},{1,5},{5,1},{2,6},{6,2},{3,7},{7,3},{8,12},{12,8},{9,1... | collective-permute-start | bytes 3145736 | tf_op jit(solution)/shard_map/ppermute | solution.py:27
  116.9 9.2 %collective-permute-start.12 = (f32[2,32,1024]{2,1,0:T(8,128)S(1)}, f32[2,32,1024]{2,1,0:T(8,128)S(1)}, u32[]{:S(2)}, u32[]{:S(2)}) collective-permute-start(f32[2,32,1024]{2,1,0:T(8,128)S(1)} %get-tuple-element.23), channel_id=1, source_target_pairs={{0,1},{1,2},{2,3},{3,0},{4,5},{5,6},{6,7},{7,4},{8,9},{9,10},{10,1... | collective-permute-start | bytes 786440 | tf_op jit(solution)/shard_map/ppermute | solution.py:36
  118.5 10.7 %collective-permute-start.13 = (f32[2,32,1024]{2,1,0:T(8,128)S(1)}, f32[2,32,1024]{2,1,0:T(8,128)S(1)}, u32[]{:S(2)}, u32[]{:S(2)}) collective-permute-start(f32[2,32,1024]{2,1,0:T(8,128)S(1)} %get-tuple-element.25), channel_id=1, source_target_pairs={{0,2},{1,3},{2,0},{3,1},{4,6},{5,7},{6,4},{7,5},{8,10},{9,11},{10,... | collective-permute-start | bytes 786440 | tf_op jit(solution)/shard_map/ppermute | solution.py:36
  119.2 13.7 %collective-permute-start.14 = (f32[2,32,1024]{2,1,0:T(8,128)S(1)}, f32[2,32,1024]{2,1,0:T(8,128)S(1)}, u32[]{:S(2)}, u32[]{:S(2)}) collective-permute-start(f32[2,32,1024]{2,1,0:T(8,128)S(1)} %get-tuple-element.24), channel_id=1, source_target_pairs={{0,3},{1,0},{2,1},{3,2},{4,7},{5,4},{6,5},{7,6},{8,11},{9,8},{10,9... | collective-permute-start | bytes 786440 | tf_op jit(solution)/shard_map/ppermute | solution.py:36
  166.7 3.0 %collective-permute-start.15 = (f32[2,4,32,1024]{3,2,1,0:T(8,128)}, f32[2,4,32,1024]{3,2,1,0:T(8,128)}, u32[]{:S(2)}, u32[]{:S(2)}) collective-permute-start(f32[2,4,32,1024]{3,2,1,0:T(8,128)} %dynamic-slice_bitcast_fusion), channel_id=1, source_target_pairs={{0,4},{4,0},{1,5},{5,1},{2,6},{6,2},{3,7},{7,3},{8,12},{12,8},{9,1... | collective-permute-start | bytes 3145736 | tf_op jit(solution)/shard_map/ppermute | solution.py:27
  166.8 9.1 %copy-start.3 = (f32[2,32,1024]{2,1,0:T(8,128)S(1)}, f32[2,32,1024]{2,1,0:T(8,128)}, u32[]{:S(2)}) copy-start(f32[2,32,1024]{2,1,0:T(8,128)} %fusion.15) | copy-start | bytes 786436
  166.8 9.2 %copy-start.4 = (f32[2,32,1024]{2,1,0:T(8,128)S(1)}, f32[2,32,1024]{2,1,0:T(8,128)}, u32[]{:S(2)}) copy-start(f32[2,32,1024]{2,1,0:T(8,128)} %fusion.13) | copy-start | bytes 786436
  171.1 9.2 %collective-permute-start.16 = (f32[2,32,1024]{2,1,0:T(8,128)S(1)}, f32[2,32,1024]{2,1,0:T(8,128)S(1)}, u32[]{:S(2)}, u32[]{:S(2)}) collective-permute-start(f32[2,32,1024]{2,1,0:T(8,128)S(1)} %get-tuple-element.20), channel_id=1, source_target_pairs={{0,1},{1,2},{2,3},{3,0},{4,5},{5,6},{6,7},{7,4},{8,9},{9,10},{10,1... | collective-permute-start | bytes 786440 | tf_op jit(solution)/shard_map/ppermute | solution.py:36
  172.7 10.7 %collective-permute-start.17 = (f32[2,32,1024]{2,1,0:T(8,128)S(1)}, f32[2,32,1024]{2,1,0:T(8,128)S(1)}, u32[]{:S(2)}, u32[]{:S(2)}) collective-permute-start(f32[2,32,1024]{2,1,0:T(8,128)S(1)} %get-tuple-element.22), channel_id=1, source_target_pairs={{0,2},{1,3},{2,0},{3,1},{4,6},{5,7},{6,4},{7,5},{8,10},{9,11},{10,... | collective-permute-start | bytes 786440 | tf_op jit(solution)/shard_map/ppermute | solution.py:36
  173.4 13.7 %collective-permute-start.18 = (f32[2,32,1024]{2,1,0:T(8,128)S(1)}, f32[2,32,1024]{2,1,0:T(8,128)S(1)}, u32[]{:S(2)}, u32[]{:S(2)}) collective-permute-start(f32[2,32,1024]{2,1,0:T(8,128)S(1)} %get-tuple-element.21), channel_id=1, source_target_pairs={{0,3},{1,0},{2,1},{3,2},{4,7},{5,4},{6,5},{7,6},{8,11},{9,8},{10,9... | collective-permute-start | bytes 786440 | tf_op jit(solution)/shard_map/ppermute | solution.py:36
  187.3 9.5 %collective-permute-start.19 = (f32[2,32,1024]{2,1,0:T(8,128)S(1)}, f32[2,32,1024]{2,1,0:T(8,128)S(1)}, u32[]{:S(2)}, u32[]{:S(2)}) collective-permute-start(f32[2,32,1024]{2,1,0:T(8,128)S(1)} %get-tuple-element.17), channel_id=1, source_target_pairs={{0,8},{8,16},{16,24},{24,0},{1,9},{9,17},{17,25},{25,1},{2,10},{10... | collective-permute-start | bytes 786440 | tf_op jit(solution)/shard_map/ppermute | solution.py:36
  189.0 14.0 %collective-permute-start.20 = (f32[2,32,1024]{2,1,0:T(8,128)S(1)}, f32[2,32,1024]{2,1,0:T(8,128)S(1)}, u32[]{:S(2)}, u32[]{:S(2)}) collective-permute-start(f32[2,32,1024]{2,1,0:T(8,128)S(1)} %get-tuple-element.19), channel_id=1, source_target_pairs={{0,16},{8,24},{16,0},{24,8},{1,17},{9,25},{17,1},{25,9},{2,18},{10... | collective-permute-start | bytes 786440 | tf_op jit(solution)/shard_map/ppermute | solution.py:36
  191.9 11.1 %collective-permute-start.21 = (f32[2,32,1024]{2,1,0:T(8,128)S(1)}, f32[2,32,1024]{2,1,0:T(8,128)S(1)}, u32[]{:S(2)}, u32[]{:S(2)}) collective-permute-start(f32[2,32,1024]{2,1,0:T(8,128)S(1)} %get-tuple-element.18), channel_id=1, source_target_pairs={{0,24},{8,0},{16,8},{24,16},{1,25},{9,1},{17,9},{25,17},{2,26},{10... | collective-permute-start | bytes 786440 | tf_op jit(solution)/shard_map/ppermute | solution.py:36
  203.1 9.8 %collective-permute-start.22 = (f32[32,1024]{1,0:T(8,128)S(1)}, f32[32,1024]{1,0:T(8,128)S(1)}, u32[]{:S(2)}, u32[]{:S(2)}) collective-permute-start(f32[32,1024]{1,0:T(8,128)S(1)} %dynamic-slice_bitcast_fusion.19), channel_id=1, source_target_pairs={{0,32},{32,0},{1,33},{33,1},{2,34},{34,2},{3,35},{35,3},{4,36},{36... | collective-permute-start | bytes 393224 | tf_op jit(solution)/shard_map/ppermute | solution.py:27

commit v8 on v7

--- a/solution.py
+++ b/solution.py
@@ -52,7 +52,10 @@
     for step in range(cycle_size):
         current = arrived
         if step > 0:
-            current, reduced = lax.optimization_barrier((current, reduced))
+            if step + 1 < cycle_size:
+                current, reduced = lax.optimization_barrier((current, reduced))
+            else:
+                left, reduced = lax.optimization_barrier((left, reduced))
             gathered = lax.dynamic_update_slice_in_dim(gathered, reduced[None], (position - step + 1) % cycle_size, 0)
         if step + 1 < cycle_size:
             arrived = from_behind(current, "row", 1)

time: 215 us -> 208 us (0.967)
  local copies, waits for them, and re-layouts: 18.1 us -> 13.9 us
  matrix products: 17.9 us -> 15.1 us
    optimization_barrier x3 -> x2, local copies, waits for them, and re-layouts: 10.6 us -> 6.43 us  [local(): current, reduced = lax.optimization_barrier((current, reduced))]
    dot_general x4, matrix products: 17.9 us -> 15.1 us  [local(): lax.dot_general(current, left, (((1,), (1,)), ((), ())), preferred_elemen...]
where the time goes in v8:
time: 208 us; the launch traced here: 206 us
  waiting for transfers between devices  132 us (63%)
  starting transfers between devices  33 us (16%)
  matrix products  15.1 us (7%)
  local copies, waits for them, and re-layouts  13.9 us (7%)
  other arithmetic  12 us (6%)
    ppermute x3, waiting for transfers between devices, from_behind(): return lax.ppermute(x, axis, [(i, (i + by) % size) for i in range(size)])  62.2 us
    ppermute x15, waiting for transfers between devices, spread_over(): lax.ppermute(send, axes, [(i, (i + shift) % n) for i in range(n)])  54.9 us
    ppermute x15, starting transfers between devices, spread_over(): lax.ppermute(send, axes, [(i, (i + shift) % n) for i in range(n)])  25.3 us
    ppermute x5, waiting for transfers between devices, pair_over(): return keep + lax.ppermute(send, axis, [(0, 1), (1, 0)])  15.2 us
    dot_general x4, matrix products, local(): lax.dot_general(current, left, (((1,), (1,)), ((), ())), preferred_elemen...  15.1 us
    optimization_barrier x2, local copies, waits for them, and re-layouts, local(): current, reduced = lax.optimization_barrier((current, reduced))  6.43 us
    ppermute x5, starting transfers between devices, pair_over(): return keep + lax.ppermute(send, axis, [(0, 1), (1, 0)])  5.74 us
    mul x2, other arithmetic, apply_pattern(): masked = values.reshape(pattern.shape[0], block, cols) * widened[:, None, :]  4.37 us
  transfers between devices with their start and end apart: 23, of which 22 were waited for; matrix products, arithmetic and copies ran while one was open for 12% of the time, Pallas kernels for 0%

profile of v8, /device:TPU:2, one launch (start us, length us, event | category | flops | bytes accessed | tf_op | source)
XLA Modules:
  0.0 206.5 jit_solution(13114291389655952542)
XLA Ops:
  4.8 2.5 %copy.11 = bf16[512,2048]{1,0:T(8,128)(2,1)} copy(bf16[512,2048]{0,1:T(8,128)(2,1)S(1)} %bitcast.125) | data formatting | bytes 4194304 | tf_op jit(solution)/shard_map/transpose | solution.py:42
  7.5 2.6 %bitcast_multiply_fusion = bf16[1024,2048]{1,0:T(8,128)(2,1)S(1)} fusion(bf16[1024,2048]{1,0:T(8,128)(2,1)} %param.4, bf16[16,2048]{1,0:T(8,128)(2,1)S(1)} %mul.30), kind=kLoop, calls=%fused_computation.6 | loop fusion | flops 2097152 | bytes 8454144 | tf_op jit(solution)/shard_map/mul | solution.py:19
  14.2 2.8 %collective-permute-done.1 = f32[2,4,32,1024]{3,2,1,0:T(8,128)} collective-permute-done((f32[2,4,32,1024]{3,2,1,0:T(8,128)S(1)}, f32[2,4,32,1024]{3,2,1,0:T(8,128)}, u32[]{:S(2)}, u32[]{:S(2)}) %collective-permute-start.1) | collective-permute-done | bytes 1048608 | tf_op jit(solution)/shard_map/ppermute | solution.py:27
  24.4 4.6 %collective-permute-done.2 = f32[2,32,1024]{2,1,0:T(8,128)S(1)} collective-permute-done((f32[2,32,1024]{2,1,0:T(8,128)}, f32[2,32,1024]{2,1,0:T(8,128)S(1)}, u32[]{:S(2)}, u32[]{:S(2)}) %collective-permute-start.2) | collective-permute-done | bytes 262176 | tf_op jit(solution)/shard_map/ppermute | solution.py:36
  29.0 3.1 %collective-permute-done.3 = f32[2,32,1024]{2,1,0:T(8,128)} collective-permute-done((f32[2,32,1024]{2,1,0:T(8,128)}, f32[2,32,1024]{2,1,0:T(8,128)}, u32[]{:S(2)}, u32[]{:S(2)}) %collective-permute-start.3) | collective-permute-done | bytes 262176 | tf_op jit(solution)/shard_map/ppermute | solution.py:36
  32.1 3.8 %collective-permute-done.4 = f32[2,32,1024]{2,1,0:T(8,128)} collective-permute-done((f32[2,32,1024]{2,1,0:T(8,128)}, f32[2,32,1024]{2,1,0:T(8,128)}, u32[]{:S(2)}, u32[]{:S(2)}) %collective-permute-start.4) | collective-permute-done | bytes 262176 | tf_op jit(solution)/shard_map/ppermute | solution.py:36
  37.1 16.1 %collective-permute-done = bf16[512,2048]{0,1:T(8,128)(2,1)} collective-permute-done((bf16[512,2048]{0,1:T(8,128)(2,1)S(1)}, bf16[512,2048]{0,1:T(8,128)(2,1)}, u32[]{:S(2)}, u32[]{:S(2)}) %collective-permute-start) | collective-permute-done | bytes 2097184 | tf_op jit(solution)/shard_map/ppermute | solution.py:12
  53.2 3.9 %copy.12 = bf16[512,2048]{1,0:T(8,128)(2,1)} copy(bf16[512,2048]{0,1:T(8,128)(2,1)} %collective-permute-done) | data formatting | bytes 4194304 | tf_op jit(solution)/shard_map/optimization_barrier | solution.py:56
  57.1 5.2 %fusion.2 = f32[2,2,4,32,1024]{4,3,2,1,0:T(8,128)S(1)} fusion(bf16[2,2,4,32,2048]{4,3,2,1,0:T(8,128)(2,1)} %bitcast.131, bf16[1024,2048]{1,0:T(8,128)(2,1)} %copy-done), kind=kOutput, calls=%fused_computation.2 | convolution fusion | flops 2147483648 | bytes 8388608 | tf_op jit(solution)/shard_map/dot_general | solution.py:62
  62.6 2.6 %collective-permute-done.6 = f32[2,4,32,1024]{3,2,1,0:T(8,128)S(1)} collective-permute-done((f32[2,4,32,1024]{3,2,1,0:T(8,128)S(1)}, f32[2,4,32,1024]{3,2,1,0:T(8,128)S(1)}, u32[]{:S(2)}, u32[]{:S(2)}) %collective-permute-start.6) | collective-permute-done | bytes 1048608 | tf_op jit(solution)/shard_map/ppermute | solution.py:27
  70.3 4.4 %collective-permute-done.7 = f32[2,32,1024]{2,1,0:T(8,128)S(1)} collective-permute-done((f32[2,32,1024]{2,1,0:T(8,128)S(1)}, f32[2,32,1024]{2,1,0:T(8,128)S(1)}, u32[]{:S(2)}, u32[]{:S(2)}) %collective-permute-start.7) | collective-permute-done | bytes 262176 | tf_op jit(solution)/shard_map/ppermute | solution.py:36
  74.7 3.0 %collective-permute-done.8 = f32[2,32,1024]{2,1,0:T(8,128)S(1)} collective-permute-done((f32[2,32,1024]{2,1,0:T(8,128)S(1)}, f32[2,32,1024]{2,1,0:T(8,128)S(1)}, u32[]{:S(2)}, u32[]{:S(2)}) %collective-permute-start.8) | collective-permute-done | bytes 262176 | tf_op jit(solution)/shard_map/ppermute | solution.py:36
  77.7 3.9 %collective-permute-done.9 = f32[2,32,1024]{2,1,0:T(8,128)S(1)} collective-permute-done((f32[2,32,1024]{2,1,0:T(8,128)S(1)}, f32[2,32,1024]{2,1,0:T(8,128)S(1)}, u32[]{:S(2)}, u32[]{:S(2)}) %collective-permute-start.9) | collective-permute-done | bytes 262176 | tf_op jit(solution)/shard_map/ppermute | solution.py:36
  82.4 23.5 %collective-permute-done.5 = bf16[512,2048]{0,1:T(8,128)(2,1)S(1)} collective-permute-done((bf16[512,2048]{0,1:T(8,128)(2,1)}, bf16[512,2048]{0,1:T(8,128)(2,1)S(1)}, u32[]{:S(2)}, u32[]{:S(2)}) %collective-permute-start.5) | collective-permute-done | bytes 2097184 | tf_op jit(solution)/shard_map/ppermute | solution.py:12
  106.0 2.5 %copy.13 = bf16[512,2048]{1,0:T(8,128)(2,1)} copy(bf16[512,2048]{0,1:T(8,128)(2,1)S(1)} %collective-permute-done.5) | data formatting | bytes 4194304 | tf_op jit(solution)/shard_map/optimization_barrier | solution.py:56
  108.5 5.2 %fusion = f32[2,2,4,32,1024]{4,3,2,1,0:T(8,128)S(1)} fusion(bf16[2,2,4,32,2048]{4,3,2,1,0:T(8,128)(2,1)} %bitcast.132, bf16[1024,2048]{1,0:T(8,128)(2,1)} %copy-done), kind=kOutput, calls=%fused_computation | convolution fusion | flops 2147483648 | bytes 8388608 | tf_op jit(solution)/shard_map/dot_general | solution.py:62
  113.9 2.6 %collective-permute-done.10 = f32[2,4,32,1024]{3,2,1,0:T(8,128)S(1)} collective-permute-done((f32[2,4,32,1024]{3,2,1,0:T(8,128)S(1)}, f32[2,4,32,1024]{3,2,1,0:T(8,128)S(1)}, u32[]{:S(2)}, u32[]{:S(2)}) %collective-permute-start.10) | collective-permute-done | bytes 1048608 | tf_op jit(solution)/shard_map/ppermute | solution.py:27
  119.1 2.5 %collective-permute-start.13 = (f32[2,32,1024]{2,1,0:T(8,128)S(1)}, f32[2,32,1024]{2,1,0:T(8,128)S(1)}, u32[]{:S(2)}, u32[]{:S(2)}) collective-permute-start(f32[2,32,1024]{2,1,0:T(8,128)S(1)} %get-tuple-element.24), channel_id=1, source_target_pairs={{0,3},{1,0},{2,1},{3,2},{4,7},{5,4},{6,5},{7,6},{8,11},{9,8},{10,9... | collective-permute-start | bytes 786440 | tf_op jit(solution)/shard_map/ppermute | solution.py:36
  121.6 4.4 %collective-permute-done.11 = f32[2,32,1024]{2,1,0:T(8,128)S(1)} collective-permute-done((f32[2,32,1024]{2,1,0:T(8,128)S(1)}, f32[2,32,1024]{2,1,0:T(8,128)S(1)}, u32[]{:S(2)}, u32[]{:S(2)}) %collective-permute-start.11) | collective-permute-done | bytes 262176 | tf_op jit(solution)/shard_map/ppermute | solution.py:36
  126.0 3.0 %collective-permute-done.12 = f32[2,32,1024]{2,1,0:T(8,128)S(1)} collective-permute-done((f32[2,32,1024]{2,1,0:T(8,128)S(1)}, f32[2,32,1024]{2,1,0:T(8,128)S(1)}, u32[]{:S(2)}, u32[]{:S(2)}) %collective-permute-start.12) | collective-permute-done | bytes 262176 | tf_op jit(solution)/shard_map/ppermute | solution.py:36
  129.1 3.7 %collective-permute-done.13 = f32[2,32,1024]{2,1,0:T(8,128)S(1)} collective-permute-done((f32[2,32,1024]{2,1,0:T(8,128)S(1)}, f32[2,32,1024]{2,1,0:T(8,128)S(1)}, u32[]{:S(2)}, u32[]{:S(2)}) %collective-permute-start.13) | collective-permute-done | bytes 262176 | tf_op jit(solution)/shard_map/ppermute | solution.py:36
  133.6 22.6 %collective-permute-done.14 = bf16[512,2048]{0,1:T(8,128)(2,1)S(1)} collective-permute-done((bf16[512,2048]{0,1:T(8,128)(2,1)S(1)}, bf16[512,2048]{0,1:T(8,128)(2,1)S(1)}, u32[]{:S(2)}, u32[]{:S(2)}) %collective-permute-start.14) | collective-permute-done | bytes 2097184 | tf_op jit(solution)/shard_map/ppermute | solution.py:12
  159.8 2.8 %collective-permute-done.15 = f32[2,4,32,1024]{3,2,1,0:T(8,128)} collective-permute-done((f32[2,4,32,1024]{3,2,1,0:T(8,128)}, f32[2,4,32,1024]{3,2,1,0:T(8,128)}, u32[]{:S(2)}, u32[]{:S(2)}) %collective-permute-start.15) | collective-permute-done | bytes 1048608 | tf_op jit(solution)/shard_map/ppermute | solution.py:27
  166.3 2.5 %collective-permute-start.18 = (f32[2,32,1024]{2,1,0:T(8,128)S(1)}, f32[2,32,1024]{2,1,0:T(8,128)S(1)}, u32[]{:S(2)}, u32[]{:S(2)}) collective-permute-start(f32[2,32,1024]{2,1,0:T(8,128)S(1)} %get-tuple-element.21), channel_id=1, source_target_pairs={{0,3},{1,0},{2,1},{3,2},{4,7},{5,4},{6,5},{7,6},{8,11},{9,8},{10,9... | collective-permute-start | bytes 786440 | tf_op jit(solution)/shard_map/ppermute | solution.py:36
  168.9 4.3 %collective-permute-done.16 = f32[2,32,1024]{2,1,0:T(8,128)S(1)} collective-permute-done((f32[2,32,1024]{2,1,0:T(8,128)S(1)}, f32[2,32,1024]{2,1,0:T(8,128)S(1)}, u32[]{:S(2)}, u32[]{:S(2)}) %collective-permute-start.16) | collective-permute-done | bytes 262176 | tf_op jit(solution)/shard_map/ppermute | solution.py:36
  173.3 3.0 %collective-permute-done.17 = f32[2,32,1024]{2,1,0:T(8,128)S(1)} collective-permute-done((f32[2,32,1024]{2,1,0:T(8,128)S(1)}, f32[2,32,1024]{2,1,0:T(8,128)S(1)}, u32[]{:S(2)}, u32[]{:S(2)}) %collective-permute-start.17) | collective-permute-done | bytes 262176 | tf_op jit(solution)/shard_map/ppermute | solution.py:36
  176.3 3.7 %collective-permute-done.18 = f32[2,32,1024]{2,1,0:T(8,128)S(1)} collective-permute-done((f32[2,32,1024]{2,1,0:T(8,128)S(1)}, f32[2,32,1024]{2,1,0:T(8,128)S(1)}, u32[]{:S(2)}, u32[]{:S(2)}) %collective-permute-start.18) | collective-permute-done | bytes 262176 | tf_op jit(solution)/shard_map/ppermute | solution.py:36
  181.9 2.9 %collective-permute-start.20 = (f32[2,32,1024]{2,1,0:T(8,128)S(1)}, f32[2,32,1024]{2,1,0:T(8,128)S(1)}, u32[]{:S(2)}, u32[]{:S(2)}) collective-permute-start(f32[2,32,1024]{2,1,0:T(8,128)S(1)} %get-tuple-element.19), channel_id=1, source_target_pairs={{0,16},{8,24},{16,0},{24,8},{1,17},{9,25},{17,1},{25,9},{2,18},{10... | collective-permute-start | bytes 786440 | tf_op jit(solution)/shard_map/ppermute | solution.py:36
  186.2 3.5 %collective-permute-done.19 = f32[2,32,1024]{2,1,0:T(8,128)S(1)} collective-permute-done((f32[2,32,1024]{2,1,0:T(8,128)S(1)}, f32[2,32,1024]{2,1,0:T(8,128)S(1)}, u32[]{:S(2)}, u32[]{:S(2)}) %collective-permute-start.19) | collective-permute-done | bytes 262176 | tf_op jit(solution)/shard_map/ppermute | solution.py:36
  189.7 6.2 %collective-permute-done.20 = f32[2,32,1024]{2,1,0:T(8,128)S(1)} collective-permute-done((f32[2,32,1024]{2,1,0:T(8,128)S(1)}, f32[2,32,1024]{2,1,0:T(8,128)S(1)}, u32[]{:S(2)}, u32[]{:S(2)}) %collective-permute-start.20) | collective-permute-done | bytes 262176 | tf_op jit(solution)/shard_map/ppermute | solution.py:36
  196.0 5.6 %collective-permute-start.22 = (f32[32,1024]{1,0:T(8,128)S(1)}, f32[32,1024]{1,0:T(8,128)S(1)}, u32[]{:S(2)}, u32[]{:S(2)}) collective-permute-start(f32[32,1024]{1,0:T(8,128)S(1)} %dynamic-slice_bitcast_fusion.19), channel_id=1, source_target_pairs={{0,32},{32,0},{1,33},{33,1},{2,34},{34,2},{3,35},{35,3},{4,36},{36... | collective-permute-start | bytes 393224 | tf_op jit(solution)/shard_map/ppermute | solution.py:27
  201.6 4.3 %collective-permute-done.22 = f32[32,1024]{1,0:T(8,128)S(1)} collective-permute-done((f32[32,1024]{1,0:T(8,128)S(1)}, f32[32,1024]{1,0:T(8,128)S(1)}, u32[]{:S(2)}, u32[]{:S(2)}) %collective-permute-start.22) | collective-permute-done | bytes 131104 | tf_op jit(solution)/shard_map/ppermute | solution.py:27
  (70 shorter events, 38.5 us)
Async XLA Ops:
  2.8 50.4 %collective-permute-start = (bf16[512,2048]{0,1:T(8,128)(2,1)S(1)}, bf16[512,2048]{0,1:T(8,128)(2,1)}, u32[]{:S(2)}, u32[]{:S(2)}) collective-permute-start(bf16[512,2048]{0,1:T(8,128)(2,1)S(1)} %bitcast.124), channel_id=1, source_target_pairs={{0,64},{64,128},{128,192},{192,0},{1,65},{65,129},{129,193},{193,1... | collective-permute-start | bytes 6291464 | tf_op jit(solution)/shard_map/ppermute | solution.py:12
  4.7 2.5 %copy-start.7 = (s32[16,32]{1,0:T(8,128)S(1)}, s32[16,32]{1,0:T(8,128)}, u32[]{:S(2)}) copy-start(s32[16,32]{1,0:T(8,128)} %param.5) | copy-start | bytes 6148
  7.5 2.9 %copy-start.3 = (bf16[512,2048]{1,0:T(8,128)(2,1)S(1)}, bf16[512,2048]{1,0:T(8,128)(2,1)}, u32[]{:S(2)}) copy-start(bf16[512,2048]{1,0:T(8,128)(2,1)} %copy.11) | copy-start | bytes 6291460
  10.2 2.6 %copy-start = (bf16[1024,2048]{1,0:T(8,128)(2,1)}, bf16[1024,2048]{1,0:T(8,128)(2,1)S(1)}, u32[]{:S(2)}) copy-start(bf16[1024,2048]{1,0:T(8,128)(2,1)S(1)} %bitcast_multiply_fusion) | copy-start | bytes 12582916
  12.8 1.4 copy-start.2
  14.2 2.8 %collective-permute-start.1 = (f32[2,4,32,1024]{3,2,1,0:T(8,128)S(1)}, f32[2,4,32,1024]{3,2,1,0:T(8,128)}, u32[]{:S(2)}, u32[]{:S(2)}) collective-permute-start(f32[2,4,32,1024]{3,2,1,0:T(8,128)S(1)} %dynamic-slice_bitcast_fusion.3), channel_id=1, source_target_pairs={{0,4},{4,0},{1,5},{5,1},{2,6},{6,2},{3,7},{7,3},{8,12},{12,8},{9,1... | collective-permute-start | bytes 3145736 | tf_op jit(solution)/shard_map/ppermute | solution.py:27
  19.6 9.4 %collective-permute-start.2 = (f32[2,32,1024]{2,1,0:T(8,128)}, f32[2,32,1024]{2,1,0:T(8,128)S(1)}, u32[]{:S(2)}, u32[]{:S(2)}) collective-permute-start(f32[2,32,1024]{2,1,0:T(8,128)} %get-tuple-element.29), channel_id=1, source_target_pairs={{0,1},{1,2},{2,3},{3,0},{4,5},{5,6},{6,7},{7,4},{8,9},{9,10},{10,1... | collective-permute-start | bytes 786440 | tf_op jit(solution)/shard_map/ppermute | solution.py:36
  21.1 11.0 %collective-permute-start.3 = (f32[2,32,1024]{2,1,0:T(8,128)}, f32[2,32,1024]{2,1,0:T(8,128)}, u32[]{:S(2)}, u32[]{:S(2)}) collective-permute-start(f32[2,32,1024]{2,1,0:T(8,128)} %get-tuple-element.31), channel_id=1, source_target_pairs={{0,2},{1,3},{2,0},{3,1},{4,6},{5,7},{6,4},{7,5},{8,10},{9,11},{10,... | collective-permute-start | bytes 786440 | tf_op jit(solution)/shard_map/ppermute | solution.py:36
  22.2 13.7 %collective-permute-start.4 = (f32[2,32,1024]{2,1,0:T(8,128)}, f32[2,32,1024]{2,1,0:T(8,128)}, u32[]{:S(2)}, u32[]{:S(2)}) collective-permute-start(f32[2,32,1024]{2,1,0:T(8,128)} %get-tuple-element.30), channel_id=1, source_target_pairs={{0,3},{1,0},{2,1},{3,2},{4,7},{5,4},{6,5},{7,6},{8,11},{9,8},{10,9... | collective-permute-start | bytes 786440 | tf_op jit(solution)/shard_map/ppermute | solution.py:36
  29.0 3.1 %copy-start.6 = (f32[2,32,1024]{2,1,0:T(8,128)}, f32[2,32,1024]{2,1,0:T(8,128)S(1)}, u32[]{:S(2)}) copy-start(f32[2,32,1024]{2,1,0:T(8,128)S(1)} %collective-permute-done.2) | copy-start | bytes 786436
  57.1 48.8 %collective-permute-start.5 = (bf16[512,2048]{0,1:T(8,128)(2,1)}, bf16[512,2048]{0,1:T(8,128)(2,1)S(1)}, u32[]{:S(2)}, u32[]{:S(2)}) collective-permute-start(bf16[512,2048]{0,1:T(8,128)(2,1)} %collective-permute-done), channel_id=1, source_target_pairs={{0,64},{64,128},{128,192},{192,0},{1,65},{65,129},{129,193},{193,1... | collective-permute-start | bytes 6291464 | tf_op jit(solution)/shard_map/ppermute | solution.py:12
  62.5 2.7 %collective-permute-start.6 = (f32[2,4,32,1024]{3,2,1,0:T(8,128)S(1)}, f32[2,4,32,1024]{3,2,1,0:T(8,128)S(1)}, u32[]{:S(2)}, u32[]{:S(2)}) collective-permute-start(f32[2,4,32,1024]{3,2,1,0:T(8,128)S(1)} %dynamic-slice_bitcast_fusion.2), channel_id=1, source_target_pairs={{0,4},{4,0},{1,5},{5,1},{2,6},{6,2},{3,7},{7,3},{8,12},{12,8},{9,1... | collective-permute-start | bytes 3145736 | tf_op jit(solution)/shard_map/ppermute | solution.py:27
  65.5 9.2 %collective-permute-start.7 = (f32[2,32,1024]{2,1,0:T(8,128)S(1)}, f32[2,32,1024]{2,1,0:T(8,128)S(1)}, u32[]{:S(2)}, u32[]{:S(2)}) collective-permute-start(f32[2,32,1024]{2,1,0:T(8,128)S(1)} %get-tuple-element.26), channel_id=1, source_target_pairs={{0,1},{1,2},{2,3},{3,0},{4,5},{5,6},{6,7},{7,4},{8,9},{9,10},{10,1... | collective-permute-start | bytes 786440 | tf_op jit(solution)/shard_map/ppermute | solution.py:36
  67.0 10.7 %collective-permute-start.8 = (f32[2,32,1024]{2,1,0:T(8,128)S(1)}, f32[2,32,1024]{2,1,0:T(8,128)S(1)}, u32[]{:S(2)}, u32[]{:S(2)}) collective-permute-start(f32[2,32,1024]{2,1,0:T(8,128)S(1)} %get-tuple-element.28), channel_id=1, source_target_pairs={{0,2},{1,3},{2,0},{3,1},{4,6},{5,7},{6,4},{7,5},{8,10},{9,11},{10,... | collective-permute-start | bytes 786440 | tf_op jit(solution)/shard_map/ppermute | solution.py:36
  68.2 13.5 %collective-permute-start.9 = (f32[2,32,1024]{2,1,0:T(8,128)S(1)}, f32[2,32,1024]{2,1,0:T(8,128)S(1)}, u32[]{:S(2)}, u32[]{:S(2)}) collective-permute-start(f32[2,32,1024]{2,1,0:T(8,128)S(1)} %get-tuple-element.27), channel_id=1, source_target_pairs={{0,3},{1,0},{2,1},{3,2},{4,7},{5,4},{6,5},{7,6},{8,11},{9,8},{10,9... | collective-permute-start | bytes 786440 | tf_op jit(solution)/shard_map/ppermute | solution.py:36
  108.5 47.7 %collective-permute-start.14 = (bf16[512,2048]{0,1:T(8,128)(2,1)S(1)}, bf16[512,2048]{0,1:T(8,128)(2,1)S(1)}, u32[]{:S(2)}, u32[]{:S(2)}) collective-permute-start(bf16[512,2048]{0,1:T(8,128)(2,1)S(1)} %collective-permute-done.5), channel_id=1, source_target_pairs={{0,64},{64,128},{128,192},{192,0},{1,65},{65,129},{129,193},{193,1... | collective-permute-start | bytes 6291464 | tf_op jit(solution)/shard_map/ppermute | solution.py:12
  113.8 2.7 %collective-permute-start.10 = (f32[2,4,32,1024]{3,2,1,0:T(8,128)S(1)}, f32[2,4,32,1024]{3,2,1,0:T(8,128)S(1)}, u32[]{:S(2)}, u32[]{:S(2)}) collective-permute-start(f32[2,4,32,1024]{3,2,1,0:T(8,128)S(1)} %dynamic-slice_bitcast_fusion.1), channel_id=1, source_target_pairs={{0,4},{4,0},{1,5},{5,1},{2,6},{6,2},{3,7},{7,3},{8,12},{12,8},{9,1... | collective-permute-start | bytes 3145736 | tf_op jit(solution)/shard_map/ppermute | solution.py:27
  116.5 39.6 %copy-start.1 = (bf16[1024,2048]{1,0:T(8,128)(2,1)S(1)}, bf16[1024,2048]{1,0:T(8,128)(2,1)}, u32[]{:S(2)}) copy-start(bf16[1024,2048]{1,0:T(8,128)(2,1)} %copy-done) | copy-start | bytes 12582916
  116.8 9.2 %collective-permute-start.11 = (f32[2,32,1024]{2,1,0:T(8,128)S(1)}, f32[2,32,1024]{2,1,0:T(8,128)S(1)}, u32[]{:S(2)}, u32[]{:S(2)}) collective-permute-start(f32[2,32,1024]{2,1,0:T(8,128)S(1)} %get-tuple-element.23), channel_id=1, source_target_pairs={{0,1},{1,2},{2,3},{3,0},{4,5},{5,6},{6,7},{7,4},{8,9},{9,10},{10,1... | collective-permute-start | bytes 786440 | tf_op jit(solution)/shard_map/ppermute | solution.py:36
  118.4 10.7 %collective-permute-start.12 = (f32[2,32,1024]{2,1,0:T(8,128)S(1)}, f32[2,32,1024]{2,1,0:T(8,128)S(1)}, u32[]{:S(2)}, u32[]{:S(2)}) collective-permute-start(f32[2,32,1024]{2,1,0:T(8,128)S(1)} %get-tuple-element.25), channel_id=1, source_target_pairs={{0,2},{1,3},{2,0},{3,1},{4,6},{5,7},{6,4},{7,5},{8,10},{9,11},{10,... | collective-permute-start | bytes 786440 | tf_op jit(solution)/shard_map/ppermute | solution.py:36
  119.1 13.7 %collective-permute-start.13 = (f32[2,32,1024]{2,1,0:T(8,128)S(1)}, f32[2,32,1024]{2,1,0:T(8,128)S(1)}, u32[]{:S(2)}, u32[]{:S(2)}) collective-permute-start(f32[2,32,1024]{2,1,0:T(8,128)S(1)} %get-tuple-element.24), channel_id=1, source_target_pairs={{0,3},{1,0},{2,1},{3,2},{4,7},{5,4},{6,5},{7,6},{8,11},{9,8},{10,9... | collective-permute-start | bytes 786440 | tf_op jit(solution)/shard_map/ppermute | solution.py:36
  159.6 3.0 %collective-permute-start.15 = (f32[2,4,32,1024]{3,2,1,0:T(8,128)}, f32[2,4,32,1024]{3,2,1,0:T(8,128)}, u32[]{:S(2)}, u32[]{:S(2)}) collective-permute-start(f32[2,4,32,1024]{3,2,1,0:T(8,128)} %dynamic-slice_bitcast_fusion), channel_id=1, source_target_pairs={{0,4},{4,0},{1,5},{5,1},{2,6},{6,2},{3,7},{7,3},{8,12},{12,8},{9,1... | collective-permute-start | bytes 3145736 | tf_op jit(solution)/shard_map/ppermute | solution.py:27
  159.7 9.1 %copy-start.4 = (f32[2,32,1024]{2,1,0:T(8,128)S(1)}, f32[2,32,1024]{2,1,0:T(8,128)}, u32[]{:S(2)}) copy-start(f32[2,32,1024]{2,1,0:T(8,128)} %fusion.13) | copy-start | bytes 786436
  159.7 9.2 %copy-start.5 = (f32[2,32,1024]{2,1,0:T(8,128)S(1)}, f32[2,32,1024]{2,1,0:T(8,128)}, u32[]{:S(2)}) copy-start(f32[2,32,1024]{2,1,0:T(8,128)} %fusion.11) | copy-start | bytes 786436
  164.0 9.2 %collective-permute-start.16 = (f32[2,32,1024]{2,1,0:T(8,128)S(1)}, f32[2,32,1024]{2,1,0:T(8,128)S(1)}, u32[]{:S(2)}, u32[]{:S(2)}) collective-permute-start(f32[2,32,1024]{2,1,0:T(8,128)S(1)} %get-tuple-element.20), channel_id=1, source_target_pairs={{0,1},{1,2},{2,3},{3,0},{4,5},{5,6},{6,7},{7,4},{8,9},{9,10},{10,1... | collective-permute-start | bytes 786440 | tf_op jit(solution)/shard_map/ppermute | solution.py:36
  165.6 10.7 %collective-permute-start.17 = (f32[2,32,1024]{2,1,0:T(8,128)S(1)}, f32[2,32,1024]{2,1,0:T(8,128)S(1)}, u32[]{:S(2)}, u32[]{:S(2)}) collective-permute-start(f32[2,32,1024]{2,1,0:T(8,128)S(1)} %get-tuple-element.22), channel_id=1, source_target_pairs={{0,2},{1,3},{2,0},{3,1},{4,6},{5,7},{6,4},{7,5},{8,10},{9,11},{10,... | collective-permute-start | bytes 786440 | tf_op jit(solution)/shard_map/ppermute | solution.py:36
  166.3 13.7 %collective-permute-start.18 = (f32[2,32,1024]{2,1,0:T(8,128)S(1)}, f32[2,32,1024]{2,1,0:T(8,128)S(1)}, u32[]{:S(2)}, u32[]{:S(2)}) collective-permute-start(f32[2,32,1024]{2,1,0:T(8,128)S(1)} %get-tuple-element.21), channel_id=1, source_target_pairs={{0,3},{1,0},{2,1},{3,2},{4,7},{5,4},{6,5},{7,6},{8,11},{9,8},{10,9... | collective-permute-start | bytes 786440 | tf_op jit(solution)/shard_map/ppermute | solution.py:36
  180.2 9.5 %collective-permute-start.19 = (f32[2,32,1024]{2,1,0:T(8,128)S(1)}, f32[2,32,1024]{2,1,0:T(8,128)S(1)}, u32[]{:S(2)}, u32[]{:S(2)}) collective-permute-start(f32[2,32,1024]{2,1,0:T(8,128)S(1)} %get-tuple-element.17), channel_id=1, source_target_pairs={{0,8},{8,16},{16,24},{24,0},{1,9},{9,17},{17,25},{25,1},{2,10},{10... | collective-permute-start | bytes 786440 | tf_op jit(solution)/shard_map/ppermute | solution.py:36
  181.9 14.0 %collective-permute-start.20 = (f32[2,32,1024]{2,1,0:T(8,128)S(1)}, f32[2,32,1024]{2,1,0:T(8,128)S(1)}, u32[]{:S(2)}, u32[]{:S(2)}) collective-permute-start(f32[2,32,1024]{2,1,0:T(8,128)S(1)} %get-tuple-element.19), channel_id=1, source_target_pairs={{0,16},{8,24},{16,0},{24,8},{1,17},{9,25},{17,1},{25,9},{2,18},{10... | collective-permute-start | bytes 786440 | tf_op jit(solution)/shard_map/ppermute | solution.py:36
  184.8 11.1 %collective-permute-start.21 = (f32[2,32,1024]{2,1,0:T(8,128)S(1)}, f32[2,32,1024]{2,1,0:T(8,128)S(1)}, u32[]{:S(2)}, u32[]{:S(2)}) collective-permute-start(f32[2,32,1024]{2,1,0:T(8,128)S(1)} %get-tuple-element.18), channel_id=1, source_target_pairs={{0,24},{8,0},{16,8},{24,16},{1,25},{9,1},{17,9},{25,17},{2,26},{10... | collective-permute-start | bytes 786440 | tf_op jit(solution)/shard_map/ppermute | solution.py:36
  196.0 9.8 %collective-permute-start.22 = (f32[32,1024]{1,0:T(8,128)S(1)}, f32[32,1024]{1,0:T(8,128)S(1)}, u32[]{:S(2)}, u32[]{:S(2)}) collective-permute-start(f32[32,1024]{1,0:T(8,128)S(1)} %dynamic-slice_bitcast_fusion.19), channel_id=1, source_target_pairs={{0,32},{32,0},{1,33},{33,1},{2,34},{34,2},{3,35},{35,3},{4,36},{36... | collective-permute-start | bytes 393224 | tf_op jit(solution)/shard_map/ppermute | solution.py:27

commit v9 on v8

--- a/solution.py
+++ b/solution.py
@@ -59,10 +59,12 @@
             gathered = lax.dynamic_update_slice_in_dim(gathered, reduced[None], (position - step + 1) % cycle_size, 0)
         if step + 1 < cycle_size:
             arrived = from_behind(current, "row", 1)
-        piece = lax.dot_general(current, left, (((1,), (1,)), ((), ())), preferred_element_type=jnp.float32)
-        piece = piece.reshape(halves, cores, layers, block, left_rows)
-        piece = pair_over(piece, "core", 1)
-        reduced = spread_over(piece, "layer", 1)
+        by_core = current.reshape(halves, cores, layers * block, current.shape[1])
+        core = lax.axis_index("core")
+        product = lambda rows: lax.dot_general(rows, left, (((2,), (1,)), ((), ())), preferred_element_type=jnp.float32)
+        sent = lax.ppermute(product(lax.dynamic_index_in_dim(by_core, 1 - core, 1, keepdims=False)), "core", [(0, 1), (1, 0)])
+        piece = product(lax.dynamic_index_in_dim(by_core, core, 1, keepdims=False)) + sent
+        reduced = spread_over(piece.reshape(halves, layers, block, left_rows), "layer", 1)
     gathered = lax.dynamic_update_slice_in_dim(gathered, reduced[None], (position + 1) % cycle_size, 0)
     ordered = gathered.reshape(zhi, ys, block, left_rows)
     ordered = spread_over(ordered, "y", 1)

time: 208 us -> 279 us (1.34)
  local copies, waits for them, and re-layouts: 13.9 us -> 63.8 us
  matrix products: 15.1 us -> 31.5 us
  waiting for transfers between devices: 132 us -> 141 us
  other arithmetic: 12 us -> 8.73 us
    unnamed x16 -> x24, local copies, waits for them, and re-layouts: 1.49 us -> 30.6 us
    dynamic_slice x0 -> x4, local copies, waits for them, and re-layouts: none -> 21.8 us  [local(): lax.dynamic_index_in_dim(by_core, core, 1, keepdims=False)]
    dot_general x4 -> x8, matrix products: 15.1 us -> 31.5 us  [local(): lax.dot_general(rows, left, (((2,), (1,)), ((), ())), preferred_element_t...]
    ppermute x3, waiting for transfers between devices: 62.2 us -> 78 us  [from_behind(): return lax.ppermute(x, axis, [(i, (i + by) % size) for i in range(size)])]
    ppermute x5 -> x1, waiting for transfers between devices: 15.2 us -> 4.24 us  [pair_over(): return keep + lax.ppermute(send, axis, [(0, 1), (1, 0)])]
    reshape x0 -> x4, local copies, waits for them, and re-layouts: none -> 10.2 us  [local(): by_core = current.reshape(halves, cores, layers * block, current.shape[1])]
    optimization_barrier x2 -> x0, local copies, waits for them, and re-layouts: 6.43 us -> none  [local(): current, reduced = lax.optimization_barrier((current, reduced))]
    add x4 -> x0, other arithmetic: 3.41 us -> none  [pair_over(): return keep + lax.ppermute(send, axis, [(0, 1), (1, 0)])]
  transfers between devices with their start and end apart: 23 -> 23, of which waited for: 22 -> 21; matrix products, arithmetic and copies ran while one was open for 12% -> 9% of each run, Pallas kernels for 0% -> 0%
where the time goes in v9:
time: 279 us; the launch traced here: 277 us
  waiting for transfers between devices  141 us (51%)
  local copies, waits for them, and re-layouts  63.8 us (23%)
  starting transfers between devices  32 us (11%)
  matrix products  31.5 us (11%)
  other arithmetic  8.73 us (3%)
    ppermute x3, waiting for transfers between devices, from_behind(): return lax.ppermute(x, axis, [(i, (i + by) % size) for i in range(size)])  78 us
    ppermute x15, waiting for transfers between devices, spread_over(): lax.ppermute(send, axes, [(i, (i + shift) % n) for i in range(n)])  57.9 us
    dot_general x8, matrix products, local(): lax.dot_general(rows, left, (((2,), (1,)), ((), ())), preferred_element_t...  31.5 us
    unnamed x24, local copies, waits for them, and re-layouts  30.6 us
    ppermute x15, starting transfers between devices, spread_over(): lax.ppermute(send, axes, [(i, (i + shift) % n) for i in range(n)])  24.6 us
    dynamic_slice x4, local copies, waits for them, and re-layouts, local(): lax.dynamic_index_in_dim(by_core, core, 1, keepdims=False)  21.8 us
    reshape x4, local copies, waits for them, and re-layouts, local(): by_core = current.reshape(halves, cores, layers * block, current.shape[1])  10.2 us
    mul x2, other arithmetic, apply_pattern(): masked = values.reshape(pattern.shape[0], block, cols) * widened[:, None, :]  5.61 us
  transfers between devices with their start and end apart: 23, of which 21 were waited for; matrix products, arithmetic and copies ran while one was open for 9% of the time, Pallas kernels for 0%

profile of v9, /device:TPU:2, one launch (start us, length us, event | category | flops | bytes accessed | tf_op | source)
XLA Modules:
  0.0 277.3 jit_solution(16007350249571506383)
XLA Ops:
  1.0 3.1 %bitcast_multiply_fusion.1 = bf16[2048,512]{1,0:T(8,128)(2,1)} fusion(bf16[2048,512]{1,0:T(8,128)(2,1)} %param.6, bf16[32,512]{1,0:T(8,128)(2,1)S(1)} %mul.26), kind=kLoop, calls=%fused_computation.17 | loop fusion | flops 1048576 | bytes 4227072 | tf_op jit(solution)/shard_map/mul | solution.py:19
  6.7 5.4 %constant_dynamic-slice_fusion.7 = (bf16[2,1,128,2048]{2,1,0,3:T(2,128)(2,1)}, bf16[2,1,128,2048]{2,1,0,3:T(2,128)(2,1)}) fusion(bf16[2,2,128,2048]{2,1,0,3:T(2,128)(2,1)S(1)} %reshape.35, s32[]{:T(128)S(6)} %select_n.130, s32[]{:T(128)S(6)} %select_n.131), kind=kLoop, calls=%fused_computation.75 | loop fusion | bytes 4194312 | tf_op jit(solution)/shard_map/jit(dynamic_index_in_dim)/dynamic_slice | solution.py:66
  12.1 4.6 %copy.24 = bf16[2,1,128,2048]{3,2,0,1:T(8,128)(2,1)S(1)} copy(bf16[2,1,128,2048]{2,1,0,3:T(2,128)(2,1)} %get-tuple-element.24) | data formatting | bytes 2097152
  26.6 3.8 %fusion.16 = f32[2,128,1024]{2,1,0:T(8,128)S(1)} fusion(f32[2,128,1024]{2,1,0:T(8,128)} %collective-permute-done.1, bf16[1024,2048]{1,0:T(8,128)(2,1)} %copy-done.4, bf16[2,1,128,2048]{3,2,0,1:T(8,128)(2,1)S(1)} %copy.23), kind=kOutput, calls=%fused_computation.18 | convolution fusion | flops 1074003968 | bytes 7340032 | tf_op jit(solution)/shard_map/dot_general | solution.py:64
  35.3 4.4 %collective-permute-done.2 = f32[2,32,1024]{2,1,0:T(8,128)S(1)} collective-permute-done((f32[2,32,1024]{2,1,0:T(8,128)S(1)}, f32[2,32,1024]{2,1,0:T(8,128)S(1)}, u32[]{:S(2)}, u32[]{:S(2)}) %collective-permute-start.2) | collective-permute-done | bytes 262176 | tf_op jit(solution)/shard_map/ppermute | solution.py:36
  42.7 4.0 %collective-permute-done.4 = f32[2,32,1024]{2,1,0:T(8,128)S(1)} collective-permute-done((f32[2,32,1024]{2,1,0:T(8,128)S(1)}, f32[2,32,1024]{2,1,0:T(8,128)S(1)}, u32[]{:S(2)}, u32[]{:S(2)}) %collective-permute-start.4) | collective-permute-done | bytes 262176 | tf_op jit(solution)/shard_map/ppermute | solution.py:36
  46.8 26.5 %collective-permute-done = bf16[512,2048]{0,1:T(8,128)(2,1)} collective-permute-done((bf16[512,2048]{0,1:T(8,128)(2,1)}, bf16[512,2048]{0,1:T(8,128)(2,1)}, u32[]{:S(2)}, u32[]{:S(2)}) %collective-permute-start) | collective-permute-done | bytes 2097184 | tf_op jit(solution)/shard_map/ppermute | solution.py:12
  75.8 5.5 %constant_dynamic-slice_fusion.5 = (bf16[2,1,128,2048]{2,1,0,3:T(2,128)(2,1)}, bf16[2,1,128,2048]{2,1,0,3:T(2,128)(2,1)}) fusion(bf16[2,2,128,2048]{2,1,0,3:T(2,128)(2,1)S(1)} %reshape.37, s32[]{:T(128)S(6)} %select_n.130, s32[]{:T(128)S(6)} %select_n.131), kind=kLoop, calls=%fused_computation.73 | loop fusion | bytes 4194312 | tf_op jit(solution)/shard_map/jit(dynamic_index_in_dim)/dynamic_slice | solution.py:66
  81.3 4.6 %copy.26 = bf16[2,1,128,2048]{3,2,0,1:T(8,128)(2,1)S(1)} copy(bf16[2,1,128,2048]{2,1,0,3:T(2,128)(2,1)} %get-tuple-element.22) | data formatting | bytes 2097152
  85.8 4.6 %fusion.8 = f32[2,128,1024]{2,1,0:T(8,128)} fusion(bf16[1024,2048]{1,0:T(8,128)(2,1)} %copy-done.4, bf16[2,1,128,2048]{3,2,0,1:T(8,128)(2,1)S(1)} %copy.26), kind=kOutput, calls=%fused_computation.8 | convolution fusion | flops 1073741824 | bytes 6291456 | tf_op jit(solution)/shard_map/dot_general | solution.py:64
  93.4 3.8 %fusion.19 = f32[2,128,1024]{2,1,0:T(8,128)S(1)} fusion(f32[2,128,1024]{2,1,0:T(8,128)} %collective-permute-done.6, bf16[1024,2048]{1,0:T(8,128)(2,1)} %copy-done.4, bf16[2,1,128,2048]{3,2,0,1:T(8,128)(2,1)S(1)} %copy.25), kind=kOutput, calls=%fused_computation.19 | convolution fusion | flops 1074003968 | bytes 7340032 | tf_op jit(solution)/shard_map/dot_general | solution.py:64
  102.1 4.4 %collective-permute-done.7 = f32[2,32,1024]{2,1,0:T(8,128)S(1)} collective-permute-done((f32[2,32,1024]{2,1,0:T(8,128)S(1)}, f32[2,32,1024]{2,1,0:T(8,128)S(1)}, u32[]{:S(2)}, u32[]{:S(2)}) %collective-permute-start.7) | collective-permute-done | bytes 262176 | tf_op jit(solution)/shard_map/ppermute | solution.py:36
  109.6 4.5 %collective-permute-done.9 = f32[2,32,1024]{2,1,0:T(8,128)S(1)} collective-permute-done((f32[2,32,1024]{2,1,0:T(8,128)S(1)}, f32[2,32,1024]{2,1,0:T(8,128)S(1)}, u32[]{:S(2)}, u32[]{:S(2)}) %collective-permute-start.9) | collective-permute-done | bytes 262176 | tf_op jit(solution)/shard_map/ppermute | solution.py:36
  114.8 25.8 %collective-permute-done.5 = bf16[512,2048]{0,1:T(8,128)(2,1)} collective-permute-done((bf16[512,2048]{0,1:T(8,128)(2,1)}, bf16[512,2048]{0,1:T(8,128)(2,1)}, u32[]{:S(2)}, u32[]{:S(2)}) %collective-permute-start.5) | collective-permute-done | bytes 2097184 | tf_op jit(solution)/shard_map/ppermute | solution.py:12
  143.1 5.4 %constant_dynamic-slice_fusion.3 = (bf16[2,1,128,2048]{2,1,0,3:T(2,128)(2,1)}, bf16[2,1,128,2048]{2,1,0,3:T(2,128)(2,1)}) fusion(bf16[2,2,128,2048]{2,1,0,3:T(2,128)(2,1)S(1)} %reshape.39, s32[]{:T(128)S(6)} %select_n.130, s32[]{:T(128)S(6)} %select_n.131), kind=kLoop, calls=%fused_computation.71 | loop fusion | bytes 4194312 | tf_op jit(solution)/shard_map/jit(dynamic_index_in_dim)/dynamic_slice | solution.py:66
  148.6 4.6 %copy.28 = bf16[2,1,128,2048]{3,2,0,1:T(8,128)(2,1)S(1)} copy(bf16[2,1,128,2048]{2,1,0,3:T(2,128)(2,1)} %get-tuple-element.20) | data formatting | bytes 2097152
  153.2 4.6 %fusion.4 = f32[2,128,1024]{2,1,0:T(8,128)} fusion(bf16[1024,2048]{1,0:T(8,128)(2,1)} %copy-done.4, bf16[2,1,128,2048]{3,2,0,1:T(8,128)(2,1)S(1)} %copy.28), kind=kOutput, calls=%fused_computation.4 | convolution fusion | flops 1073741824 | bytes 6291456 | tf_op jit(solution)/shard_map/dot_general | solution.py:64
  160.7 3.8 %fusion.22 = f32[2,128,1024]{2,1,0:T(8,128)S(1)} fusion(f32[2,128,1024]{2,1,0:T(8,128)} %collective-permute-done.10, bf16[1024,2048]{1,0:T(8,128)(2,1)} %copy-done.4, bf16[2,1,128,2048]{3,2,0,1:T(8,128)(2,1)S(1)} %copy.27), kind=kOutput, calls=%fused_computation.20 | convolution fusion | flops 1074003968 | bytes 7340032 | tf_op jit(solution)/shard_map/dot_general | solution.py:64
  169.4 4.4 %collective-permute-done.11 = f32[2,32,1024]{2,1,0:T(8,128)S(1)} collective-permute-done((f32[2,32,1024]{2,1,0:T(8,128)S(1)}, f32[2,32,1024]{2,1,0:T(8,128)S(1)}, u32[]{:S(2)}, u32[]{:S(2)}) %collective-permute-start.11) | collective-permute-done | bytes 262176 | tf_op jit(solution)/shard_map/ppermute | solution.py:36
  176.9 4.5 %collective-permute-done.13 = f32[2,32,1024]{2,1,0:T(8,128)S(1)} collective-permute-done((f32[2,32,1024]{2,1,0:T(8,128)S(1)}, f32[2,32,1024]{2,1,0:T(8,128)S(1)}, u32[]{:S(2)}, u32[]{:S(2)}) %collective-permute-start.13) | collective-permute-done | bytes 262176 | tf_op jit(solution)/shard_map/ppermute | solution.py:36
  182.1 25.8 %collective-permute-done.14 = bf16[512,2048]{0,1:T(8,128)(2,1)} collective-permute-done((bf16[512,2048]{0,1:T(8,128)(2,1)}, bf16[512,2048]{0,1:T(8,128)(2,1)}, u32[]{:S(2)}, u32[]{:S(2)}) %collective-permute-start.14) | collective-permute-done | bytes 2097184 | tf_op jit(solution)/shard_map/ppermute | solution.py:12
  210.5 5.4 %constant_dynamic-slice_fusion.1 = (bf16[2,1,128,2048]{2,1,0,3:T(2,128)(2,1)}, bf16[2,1,128,2048]{2,1,0,3:T(2,128)(2,1)}) fusion(bf16[2,2,128,2048]{2,1,0,3:T(2,128)(2,1)S(1)} %reshape.41, s32[]{:T(128)S(6)} %select_n.130, s32[]{:T(128)S(6)} %select_n.131), kind=kLoop, calls=%fused_computation.69 | loop fusion | bytes 4194312 | tf_op jit(solution)/shard_map/jit(dynamic_index_in_dim)/dynamic_slice | solution.py:66
  215.9 4.6 %copy.30 = bf16[2,1,128,2048]{3,2,0,1:T(8,128)(2,1)S(1)} copy(bf16[2,1,128,2048]{2,1,0,3:T(2,128)(2,1)} %get-tuple-element.18) | data formatting | bytes 2097152
  220.5 4.7 %fusion = f32[2,128,1024]{2,1,0:T(8,128)} fusion(bf16[1024,2048]{1,0:T(8,128)(2,1)} %copy-done.4, bf16[2,1,128,2048]{3,2,0,1:T(8,128)(2,1)S(1)} %copy.30), kind=kOutput, calls=%fused_computation | convolution fusion | flops 1073741824 | bytes 6291456 | tf_op jit(solution)/shard_map/dot_general | solution.py:64
  225.3 4.3 %copy.29 = bf16[2,1,128,2048]{3,2,0,1:T(8,128)(2,1)} copy(bf16[2,1,128,2048]{2,1,0,3:T(2,128)(2,1)S(1)} %copy-done) | data formatting | bytes 2097152
  229.6 4.1 %fusion.25 = f32[2,128,1024]{2,1,0:T(8,128)S(1)} fusion(f32[2,128,1024]{2,1,0:T(8,128)} %collective-permute-done.15, bf16[1024,2048]{1,0:T(8,128)(2,1)} %copy-done.4, bf16[2,1,128,2048]{3,2,0,1:T(8,128)(2,1)} %copy.29), kind=kOutput, calls=%fused_computation.21 | convolution fusion | flops 1074003968 | bytes 7340032 | tf_op jit(solution)/shard_map/dot_general | solution.py:64
  238.7 4.3 %collective-permute-done.16 = f32[2,32,1024]{2,1,0:T(8,128)S(1)} collective-permute-done((f32[2,32,1024]{2,1,0:T(8,128)S(1)}, f32[2,32,1024]{2,1,0:T(8,128)S(1)}, u32[]{:S(2)}, u32[]{:S(2)}) %collective-permute-start.16) | collective-permute-done | bytes 262176 | tf_op jit(solution)/shard_map/ppermute | solution.py:36
  246.1 4.8 %collective-permute-done.18 = f32[2,32,1024]{2,1,0:T(8,128)S(1)} collective-permute-done((f32[2,32,1024]{2,1,0:T(8,128)S(1)}, f32[2,32,1024]{2,1,0:T(8,128)S(1)}, u32[]{:S(2)}, u32[]{:S(2)}) %collective-permute-start.18) | collective-permute-done | bytes 262176 | tf_op jit(solution)/shard_map/ppermute | solution.py:36
  256.4 5.9 %collective-permute-done.19 = f32[2,32,1024]{2,1,0:T(8,128)S(1)} collective-permute-done((f32[2,32,1024]{2,1,0:T(8,128)S(1)}, f32[2,32,1024]{2,1,0:T(8,128)S(1)}, u32[]{:S(2)}, u32[]{:S(2)}) %collective-permute-start.19) | collective-permute-done | bytes 262176 | tf_op jit(solution)/shard_map/ppermute | solution.py:36
  262.3 3.9 %collective-permute-done.20 = f32[2,32,1024]{2,1,0:T(8,128)S(1)} collective-permute-done((f32[2,32,1024]{2,1,0:T(8,128)S(1)}, f32[2,32,1024]{2,1,0:T(8,128)S(1)}, u32[]{:S(2)}, u32[]{:S(2)}) %collective-permute-start.20) | collective-permute-done | bytes 262176 | tf_op jit(solution)/shard_map/ppermute | solution.py:36
  266.9 5.5 %collective-permute-start.22 = (f32[32,1024]{1,0:T(8,128)S(1)}, f32[32,1024]{1,0:T(8,128)S(1)}, u32[]{:S(2)}, u32[]{:S(2)}) collective-permute-start(f32[32,1024]{1,0:T(8,128)S(1)} %dynamic-slice_bitcast_fusion.15), channel_id=1, source_target_pairs={{0,32},{32,0},{1,33},{33,1},{2,34},{34,2},{3,35},{35,3},{4,36},{36... | collective-permute-start | bytes 393224 | tf_op jit(solution)/shard_map/ppermute | solution.py:27
  272.4 4.2 %collective-permute-done.22 = f32[32,1024]{1,0:T(8,128)S(1)} collective-permute-done((f32[32,1024]{1,0:T(8,128)S(1)}, f32[32,1024]{1,0:T(8,128)S(1)}, u32[]{:S(2)}, u32[]{:S(2)}) %collective-permute-start.22) | collective-permute-done | bytes 131104 | tf_op jit(solution)/shard_map/ppermute | solution.py:27
  (79 shorter events, 67.4 us)
Async XLA Ops:
  12.1 4.6 %copy-start.7 = (s32[16,32]{1,0:T(8,128)S(1)}, s32[16,32]{1,0:T(8,128)}, u32[]{:S(2)}) copy-start(s32[16,32]{1,0:T(8,128)} %param.5) | copy-start | bytes 6148
  19.5 2.5 copy-start.4
  19.6 4.4 %copy-start.1 = (bf16[2,1,128,2048]{2,1,0,3:T(2,128)(2,1)S(1)}, bf16[2,1,128,2048]{2,1,0,3:T(2,128)(2,1)}, u32[]{:S(2)}) copy-start(bf16[2,1,128,2048]{2,1,0,3:T(2,128)(2,1)} %get-tuple-element.23) | copy-start | bytes 3145732
  22.0 4.6 %collective-permute-start.1 = (f32[2,128,1024]{2,1,0:T(8,128)}, f32[2,128,1024]{2,1,0:T(8,128)}, u32[]{:S(2)}, u32[]{:S(2)}) collective-permute-start(f32[2,128,1024]{2,1,0:T(8,128)} %fusion.12), channel_id=1, source_target_pairs={{0,4},{4,0},{1,5},{5,1},{2,6},{6,2},{3,7},{7,3},{8,12},{12,8},{9,1... | collective-permute-start | bytes 3145736 | tf_op jit(solution)/shard_map/ppermute | solution.py:65
  22.0 51.2 %collective-permute-start = (bf16[512,2048]{0,1:T(8,128)(2,1)}, bf16[512,2048]{0,1:T(8,128)(2,1)}, u32[]{:S(2)}, u32[]{:S(2)}) collective-permute-start(bf16[512,2048]{0,1:T(8,128)(2,1)} %bitcast.1), channel_id=1, source_target_pairs={{0,64},{64,128},{128,192},{192,0},{1,65},{65,129},{129,193},{193,1... | collective-permute-start | bytes 6291464 | tf_op jit(solution)/shard_map/ppermute | solution.py:12
  30.4 9.2 %collective-permute-start.2 = (f32[2,32,1024]{2,1,0:T(8,128)S(1)}, f32[2,32,1024]{2,1,0:T(8,128)S(1)}, u32[]{:S(2)}, u32[]{:S(2)}) collective-permute-start(f32[2,32,1024]{2,1,0:T(8,128)S(1)} %get-tuple-element.37), channel_id=1, source_target_pairs={{0,1},{1,2},{2,3},{3,0},{4,5},{5,6},{6,7},{7,4},{8,9},{9,10},{10,1... | collective-permute-start | bytes 786440 | tf_op jit(solution)/shard_map/ppermute | solution.py:36
  32.0 10.7 %collective-permute-start.3 = (f32[2,32,1024]{2,1,0:T(8,128)S(1)}, f32[2,32,1024]{2,1,0:T(8,128)S(1)}, u32[]{:S(2)}, u32[]{:S(2)}) collective-permute-start(f32[2,32,1024]{2,1,0:T(8,128)S(1)} %get-tuple-element.39), channel_id=1, source_target_pairs={{0,2},{1,3},{2,0},{3,1},{4,6},{5,7},{6,4},{7,5},{8,10},{9,11},{10,... | collective-permute-start | bytes 786440 | tf_op jit(solution)/shard_map/ppermute | solution.py:36
  33.6 13.1 %collective-permute-start.4 = (f32[2,32,1024]{2,1,0:T(8,128)S(1)}, f32[2,32,1024]{2,1,0:T(8,128)S(1)}, u32[]{:S(2)}, u32[]{:S(2)}) collective-permute-start(f32[2,32,1024]{2,1,0:T(8,128)S(1)} %get-tuple-element.38), channel_id=1, source_target_pairs={{0,3},{1,0},{2,1},{3,2},{4,7},{5,4},{6,5},{7,6},{8,11},{9,8},{10,9... | collective-permute-start | bytes 786440 | tf_op jit(solution)/shard_map/ppermute | solution.py:36
  85.8 4.6 %copy-start.2 = (bf16[2,1,128,2048]{2,1,0,3:T(2,128)(2,1)S(1)}, bf16[2,1,128,2048]{2,1,0,3:T(2,128)(2,1)}, u32[]{:S(2)}) copy-start(bf16[2,1,128,2048]{2,1,0,3:T(2,128)(2,1)} %get-tuple-element.21) | copy-start | bytes 3145732
  90.4 3.0 %collective-permute-start.6 = (f32[2,128,1024]{2,1,0:T(8,128)}, f32[2,128,1024]{2,1,0:T(8,128)}, u32[]{:S(2)}, u32[]{:S(2)}) collective-permute-start(f32[2,128,1024]{2,1,0:T(8,128)} %fusion.8), channel_id=1, source_target_pairs={{0,4},{4,0},{1,5},{5,1},{2,6},{6,2},{3,7},{7,3},{8,12},{12,8},{9,1... | collective-permute-start | bytes 3145736 | tf_op jit(solution)/shard_map/ppermute | solution.py:65
  90.4 50.2 %collective-permute-start.5 = (bf16[512,2048]{0,1:T(8,128)(2,1)}, bf16[512,2048]{0,1:T(8,128)(2,1)}, u32[]{:S(2)}, u32[]{:S(2)}) collective-permute-start(bf16[512,2048]{0,1:T(8,128)(2,1)} %collective-permute-done), channel_id=1, source_target_pairs={{0,64},{64,128},{128,192},{192,0},{1,65},{65,129},{129,193},{193,1... | collective-permute-start | bytes 6291464 | tf_op jit(solution)/shard_map/ppermute | solution.py:12
  97.3 9.2 %collective-permute-start.7 = (f32[2,32,1024]{2,1,0:T(8,128)S(1)}, f32[2,32,1024]{2,1,0:T(8,128)S(1)}, u32[]{:S(2)}, u32[]{:S(2)}) collective-permute-start(f32[2,32,1024]{2,1,0:T(8,128)S(1)} %get-tuple-element.34), channel_id=1, source_target_pairs={{0,1},{1,2},{2,3},{3,0},{4,5},{5,6},{6,7},{7,4},{8,9},{9,10},{10,1... | collective-permute-start | bytes 786440 | tf_op jit(solution)/shard_map/ppermute | solution.py:36
  98.9 10.7 %collective-permute-start.8 = (f32[2,32,1024]{2,1,0:T(8,128)S(1)}, f32[2,32,1024]{2,1,0:T(8,128)S(1)}, u32[]{:S(2)}, u32[]{:S(2)}) collective-permute-start(f32[2,32,1024]{2,1,0:T(8,128)S(1)} %get-tuple-element.36), channel_id=1, source_target_pairs={{0,2},{1,3},{2,0},{3,1},{4,6},{5,7},{6,4},{7,5},{8,10},{9,11},{10,... | collective-permute-start | bytes 786440 | tf_op jit(solution)/shard_map/ppermute | solution.py:36
  100.6 13.4 %collective-permute-start.9 = (f32[2,32,1024]{2,1,0:T(8,128)S(1)}, f32[2,32,1024]{2,1,0:T(8,128)S(1)}, u32[]{:S(2)}, u32[]{:S(2)}) collective-permute-start(f32[2,32,1024]{2,1,0:T(8,128)S(1)} %get-tuple-element.35), channel_id=1, source_target_pairs={{0,3},{1,0},{2,1},{3,2},{4,7},{5,4},{6,5},{7,6},{8,11},{9,8},{10,9... | collective-permute-start | bytes 786440 | tf_op jit(solution)/shard_map/ppermute | solution.py:36
  153.2 4.6 %copy-start.3 = (bf16[2,1,128,2048]{2,1,0,3:T(2,128)(2,1)S(1)}, bf16[2,1,128,2048]{2,1,0,3:T(2,128)(2,1)}, u32[]{:S(2)}) copy-start(bf16[2,1,128,2048]{2,1,0,3:T(2,128)(2,1)} %get-tuple-element.19) | copy-start | bytes 3145732
  157.7 3.0 %collective-permute-start.10 = (f32[2,128,1024]{2,1,0:T(8,128)}, f32[2,128,1024]{2,1,0:T(8,128)}, u32[]{:S(2)}, u32[]{:S(2)}) collective-permute-start(f32[2,128,1024]{2,1,0:T(8,128)} %fusion.4), channel_id=1, source_target_pairs={{0,4},{4,0},{1,5},{5,1},{2,6},{6,2},{3,7},{7,3},{8,12},{12,8},{9,1... | collective-permute-start | bytes 3145736 | tf_op jit(solution)/shard_map/ppermute | solution.py:65
  157.7 50.2 %collective-permute-start.14 = (bf16[512,2048]{0,1:T(8,128)(2,1)}, bf16[512,2048]{0,1:T(8,128)(2,1)}, u32[]{:S(2)}, u32[]{:S(2)}) collective-permute-start(bf16[512,2048]{0,1:T(8,128)(2,1)} %collective-permute-done.5), channel_id=1, source_target_pairs={{0,64},{64,128},{128,192},{192,0},{1,65},{65,129},{129,193},{193,1... | collective-permute-start | bytes 6291464 | tf_op jit(solution)/shard_map/ppermute | solution.py:12
  164.6 9.2 %collective-permute-start.11 = (f32[2,32,1024]{2,1,0:T(8,128)S(1)}, f32[2,32,1024]{2,1,0:T(8,128)S(1)}, u32[]{:S(2)}, u32[]{:S(2)}) collective-permute-start(f32[2,32,1024]{2,1,0:T(8,128)S(1)} %get-tuple-element.31), channel_id=1, source_target_pairs={{0,1},{1,2},{2,3},{3,0},{4,5},{5,6},{6,7},{7,4},{8,9},{9,10},{10,1... | collective-permute-start | bytes 786440 | tf_op jit(solution)/shard_map/ppermute | solution.py:36
  166.2 10.7 %collective-permute-start.12 = (f32[2,32,1024]{2,1,0:T(8,128)S(1)}, f32[2,32,1024]{2,1,0:T(8,128)S(1)}, u32[]{:S(2)}, u32[]{:S(2)}) collective-permute-start(f32[2,32,1024]{2,1,0:T(8,128)S(1)} %get-tuple-element.33), channel_id=1, source_target_pairs={{0,2},{1,3},{2,0},{3,1},{4,6},{5,7},{6,4},{7,5},{8,10},{9,11},{10,... | collective-permute-start | bytes 786440 | tf_op jit(solution)/shard_map/ppermute | solution.py:36
  167.9 13.4 %collective-permute-start.13 = (f32[2,32,1024]{2,1,0:T(8,128)S(1)}, f32[2,32,1024]{2,1,0:T(8,128)S(1)}, u32[]{:S(2)}, u32[]{:S(2)}) collective-permute-start(f32[2,32,1024]{2,1,0:T(8,128)S(1)} %get-tuple-element.32), channel_id=1, source_target_pairs={{0,3},{1,0},{2,1},{3,2},{4,7},{5,4},{6,5},{7,6},{8,11},{9,8},{10,9... | collective-permute-start | bytes 786440 | tf_op jit(solution)/shard_map/ppermute | solution.py:36
  220.5 4.9 %copy-start = (bf16[2,1,128,2048]{2,1,0,3:T(2,128)(2,1)S(1)}, bf16[2,1,128,2048]{2,1,0,3:T(2,128)(2,1)}, u32[]{:S(2)}) copy-start(bf16[2,1,128,2048]{2,1,0,3:T(2,128)(2,1)} %get-tuple-element.17) | copy-start | bytes 3145732
  225.2 4.5 %collective-permute-start.15 = (f32[2,128,1024]{2,1,0:T(8,128)}, f32[2,128,1024]{2,1,0:T(8,128)}, u32[]{:S(2)}, u32[]{:S(2)}) collective-permute-start(f32[2,128,1024]{2,1,0:T(8,128)} %fusion), channel_id=1, source_target_pairs={{0,4},{4,0},{1,5},{5,1},{2,6},{6,2},{3,7},{7,3},{8,12},{12,8},{9,1... | collective-permute-start | bytes 3145736 | tf_op jit(solution)/shard_map/ppermute | solution.py:65
  229.6 9.1 %copy-start.5 = (f32[2,32,1024]{2,1,0:T(8,128)S(1)}, f32[2,32,1024]{2,1,0:T(8,128)}, u32[]{:S(2)}) copy-start(f32[2,32,1024]{2,1,0:T(8,128)} %fusion.43) | copy-start | bytes 786436
  233.7 5.0 %copy-start.6 = (f32[2,32,1024]{2,1,0:T(8,128)S(1)}, f32[2,32,1024]{2,1,0:T(8,128)}, u32[]{:S(2)}) copy-start(f32[2,32,1024]{2,1,0:T(8,128)} %fusion.41) | copy-start | bytes 786436
  233.8 9.2 %collective-permute-start.16 = (f32[2,32,1024]{2,1,0:T(8,128)S(1)}, f32[2,32,1024]{2,1,0:T(8,128)S(1)}, u32[]{:S(2)}, u32[]{:S(2)}) collective-permute-start(f32[2,32,1024]{2,1,0:T(8,128)S(1)} %get-tuple-element.28), channel_id=1, source_target_pairs={{0,1},{1,2},{2,3},{3,0},{4,5},{5,6},{6,7},{7,4},{8,9},{9,10},{10,1... | collective-permute-start | bytes 786440 | tf_op jit(solution)/shard_map/ppermute | solution.py:36
  235.4 10.7 %collective-permute-start.17 = (f32[2,32,1024]{2,1,0:T(8,128)S(1)}, f32[2,32,1024]{2,1,0:T(8,128)S(1)}, u32[]{:S(2)}, u32[]{:S(2)}) collective-permute-start(f32[2,32,1024]{2,1,0:T(8,128)S(1)} %get-tuple-element.30), channel_id=1, source_target_pairs={{0,2},{1,3},{2,0},{3,1},{4,6},{5,7},{6,4},{7,5},{8,10},{9,11},{10,... | collective-permute-start | bytes 786440 | tf_op jit(solution)/shard_map/ppermute | solution.py:36
  237.2 13.8 %collective-permute-start.18 = (f32[2,32,1024]{2,1,0:T(8,128)S(1)}, f32[2,32,1024]{2,1,0:T(8,128)S(1)}, u32[]{:S(2)}, u32[]{:S(2)}) collective-permute-start(f32[2,32,1024]{2,1,0:T(8,128)S(1)} %get-tuple-element.29), channel_id=1, source_target_pairs={{0,3},{1,0},{2,1},{3,2},{4,7},{5,4},{6,5},{7,6},{8,11},{9,8},{10,9... | collective-permute-start | bytes 786440 | tf_op jit(solution)/shard_map/ppermute | solution.py:36
  251.1 11.2 %collective-permute-start.19 = (f32[2,32,1024]{2,1,0:T(8,128)S(1)}, f32[2,32,1024]{2,1,0:T(8,128)S(1)}, u32[]{:S(2)}, u32[]{:S(2)}) collective-permute-start(f32[2,32,1024]{2,1,0:T(8,128)S(1)} %get-tuple-element.25), channel_id=1, source_target_pairs={{0,8},{8,16},{16,24},{24,0},{1,9},{9,17},{17,25},{25,1},{2,10},{10... | collective-permute-start | bytes 786440 | tf_op jit(solution)/shard_map/ppermute | solution.py:36
  252.1 14.1 %collective-permute-start.20 = (f32[2,32,1024]{2,1,0:T(8,128)S(1)}, f32[2,32,1024]{2,1,0:T(8,128)S(1)}, u32[]{:S(2)}, u32[]{:S(2)}) collective-permute-start(f32[2,32,1024]{2,1,0:T(8,128)S(1)} %get-tuple-element.27), channel_id=1, source_target_pairs={{0,16},{8,24},{16,0},{24,8},{1,17},{9,25},{17,1},{25,9},{2,18},{10... | collective-permute-start | bytes 786440 | tf_op jit(solution)/shard_map/ppermute | solution.py:36
  255.0 11.8 %collective-permute-start.21 = (f32[2,32,1024]{2,1,0:T(8,128)S(1)}, f32[2,32,1024]{2,1,0:T(8,128)S(1)}, u32[]{:S(2)}, u32[]{:S(2)}) collective-permute-start(f32[2,32,1024]{2,1,0:T(8,128)S(1)} %get-tuple-element.26), channel_id=1, source_target_pairs={{0,24},{8,0},{16,8},{24,16},{1,25},{9,1},{17,9},{25,17},{2,26},{10... | collective-permute-start | bytes 786440 | tf_op jit(solution)/shard_map/ppermute | solution.py:36
  266.9 9.8 %collective-permute-start.22 = (f32[32,1024]{1,0:T(8,128)S(1)}, f32[32,1024]{1,0:T(8,128)S(1)}, u32[]{:S(2)}, u32[]{:S(2)}) collective-permute-start(f32[32,1024]{1,0:T(8,128)S(1)} %dynamic-slice_bitcast_fusion.15), channel_id=1, source_target_pairs={{0,32},{32,0},{1,33},{33,1},{2,34},{34,2},{3,35},{35,3},{4,36},{36... | collective-permute-start | bytes 393224 | tf_op jit(solution)/shard_map/ppermute | solution.py:27

commit v10 on v8

--- a/solution.py
+++ b/solution.py
@@ -46,7 +46,8 @@
     zhi, ys, cores, layers = (lax.axis_size(a) for a in COL_PARTS + ("layer",))
     halves = ys // 2
     block = right.shape[0] // (halves * cores * layers)
-    gathered = jnp.zeros((cycle_size, halves, block, left_rows), jnp.float32)
+    gathered = jnp.zeros((ys, zhi, block, left_rows), jnp.float32)
+    store = lambda into, part, owner: lax.dynamic_update_slice(into, part[:, None], (owner % 2 * halves, owner // 2, 0, 0))
     arrived = right
     reduced = None
     for step in range(cycle_size):
@@ -56,16 +57,15 @@
                 current, reduced = lax.optimization_barrier((current, reduced))
             else:
                 left, reduced = lax.optimization_barrier((left, reduced))
-            gathered = lax.dynamic_update_slice_in_dim(gathered, reduced[None], (position - step + 1) % cycle_size, 0)
+            gathered = store(gathered, reduced, (position - step + 1) % cycle_size)
         if step + 1 < cycle_size:
             arrived = from_behind(current, "row", 1)
         piece = lax.dot_general(current, left, (((1,), (1,)), ((), ())), preferred_element_type=jnp.float32)
         piece = piece.reshape(halves, cores, layers, block, left_rows)
         piece = pair_over(piece, "core", 1)
         reduced = spread_over(piece, "layer", 1)
-    gathered = lax.dynamic_update_slice_in_dim(gathered, reduced[None], (position + 1) % cycle_size, 0)
-    ordered = gathered.reshape(zhi, ys, block, left_rows)
-    ordered = spread_over(ordered, "y", 1)
+    gathered = store(gathered, reduced, (position + 1) % cycle_size)
+    ordered = spread_over(gathered, "y", 0)
     ordered = pair_over(ordered, "zhi", 0)
     return ordered.T.astype(jnp.bfloat16)
 

time: 208 us -> 208 us (level)
  transfers between devices with their start and end apart: 23 -> 23, of which waited for: 22 -> 22; matrix products, arithmetic and copies ran while one was open for 12% -> 11% of each run, Pallas kernels for 0% -> 0%
where the time goes in v10:
time: 208 us; the launch traced here: 206 us
  waiting for transfers between devices  134 us (64%)
  starting transfers between devices  33.2 us (16%)
  matrix products  13.8 us (7%)
  local copies, waits for them, and re-layouts  13.2 us (6%)
  other arithmetic  11.9 us (6%)
    ppermute x3, waiting for transfers between devices, from_behind(): return lax.ppermute(x, axis, [(i, (i + by) % size) for i in range(size)])  63.9 us
    ppermute x15, waiting for transfers between devices, spread_over(): lax.ppermute(send, axes, [(i, (i + shift) % n) for i in range(n)])  54.9 us
    ppermute x15, starting transfers between devices, spread_over(): lax.ppermute(send, axes, [(i, (i + shift) % n) for i in range(n)])  25.3 us
    ppermute x5, waiting for transfers between devices, pair_over(): return keep + lax.ppermute(send, axis, [(0, 1), (1, 0)])  15.2 us
    dot_general x4, matrix products, local(): lax.dot_general(current, left, (((1,), (1,)), ((), ())), preferred_elemen...  13.8 us
    optimization_barrier x2, local copies, waits for them, and re-layouts, local(): current, reduced = lax.optimization_barrier((current, reduced))  5.85 us
    ppermute x5, starting transfers between devices, pair_over(): return keep + lax.ppermute(send, axis, [(0, 1), (1, 0)])  5.74 us
    mul x2, other arithmetic, apply_pattern(): masked = values.reshape(pattern.shape[0], block, cols) * widened[:, None, :]  4.37 us
  transfers between devices with their start and end apart: 23, of which 22 were waited for; matrix products, arithmetic and copies ran while one was open for 11% of the time, Pallas kernels for 0%

profile of v10, /device:TPU:2, one launch (start us, length us, event | category | flops | bytes accessed | tf_op | source)
XLA Modules:
  0.0 206.4 jit_solution(13524239734070324261)
XLA Ops:
  4.8 2.5 %copy.11 = bf16[512,2048]{1,0:T(8,128)(2,1)} copy(bf16[512,2048]{0,1:T(8,128)(2,1)S(1)} %bitcast.120) | data formatting | bytes 4194304 | tf_op jit(solution)/shard_map/transpose | solution.py:42
  7.5 2.6 %bitcast_multiply_fusion = bf16[1024,2048]{1,0:T(8,128)(2,1)S(1)} fusion(bf16[1024,2048]{1,0:T(8,128)(2,1)} %param.4, bf16[16,2048]{1,0:T(8,128)(2,1)S(1)} %mul.42), kind=kLoop, calls=%fused_computation.6 | loop fusion | flops 2097152 | bytes 8454144 | tf_op jit(solution)/shard_map/mul | solution.py:19
  14.2 2.8 %collective-permute-done.1 = f32[2,4,32,1024]{3,2,1,0:T(8,128)} collective-permute-done((f32[2,4,32,1024]{3,2,1,0:T(8,128)S(1)}, f32[2,4,32,1024]{3,2,1,0:T(8,128)}, u32[]{:S(2)}, u32[]{:S(2)}) %collective-permute-start.1) | collective-permute-done | bytes 1048608 | tf_op jit(solution)/shard_map/ppermute | solution.py:27
  24.4 4.6 %collective-permute-done.2 = f32[2,32,1024]{2,1,0:T(8,128)S(1)} collective-permute-done((f32[2,32,1024]{2,1,0:T(8,128)}, f32[2,32,1024]{2,1,0:T(8,128)S(1)}, u32[]{:S(2)}, u32[]{:S(2)}) %collective-permute-start.2) | collective-permute-done | bytes 262176 | tf_op jit(solution)/shard_map/ppermute | solution.py:36
  29.0 3.1 %collective-permute-done.3 = f32[2,32,1024]{2,1,0:T(8,128)} collective-permute-done((f32[2,32,1024]{2,1,0:T(8,128)}, f32[2,32,1024]{2,1,0:T(8,128)}, u32[]{:S(2)}, u32[]{:S(2)}) %collective-permute-start.3) | collective-permute-done | bytes 262176 | tf_op jit(solution)/shard_map/ppermute | solution.py:36
  32.1 3.8 %collective-permute-done.4 = f32[2,32,1024]{2,1,0:T(8,128)} collective-permute-done((f32[2,32,1024]{2,1,0:T(8,128)}, f32[2,32,1024]{2,1,0:T(8,128)}, u32[]{:S(2)}, u32[]{:S(2)}) %collective-permute-start.4) | collective-permute-done | bytes 262176 | tf_op jit(solution)/shard_map/ppermute | solution.py:36
  37.1 16.1 %collective-permute-done = bf16[512,2048]{0,1:T(8,128)(2,1)} collective-permute-done((bf16[512,2048]{0,1:T(8,128)(2,1)S(1)}, bf16[512,2048]{0,1:T(8,128)(2,1)}, u32[]{:S(2)}, u32[]{:S(2)}) %collective-permute-start) | collective-permute-done | bytes 2097184 | tf_op jit(solution)/shard_map/ppermute | solution.py:12
  53.2 2.9 %copy.12 = bf16[512,2048]{1,0:T(8,128)(2,1)S(1)} copy(bf16[512,2048]{0,1:T(8,128)(2,1)} %collective-permute-done) | data formatting | bytes 4194304 | tf_op jit(solution)/shard_map/optimization_barrier | solution.py:57
  56.2 4.5 %fusion.2 = f32[2,2,4,32,1024]{4,3,2,1,0:T(8,128)S(1)} fusion(bf16[2,2,4,32,2048]{4,3,2,1,0:T(8,128)(2,1)S(1)} %bitcast.124, bf16[1024,2048]{1,0:T(8,128)(2,1)} %copy-done), kind=kOutput, calls=%fused_computation.2 | convolution fusion | flops 2147483648 | bytes 8388608 | tf_op jit(solution)/shard_map/dot_general | solution.py:63
  61.0 2.6 %collective-permute-done.6 = f32[2,4,32,1024]{3,2,1,0:T(8,128)S(1)} collective-permute-done((f32[2,4,32,1024]{3,2,1,0:T(8,128)S(1)}, f32[2,4,32,1024]{3,2,1,0:T(8,128)S(1)}, u32[]{:S(2)}, u32[]{:S(2)}) %collective-permute-start.6) | collective-permute-done | bytes 1048608 | tf_op jit(solution)/shard_map/ppermute | solution.py:27
  68.7 4.4 %collective-permute-done.7 = f32[2,32,1024]{2,1,0:T(8,128)S(1)} collective-permute-done((f32[2,32,1024]{2,1,0:T(8,128)S(1)}, f32[2,32,1024]{2,1,0:T(8,128)S(1)}, u32[]{:S(2)}, u32[]{:S(2)}) %collective-permute-start.7) | collective-permute-done | bytes 262176 | tf_op jit(solution)/shard_map/ppermute | solution.py:36
  73.1 3.0 %collective-permute-done.8 = f32[2,32,1024]{2,1,0:T(8,128)S(1)} collective-permute-done((f32[2,32,1024]{2,1,0:T(8,128)S(1)}, f32[2,32,1024]{2,1,0:T(8,128)S(1)}, u32[]{:S(2)}, u32[]{:S(2)}) %collective-permute-start.8) | collective-permute-done | bytes 262176 | tf_op jit(solution)/shard_map/ppermute | solution.py:36
  76.1 3.9 %collective-permute-done.9 = f32[2,32,1024]{2,1,0:T(8,128)S(1)} collective-permute-done((f32[2,32,1024]{2,1,0:T(8,128)S(1)}, f32[2,32,1024]{2,1,0:T(8,128)S(1)}, u32[]{:S(2)}, u32[]{:S(2)}) %collective-permute-start.9) | collective-permute-done | bytes 262176 | tf_op jit(solution)/shard_map/ppermute | solution.py:36
  80.8 24.3 %collective-permute-done.5 = bf16[512,2048]{0,1:T(8,128)(2,1)} collective-permute-done((bf16[512,2048]{0,1:T(8,128)(2,1)}, bf16[512,2048]{0,1:T(8,128)(2,1)}, u32[]{:S(2)}, u32[]{:S(2)}) %collective-permute-start.5) | collective-permute-done | bytes 2097184 | tf_op jit(solution)/shard_map/ppermute | solution.py:12
  105.1 2.9 %copy.13 = bf16[512,2048]{1,0:T(8,128)(2,1)S(1)} copy(bf16[512,2048]{0,1:T(8,128)(2,1)} %collective-permute-done.5) | data formatting | bytes 4194304 | tf_op jit(solution)/shard_map/optimization_barrier | solution.py:57
  108.2 4.5 %fusion = f32[2,2,4,32,1024]{4,3,2,1,0:T(8,128)S(1)} fusion(bf16[2,2,4,32,2048]{4,3,2,1,0:T(8,128)(2,1)S(1)} %bitcast.125, bf16[1024,2048]{1,0:T(8,128)(2,1)} %copy-done), kind=kOutput, calls=%fused_computation | convolution fusion | flops 2147483648 | bytes 8388608 | tf_op jit(solution)/shard_map/dot_general | solution.py:63
  112.9 2.6 %collective-permute-done.10 = f32[2,4,32,1024]{3,2,1,0:T(8,128)S(1)} collective-permute-done((f32[2,4,32,1024]{3,2,1,0:T(8,128)S(1)}, f32[2,4,32,1024]{3,2,1,0:T(8,128)S(1)}, u32[]{:S(2)}, u32[]{:S(2)}) %collective-permute-start.10) | collective-permute-done | bytes 1048608 | tf_op jit(solution)/shard_map/ppermute | solution.py:27
  118.1 2.5 %collective-permute-start.13 = (f32[2,32,1024]{2,1,0:T(8,128)S(1)}, f32[2,32,1024]{2,1,0:T(8,128)S(1)}, u32[]{:S(2)}, u32[]{:S(2)}) collective-permute-start(f32[2,32,1024]{2,1,0:T(8,128)S(1)} %get-tuple-element.24), channel_id=1, source_target_pairs={{0,3},{1,0},{2,1},{3,2},{4,7},{5,4},{6,5},{7,6},{8,11},{9,8},{10,9... | collective-permute-start | bytes 786440 | tf_op jit(solution)/shard_map/ppermute | solution.py:36
  120.6 4.4 %collective-permute-done.11 = f32[2,32,1024]{2,1,0:T(8,128)S(1)} collective-permute-done((f32[2,32,1024]{2,1,0:T(8,128)S(1)}, f32[2,32,1024]{2,1,0:T(8,128)S(1)}, u32[]{:S(2)}, u32[]{:S(2)}) %collective-permute-start.11) | collective-permute-done | bytes 262176 | tf_op jit(solution)/shard_map/ppermute | solution.py:36
  125.0 3.0 %collective-permute-done.12 = f32[2,32,1024]{2,1,0:T(8,128)S(1)} collective-permute-done((f32[2,32,1024]{2,1,0:T(8,128)S(1)}, f32[2,32,1024]{2,1,0:T(8,128)S(1)}, u32[]{:S(2)}, u32[]{:S(2)}) %collective-permute-start.12) | collective-permute-done | bytes 262176 | tf_op jit(solution)/shard_map/ppermute | solution.py:36
  128.0 3.7 %collective-permute-done.13 = f32[2,32,1024]{2,1,0:T(8,128)S(1)} collective-permute-done((f32[2,32,1024]{2,1,0:T(8,128)S(1)}, f32[2,32,1024]{2,1,0:T(8,128)S(1)}, u32[]{:S(2)}, u32[]{:S(2)}) %collective-permute-start.13) | collective-permute-done | bytes 262176 | tf_op jit(solution)/shard_map/ppermute | solution.py:36
  132.5 23.5 %collective-permute-done.14 = bf16[512,2048]{0,1:T(8,128)(2,1)S(1)} collective-permute-done((bf16[512,2048]{0,1:T(8,128)(2,1)}, bf16[512,2048]{0,1:T(8,128)(2,1)S(1)}, u32[]{:S(2)}, u32[]{:S(2)}) %collective-permute-start.14) | collective-permute-done | bytes 2097184 | tf_op jit(solution)/shard_map/ppermute | solution.py:12
  159.7 2.8 %collective-permute-done.15 = f32[2,4,32,1024]{3,2,1,0:T(8,128)} collective-permute-done((f32[2,4,32,1024]{3,2,1,0:T(8,128)}, f32[2,4,32,1024]{3,2,1,0:T(8,128)}, u32[]{:S(2)}, u32[]{:S(2)}) %collective-permute-start.15) | collective-permute-done | bytes 1048608 | tf_op jit(solution)/shard_map/ppermute | solution.py:27
  166.3 2.5 %collective-permute-start.18 = (f32[2,32,1024]{2,1,0:T(8,128)S(1)}, f32[2,32,1024]{2,1,0:T(8,128)S(1)}, u32[]{:S(2)}, u32[]{:S(2)}) collective-permute-start(f32[2,32,1024]{2,1,0:T(8,128)S(1)} %get-tuple-element.21), channel_id=1, source_target_pairs={{0,3},{1,0},{2,1},{3,2},{4,7},{5,4},{6,5},{7,6},{8,11},{9,8},{10,9... | collective-permute-start | bytes 786440 | tf_op jit(solution)/shard_map/ppermute | solution.py:36
  168.9 4.3 %collective-permute-done.16 = f32[2,32,1024]{2,1,0:T(8,128)S(1)} collective-permute-done((f32[2,32,1024]{2,1,0:T(8,128)S(1)}, f32[2,32,1024]{2,1,0:T(8,128)S(1)}, u32[]{:S(2)}, u32[]{:S(2)}) %collective-permute-start.16) | collective-permute-done | bytes 262176 | tf_op jit(solution)/shard_map/ppermute | solution.py:36
  173.2 3.0 %collective-permute-done.17 = f32[2,32,1024]{2,1,0:T(8,128)S(1)} collective-permute-done((f32[2,32,1024]{2,1,0:T(8,128)S(1)}, f32[2,32,1024]{2,1,0:T(8,128)S(1)}, u32[]{:S(2)}, u32[]{:S(2)}) %collective-permute-start.17) | collective-permute-done | bytes 262176 | tf_op jit(solution)/shard_map/ppermute | solution.py:36
  176.2 3.7 %collective-permute-done.18 = f32[2,32,1024]{2,1,0:T(8,128)S(1)} collective-permute-done((f32[2,32,1024]{2,1,0:T(8,128)S(1)}, f32[2,32,1024]{2,1,0:T(8,128)S(1)}, u32[]{:S(2)}, u32[]{:S(2)}) %collective-permute-start.18) | collective-permute-done | bytes 262176 | tf_op jit(solution)/shard_map/ppermute | solution.py:36
  181.8 2.9 %collective-permute-start.20 = (f32[2,32,1024]{2,1,0:T(8,128)S(1)}, f32[2,32,1024]{2,1,0:T(8,128)S(1)}, u32[]{:S(2)}, u32[]{:S(2)}) collective-permute-start(f32[2,32,1024]{2,1,0:T(8,128)S(1)} %get-tuple-element.19), channel_id=1, source_target_pairs={{0,16},{8,24},{16,0},{24,8},{1,17},{9,25},{17,1},{25,9},{2,18},{10... | collective-permute-start | bytes 786440 | tf_op jit(solution)/shard_map/ppermute | solution.py:36
  186.1 3.5 %collective-permute-done.19 = f32[2,32,1024]{2,1,0:T(8,128)S(1)} collective-permute-done((f32[2,32,1024]{2,1,0:T(8,128)S(1)}, f32[2,32,1024]{2,1,0:T(8,128)S(1)}, u32[]{:S(2)}, u32[]{:S(2)}) %collective-permute-start.19) | collective-permute-done | bytes 262176 | tf_op jit(solution)/shard_map/ppermute | solution.py:36
  189.6 6.2 %collective-permute-done.20 = f32[2,32,1024]{2,1,0:T(8,128)S(1)} collective-permute-done((f32[2,32,1024]{2,1,0:T(8,128)S(1)}, f32[2,32,1024]{2,1,0:T(8,128)S(1)}, u32[]{:S(2)}, u32[]{:S(2)}) %collective-permute-start.20) | collective-permute-done | bytes 262176 | tf_op jit(solution)/shard_map/ppermute | solution.py:36
  195.9 5.5 %collective-permute-start.22 = (f32[32,1024]{1,0:T(8,128)S(1)}, f32[32,1024]{1,0:T(8,128)S(1)}, u32[]{:S(2)}, u32[]{:S(2)}) collective-permute-start(f32[32,1024]{1,0:T(8,128)S(1)} %dynamic-slice_bitcast_fusion.19), channel_id=1, source_target_pairs={{0,32},{32,0},{1,33},{33,1},{2,34},{34,2},{3,35},{35,3},{4,36},{36... | collective-permute-start | bytes 393224 | tf_op jit(solution)/shard_map/ppermute | solution.py:27
  201.5 4.3 %collective-permute-done.22 = f32[32,1024]{1,0:T(8,128)S(1)} collective-permute-done((f32[32,1024]{1,0:T(8,128)S(1)}, f32[32,1024]{1,0:T(8,128)S(1)}, u32[]{:S(2)}, u32[]{:S(2)}) %collective-permute-start.22) | collective-permute-done | bytes 131104 | tf_op jit(solution)/shard_map/ppermute | solution.py:27
  (70 shorter events, 38.6 us)
Async XLA Ops:
  2.8 50.4 %collective-permute-start = (bf16[512,2048]{0,1:T(8,128)(2,1)S(1)}, bf16[512,2048]{0,1:T(8,128)(2,1)}, u32[]{:S(2)}, u32[]{:S(2)}) collective-permute-start(bf16[512,2048]{0,1:T(8,128)(2,1)S(1)} %bitcast.119), channel_id=1, source_target_pairs={{0,64},{64,128},{128,192},{192,0},{1,65},{65,129},{129,193},{193,1... | collective-permute-start | bytes 6291464 | tf_op jit(solution)/shard_map/ppermute | solution.py:12
  4.7 2.5 %copy-start.7 = (s32[16,32]{1,0:T(8,128)S(1)}, s32[16,32]{1,0:T(8,128)}, u32[]{:S(2)}) copy-start(s32[16,32]{1,0:T(8,128)} %param.5) | copy-start | bytes 6148
  7.5 2.9 %copy-start.3 = (bf16[512,2048]{1,0:T(8,128)(2,1)S(1)}, bf16[512,2048]{1,0:T(8,128)(2,1)}, u32[]{:S(2)}) copy-start(bf16[512,2048]{1,0:T(8,128)(2,1)} %copy.11) | copy-start | bytes 6291460
  10.2 2.6 %copy-start = (bf16[1024,2048]{1,0:T(8,128)(2,1)}, bf16[1024,2048]{1,0:T(8,128)(2,1)S(1)}, u32[]{:S(2)}) copy-start(bf16[1024,2048]{1,0:T(8,128)(2,1)S(1)} %bitcast_multiply_fusion) | copy-start | bytes 12582916
  12.8 1.4 copy-start.2
  14.2 2.8 %collective-permute-start.1 = (f32[2,4,32,1024]{3,2,1,0:T(8,128)S(1)}, f32[2,4,32,1024]{3,2,1,0:T(8,128)}, u32[]{:S(2)}, u32[]{:S(2)}) collective-permute-start(f32[2,4,32,1024]{3,2,1,0:T(8,128)S(1)} %dynamic-slice_bitcast_fusion.3), channel_id=1, source_target_pairs={{0,4},{4,0},{1,5},{5,1},{2,6},{6,2},{3,7},{7,3},{8,12},{12,8},{9,1... | collective-permute-start | bytes 3145736 | tf_op jit(solution)/shard_map/ppermute | solution.py:27
  19.6 9.4 %collective-permute-start.2 = (f32[2,32,1024]{2,1,0:T(8,128)}, f32[2,32,1024]{2,1,0:T(8,128)S(1)}, u32[]{:S(2)}, u32[]{:S(2)}) collective-permute-start(f32[2,32,1024]{2,1,0:T(8,128)} %get-tuple-element.29), channel_id=1, source_target_pairs={{0,1},{1,2},{2,3},{3,0},{4,5},{5,6},{6,7},{7,4},{8,9},{9,10},{10,1... | collective-permute-start | bytes 786440 | tf_op jit(solution)/shard_map/ppermute | solution.py:36
  21.1 11.0 %collective-permute-start.3 = (f32[2,32,1024]{2,1,0:T(8,128)}, f32[2,32,1024]{2,1,0:T(8,128)}, u32[]{:S(2)}, u32[]{:S(2)}) collective-permute-start(f32[2,32,1024]{2,1,0:T(8,128)} %get-tuple-element.31), channel_id=1, source_target_pairs={{0,2},{1,3},{2,0},{3,1},{4,6},{5,7},{6,4},{7,5},{8,10},{9,11},{10,... | collective-permute-start | bytes 786440 | tf_op jit(solution)/shard_map/ppermute | solution.py:36
  22.2 13.7 %collective-permute-start.4 = (f32[2,32,1024]{2,1,0:T(8,128)}, f32[2,32,1024]{2,1,0:T(8,128)}, u32[]{:S(2)}, u32[]{:S(2)}) collective-permute-start(f32[2,32,1024]{2,1,0:T(8,128)} %get-tuple-element.30), channel_id=1, source_target_pairs={{0,3},{1,0},{2,1},{3,2},{4,7},{5,4},{6,5},{7,6},{8,11},{9,8},{10,9... | collective-permute-start | bytes 786440 | tf_op jit(solution)/shard_map/ppermute | solution.py:36
  29.0 3.1 %copy-start.6 = (f32[2,32,1024]{2,1,0:T(8,128)}, f32[2,32,1024]{2,1,0:T(8,128)S(1)}, u32[]{:S(2)}) copy-start(f32[2,32,1024]{2,1,0:T(8,128)S(1)} %collective-permute-done.2) | copy-start | bytes 786436
  56.1 49.0 %collective-permute-start.5 = (bf16[512,2048]{0,1:T(8,128)(2,1)}, bf16[512,2048]{0,1:T(8,128)(2,1)}, u32[]{:S(2)}, u32[]{:S(2)}) collective-permute-start(bf16[512,2048]{0,1:T(8,128)(2,1)} %collective-permute-done), channel_id=1, source_target_pairs={{0,64},{64,128},{128,192},{192,0},{1,65},{65,129},{129,193},{193,1... | collective-permute-start | bytes 6291464 | tf_op jit(solution)/shard_map/ppermute | solution.py:12
  60.9 2.7 %collective-permute-start.6 = (f32[2,4,32,1024]{3,2,1,0:T(8,128)S(1)}, f32[2,4,32,1024]{3,2,1,0:T(8,128)S(1)}, u32[]{:S(2)}, u32[]{:S(2)}) collective-permute-start(f32[2,4,32,1024]{3,2,1,0:T(8,128)S(1)} %dynamic-slice_bitcast_fusion.2), channel_id=1, source_target_pairs={{0,4},{4,0},{1,5},{5,1},{2,6},{6,2},{3,7},{7,3},{8,12},{12,8},{9,1... | collective-permute-start | bytes 3145736 | tf_op jit(solution)/shard_map/ppermute | solution.py:27
  63.8 9.2 %collective-permute-start.7 = (f32[2,32,1024]{2,1,0:T(8,128)S(1)}, f32[2,32,1024]{2,1,0:T(8,128)S(1)}, u32[]{:S(2)}, u32[]{:S(2)}) collective-permute-start(f32[2,32,1024]{2,1,0:T(8,128)S(1)} %get-tuple-element.26), channel_id=1, source_target_pairs={{0,1},{1,2},{2,3},{3,0},{4,5},{5,6},{6,7},{7,4},{8,9},{9,10},{10,1... | collective-permute-start | bytes 786440 | tf_op jit(solution)/shard_map/ppermute | solution.py:36
  65.4 10.7 %collective-permute-start.8 = (f32[2,32,1024]{2,1,0:T(8,128)S(1)}, f32[2,32,1024]{2,1,0:T(8,128)S(1)}, u32[]{:S(2)}, u32[]{:S(2)}) collective-permute-start(f32[2,32,1024]{2,1,0:T(8,128)S(1)} %get-tuple-element.28), channel_id=1, source_target_pairs={{0,2},{1,3},{2,0},{3,1},{4,6},{5,7},{6,4},{7,5},{8,10},{9,11},{10,... | collective-permute-start | bytes 786440 | tf_op jit(solution)/shard_map/ppermute | solution.py:36
  66.5 13.5 %collective-permute-start.9 = (f32[2,32,1024]{2,1,0:T(8,128)S(1)}, f32[2,32,1024]{2,1,0:T(8,128)S(1)}, u32[]{:S(2)}, u32[]{:S(2)}) collective-permute-start(f32[2,32,1024]{2,1,0:T(8,128)S(1)} %get-tuple-element.27), channel_id=1, source_target_pairs={{0,3},{1,0},{2,1},{3,2},{4,7},{5,4},{6,5},{7,6},{8,11},{9,8},{10,9... | collective-permute-start | bytes 786440 | tf_op jit(solution)/shard_map/ppermute | solution.py:36
  108.1 48.0 %collective-permute-start.14 = (bf16[512,2048]{0,1:T(8,128)(2,1)}, bf16[512,2048]{0,1:T(8,128)(2,1)S(1)}, u32[]{:S(2)}, u32[]{:S(2)}) collective-permute-start(bf16[512,2048]{0,1:T(8,128)(2,1)} %collective-permute-done.5), channel_id=1, source_target_pairs={{0,64},{64,128},{128,192},{192,0},{1,65},{65,129},{129,193},{193,1... | collective-permute-start | bytes 6291464 | tf_op jit(solution)/shard_map/ppermute | solution.py:12
  112.8 2.7 %collective-permute-start.10 = (f32[2,4,32,1024]{3,2,1,0:T(8,128)S(1)}, f32[2,4,32,1024]{3,2,1,0:T(8,128)S(1)}, u32[]{:S(2)}, u32[]{:S(2)}) collective-permute-start(f32[2,4,32,1024]{3,2,1,0:T(8,128)S(1)} %dynamic-slice_bitcast_fusion.1), channel_id=1, source_target_pairs={{0,4},{4,0},{1,5},{5,1},{2,6},{6,2},{3,7},{7,3},{8,12},{12,8},{9,1... | collective-permute-start | bytes 3145736 | tf_op jit(solution)/shard_map/ppermute | solution.py:27
  115.5 40.5 %copy-start.1 = (bf16[1024,2048]{1,0:T(8,128)(2,1)S(1)}, bf16[1024,2048]{1,0:T(8,128)(2,1)}, u32[]{:S(2)}) copy-start(bf16[1024,2048]{1,0:T(8,128)(2,1)} %copy-done) | copy-start | bytes 12582916
  115.8 9.2 %collective-permute-start.11 = (f32[2,32,1024]{2,1,0:T(8,128)S(1)}, f32[2,32,1024]{2,1,0:T(8,128)S(1)}, u32[]{:S(2)}, u32[]{:S(2)}) collective-permute-start(f32[2,32,1024]{2,1,0:T(8,128)S(1)} %get-tuple-element.23), channel_id=1, source_target_pairs={{0,1},{1,2},{2,3},{3,0},{4,5},{5,6},{6,7},{7,4},{8,9},{9,10},{10,1... | collective-permute-start | bytes 786440 | tf_op jit(solution)/shard_map/ppermute | solution.py:36
  117.3 10.7 %collective-permute-start.12 = (f32[2,32,1024]{2,1,0:T(8,128)S(1)}, f32[2,32,1024]{2,1,0:T(8,128)S(1)}, u32[]{:S(2)}, u32[]{:S(2)}) collective-permute-start(f32[2,32,1024]{2,1,0:T(8,128)S(1)} %get-tuple-element.25), channel_id=1, source_target_pairs={{0,2},{1,3},{2,0},{3,1},{4,6},{5,7},{6,4},{7,5},{8,10},{9,11},{10,... | collective-permute-start | bytes 786440 | tf_op jit(solution)/shard_map/ppermute | solution.py:36
  118.1 13.7 %collective-permute-start.13 = (f32[2,32,1024]{2,1,0:T(8,128)S(1)}, f32[2,32,1024]{2,1,0:T(8,128)S(1)}, u32[]{:S(2)}, u32[]{:S(2)}) collective-permute-start(f32[2,32,1024]{2,1,0:T(8,128)S(1)} %get-tuple-element.24), channel_id=1, source_target_pairs={{0,3},{1,0},{2,1},{3,2},{4,7},{5,4},{6,5},{7,6},{8,11},{9,8},{10,9... | collective-permute-start | bytes 786440 | tf_op jit(solution)/shard_map/ppermute | solution.py:36
  159.5 3.0 %collective-permute-start.15 = (f32[2,4,32,1024]{3,2,1,0:T(8,128)}, f32[2,4,32,1024]{3,2,1,0:T(8,128)}, u32[]{:S(2)}, u32[]{:S(2)}) collective-permute-start(f32[2,4,32,1024]{3,2,1,0:T(8,128)} %dynamic-slice_bitcast_fusion), channel_id=1, source_target_pairs={{0,4},{4,0},{1,5},{5,1},{2,6},{6,2},{3,7},{7,3},{8,12},{12,8},{9,1... | collective-permute-start | bytes 3145736 | tf_op jit(solution)/shard_map/ppermute | solution.py:27
  159.7 9.1 %copy-start.4 = (f32[2,32,1024]{2,1,0:T(8,128)S(1)}, f32[2,32,1024]{2,1,0:T(8,128)}, u32[]{:S(2)}) copy-start(f32[2,32,1024]{2,1,0:T(8,128)} %fusion.13) | copy-start | bytes 786436
  159.7 9.1 %copy-start.5 = (f32[2,32,1024]{2,1,0:T(8,128)S(1)}, f32[2,32,1024]{2,1,0:T(8,128)}, u32[]{:S(2)}) copy-start(f32[2,32,1024]{2,1,0:T(8,128)} %fusion.11) | copy-start | bytes 786436
  164.0 9.2 %collective-permute-start.16 = (f32[2,32,1024]{2,1,0:T(8,128)S(1)}, f32[2,32,1024]{2,1,0:T(8,128)S(1)}, u32[]{:S(2)}, u32[]{:S(2)}) collective-permute-start(f32[2,32,1024]{2,1,0:T(8,128)S(1)} %get-tuple-element.20), channel_id=1, source_target_pairs={{0,1},{1,2},{2,3},{3,0},{4,5},{5,6},{6,7},{7,4},{8,9},{9,10},{10,1... | collective-permute-start | bytes 786440 | tf_op jit(solution)/shard_map/ppermute | solution.py:36
  165.5 10.7 %collective-permute-start.17 = (f32[2,32,1024]{2,1,0:T(8,128)S(1)}, f32[2,32,1024]{2,1,0:T(8,128)S(1)}, u32[]{:S(2)}, u32[]{:S(2)}) collective-permute-start(f32[2,32,1024]{2,1,0:T(8,128)S(1)} %get-tuple-element.22), channel_id=1, source_target_pairs={{0,2},{1,3},{2,0},{3,1},{4,6},{5,7},{6,4},{7,5},{8,10},{9,11},{10,... | collective-permute-start | bytes 786440 | tf_op jit(solution)/shard_map/ppermute | solution.py:36
  166.3 13.7 %collective-permute-start.18 = (f32[2,32,1024]{2,1,0:T(8,128)S(1)}, f32[2,32,1024]{2,1,0:T(8,128)S(1)}, u32[]{:S(2)}, u32[]{:S(2)}) collective-permute-start(f32[2,32,1024]{2,1,0:T(8,128)S(1)} %get-tuple-element.21), channel_id=1, source_target_pairs={{0,3},{1,0},{2,1},{3,2},{4,7},{5,4},{6,5},{7,6},{8,11},{9,8},{10,9... | collective-permute-start | bytes 786440 | tf_op jit(solution)/shard_map/ppermute | solution.py:36
  180.1 9.5 %collective-permute-start.19 = (f32[2,32,1024]{2,1,0:T(8,128)S(1)}, f32[2,32,1024]{2,1,0:T(8,128)S(1)}, u32[]{:S(2)}, u32[]{:S(2)}) collective-permute-start(f32[2,32,1024]{2,1,0:T(8,128)S(1)} %get-tuple-element.17), channel_id=1, source_target_pairs={{0,8},{8,16},{16,24},{24,0},{1,9},{9,17},{17,25},{25,1},{2,10},{10... | collective-permute-start | bytes 786440 | tf_op jit(solution)/shard_map/ppermute | solution.py:36
  181.8 14.0 %collective-permute-start.20 = (f32[2,32,1024]{2,1,0:T(8,128)S(1)}, f32[2,32,1024]{2,1,0:T(8,128)S(1)}, u32[]{:S(2)}, u32[]{:S(2)}) collective-permute-start(f32[2,32,1024]{2,1,0:T(8,128)S(1)} %get-tuple-element.19), channel_id=1, source_target_pairs={{0,16},{8,24},{16,0},{24,8},{1,17},{9,25},{17,1},{25,9},{2,18},{10... | collective-permute-start | bytes 786440 | tf_op jit(solution)/shard_map/ppermute | solution.py:36
  184.7 11.1 %collective-permute-start.21 = (f32[2,32,1024]{2,1,0:T(8,128)S(1)}, f32[2,32,1024]{2,1,0:T(8,128)S(1)}, u32[]{:S(2)}, u32[]{:S(2)}) collective-permute-start(f32[2,32,1024]{2,1,0:T(8,128)S(1)} %get-tuple-element.18), channel_id=1, source_target_pairs={{0,24},{8,0},{16,8},{24,16},{1,25},{9,1},{17,9},{25,17},{2,26},{10... | collective-permute-start | bytes 786440 | tf_op jit(solution)/shard_map/ppermute | solution.py:36
  195.9 9.8 %collective-permute-start.22 = (f32[32,1024]{1,0:T(8,128)S(1)}, f32[32,1024]{1,0:T(8,128)S(1)}, u32[]{:S(2)}, u32[]{:S(2)}) collective-permute-start(f32[32,1024]{1,0:T(8,128)S(1)} %dynamic-slice_bitcast_fusion.19), channel_id=1, source_target_pairs={{0,32},{32,0},{1,33},{33,1},{2,34},{34,2},{3,35},{35,3},{4,36},{36... | collective-permute-start | bytes 393224 | tf_op jit(solution)/shard_map/ppermute | solution.py:27

commit v11 on v8

--- a/solution.py
+++ b/solution.py
@@ -39,7 +39,7 @@
 
 def local(left_blocks, left_pattern, right_blocks, right_pattern):
     left = apply_pattern(left_blocks, left_pattern)
-    right = apply_pattern(right_blocks, right_pattern).T
+    right = apply_pattern(right_blocks.T, right_pattern.T)
     left_rows = left.shape[0]
     cycle_size = lax.axis_size("row")
     position = lax.axis_index("row")

time: 208 us -> 204 us (0.981)
  local copies, waits for them, and re-layouts: 13.9 us -> 5.4 us
  waiting for transfers between devices: 132 us -> 138 us
  other arithmetic: 12 us -> 9.54 us
    ppermute x3, waiting for transfers between devices: 62.2 us -> 68.8 us  [from_behind(): return lax.ppermute(x, axis, [(i, (i + by) % size) for i in range(size)])]
    optimization_barrier x2 -> x0, local copies, waits for them, and re-layouts: 6.43 us -> none  [local(): current, reduced = lax.optimization_barrier((current, reduced))]
    transpose x1 -> x0, local copies, waits for them, and re-layouts: 2.46 us -> none  [local(): right = apply_pattern(right_blocks, right_pattern).T]
  transfers between devices with their start and end apart: 23 -> 23, of which waited for: 22 -> 22; matrix products, arithmetic and copies ran while one was open for 12% -> 10% of each run, Pallas kernels for 0% -> 0%
where the time goes in v11:
time: 204 us; the launch traced here: 202 us
  waiting for transfers between devices  138 us (68%)
  starting transfers between devices  33.1 us (16%)
  matrix products  15.4 us (8%)
  other arithmetic  9.54 us (5%)
  local copies, waits for them, and re-layouts  5.4 us (3%)
    ppermute x3, waiting for transfers between devices, from_behind(): return lax.ppermute(x, axis, [(i, (i + by) % size) for i in range(size)])  68.8 us
    ppermute x15, waiting for transfers between devices, spread_over(): lax.ppermute(send, axes, [(i, (i + shift) % n) for i in range(n)])  54.5 us
    ppermute x15, starting transfers between devices, spread_over(): lax.ppermute(send, axes, [(i, (i + shift) % n) for i in range(n)])  25.3 us
    dot_general x4, matrix products, local(): lax.dot_general(current, left, (((1,), (1,)), ((), ())), preferred_elemen...  15.4 us
    ppermute x5, waiting for transfers between devices, pair_over(): return keep + lax.ppermute(send, axis, [(0, 1), (1, 0)])  15.1 us
    ppermute x5, starting transfers between devices, pair_over(): return keep + lax.ppermute(send, axis, [(0, 1), (1, 0)])  5.83 us
  transfers between devices with their start and end apart: 23, of which 22 were waited for; matrix products, arithmetic and copies ran while one was open for 10% of the time, Pallas kernels for 0%

profile of v11, /device:TPU:2, one launch (start us, length us, event | category | flops | bytes accessed | tf_op | source)
XLA Modules:
  0.0 202.2 jit_solution(12589861606815794536)
XLA Ops:
  0.0 2.9 %copy.10 = bf16[2048,512]{0,1:T(8,128)(2,1)S(1)} copy(bf16[2048,512]{1,0:T(8,128)(2,1)} %param.6) | data formatting | bytes 4194304 | tf_op args[2]
  7.0 2.5 %bitcast_multiply_fusion = bf16[1024,2048]{1,0:T(8,128)(2,1)S(1)} fusion(bf16[1024,2048]{1,0:T(8,128)(2,1)} %param.4, bf16[16,2048]{1,0:T(8,128)(2,1)S(1)} %mul.30), kind=kLoop, calls=%fused_computation.6 | loop fusion | flops 2097152 | bytes 8454144 | tf_op jit(solution)/shard_map/mul | solution.py:19
  9.5 5.5 %fusion.4 = f32[2,2,4,32,1024]{4,3,2,1,0:T(8,128)S(1)} fusion(bf16[2,2,4,32,2048]{4,3,2,1,0:T(8,128)(2,1)} %bitcast.3, bf16[1024,2048]{1,0:T(8,128)(2,1)S(1)} %bitcast_multiply_fusion), kind=kOutput, calls=%fused_computation.4 | convolution fusion | flops 2147483648 | bytes 8388608 | tf_op jit(solution)/shard_map/dot_general | solution.py:62
  15.3 2.7 %collective-permute-done.1 = f32[2,4,32,1024]{3,2,1,0:T(8,128)} collective-permute-done((f32[2,4,32,1024]{3,2,1,0:T(8,128)S(1)}, f32[2,4,32,1024]{3,2,1,0:T(8,128)}, u32[]{:S(2)}, u32[]{:S(2)}) %collective-permute-start.1) | collective-permute-done | bytes 1048608 | tf_op jit(solution)/shard_map/ppermute | solution.py:27
  24.3 4.4 %collective-permute-done.2 = f32[2,32,1024]{2,1,0:T(8,128)S(1)} collective-permute-done((f32[2,32,1024]{2,1,0:T(8,128)S(1)}, f32[2,32,1024]{2,1,0:T(8,128)S(1)}, u32[]{:S(2)}, u32[]{:S(2)}) %collective-permute-start.2) | collective-permute-done | bytes 262176 | tf_op jit(solution)/shard_map/ppermute | solution.py:36
  28.7 3.0 %collective-permute-done.3 = f32[2,32,1024]{2,1,0:T(8,128)S(1)} collective-permute-done((f32[2,32,1024]{2,1,0:T(8,128)S(1)}, f32[2,32,1024]{2,1,0:T(8,128)S(1)}, u32[]{:S(2)}, u32[]{:S(2)}) %collective-permute-start.3) | collective-permute-done | bytes 262176 | tf_op jit(solution)/shard_map/ppermute | solution.py:36
  31.7 3.8 %collective-permute-done.4 = f32[2,32,1024]{2,1,0:T(8,128)S(1)} collective-permute-done((f32[2,32,1024]{2,1,0:T(8,128)S(1)}, f32[2,32,1024]{2,1,0:T(8,128)S(1)}, u32[]{:S(2)}, u32[]{:S(2)}) %collective-permute-start.4) | collective-permute-done | bytes 262176 | tf_op jit(solution)/shard_map/ppermute | solution.py:36
  35.6 19.7 %collective-permute-done = bf16[512,2048]{1,0:T(8,128)(2,1)} collective-permute-done((bf16[512,2048]{1,0:T(8,128)(2,1)}, bf16[512,2048]{1,0:T(8,128)(2,1)}, u32[]{:S(2)}, u32[]{:S(2)}) %collective-permute-start) | collective-permute-done | bytes 2097184 | tf_op jit(solution)/shard_map/ppermute | solution.py:12
  55.3 5.2 %fusion.2 = f32[2,2,4,32,1024]{4,3,2,1,0:T(8,128)S(1)} fusion(bf16[2,2,4,32,2048]{4,3,2,1,0:T(8,128)(2,1)} %bitcast.14, bf16[1024,2048]{1,0:T(8,128)(2,1)} %copy-done), kind=kOutput, calls=%fused_computation.2 | convolution fusion | flops 2147483648 | bytes 8388608 | tf_op jit(solution)/shard_map/dot_general | solution.py:62
  60.7 2.6 %collective-permute-done.6 = f32[2,4,32,1024]{3,2,1,0:T(8,128)S(1)} collective-permute-done((f32[2,4,32,1024]{3,2,1,0:T(8,128)S(1)}, f32[2,4,32,1024]{3,2,1,0:T(8,128)S(1)}, u32[]{:S(2)}, u32[]{:S(2)}) %collective-permute-start.6) | collective-permute-done | bytes 1048608 | tf_op jit(solution)/shard_map/ppermute | solution.py:27
  68.5 4.4 %collective-permute-done.7 = f32[2,32,1024]{2,1,0:T(8,128)S(1)} collective-permute-done((f32[2,32,1024]{2,1,0:T(8,128)S(1)}, f32[2,32,1024]{2,1,0:T(8,128)S(1)}, u32[]{:S(2)}, u32[]{:S(2)}) %collective-permute-start.7) | collective-permute-done | bytes 262176 | tf_op jit(solution)/shard_map/ppermute | solution.py:36
  72.9 3.0 %collective-permute-done.8 = f32[2,32,1024]{2,1,0:T(8,128)S(1)} collective-permute-done((f32[2,32,1024]{2,1,0:T(8,128)S(1)}, f32[2,32,1024]{2,1,0:T(8,128)S(1)}, u32[]{:S(2)}, u32[]{:S(2)}) %collective-permute-start.8) | collective-permute-done | bytes 262176 | tf_op jit(solution)/shard_map/ppermute | solution.py:36
  75.9 3.8 %collective-permute-done.9 = f32[2,32,1024]{2,1,0:T(8,128)S(1)} collective-permute-done((f32[2,32,1024]{2,1,0:T(8,128)S(1)}, f32[2,32,1024]{2,1,0:T(8,128)S(1)}, u32[]{:S(2)}, u32[]{:S(2)}) %collective-permute-start.9) | collective-permute-done | bytes 262176 | tf_op jit(solution)/shard_map/ppermute | solution.py:36
  80.5 23.6 %collective-permute-done.5 = bf16[512,2048]{1,0:T(8,128)(2,1)S(1)} collective-permute-done((bf16[512,2048]{1,0:T(8,128)(2,1)}, bf16[512,2048]{1,0:T(8,128)(2,1)S(1)}, u32[]{:S(2)}, u32[]{:S(2)}) %collective-permute-start.5) | collective-permute-done | bytes 2097184 | tf_op jit(solution)/shard_map/ppermute | solution.py:12
  104.2 2.4 %fusion = f32[2,2,4,32,1024]{4,3,2,1,0:T(8,128)S(1)} fusion(bf16[2,2,4,32,2048]{4,3,2,1,0:T(8,128)(2,1)S(1)} %bitcast.131, bf16[1024,2048]{1,0:T(8,128)(2,1)S(1)} %copy-done.1), kind=kOutput, calls=%fused_computation | convolution fusion | flops 2147483648 | bytes 8388608 | tf_op jit(solution)/shard_map/dot_general | solution.py:62
  106.7 2.6 %collective-permute-done.10 = f32[2,4,32,1024]{3,2,1,0:T(8,128)S(1)} collective-permute-done((f32[2,4,32,1024]{3,2,1,0:T(8,128)S(1)}, f32[2,4,32,1024]{3,2,1,0:T(8,128)S(1)}, u32[]{:S(2)}, u32[]{:S(2)}) %collective-permute-start.10) | collective-permute-done | bytes 1048608 | tf_op jit(solution)/shard_map/ppermute | solution.py:27
  111.9 2.5 %collective-permute-start.13 = (f32[2,32,1024]{2,1,0:T(8,128)S(1)}, f32[2,32,1024]{2,1,0:T(8,128)S(1)}, u32[]{:S(2)}, u32[]{:S(2)}) collective-permute-start(f32[2,32,1024]{2,1,0:T(8,128)S(1)} %get-tuple-element.24), channel_id=1, source_target_pairs={{0,3},{1,0},{2,1},{3,2},{4,7},{5,4},{6,5},{7,6},{8,11},{9,8},{10,9... | collective-permute-start | bytes 786440 | tf_op jit(solution)/shard_map/ppermute | solution.py:36
  114.5 4.4 %collective-permute-done.11 = f32[2,32,1024]{2,1,0:T(8,128)S(1)} collective-permute-done((f32[2,32,1024]{2,1,0:T(8,128)S(1)}, f32[2,32,1024]{2,1,0:T(8,128)S(1)}, u32[]{:S(2)}, u32[]{:S(2)}) %collective-permute-start.11) | collective-permute-done | bytes 262176 | tf_op jit(solution)/shard_map/ppermute | solution.py:36
  118.9 3.0 %collective-permute-done.12 = f32[2,32,1024]{2,1,0:T(8,128)S(1)} collective-permute-done((f32[2,32,1024]{2,1,0:T(8,128)S(1)}, f32[2,32,1024]{2,1,0:T(8,128)S(1)}, u32[]{:S(2)}, u32[]{:S(2)}) %collective-permute-start.12) | collective-permute-done | bytes 262176 | tf_op jit(solution)/shard_map/ppermute | solution.py:36
  121.9 3.7 %collective-permute-done.13 = f32[2,32,1024]{2,1,0:T(8,128)S(1)} collective-permute-done((f32[2,32,1024]{2,1,0:T(8,128)S(1)}, f32[2,32,1024]{2,1,0:T(8,128)S(1)}, u32[]{:S(2)}, u32[]{:S(2)}) %collective-permute-start.13) | collective-permute-done | bytes 262176 | tf_op jit(solution)/shard_map/ppermute | solution.py:36
  126.4 25.4 %collective-permute-done.14 = bf16[512,2048]{1,0:T(8,128)(2,1)S(1)} collective-permute-done((bf16[512,2048]{1,0:T(8,128)(2,1)S(1)}, bf16[512,2048]{1,0:T(8,128)(2,1)S(1)}, u32[]{:S(2)}, u32[]{:S(2)}) %collective-permute-start.14) | collective-permute-done | bytes 2097184 | tf_op jit(solution)/shard_map/ppermute | solution.py:12
  151.9 2.4 %fusion.18 = f32[512,1024]{1,0:T(8,128)S(1)} fusion(bf16[512,2048]{1,0:T(8,128)(2,1)S(1)} %collective-permute-done.14, bf16[1024,2048]{1,0:T(8,128)(2,1)S(1)} %copy-done.1), kind=kOutput, calls=%fused_computation.55 | convolution fusion | flops 2147483648 | bytes 8388608 | tf_op jit(solution)/shard_map/dot_general | solution.py:62
  155.4 2.8 %collective-permute-done.15 = f32[2,4,32,1024]{3,2,1,0:T(8,128)} collective-permute-done((f32[2,4,32,1024]{3,2,1,0:T(8,128)}, f32[2,4,32,1024]{3,2,1,0:T(8,128)}, u32[]{:S(2)}, u32[]{:S(2)}) %collective-permute-start.15) | collective-permute-done | bytes 1048608 | tf_op jit(solution)/shard_map/ppermute | solution.py:27
  162.0 2.5 %collective-permute-start.18 = (f32[2,32,1024]{2,1,0:T(8,128)S(1)}, f32[2,32,1024]{2,1,0:T(8,128)S(1)}, u32[]{:S(2)}, u32[]{:S(2)}) collective-permute-start(f32[2,32,1024]{2,1,0:T(8,128)S(1)} %get-tuple-element.21), channel_id=1, source_target_pairs={{0,3},{1,0},{2,1},{3,2},{4,7},{5,4},{6,5},{7,6},{8,11},{9,8},{10,9... | collective-permute-start | bytes 786440 | tf_op jit(solution)/shard_map/ppermute | solution.py:36
  164.6 4.3 %collective-permute-done.16 = f32[2,32,1024]{2,1,0:T(8,128)S(1)} collective-permute-done((f32[2,32,1024]{2,1,0:T(8,128)S(1)}, f32[2,32,1024]{2,1,0:T(8,128)S(1)}, u32[]{:S(2)}, u32[]{:S(2)}) %collective-permute-start.16) | collective-permute-done | bytes 262176 | tf_op jit(solution)/shard_map/ppermute | solution.py:36
  168.9 3.0 %collective-permute-done.17 = f32[2,32,1024]{2,1,0:T(8,128)S(1)} collective-permute-done((f32[2,32,1024]{2,1,0:T(8,128)S(1)}, f32[2,32,1024]{2,1,0:T(8,128)S(1)}, u32[]{:S(2)}, u32[]{:S(2)}) %collective-permute-start.17) | collective-permute-done | bytes 262176 | tf_op jit(solution)/shard_map/ppermute | solution.py:36
  172.0 3.7 %collective-permute-done.18 = f32[2,32,1024]{2,1,0:T(8,128)S(1)} collective-permute-done((f32[2,32,1024]{2,1,0:T(8,128)S(1)}, f32[2,32,1024]{2,1,0:T(8,128)S(1)}, u32[]{:S(2)}, u32[]{:S(2)}) %collective-permute-start.18) | collective-permute-done | bytes 262176 | tf_op jit(solution)/shard_map/ppermute | solution.py:36
  177.6 2.9 %collective-permute-start.20 = (f32[2,32,1024]{2,1,0:T(8,128)S(1)}, f32[2,32,1024]{2,1,0:T(8,128)S(1)}, u32[]{:S(2)}, u32[]{:S(2)}) collective-permute-start(f32[2,32,1024]{2,1,0:T(8,128)S(1)} %get-tuple-element.19), channel_id=1, source_target_pairs={{0,16},{8,24},{16,0},{24,8},{1,17},{9,25},{17,1},{25,9},{2,18},{10... | collective-permute-start | bytes 786440 | tf_op jit(solution)/shard_map/ppermute | solution.py:36
  181.9 3.5 %collective-permute-done.19 = f32[2,32,1024]{2,1,0:T(8,128)S(1)} collective-permute-done((f32[2,32,1024]{2,1,0:T(8,128)S(1)}, f32[2,32,1024]{2,1,0:T(8,128)S(1)}, u32[]{:S(2)}, u32[]{:S(2)}) %collective-permute-start.19) | collective-permute-done | bytes 262176 | tf_op jit(solution)/shard_map/ppermute | solution.py:36
  185.4 6.2 %collective-permute-done.20 = f32[2,32,1024]{2,1,0:T(8,128)S(1)} collective-permute-done((f32[2,32,1024]{2,1,0:T(8,128)S(1)}, f32[2,32,1024]{2,1,0:T(8,128)S(1)}, u32[]{:S(2)}, u32[]{:S(2)}) %collective-permute-start.20) | collective-permute-done | bytes 262176 | tf_op jit(solution)/shard_map/ppermute | solution.py:36
  191.7 5.5 %collective-permute-start.22 = (f32[32,1024]{1,0:T(8,128)S(1)}, f32[32,1024]{1,0:T(8,128)S(1)}, u32[]{:S(2)}, u32[]{:S(2)}) collective-permute-start(f32[32,1024]{1,0:T(8,128)S(1)} %dynamic-slice_bitcast_fusion.19), channel_id=1, source_target_pairs={{0,32},{32,0},{1,33},{33,1},{2,34},{34,2},{3,35},{35,3},{4,36},{36... | collective-permute-start | bytes 393224 | tf_op jit(solution)/shard_map/ppermute | solution.py:27
  197.3 4.3 %collective-permute-done.22 = f32[32,1024]{1,0:T(8,128)S(1)} collective-permute-done((f32[32,1024]{1,0:T(8,128)S(1)}, f32[32,1024]{1,0:T(8,128)S(1)}, u32[]{:S(2)}, u32[]{:S(2)}) %collective-permute-start.22) | collective-permute-done | bytes 131104 | tf_op jit(solution)/shard_map/ppermute | solution.py:27
  (63 shorter events, 29.1 us)
Async XLA Ops:
  0.0 3.0 %copy-start.5 = (s32[32,8]{0,1:T(8,128)S(1)}, s32[32,8]{0,1:T(8,128)}, u32[]{:S(2)}) copy-start(s32[32,8]{0,1:T(8,128)} %param.7) | copy-start | bytes 3076
  3.2 3.5 %copy-start.4 = (s32[16,32]{1,0:T(8,128)S(1)}, s32[16,32]{1,0:T(8,128)}, u32[]{:S(2)}) copy-start(s32[16,32]{1,0:T(8,128)} %param.5) | copy-start | bytes 6148
  4.8 50.6 %collective-permute-start = (bf16[512,2048]{1,0:T(8,128)(2,1)}, bf16[512,2048]{1,0:T(8,128)(2,1)}, u32[]{:S(2)}, u32[]{:S(2)}) collective-permute-start(bf16[512,2048]{1,0:T(8,128)(2,1)} %bitcast_multiply_fusion.1), channel_id=1, source_target_pairs={{0,64},{64,128},{128,192},{192,0},{1,65},{65,129},{129,193},{193,1... | collective-permute-start | bytes 6291464 | tf_op jit(solution)/shard_map/ppermute | solution.py:12
  9.5 5.5 %copy-start = (bf16[1024,2048]{1,0:T(8,128)(2,1)}, bf16[1024,2048]{1,0:T(8,128)(2,1)S(1)}, u32[]{:S(2)}) copy-start(bf16[1024,2048]{1,0:T(8,128)(2,1)S(1)} %bitcast_multiply_fusion) | copy-start | bytes 12582916
  15.1 2.9 %collective-permute-start.1 = (f32[2,4,32,1024]{3,2,1,0:T(8,128)S(1)}, f32[2,4,32,1024]{3,2,1,0:T(8,128)}, u32[]{:S(2)}, u32[]{:S(2)}) collective-permute-start(f32[2,4,32,1024]{3,2,1,0:T(8,128)S(1)} %dynamic-slice_bitcast_fusion.3), channel_id=1, source_target_pairs={{0,4},{4,0},{1,5},{5,1},{2,6},{6,2},{3,7},{7,3},{8,12},{12,8},{9,1... | collective-permute-start | bytes 3145736 | tf_op jit(solution)/shard_map/ppermute | solution.py:27
  19.5 9.2 %collective-permute-start.2 = (f32[2,32,1024]{2,1,0:T(8,128)S(1)}, f32[2,32,1024]{2,1,0:T(8,128)S(1)}, u32[]{:S(2)}, u32[]{:S(2)}) collective-permute-start(f32[2,32,1024]{2,1,0:T(8,128)S(1)} %get-tuple-element.29), channel_id=1, source_target_pairs={{0,1},{1,2},{2,3},{3,0},{4,5},{5,6},{6,7},{7,4},{8,9},{9,10},{10,1... | collective-permute-start | bytes 786440 | tf_op jit(solution)/shard_map/ppermute | solution.py:36
  21.0 10.7 %collective-permute-start.3 = (f32[2,32,1024]{2,1,0:T(8,128)S(1)}, f32[2,32,1024]{2,1,0:T(8,128)S(1)}, u32[]{:S(2)}, u32[]{:S(2)}) collective-permute-start(f32[2,32,1024]{2,1,0:T(8,128)S(1)} %get-tuple-element.31), channel_id=1, source_target_pairs={{0,2},{1,3},{2,0},{3,1},{4,6},{5,7},{6,4},{7,5},{8,10},{9,11},{10,... | collective-permute-start | bytes 786440 | tf_op jit(solution)/shard_map/ppermute | solution.py:36
  22.1 13.4 %collective-permute-start.4 = (f32[2,32,1024]{2,1,0:T(8,128)S(1)}, f32[2,32,1024]{2,1,0:T(8,128)S(1)}, u32[]{:S(2)}, u32[]{:S(2)}) collective-permute-start(f32[2,32,1024]{2,1,0:T(8,128)S(1)} %get-tuple-element.30), channel_id=1, source_target_pairs={{0,3},{1,0},{2,1},{3,2},{4,7},{5,4},{6,5},{7,6},{8,11},{9,8},{10,9... | collective-permute-start | bytes 786440 | tf_op jit(solution)/shard_map/ppermute | solution.py:36
  55.3 48.8 %collective-permute-start.5 = (bf16[512,2048]{1,0:T(8,128)(2,1)}, bf16[512,2048]{1,0:T(8,128)(2,1)S(1)}, u32[]{:S(2)}, u32[]{:S(2)}) collective-permute-start(bf16[512,2048]{1,0:T(8,128)(2,1)} %collective-permute-done), channel_id=1, source_target_pairs={{0,64},{64,128},{128,192},{192,0},{1,65},{65,129},{129,193},{193,1... | collective-permute-start | bytes 6291464 | tf_op jit(solution)/shard_map/ppermute | solution.py:12
  60.6 2.7 %collective-permute-start.6 = (f32[2,4,32,1024]{3,2,1,0:T(8,128)S(1)}, f32[2,4,32,1024]{3,2,1,0:T(8,128)S(1)}, u32[]{:S(2)}, u32[]{:S(2)}) collective-permute-start(f32[2,4,32,1024]{3,2,1,0:T(8,128)S(1)} %dynamic-slice_bitcast_fusion.2), channel_id=1, source_target_pairs={{0,4},{4,0},{1,5},{5,1},{2,6},{6,2},{3,7},{7,3},{8,12},{12,8},{9,1... | collective-permute-start | bytes 3145736 | tf_op jit(solution)/shard_map/ppermute | solution.py:27
  63.4 40.8 %copy-start.1 = (bf16[1024,2048]{1,0:T(8,128)(2,1)S(1)}, bf16[1024,2048]{1,0:T(8,128)(2,1)}, u32[]{:S(2)}) copy-start(bf16[1024,2048]{1,0:T(8,128)(2,1)} %copy-done) | copy-start | bytes 12582916
  63.6 9.2 %collective-permute-start.7 = (f32[2,32,1024]{2,1,0:T(8,128)S(1)}, f32[2,32,1024]{2,1,0:T(8,128)S(1)}, u32[]{:S(2)}, u32[]{:S(2)}) collective-permute-start(f32[2,32,1024]{2,1,0:T(8,128)S(1)} %get-tuple-element.26), channel_id=1, source_target_pairs={{0,1},{1,2},{2,3},{3,0},{4,5},{5,6},{6,7},{7,4},{8,9},{9,10},{10,1... | collective-permute-start | bytes 786440 | tf_op jit(solution)/shard_map/ppermute | solution.py:36
  65.2 10.7 %collective-permute-start.8 = (f32[2,32,1024]{2,1,0:T(8,128)S(1)}, f32[2,32,1024]{2,1,0:T(8,128)S(1)}, u32[]{:S(2)}, u32[]{:S(2)}) collective-permute-start(f32[2,32,1024]{2,1,0:T(8,128)S(1)} %get-tuple-element.28), channel_id=1, source_target_pairs={{0,2},{1,3},{2,0},{3,1},{4,6},{5,7},{6,4},{7,5},{8,10},{9,11},{10,... | collective-permute-start | bytes 786440 | tf_op jit(solution)/shard_map/ppermute | solution.py:36
  66.3 13.4 %collective-permute-start.9 = (f32[2,32,1024]{2,1,0:T(8,128)S(1)}, f32[2,32,1024]{2,1,0:T(8,128)S(1)}, u32[]{:S(2)}, u32[]{:S(2)}) collective-permute-start(f32[2,32,1024]{2,1,0:T(8,128)S(1)} %get-tuple-element.27), channel_id=1, source_target_pairs={{0,3},{1,0},{2,1},{3,2},{4,7},{5,4},{6,5},{7,6},{8,11},{9,8},{10,9... | collective-permute-start | bytes 786440 | tf_op jit(solution)/shard_map/ppermute | solution.py:36
  104.2 47.7 %collective-permute-start.14 = (bf16[512,2048]{1,0:T(8,128)(2,1)S(1)}, bf16[512,2048]{1,0:T(8,128)(2,1)S(1)}, u32[]{:S(2)}, u32[]{:S(2)}) collective-permute-start(bf16[512,2048]{1,0:T(8,128)(2,1)S(1)} %collective-permute-done.5), channel_id=1, source_target_pairs={{0,64},{64,128},{128,192},{192,0},{1,65},{65,129},{129,193},{193,1... | collective-permute-start | bytes 6291464 | tf_op jit(solution)/shard_map/ppermute | solution.py:12
  106.6 2.7 %collective-permute-start.10 = (f32[2,4,32,1024]{3,2,1,0:T(8,128)S(1)}, f32[2,4,32,1024]{3,2,1,0:T(8,128)S(1)}, u32[]{:S(2)}, u32[]{:S(2)}) collective-permute-start(f32[2,4,32,1024]{3,2,1,0:T(8,128)S(1)} %dynamic-slice_bitcast_fusion.1), channel_id=1, source_target_pairs={{0,4},{4,0},{1,5},{5,1},{2,6},{6,2},{3,7},{7,3},{8,12},{12,8},{9,1... | collective-permute-start | bytes 3145736 | tf_op jit(solution)/shard_map/ppermute | solution.py:27
  109.6 9.2 %collective-permute-start.11 = (f32[2,32,1024]{2,1,0:T(8,128)S(1)}, f32[2,32,1024]{2,1,0:T(8,128)S(1)}, u32[]{:S(2)}, u32[]{:S(2)}) collective-permute-start(f32[2,32,1024]{2,1,0:T(8,128)S(1)} %get-tuple-element.23), channel_id=1, source_target_pairs={{0,1},{1,2},{2,3},{3,0},{4,5},{5,6},{6,7},{7,4},{8,9},{9,10},{10,1... | collective-permute-start | bytes 786440 | tf_op jit(solution)/shard_map/ppermute | solution.py:36
  111.2 10.7 %collective-permute-start.12 = (f32[2,32,1024]{2,1,0:T(8,128)S(1)}, f32[2,32,1024]{2,1,0:T(8,128)S(1)}, u32[]{:S(2)}, u32[]{:S(2)}) collective-permute-start(f32[2,32,1024]{2,1,0:T(8,128)S(1)} %get-tuple-element.25), channel_id=1, source_target_pairs={{0,2},{1,3},{2,0},{3,1},{4,6},{5,7},{6,4},{7,5},{8,10},{9,11},{10,... | collective-permute-start | bytes 786440 | tf_op jit(solution)/shard_map/ppermute | solution.py:36
  111.9 13.7 %collective-permute-start.13 = (f32[2,32,1024]{2,1,0:T(8,128)S(1)}, f32[2,32,1024]{2,1,0:T(8,128)S(1)}, u32[]{:S(2)}, u32[]{:S(2)}) collective-permute-start(f32[2,32,1024]{2,1,0:T(8,128)S(1)} %get-tuple-element.24), channel_id=1, source_target_pairs={{0,3},{1,0},{2,1},{3,2},{4,7},{5,4},{6,5},{7,6},{8,11},{9,8},{10,9... | collective-permute-start | bytes 786440 | tf_op jit(solution)/shard_map/ppermute | solution.py:36
  155.3 3.0 %collective-permute-start.15 = (f32[2,4,32,1024]{3,2,1,0:T(8,128)}, f32[2,4,32,1024]{3,2,1,0:T(8,128)}, u32[]{:S(2)}, u32[]{:S(2)}) collective-permute-start(f32[2,4,32,1024]{3,2,1,0:T(8,128)} %dynamic-slice_bitcast_fusion), channel_id=1, source_target_pairs={{0,4},{4,0},{1,5},{5,1},{2,6},{6,2},{3,7},{7,3},{8,12},{12,8},{9,1... | collective-permute-start | bytes 3145736 | tf_op jit(solution)/shard_map/ppermute | solution.py:27
  155.4 9.1 %copy-start.2 = (f32[2,32,1024]{2,1,0:T(8,128)S(1)}, f32[2,32,1024]{2,1,0:T(8,128)}, u32[]{:S(2)}) copy-start(f32[2,32,1024]{2,1,0:T(8,128)} %fusion.13) | copy-start | bytes 786436
  155.4 9.2 %copy-start.3 = (f32[2,32,1024]{2,1,0:T(8,128)S(1)}, f32[2,32,1024]{2,1,0:T(8,128)}, u32[]{:S(2)}) copy-start(f32[2,32,1024]{2,1,0:T(8,128)} %fusion.11) | copy-start | bytes 786436
  159.7 9.2 %collective-permute-start.16 = (f32[2,32,1024]{2,1,0:T(8,128)S(1)}, f32[2,32,1024]{2,1,0:T(8,128)S(1)}, u32[]{:S(2)}, u32[]{:S(2)}) collective-permute-start(f32[2,32,1024]{2,1,0:T(8,128)S(1)} %get-tuple-element.20), channel_id=1, source_target_pairs={{0,1},{1,2},{2,3},{3,0},{4,5},{5,6},{6,7},{7,4},{8,9},{9,10},{10,1... | collective-permute-start | bytes 786440 | tf_op jit(solution)/shard_map/ppermute | solution.py:36
  161.3 10.7 %collective-permute-start.17 = (f32[2,32,1024]{2,1,0:T(8,128)S(1)}, f32[2,32,1024]{2,1,0:T(8,128)S(1)}, u32[]{:S(2)}, u32[]{:S(2)}) collective-permute-start(f32[2,32,1024]{2,1,0:T(8,128)S(1)} %get-tuple-element.22), channel_id=1, source_target_pairs={{0,2},{1,3},{2,0},{3,1},{4,6},{5,7},{6,4},{7,5},{8,10},{9,11},{10,... | collective-permute-start | bytes 786440 | tf_op jit(solution)/shard_map/ppermute | solution.py:36
  162.0 13.7 %collective-permute-start.18 = (f32[2,32,1024]{2,1,0:T(8,128)S(1)}, f32[2,32,1024]{2,1,0:T(8,128)S(1)}, u32[]{:S(2)}, u32[]{:S(2)}) collective-permute-start(f32[2,32,1024]{2,1,0:T(8,128)S(1)} %get-tuple-element.21), channel_id=1, source_target_pairs={{0,3},{1,0},{2,1},{3,2},{4,7},{5,4},{6,5},{7,6},{8,11},{9,8},{10,9... | collective-permute-start | bytes 786440 | tf_op jit(solution)/shard_map/ppermute | solution.py:36
  175.9 9.5 %collective-permute-start.19 = (f32[2,32,1024]{2,1,0:T(8,128)S(1)}, f32[2,32,1024]{2,1,0:T(8,128)S(1)}, u32[]{:S(2)}, u32[]{:S(2)}) collective-permute-start(f32[2,32,1024]{2,1,0:T(8,128)S(1)} %get-tuple-element.17), channel_id=1, source_target_pairs={{0,8},{8,16},{16,24},{24,0},{1,9},{9,17},{17,25},{25,1},{2,10},{10... | collective-permute-start | bytes 786440 | tf_op jit(solution)/shard_map/ppermute | solution.py:36
  177.6 14.0 %collective-permute-start.20 = (f32[2,32,1024]{2,1,0:T(8,128)S(1)}, f32[2,32,1024]{2,1,0:T(8,128)S(1)}, u32[]{:S(2)}, u32[]{:S(2)}) collective-permute-start(f32[2,32,1024]{2,1,0:T(8,128)S(1)} %get-tuple-element.19), channel_id=1, source_target_pairs={{0,16},{8,24},{16,0},{24,8},{1,17},{9,25},{17,1},{25,9},{2,18},{10... | collective-permute-start | bytes 786440 | tf_op jit(solution)/shard_map/ppermute | solution.py:36
  180.5 11.1 %collective-permute-start.21 = (f32[2,32,1024]{2,1,0:T(8,128)S(1)}, f32[2,32,1024]{2,1,0:T(8,128)S(1)}, u32[]{:S(2)}, u32[]{:S(2)}) collective-permute-start(f32[2,32,1024]{2,1,0:T(8,128)S(1)} %get-tuple-element.18), channel_id=1, source_target_pairs={{0,24},{8,0},{16,8},{24,16},{1,25},{9,1},{17,9},{25,17},{2,26},{10... | collective-permute-start | bytes 786440 | tf_op jit(solution)/shard_map/ppermute | solution.py:36
  191.7 9.8 %collective-permute-start.22 = (f32[32,1024]{1,0:T(8,128)S(1)}, f32[32,1024]{1,0:T(8,128)S(1)}, u32[]{:S(2)}, u32[]{:S(2)}) collective-permute-start(f32[32,1024]{1,0:T(8,128)S(1)} %dynamic-slice_bitcast_fusion.19), channel_id=1, source_target_pairs={{0,32},{32,0},{1,33},{33,1},{2,34},{34,2},{3,35},{35,3},{4,36},{36... | collective-permute-start | bytes 393224 | tf_op jit(solution)/shard_map/ppermute | solution.py:27

commit v12 on v11

--- a/solution.py
+++ b/solution.py
@@ -46,6 +46,7 @@
     zhi, ys, cores, layers = (lax.axis_size(a) for a in COL_PARTS + ("layer",))
     halves = ys // 2
     block = right.shape[0] // (halves * cores * layers)
+    right = right.reshape(halves, cores, layers, block, -1).transpose(1, 2, 0, 3, 4).reshape(right.shape)
     gathered = jnp.zeros((cycle_size, halves, block, left_rows), jnp.float32)
     arrived = right
     reduced = None
@@ -60,9 +61,9 @@
         if step + 1 < cycle_size:
             arrived = from_behind(current, "row", 1)
         piece = lax.dot_general(current, left, (((1,), (1,)), ((), ())), preferred_element_type=jnp.float32)
-        piece = piece.reshape(halves, cores, layers, block, left_rows)
-        piece = pair_over(piece, "core", 1)
-        reduced = spread_over(piece, "layer", 1)
+        piece = piece.reshape(cores, layers, halves, block, left_rows)
+        piece = pair_over(piece, "core", 0)
+        reduced = spread_over(piece, "layer", 0)
     gathered = lax.dynamic_update_slice_in_dim(gathered, reduced[None], (position + 1) % cycle_size, 0)
     ordered = gathered.reshape(zhi, ys, block, left_rows)
     ordered = spread_over(ordered, "y", 1)

time: 204 us -> 207 us (1.015)
  local copies, waits for them, and re-layouts: 5.4 us -> 11.3 us
    unnamed x13 -> x15, local copies, waits for them, and re-layouts: 2.96 us -> 5.96 us
  transfers between devices with their start and end apart: 23 -> 23, of which waited for: 22 -> 22; matrix products, arithmetic and copies ran while one was open for 10% -> 9% of each run, Pallas kernels for 0% -> 0%
where the time goes in v12:
time: 207 us; the launch traced here: 205 us
  waiting for transfers between devices  137 us (66%)
  starting transfers between devices  33.1 us (16%)
  matrix products  13.6 us (7%)
  local copies, waits for them, and re-layouts  11.3 us (5%)
  other arithmetic  9.74 us (5%)
    ppermute x3, waiting for transfers between devices, from_behind(): return lax.ppermute(x, axis, [(i, (i + by) % size) for i in range(size)])  67.2 us
    ppermute x15, waiting for transfers between devices, spread_over(): lax.ppermute(send, axes, [(i, (i + shift) % n) for i in range(n)])  54.6 us
    ppermute x15, starting transfers between devices, spread_over(): lax.ppermute(send, axes, [(i, (i + shift) % n) for i in range(n)])  25.3 us
    ppermute x5, waiting for transfers between devices, pair_over(): return keep + lax.ppermute(send, axis, [(0, 1), (1, 0)])  15.1 us
    dot_general x4, matrix products, local(): lax.dot_general(current, left, (((1,), (1,)), ((), ())), preferred_elemen...  13.6 us
    unnamed x15, local copies, waits for them, and re-layouts  5.96 us
    ppermute x5, starting transfers between devices, pair_over(): return keep + lax.ppermute(send, axis, [(0, 1), (1, 0)])  5.83 us
  transfers between devices with their start and end apart: 23, of which 22 were waited for; matrix products, arithmetic and copies ran while one was open for 9% of the time, Pallas kernels for 0%

profile of v12, /device:TPU:2, one launch (start us, length us, event | category | flops | bytes accessed | tf_op | source)
XLA Modules:
  0.0 205.0 jit_solution(16432495312427054457)
XLA Ops:
  0.0 4.0 %copy.8 = bf16[2048,512]{0,1:T(8,128)(2,1)} copy(bf16[2048,512]{1,0:T(8,128)(2,1)} %param.6) | data formatting | bytes 4194304 | tf_op args[2]
  9.9 2.5 %bitcast_multiply_fusion = bf16[1024,2048]{1,0:T(8,128)(2,1)S(1)} fusion(bf16[1024,2048]{1,0:T(8,128)(2,1)} %param.4, bf16[16,2048]{1,0:T(8,128)(2,1)S(1)} %mul.33), kind=kLoop, calls=%fused_computation.6 | loop fusion | flops 2097152 | bytes 8454144 | tf_op jit(solution)/shard_map/mul | solution.py:19
  14.3 3.7 %fusion.4 = f32[2,4,2,32,1024]{4,3,2,1,0:T(8,128)} fusion(bf16[1024,2048]{1,0:T(8,128)(2,1)S(1)} %bitcast_multiply_fusion, bf16[2,4,2,32,2048]{4,3,1,0,2:T(8,128)(2,1)S(1)} %multiply_bitcast_fusion), kind=kOutput, calls=%fused_computation.4 | convolution fusion | flops 2147483648 | bytes 8388608 | tf_op jit(solution)/shard_map/dot_general | solution.py:63
  19.6 2.7 %collective-permute-done.1 = f32[4,2,32,1024]{3,2,1,0:T(8,128)} collective-permute-done((f32[4,2,32,1024]{3,2,1,0:T(8,128)S(1)}, f32[4,2,32,1024]{3,2,1,0:T(8,128)}, u32[]{:S(2)}, u32[]{:S(2)}) %collective-permute-start.1) | collective-permute-done | bytes 1048608 | tf_op jit(solution)/shard_map/ppermute | solution.py:27
  28.7 4.4 %collective-permute-done.2 = f32[2,32,1024]{2,1,0:T(8,128)S(1)} collective-permute-done((f32[2,32,1024]{2,1,0:T(8,128)S(1)}, f32[2,32,1024]{2,1,0:T(8,128)S(1)}, u32[]{:S(2)}, u32[]{:S(2)}) %collective-permute-start.2) | collective-permute-done | bytes 262176 | tf_op jit(solution)/shard_map/ppermute | solution.py:36
  33.1 3.0 %collective-permute-done.3 = f32[2,32,1024]{2,1,0:T(8,128)S(1)} collective-permute-done((f32[2,32,1024]{2,1,0:T(8,128)S(1)}, f32[2,32,1024]{2,1,0:T(8,128)S(1)}, u32[]{:S(2)}, u32[]{:S(2)}) %collective-permute-start.3) | collective-permute-done | bytes 262176 | tf_op jit(solution)/shard_map/ppermute | solution.py:36
  36.1 3.8 %collective-permute-done.4 = f32[2,32,1024]{2,1,0:T(8,128)S(1)} collective-permute-done((f32[2,32,1024]{2,1,0:T(8,128)S(1)}, f32[2,32,1024]{2,1,0:T(8,128)S(1)}, u32[]{:S(2)}, u32[]{:S(2)}) %collective-permute-start.4) | collective-permute-done | bytes 262176 | tf_op jit(solution)/shard_map/ppermute | solution.py:36
  40.0 18.2 %collective-permute-done = bf16[512,2048]{1,0:T(8,128)(2,1)} collective-permute-done((bf16[512,2048]{1,0:T(8,128)(2,1)}, bf16[512,2048]{1,0:T(8,128)(2,1)}, u32[]{:S(2)}, u32[]{:S(2)}) %collective-permute-start) | collective-permute-done | bytes 2097184 | tf_op jit(solution)/shard_map/ppermute | solution.py:12
  58.2 5.2 %fusion.2 = f32[2,4,2,32,1024]{4,3,2,1,0:T(8,128)S(1)} fusion(bf16[2,4,2,32,2048]{4,3,2,1,0:T(8,128)(2,1)} %bitcast.15, bf16[1024,2048]{1,0:T(8,128)(2,1)} %copy-done), kind=kOutput, calls=%fused_computation.2 | convolution fusion | flops 2147483648 | bytes 8388608 | tf_op jit(solution)/shard_map/dot_general | solution.py:63
  63.6 2.6 %collective-permute-done.6 = f32[4,2,32,1024]{3,2,1,0:T(8,128)S(1)} collective-permute-done((f32[4,2,32,1024]{3,2,1,0:T(8,128)S(1)}, f32[4,2,32,1024]{3,2,1,0:T(8,128)S(1)}, u32[]{:S(2)}, u32[]{:S(2)}) %collective-permute-start.6) | collective-permute-done | bytes 1048608 | tf_op jit(solution)/shard_map/ppermute | solution.py:27
  71.3 4.4 %collective-permute-done.7 = f32[2,32,1024]{2,1,0:T(8,128)S(1)} collective-permute-done((f32[2,32,1024]{2,1,0:T(8,128)S(1)}, f32[2,32,1024]{2,1,0:T(8,128)S(1)}, u32[]{:S(2)}, u32[]{:S(2)}) %collective-permute-start.7) | collective-permute-done | bytes 262176 | tf_op jit(solution)/shard_map/ppermute | solution.py:36
  75.7 3.0 %collective-permute-done.8 = f32[2,32,1024]{2,1,0:T(8,128)S(1)} collective-permute-done((f32[2,32,1024]{2,1,0:T(8,128)S(1)}, f32[2,32,1024]{2,1,0:T(8,128)S(1)}, u32[]{:S(2)}, u32[]{:S(2)}) %collective-permute-start.8) | collective-permute-done | bytes 262176 | tf_op jit(solution)/shard_map/ppermute | solution.py:36
  78.7 3.9 %collective-permute-done.9 = f32[2,32,1024]{2,1,0:T(8,128)S(1)} collective-permute-done((f32[2,32,1024]{2,1,0:T(8,128)S(1)}, f32[2,32,1024]{2,1,0:T(8,128)S(1)}, u32[]{:S(2)}, u32[]{:S(2)}) %collective-permute-start.9) | collective-permute-done | bytes 262176 | tf_op jit(solution)/shard_map/ppermute | solution.py:36
  83.4 23.6 %collective-permute-done.5 = bf16[512,2048]{1,0:T(8,128)(2,1)S(1)} collective-permute-done((bf16[512,2048]{1,0:T(8,128)(2,1)}, bf16[512,2048]{1,0:T(8,128)(2,1)S(1)}, u32[]{:S(2)}, u32[]{:S(2)}) %collective-permute-start.5) | collective-permute-done | bytes 2097184 | tf_op jit(solution)/shard_map/ppermute | solution.py:12
  107.0 2.4 %fusion = f32[2,4,2,32,1024]{4,3,2,1,0:T(8,128)S(1)} fusion(bf16[2,4,2,32,2048]{4,3,2,1,0:T(8,128)(2,1)S(1)} %bitcast.128, bf16[1024,2048]{1,0:T(8,128)(2,1)S(1)} %copy-done.1), kind=kOutput, calls=%fused_computation | convolution fusion | flops 2147483648 | bytes 8388608 | tf_op jit(solution)/shard_map/dot_general | solution.py:63
  109.6 2.6 %collective-permute-done.10 = f32[4,2,32,1024]{3,2,1,0:T(8,128)S(1)} collective-permute-done((f32[4,2,32,1024]{3,2,1,0:T(8,128)S(1)}, f32[4,2,32,1024]{3,2,1,0:T(8,128)S(1)}, u32[]{:S(2)}, u32[]{:S(2)}) %collective-permute-start.10) | collective-permute-done | bytes 1048608 | tf_op jit(solution)/shard_map/ppermute | solution.py:27
  114.8 2.5 %collective-permute-start.13 = (f32[2,32,1024]{2,1,0:T(8,128)S(1)}, f32[2,32,1024]{2,1,0:T(8,128)S(1)}, u32[]{:S(2)}, u32[]{:S(2)}) collective-permute-start(f32[2,32,1024]{2,1,0:T(8,128)S(1)} %get-tuple-element.24), channel_id=1, source_target_pairs={{0,3},{1,0},{2,1},{3,2},{4,7},{5,4},{6,5},{7,6},{8,11},{9,8},{10,9... | collective-permute-start | bytes 786440 | tf_op jit(solution)/shard_map/ppermute | solution.py:36
  117.3 4.4 %collective-permute-done.11 = f32[2,32,1024]{2,1,0:T(8,128)S(1)} collective-permute-done((f32[2,32,1024]{2,1,0:T(8,128)S(1)}, f32[2,32,1024]{2,1,0:T(8,128)S(1)}, u32[]{:S(2)}, u32[]{:S(2)}) %collective-permute-start.11) | collective-permute-done | bytes 262176 | tf_op jit(solution)/shard_map/ppermute | solution.py:36
  121.7 3.0 %collective-permute-done.12 = f32[2,32,1024]{2,1,0:T(8,128)S(1)} collective-permute-done((f32[2,32,1024]{2,1,0:T(8,128)S(1)}, f32[2,32,1024]{2,1,0:T(8,128)S(1)}, u32[]{:S(2)}, u32[]{:S(2)}) %collective-permute-start.12) | collective-permute-done | bytes 262176 | tf_op jit(solution)/shard_map/ppermute | solution.py:36
  124.8 3.7 %collective-permute-done.13 = f32[2,32,1024]{2,1,0:T(8,128)S(1)} collective-permute-done((f32[2,32,1024]{2,1,0:T(8,128)S(1)}, f32[2,32,1024]{2,1,0:T(8,128)S(1)}, u32[]{:S(2)}, u32[]{:S(2)}) %collective-permute-start.13) | collective-permute-done | bytes 262176 | tf_op jit(solution)/shard_map/ppermute | solution.py:36
  129.3 25.4 %collective-permute-done.14 = bf16[512,2048]{1,0:T(8,128)(2,1)S(1)} collective-permute-done((bf16[512,2048]{1,0:T(8,128)(2,1)S(1)}, bf16[512,2048]{1,0:T(8,128)(2,1)S(1)}, u32[]{:S(2)}, u32[]{:S(2)}) %collective-permute-start.14) | collective-permute-done | bytes 2097184 | tf_op jit(solution)/shard_map/ppermute | solution.py:12
  154.7 2.4 %fusion.19 = f32[512,1024]{1,0:T(8,128)S(1)} fusion(bf16[512,2048]{1,0:T(8,128)(2,1)S(1)} %collective-permute-done.14, bf16[1024,2048]{1,0:T(8,128)(2,1)S(1)} %copy-done.1), kind=kOutput, calls=%fused_computation.56 | convolution fusion | flops 2147483648 | bytes 8388608 | tf_op jit(solution)/shard_map/dot_general | solution.py:63
  158.3 2.8 %collective-permute-done.15 = f32[4,2,32,1024]{3,2,1,0:T(8,128)} collective-permute-done((f32[4,2,32,1024]{3,2,1,0:T(8,128)}, f32[4,2,32,1024]{3,2,1,0:T(8,128)}, u32[]{:S(2)}, u32[]{:S(2)}) %collective-permute-start.15) | collective-permute-done | bytes 1048608 | tf_op jit(solution)/shard_map/ppermute | solution.py:27
  164.9 2.5 %collective-permute-start.18 = (f32[2,32,1024]{2,1,0:T(8,128)S(1)}, f32[2,32,1024]{2,1,0:T(8,128)S(1)}, u32[]{:S(2)}, u32[]{:S(2)}) collective-permute-start(f32[2,32,1024]{2,1,0:T(8,128)S(1)} %get-tuple-element.21), channel_id=1, source_target_pairs={{0,3},{1,0},{2,1},{3,2},{4,7},{5,4},{6,5},{7,6},{8,11},{9,8},{10,9... | collective-permute-start | bytes 786440 | tf_op jit(solution)/shard_map/ppermute | solution.py:36
  167.5 4.3 %collective-permute-done.16 = f32[2,32,1024]{2,1,0:T(8,128)S(1)} collective-permute-done((f32[2,32,1024]{2,1,0:T(8,128)S(1)}, f32[2,32,1024]{2,1,0:T(8,128)S(1)}, u32[]{:S(2)}, u32[]{:S(2)}) %collective-permute-start.16) | collective-permute-done | bytes 262176 | tf_op jit(solution)/shard_map/ppermute | solution.py:36
  171.8 3.0 %collective-permute-done.17 = f32[2,32,1024]{2,1,0:T(8,128)S(1)} collective-permute-done((f32[2,32,1024]{2,1,0:T(8,128)S(1)}, f32[2,32,1024]{2,1,0:T(8,128)S(1)}, u32[]{:S(2)}, u32[]{:S(2)}) %collective-permute-start.17) | collective-permute-done | bytes 262176 | tf_op jit(solution)/shard_map/ppermute | solution.py:36
  174.9 3.7 %collective-permute-done.18 = f32[2,32,1024]{2,1,0:T(8,128)S(1)} collective-permute-done((f32[2,32,1024]{2,1,0:T(8,128)S(1)}, f32[2,32,1024]{2,1,0:T(8,128)S(1)}, u32[]{:S(2)}, u32[]{:S(2)}) %collective-permute-start.18) | collective-permute-done | bytes 262176 | tf_op jit(solution)/shard_map/ppermute | solution.py:36
  180.5 2.9 %collective-permute-start.20 = (f32[2,32,1024]{2,1,0:T(8,128)S(1)}, f32[2,32,1024]{2,1,0:T(8,128)S(1)}, u32[]{:S(2)}, u32[]{:S(2)}) collective-permute-start(f32[2,32,1024]{2,1,0:T(8,128)S(1)} %get-tuple-element.19), channel_id=1, source_target_pairs={{0,16},{8,24},{16,0},{24,8},{1,17},{9,25},{17,1},{25,9},{2,18},{10... | collective-permute-start | bytes 786440 | tf_op jit(solution)/shard_map/ppermute | solution.py:36
  184.7 3.5 %collective-permute-done.19 = f32[2,32,1024]{2,1,0:T(8,128)S(1)} collective-permute-done((f32[2,32,1024]{2,1,0:T(8,128)S(1)}, f32[2,32,1024]{2,1,0:T(8,128)S(1)}, u32[]{:S(2)}, u32[]{:S(2)}) %collective-permute-start.19) | collective-permute-done | bytes 262176 | tf_op jit(solution)/shard_map/ppermute | solution.py:36
  188.2 6.2 %collective-permute-done.20 = f32[2,32,1024]{2,1,0:T(8,128)S(1)} collective-permute-done((f32[2,32,1024]{2,1,0:T(8,128)S(1)}, f32[2,32,1024]{2,1,0:T(8,128)S(1)}, u32[]{:S(2)}, u32[]{:S(2)}) %collective-permute-start.20) | collective-permute-done | bytes 262176 | tf_op jit(solution)/shard_map/ppermute | solution.py:36
  194.6 5.5 %collective-permute-start.22 = (f32[32,1024]{1,0:T(8,128)S(1)}, f32[32,1024]{1,0:T(8,128)S(1)}, u32[]{:S(2)}, u32[]{:S(2)}) collective-permute-start(f32[32,1024]{1,0:T(8,128)S(1)} %dynamic-slice_bitcast_fusion.19), channel_id=1, source_target_pairs={{0,32},{32,0},{1,33},{33,1},{2,34},{34,2},{3,35},{35,3},{4,36},{36... | collective-permute-start | bytes 393224 | tf_op jit(solution)/shard_map/ppermute | solution.py:27
  200.1 4.3 %collective-permute-done.22 = f32[32,1024]{1,0:T(8,128)S(1)} collective-permute-done((f32[32,1024]{1,0:T(8,128)S(1)}, f32[32,1024]{1,0:T(8,128)S(1)}, u32[]{:S(2)}, u32[]{:S(2)}) %collective-permute-start.22) | collective-permute-done | bytes 131104 | tf_op jit(solution)/shard_map/ppermute | solution.py:27
  (68 shorter events, 34.2 us)
Async XLA Ops:
  0.0 4.0 %copy-start.6 = (s32[32,8]{0,1:T(8,128)S(1)}, s32[32,8]{0,1:T(8,128)}, u32[]{:S(2)}) copy-start(s32[32,8]{0,1:T(8,128)} %param.7) | copy-start | bytes 3076
  6.1 3.5 %copy-start.5 = (s32[16,32]{1,0:T(8,128)S(1)}, s32[16,32]{1,0:T(8,128)}, u32[]{:S(2)}) copy-start(s32[16,32]{1,0:T(8,128)} %param.5) | copy-start | bytes 6148
  7.6 50.6 %collective-permute-start = (bf16[512,2048]{1,0:T(8,128)(2,1)}, bf16[512,2048]{1,0:T(8,128)(2,1)}, u32[]{:S(2)}, u32[]{:S(2)}) collective-permute-start(bf16[512,2048]{1,0:T(8,128)(2,1)} %bitcast.4), channel_id=1, source_target_pairs={{0,64},{64,128},{128,192},{192,0},{1,65},{65,129},{129,193},{193,1... | collective-permute-start | bytes 6291464 | tf_op jit(solution)/shard_map/ppermute | solution.py:12
  12.3 2.0 copy-start
  18.1 4.3 %copy-start.2 = (f32[2,4,2,32,1024]{4,3,2,1,0:T(8,128)S(1)}, f32[2,4,2,32,1024]{4,3,2,1,0:T(8,128)}, u32[]{:S(2)}) copy-start(f32[2,4,2,32,1024]{4,3,2,1,0:T(8,128)} %fusion.4) | copy-start | bytes 6291460
  19.5 2.9 %collective-permute-start.1 = (f32[4,2,32,1024]{3,2,1,0:T(8,128)S(1)}, f32[4,2,32,1024]{3,2,1,0:T(8,128)}, u32[]{:S(2)}, u32[]{:S(2)}) collective-permute-start(f32[4,2,32,1024]{3,2,1,0:T(8,128)S(1)} %dynamic-slice_bitcast_fusion.3), channel_id=1, source_target_pairs={{0,4},{4,0},{1,5},{5,1},{2,6},{6,2},{3,7},{7,3},{8,12},{12,8},{9,1... | collective-permute-start | bytes 3145736 | tf_op jit(solution)/shard_map/ppermute | solution.py:27
  23.8 9.2 %collective-permute-start.2 = (f32[2,32,1024]{2,1,0:T(8,128)S(1)}, f32[2,32,1024]{2,1,0:T(8,128)S(1)}, u32[]{:S(2)}, u32[]{:S(2)}) collective-permute-start(f32[2,32,1024]{2,1,0:T(8,128)S(1)} %get-tuple-element.29), channel_id=1, source_target_pairs={{0,1},{1,2},{2,3},{3,0},{4,5},{5,6},{6,7},{7,4},{8,9},{9,10},{10,1... | collective-permute-start | bytes 786440 | tf_op jit(solution)/shard_map/ppermute | solution.py:36
  25.4 10.7 %collective-permute-start.3 = (f32[2,32,1024]{2,1,0:T(8,128)S(1)}, f32[2,32,1024]{2,1,0:T(8,128)S(1)}, u32[]{:S(2)}, u32[]{:S(2)}) collective-permute-start(f32[2,32,1024]{2,1,0:T(8,128)S(1)} %get-tuple-element.31), channel_id=1, source_target_pairs={{0,2},{1,3},{2,0},{3,1},{4,6},{5,7},{6,4},{7,5},{8,10},{9,11},{10,... | collective-permute-start | bytes 786440 | tf_op jit(solution)/shard_map/ppermute | solution.py:36
  26.5 13.4 %collective-permute-start.4 = (f32[2,32,1024]{2,1,0:T(8,128)S(1)}, f32[2,32,1024]{2,1,0:T(8,128)S(1)}, u32[]{:S(2)}, u32[]{:S(2)}) collective-permute-start(f32[2,32,1024]{2,1,0:T(8,128)S(1)} %get-tuple-element.30), channel_id=1, source_target_pairs={{0,3},{1,0},{2,1},{3,2},{4,7},{5,4},{6,5},{7,6},{8,11},{9,8},{10,9... | collective-permute-start | bytes 786440 | tf_op jit(solution)/shard_map/ppermute | solution.py:36
  58.2 48.8 %collective-permute-start.5 = (bf16[512,2048]{1,0:T(8,128)(2,1)}, bf16[512,2048]{1,0:T(8,128)(2,1)S(1)}, u32[]{:S(2)}, u32[]{:S(2)}) collective-permute-start(bf16[512,2048]{1,0:T(8,128)(2,1)} %collective-permute-done), channel_id=1, source_target_pairs={{0,64},{64,128},{128,192},{192,0},{1,65},{65,129},{129,193},{193,1... | collective-permute-start | bytes 6291464 | tf_op jit(solution)/shard_map/ppermute | solution.py:12
  63.5 2.7 %collective-permute-start.6 = (f32[4,2,32,1024]{3,2,1,0:T(8,128)S(1)}, f32[4,2,32,1024]{3,2,1,0:T(8,128)S(1)}, u32[]{:S(2)}, u32[]{:S(2)}) collective-permute-start(f32[4,2,32,1024]{3,2,1,0:T(8,128)S(1)} %dynamic-slice_bitcast_fusion.2), channel_id=1, source_target_pairs={{0,4},{4,0},{1,5},{5,1},{2,6},{6,2},{3,7},{7,3},{8,12},{12,8},{9,1... | collective-permute-start | bytes 3145736 | tf_op jit(solution)/shard_map/ppermute | solution.py:27
  66.2 40.8 %copy-start.1 = (bf16[1024,2048]{1,0:T(8,128)(2,1)S(1)}, bf16[1024,2048]{1,0:T(8,128)(2,1)}, u32[]{:S(2)}) copy-start(bf16[1024,2048]{1,0:T(8,128)(2,1)} %copy-done) | copy-start | bytes 12582916
  66.5 9.2 %collective-permute-start.7 = (f32[2,32,1024]{2,1,0:T(8,128)S(1)}, f32[2,32,1024]{2,1,0:T(8,128)S(1)}, u32[]{:S(2)}, u32[]{:S(2)}) collective-permute-start(f32[2,32,1024]{2,1,0:T(8,128)S(1)} %get-tuple-element.26), channel_id=1, source_target_pairs={{0,1},{1,2},{2,3},{3,0},{4,5},{5,6},{6,7},{7,4},{8,9},{9,10},{10,1... | collective-permute-start | bytes 786440 | tf_op jit(solution)/shard_map/ppermute | solution.py:36
  68.0 10.7 %collective-permute-start.8 = (f32[2,32,1024]{2,1,0:T(8,128)S(1)}, f32[2,32,1024]{2,1,0:T(8,128)S(1)}, u32[]{:S(2)}, u32[]{:S(2)}) collective-permute-start(f32[2,32,1024]{2,1,0:T(8,128)S(1)} %get-tuple-element.28), channel_id=1, source_target_pairs={{0,2},{1,3},{2,0},{3,1},{4,6},{5,7},{6,4},{7,5},{8,10},{9,11},{10,... | collective-permute-start | bytes 786440 | tf_op jit(solution)/shard_map/ppermute | solution.py:36
  69.2 13.5 %collective-permute-start.9 = (f32[2,32,1024]{2,1,0:T(8,128)S(1)}, f32[2,32,1024]{2,1,0:T(8,128)S(1)}, u32[]{:S(2)}, u32[]{:S(2)}) collective-permute-start(f32[2,32,1024]{2,1,0:T(8,128)S(1)} %get-tuple-element.27), channel_id=1, source_target_pairs={{0,3},{1,0},{2,1},{3,2},{4,7},{5,4},{6,5},{7,6},{8,11},{9,8},{10,9... | collective-permute-start | bytes 786440 | tf_op jit(solution)/shard_map/ppermute | solution.py:36
  107.0 47.7 %collective-permute-start.14 = (bf16[512,2048]{1,0:T(8,128)(2,1)S(1)}, bf16[512,2048]{1,0:T(8,128)(2,1)S(1)}, u32[]{:S(2)}, u32[]{:S(2)}) collective-permute-start(bf16[512,2048]{1,0:T(8,128)(2,1)S(1)} %collective-permute-done.5), channel_id=1, source_target_pairs={{0,64},{64,128},{128,192},{192,0},{1,65},{65,129},{129,193},{193,1... | collective-permute-start | bytes 6291464 | tf_op jit(solution)/shard_map/ppermute | solution.py:12
  109.5 2.7 %collective-permute-start.10 = (f32[4,2,32,1024]{3,2,1,0:T(8,128)S(1)}, f32[4,2,32,1024]{3,2,1,0:T(8,128)S(1)}, u32[]{:S(2)}, u32[]{:S(2)}) collective-permute-start(f32[4,2,32,1024]{3,2,1,0:T(8,128)S(1)} %dynamic-slice_bitcast_fusion.1), channel_id=1, source_target_pairs={{0,4},{4,0},{1,5},{5,1},{2,6},{6,2},{3,7},{7,3},{8,12},{12,8},{9,1... | collective-permute-start | bytes 3145736 | tf_op jit(solution)/shard_map/ppermute | solution.py:27
  112.5 9.2 %collective-permute-start.11 = (f32[2,32,1024]{2,1,0:T(8,128)S(1)}, f32[2,32,1024]{2,1,0:T(8,128)S(1)}, u32[]{:S(2)}, u32[]{:S(2)}) collective-permute-start(f32[2,32,1024]{2,1,0:T(8,128)S(1)} %get-tuple-element.23), channel_id=1, source_target_pairs={{0,1},{1,2},{2,3},{3,0},{4,5},{5,6},{6,7},{7,4},{8,9},{9,10},{10,1... | collective-permute-start | bytes 786440 | tf_op jit(solution)/shard_map/ppermute | solution.py:36
  114.1 10.7 %collective-permute-start.12 = (f32[2,32,1024]{2,1,0:T(8,128)S(1)}, f32[2,32,1024]{2,1,0:T(8,128)S(1)}, u32[]{:S(2)}, u32[]{:S(2)}) collective-permute-start(f32[2,32,1024]{2,1,0:T(8,128)S(1)} %get-tuple-element.25), channel_id=1, source_target_pairs={{0,2},{1,3},{2,0},{3,1},{4,6},{5,7},{6,4},{7,5},{8,10},{9,11},{10,... | collective-permute-start | bytes 786440 | tf_op jit(solution)/shard_map/ppermute | solution.py:36
  114.8 13.7 %collective-permute-start.13 = (f32[2,32,1024]{2,1,0:T(8,128)S(1)}, f32[2,32,1024]{2,1,0:T(8,128)S(1)}, u32[]{:S(2)}, u32[]{:S(2)}) collective-permute-start(f32[2,32,1024]{2,1,0:T(8,128)S(1)} %get-tuple-element.24), channel_id=1, source_target_pairs={{0,3},{1,0},{2,1},{3,2},{4,7},{5,4},{6,5},{7,6},{8,11},{9,8},{10,9... | collective-permute-start | bytes 786440 | tf_op jit(solution)/shard_map/ppermute | solution.py:36
  158.1 3.0 %collective-permute-start.15 = (f32[4,2,32,1024]{3,2,1,0:T(8,128)}, f32[4,2,32,1024]{3,2,1,0:T(8,128)}, u32[]{:S(2)}, u32[]{:S(2)}) collective-permute-start(f32[4,2,32,1024]{3,2,1,0:T(8,128)} %dynamic-slice_bitcast_fusion), channel_id=1, source_target_pairs={{0,4},{4,0},{1,5},{5,1},{2,6},{6,2},{3,7},{7,3},{8,12},{12,8},{9,1... | collective-permute-start | bytes 3145736 | tf_op jit(solution)/shard_map/ppermute | solution.py:27
  158.3 9.1 %copy-start.3 = (f32[2,32,1024]{2,1,0:T(8,128)S(1)}, f32[2,32,1024]{2,1,0:T(8,128)}, u32[]{:S(2)}) copy-start(f32[2,32,1024]{2,1,0:T(8,128)} %fusion.13) | copy-start | bytes 786436
  158.3 9.2 %copy-start.4 = (f32[2,32,1024]{2,1,0:T(8,128)S(1)}, f32[2,32,1024]{2,1,0:T(8,128)}, u32[]{:S(2)}) copy-start(f32[2,32,1024]{2,1,0:T(8,128)} %fusion.11) | copy-start | bytes 786436
  162.6 9.2 %collective-permute-start.16 = (f32[2,32,1024]{2,1,0:T(8,128)S(1)}, f32[2,32,1024]{2,1,0:T(8,128)S(1)}, u32[]{:S(2)}, u32[]{:S(2)}) collective-permute-start(f32[2,32,1024]{2,1,0:T(8,128)S(1)} %get-tuple-element.20), channel_id=1, source_target_pairs={{0,1},{1,2},{2,3},{3,0},{4,5},{5,6},{6,7},{7,4},{8,9},{9,10},{10,1... | collective-permute-start | bytes 786440 | tf_op jit(solution)/shard_map/ppermute | solution.py:36
  164.2 10.7 %collective-permute-start.17 = (f32[2,32,1024]{2,1,0:T(8,128)S(1)}, f32[2,32,1024]{2,1,0:T(8,128)S(1)}, u32[]{:S(2)}, u32[]{:S(2)}) collective-permute-start(f32[2,32,1024]{2,1,0:T(8,128)S(1)} %get-tuple-element.22), channel_id=1, source_target_pairs={{0,2},{1,3},{2,0},{3,1},{4,6},{5,7},{6,4},{7,5},{8,10},{9,11},{10,... | collective-permute-start | bytes 786440 | tf_op jit(solution)/shard_map/ppermute | solution.py:36
  164.9 13.7 %collective-permute-start.18 = (f32[2,32,1024]{2,1,0:T(8,128)S(1)}, f32[2,32,1024]{2,1,0:T(8,128)S(1)}, u32[]{:S(2)}, u32[]{:S(2)}) collective-permute-start(f32[2,32,1024]{2,1,0:T(8,128)S(1)} %get-tuple-element.21), channel_id=1, source_target_pairs={{0,3},{1,0},{2,1},{3,2},{4,7},{5,4},{6,5},{7,6},{8,11},{9,8},{10,9... | collective-permute-start | bytes 786440 | tf_op jit(solution)/shard_map/ppermute | solution.py:36
  178.7 9.5 %collective-permute-start.19 = (f32[2,32,1024]{2,1,0:T(8,128)S(1)}, f32[2,32,1024]{2,1,0:T(8,128)S(1)}, u32[]{:S(2)}, u32[]{:S(2)}) collective-permute-start(f32[2,32,1024]{2,1,0:T(8,128)S(1)} %get-tuple-element.17), channel_id=1, source_target_pairs={{0,8},{8,16},{16,24},{24,0},{1,9},{9,17},{17,25},{25,1},{2,10},{10... | collective-permute-start | bytes 786440 | tf_op jit(solution)/shard_map/ppermute | solution.py:36
  180.5 14.0 %collective-permute-start.20 = (f32[2,32,1024]{2,1,0:T(8,128)S(1)}, f32[2,32,1024]{2,1,0:T(8,128)S(1)}, u32[]{:S(2)}, u32[]{:S(2)}) collective-permute-start(f32[2,32,1024]{2,1,0:T(8,128)S(1)} %get-tuple-element.19), channel_id=1, source_target_pairs={{0,16},{8,24},{16,0},{24,8},{1,17},{9,25},{17,1},{25,9},{2,18},{10... | collective-permute-start | bytes 786440 | tf_op jit(solution)/shard_map/ppermute | solution.py:36
  183.4 11.1 %collective-permute-start.21 = (f32[2,32,1024]{2,1,0:T(8,128)S(1)}, f32[2,32,1024]{2,1,0:T(8,128)S(1)}, u32[]{:S(2)}, u32[]{:S(2)}) collective-permute-start(f32[2,32,1024]{2,1,0:T(8,128)S(1)} %get-tuple-element.18), channel_id=1, source_target_pairs={{0,24},{8,0},{16,8},{24,16},{1,25},{9,1},{17,9},{25,17},{2,26},{10... | collective-permute-start | bytes 786440 | tf_op jit(solution)/shard_map/ppermute | solution.py:36
  194.6 9.8 %collective-permute-start.22 = (f32[32,1024]{1,0:T(8,128)S(1)}, f32[32,1024]{1,0:T(8,128)S(1)}, u32[]{:S(2)}, u32[]{:S(2)}) collective-permute-start(f32[32,1024]{1,0:T(8,128)S(1)} %dynamic-slice_bitcast_fusion.19), channel_id=1, source_target_pairs={{0,32},{32,0},{1,33},{33,1},{2,34},{34,2},{3,35},{35,3},{4,36},{36... | collective-permute-start | bytes 393224 | tf_op jit(solution)/shard_map/ppermute | solution.py:27

commit v13 on v10

--- a/solution.py
+++ b/solution.py
@@ -39,7 +39,7 @@
 
 def local(left_blocks, left_pattern, right_blocks, right_pattern):
     left = apply_pattern(left_blocks, left_pattern)
-    right = apply_pattern(right_blocks, right_pattern).T
+    right = apply_pattern(right_blocks.T, right_pattern.T)
     left_rows = left.shape[0]
     cycle_size = lax.axis_size("row")
     position = lax.axis_index("row")

time: 208 us -> 204 us (0.981)
  local copies, waits for them, and re-layouts: 13.2 us -> 5.35 us
  waiting for transfers between devices: 134 us -> 139 us
  other arithmetic: 11.9 us -> 9.45 us
    optimization_barrier x2 -> x0, local copies, waits for them, and re-layouts: 5.85 us -> none  [local(): current, reduced = lax.optimization_barrier((current, reduced))]
    ppermute x3, waiting for transfers between devices: 63.9 us -> 68.9 us  [from_behind(): return lax.ppermute(x, axis, [(i, (i + by) % size) for i in range(size)])]
    transpose x1 -> x0, local copies, waits for them, and re-layouts: 2.46 us -> none  [local(): right = apply_pattern(right_blocks, right_pattern).T]
  transfers between devices with their start and end apart: 23 -> 23, of which waited for: 22 -> 22; matrix products, arithmetic and copies ran while one was open for 11% -> 10% of each run, Pallas kernels for 0% -> 0%
where the time goes in v13:
time: 204 us; the launch traced here: 202 us
  waiting for transfers between devices  139 us (68%)
  starting transfers between devices  33.1 us (16%)
  matrix products  15.4 us (8%)
  other arithmetic  9.45 us (5%)
  local copies, waits for them, and re-layouts  5.35 us (3%)
    ppermute x3, waiting for transfers between devices, from_behind(): return lax.ppermute(x, axis, [(i, (i + by) % size) for i in range(size)])  68.9 us
    ppermute x15, waiting for transfers between devices, spread_over(): lax.ppermute(send, axes, [(i, (i + shift) % n) for i in range(n)])  54.5 us
    ppermute x15, starting transfers between devices, spread_over(): lax.ppermute(send, axes, [(i, (i + shift) % n) for i in range(n)])  25.3 us
    dot_general x4, matrix products, local(): lax.dot_general(current, left, (((1,), (1,)), ((), ())), preferred_elemen...  15.4 us
    ppermute x5, waiting for transfers between devices, pair_over(): return keep + lax.ppermute(send, axis, [(0, 1), (1, 0)])  15.1 us
    ppermute x5, starting transfers between devices, pair_over(): return keep + lax.ppermute(send, axis, [(0, 1), (1, 0)])  5.83 us
  transfers between devices with their start and end apart: 23, of which 22 were waited for; matrix products, arithmetic and copies ran while one was open for 10% of the time, Pallas kernels for 0%

profile of v13, /device:TPU:2, one launch (start us, length us, event | category | flops | bytes accessed | tf_op | source)
XLA Modules:
  0.0 202.2 jit_solution(916010410114548543)
XLA Ops:
  0.0 2.9 %copy.9 = bf16[2048,512]{0,1:T(8,128)(2,1)S(1)} copy(bf16[2048,512]{1,0:T(8,128)(2,1)} %param.6) | data formatting | bytes 4194304 | tf_op args[2]
  7.0 2.5 %bitcast_multiply_fusion = bf16[1024,2048]{1,0:T(8,128)(2,1)S(1)} fusion(bf16[1024,2048]{1,0:T(8,128)(2,1)} %param.4, bf16[16,2048]{1,0:T(8,128)(2,1)S(1)} %mul.42), kind=kLoop, calls=%fused_computation.6 | loop fusion | flops 2097152 | bytes 8454144 | tf_op jit(solution)/shard_map/mul | solution.py:19
  9.5 5.5 %fusion.4 = f32[2,2,4,32,1024]{4,3,2,1,0:T(8,128)S(1)} fusion(bf16[2,2,4,32,2048]{4,3,2,1,0:T(8,128)(2,1)} %bitcast.3, bf16[1024,2048]{1,0:T(8,128)(2,1)S(1)} %bitcast_multiply_fusion), kind=kOutput, calls=%fused_computation.4 | convolution fusion | flops 2147483648 | bytes 8388608 | tf_op jit(solution)/shard_map/dot_general | solution.py:63
  15.2 2.7 %collective-permute-done.1 = f32[2,4,32,1024]{3,2,1,0:T(8,128)} collective-permute-done((f32[2,4,32,1024]{3,2,1,0:T(8,128)S(1)}, f32[2,4,32,1024]{3,2,1,0:T(8,128)}, u32[]{:S(2)}, u32[]{:S(2)}) %collective-permute-start.1) | collective-permute-done | bytes 1048608 | tf_op jit(solution)/shard_map/ppermute | solution.py:27
  24.2 4.4 %collective-permute-done.2 = f32[2,32,1024]{2,1,0:T(8,128)S(1)} collective-permute-done((f32[2,32,1024]{2,1,0:T(8,128)S(1)}, f32[2,32,1024]{2,1,0:T(8,128)S(1)}, u32[]{:S(2)}, u32[]{:S(2)}) %collective-permute-start.2) | collective-permute-done | bytes 262176 | tf_op jit(solution)/shard_map/ppermute | solution.py:36
  28.6 3.0 %collective-permute-done.3 = f32[2,32,1024]{2,1,0:T(8,128)S(1)} collective-permute-done((f32[2,32,1024]{2,1,0:T(8,128)S(1)}, f32[2,32,1024]{2,1,0:T(8,128)S(1)}, u32[]{:S(2)}, u32[]{:S(2)}) %collective-permute-start.3) | collective-permute-done | bytes 262176 | tf_op jit(solution)/shard_map/ppermute | solution.py:36
  31.7 3.8 %collective-permute-done.4 = f32[2,32,1024]{2,1,0:T(8,128)S(1)} collective-permute-done((f32[2,32,1024]{2,1,0:T(8,128)S(1)}, f32[2,32,1024]{2,1,0:T(8,128)S(1)}, u32[]{:S(2)}, u32[]{:S(2)}) %collective-permute-start.4) | collective-permute-done | bytes 262176 | tf_op jit(solution)/shard_map/ppermute | solution.py:36
  35.6 19.8 %collective-permute-done = bf16[512,2048]{1,0:T(8,128)(2,1)} collective-permute-done((bf16[512,2048]{1,0:T(8,128)(2,1)}, bf16[512,2048]{1,0:T(8,128)(2,1)}, u32[]{:S(2)}, u32[]{:S(2)}) %collective-permute-start) | collective-permute-done | bytes 2097184 | tf_op jit(solution)/shard_map/ppermute | solution.py:12
  55.3 5.2 %fusion.2 = f32[2,2,4,32,1024]{4,3,2,1,0:T(8,128)S(1)} fusion(bf16[2,2,4,32,2048]{4,3,2,1,0:T(8,128)(2,1)} %bitcast.14, bf16[1024,2048]{1,0:T(8,128)(2,1)} %copy-done), kind=kOutput, calls=%fused_computation.2 | convolution fusion | flops 2147483648 | bytes 8388608 | tf_op jit(solution)/shard_map/dot_general | solution.py:63
  60.7 2.6 %collective-permute-done.6 = f32[2,4,32,1024]{3,2,1,0:T(8,128)S(1)} collective-permute-done((f32[2,4,32,1024]{3,2,1,0:T(8,128)S(1)}, f32[2,4,32,1024]{3,2,1,0:T(8,128)S(1)}, u32[]{:S(2)}, u32[]{:S(2)}) %collective-permute-start.6) | collective-permute-done | bytes 1048608 | tf_op jit(solution)/shard_map/ppermute | solution.py:27
  68.4 4.4 %collective-permute-done.7 = f32[2,32,1024]{2,1,0:T(8,128)S(1)} collective-permute-done((f32[2,32,1024]{2,1,0:T(8,128)S(1)}, f32[2,32,1024]{2,1,0:T(8,128)S(1)}, u32[]{:S(2)}, u32[]{:S(2)}) %collective-permute-start.7) | collective-permute-done | bytes 262176 | tf_op jit(solution)/shard_map/ppermute | solution.py:36
  72.8 3.0 %collective-permute-done.8 = f32[2,32,1024]{2,1,0:T(8,128)S(1)} collective-permute-done((f32[2,32,1024]{2,1,0:T(8,128)S(1)}, f32[2,32,1024]{2,1,0:T(8,128)S(1)}, u32[]{:S(2)}, u32[]{:S(2)}) %collective-permute-start.8) | collective-permute-done | bytes 262176 | tf_op jit(solution)/shard_map/ppermute | solution.py:36
  75.8 3.8 %collective-permute-done.9 = f32[2,32,1024]{2,1,0:T(8,128)S(1)} collective-permute-done((f32[2,32,1024]{2,1,0:T(8,128)S(1)}, f32[2,32,1024]{2,1,0:T(8,128)S(1)}, u32[]{:S(2)}, u32[]{:S(2)}) %collective-permute-start.9) | collective-permute-done | bytes 262176 | tf_op jit(solution)/shard_map/ppermute | solution.py:36
  80.5 23.7 %collective-permute-done.5 = bf16[512,2048]{1,0:T(8,128)(2,1)S(1)} collective-permute-done((bf16[512,2048]{1,0:T(8,128)(2,1)}, bf16[512,2048]{1,0:T(8,128)(2,1)S(1)}, u32[]{:S(2)}, u32[]{:S(2)}) %collective-permute-start.5) | collective-permute-done | bytes 2097184 | tf_op jit(solution)/shard_map/ppermute | solution.py:12
  104.2 2.4 %fusion = f32[2,2,4,32,1024]{4,3,2,1,0:T(8,128)S(1)} fusion(bf16[2,2,4,32,2048]{4,3,2,1,0:T(8,128)(2,1)S(1)} %bitcast.124, bf16[1024,2048]{1,0:T(8,128)(2,1)S(1)} %copy-done.1), kind=kOutput, calls=%fused_computation | convolution fusion | flops 2147483648 | bytes 8388608 | tf_op jit(solution)/shard_map/dot_general | solution.py:63
  106.7 2.6 %collective-permute-done.10 = f32[2,4,32,1024]{3,2,1,0:T(8,128)S(1)} collective-permute-done((f32[2,4,32,1024]{3,2,1,0:T(8,128)S(1)}, f32[2,4,32,1024]{3,2,1,0:T(8,128)S(1)}, u32[]{:S(2)}, u32[]{:S(2)}) %collective-permute-start.10) | collective-permute-done | bytes 1048608 | tf_op jit(solution)/shard_map/ppermute | solution.py:27
  111.9 2.5 %collective-permute-start.13 = (f32[2,32,1024]{2,1,0:T(8,128)S(1)}, f32[2,32,1024]{2,1,0:T(8,128)S(1)}, u32[]{:S(2)}, u32[]{:S(2)}) collective-permute-start(f32[2,32,1024]{2,1,0:T(8,128)S(1)} %get-tuple-element.24), channel_id=1, source_target_pairs={{0,3},{1,0},{2,1},{3,2},{4,7},{5,4},{6,5},{7,6},{8,11},{9,8},{10,9... | collective-permute-start | bytes 786440 | tf_op jit(solution)/shard_map/ppermute | solution.py:36
  114.4 4.4 %collective-permute-done.11 = f32[2,32,1024]{2,1,0:T(8,128)S(1)} collective-permute-done((f32[2,32,1024]{2,1,0:T(8,128)S(1)}, f32[2,32,1024]{2,1,0:T(8,128)S(1)}, u32[]{:S(2)}, u32[]{:S(2)}) %collective-permute-start.11) | collective-permute-done | bytes 262176 | tf_op jit(solution)/shard_map/ppermute | solution.py:36
  118.8 3.0 %collective-permute-done.12 = f32[2,32,1024]{2,1,0:T(8,128)S(1)} collective-permute-done((f32[2,32,1024]{2,1,0:T(8,128)S(1)}, f32[2,32,1024]{2,1,0:T(8,128)S(1)}, u32[]{:S(2)}, u32[]{:S(2)}) %collective-permute-start.12) | collective-permute-done | bytes 262176 | tf_op jit(solution)/shard_map/ppermute | solution.py:36
  121.9 3.7 %collective-permute-done.13 = f32[2,32,1024]{2,1,0:T(8,128)S(1)} collective-permute-done((f32[2,32,1024]{2,1,0:T(8,128)S(1)}, f32[2,32,1024]{2,1,0:T(8,128)S(1)}, u32[]{:S(2)}, u32[]{:S(2)}) %collective-permute-start.13) | collective-permute-done | bytes 262176 | tf_op jit(solution)/shard_map/ppermute | solution.py:36
  126.4 25.5 %collective-permute-done.14 = bf16[512,2048]{1,0:T(8,128)(2,1)S(1)} collective-permute-done((bf16[512,2048]{1,0:T(8,128)(2,1)S(1)}, bf16[512,2048]{1,0:T(8,128)(2,1)S(1)}, u32[]{:S(2)}, u32[]{:S(2)}) %collective-permute-start.14) | collective-permute-done | bytes 2097184 | tf_op jit(solution)/shard_map/ppermute | solution.py:12
  151.9 2.4 %fusion.18 = f32[512,1024]{1,0:T(8,128)S(1)} fusion(bf16[512,2048]{1,0:T(8,128)(2,1)S(1)} %collective-permute-done.14, bf16[1024,2048]{1,0:T(8,128)(2,1)S(1)} %copy-done.1), kind=kOutput, calls=%fused_computation.55 | convolution fusion | flops 2147483648 | bytes 8388608 | tf_op jit(solution)/shard_map/dot_general | solution.py:63
  155.5 2.8 %collective-permute-done.15 = f32[2,4,32,1024]{3,2,1,0:T(8,128)} collective-permute-done((f32[2,4,32,1024]{3,2,1,0:T(8,128)}, f32[2,4,32,1024]{3,2,1,0:T(8,128)}, u32[]{:S(2)}, u32[]{:S(2)}) %collective-permute-start.15) | collective-permute-done | bytes 1048608 | tf_op jit(solution)/shard_map/ppermute | solution.py:27
  162.1 2.5 %collective-permute-start.18 = (f32[2,32,1024]{2,1,0:T(8,128)S(1)}, f32[2,32,1024]{2,1,0:T(8,128)S(1)}, u32[]{:S(2)}, u32[]{:S(2)}) collective-permute-start(f32[2,32,1024]{2,1,0:T(8,128)S(1)} %get-tuple-element.21), channel_id=1, source_target_pairs={{0,3},{1,0},{2,1},{3,2},{4,7},{5,4},{6,5},{7,6},{8,11},{9,8},{10,9... | collective-permute-start | bytes 786440 | tf_op jit(solution)/shard_map/ppermute | solution.py:36
  164.7 4.3 %collective-permute-done.16 = f32[2,32,1024]{2,1,0:T(8,128)S(1)} collective-permute-done((f32[2,32,1024]{2,1,0:T(8,128)S(1)}, f32[2,32,1024]{2,1,0:T(8,128)S(1)}, u32[]{:S(2)}, u32[]{:S(2)}) %collective-permute-start.16) | collective-permute-done | bytes 262176 | tf_op jit(solution)/shard_map/ppermute | solution.py:36
  169.0 3.0 %collective-permute-done.17 = f32[2,32,1024]{2,1,0:T(8,128)S(1)} collective-permute-done((f32[2,32,1024]{2,1,0:T(8,128)S(1)}, f32[2,32,1024]{2,1,0:T(8,128)S(1)}, u32[]{:S(2)}, u32[]{:S(2)}) %collective-permute-start.17) | collective-permute-done | bytes 262176 | tf_op jit(solution)/shard_map/ppermute | solution.py:36
  172.0 3.7 %collective-permute-done.18 = f32[2,32,1024]{2,1,0:T(8,128)S(1)} collective-permute-done((f32[2,32,1024]{2,1,0:T(8,128)S(1)}, f32[2,32,1024]{2,1,0:T(8,128)S(1)}, u32[]{:S(2)}, u32[]{:S(2)}) %collective-permute-start.18) | collective-permute-done | bytes 262176 | tf_op jit(solution)/shard_map/ppermute | solution.py:36
  177.6 2.9 %collective-permute-start.20 = (f32[2,32,1024]{2,1,0:T(8,128)S(1)}, f32[2,32,1024]{2,1,0:T(8,128)S(1)}, u32[]{:S(2)}, u32[]{:S(2)}) collective-permute-start(f32[2,32,1024]{2,1,0:T(8,128)S(1)} %get-tuple-element.19), channel_id=1, source_target_pairs={{0,16},{8,24},{16,0},{24,8},{1,17},{9,25},{17,1},{25,9},{2,18},{10... | collective-permute-start | bytes 786440 | tf_op jit(solution)/shard_map/ppermute | solution.py:36
  181.9 3.5 %collective-permute-done.19 = f32[2,32,1024]{2,1,0:T(8,128)S(1)} collective-permute-done((f32[2,32,1024]{2,1,0:T(8,128)S(1)}, f32[2,32,1024]{2,1,0:T(8,128)S(1)}, u32[]{:S(2)}, u32[]{:S(2)}) %collective-permute-start.19) | collective-permute-done | bytes 262176 | tf_op jit(solution)/shard_map/ppermute | solution.py:36
  185.4 6.2 %collective-permute-done.20 = f32[2,32,1024]{2,1,0:T(8,128)S(1)} collective-permute-done((f32[2,32,1024]{2,1,0:T(8,128)S(1)}, f32[2,32,1024]{2,1,0:T(8,128)S(1)}, u32[]{:S(2)}, u32[]{:S(2)}) %collective-permute-start.20) | collective-permute-done | bytes 262176 | tf_op jit(solution)/shard_map/ppermute | solution.py:36
  191.7 5.5 %collective-permute-start.22 = (f32[32,1024]{1,0:T(8,128)S(1)}, f32[32,1024]{1,0:T(8,128)S(1)}, u32[]{:S(2)}, u32[]{:S(2)}) collective-permute-start(f32[32,1024]{1,0:T(8,128)S(1)} %dynamic-slice_bitcast_fusion.19), channel_id=1, source_target_pairs={{0,32},{32,0},{1,33},{33,1},{2,34},{34,2},{3,35},{35,3},{4,36},{36... | collective-permute-start | bytes 393224 | tf_op jit(solution)/shard_map/ppermute | solution.py:27
  197.3 4.3 %collective-permute-done.22 = f32[32,1024]{1,0:T(8,128)S(1)} collective-permute-done((f32[32,1024]{1,0:T(8,128)S(1)}, f32[32,1024]{1,0:T(8,128)S(1)}, u32[]{:S(2)}, u32[]{:S(2)}) %collective-permute-start.22) | collective-permute-done | bytes 131104 | tf_op jit(solution)/shard_map/ppermute | solution.py:27
  (63 shorter events, 29.0 us)
Async XLA Ops:
  0.0 2.9 %copy-start.5 = (s32[32,8]{0,1:T(8,128)S(1)}, s32[32,8]{0,1:T(8,128)}, u32[]{:S(2)}) copy-start(s32[32,8]{0,1:T(8,128)} %param.7) | copy-start | bytes 3076
  3.2 3.5 %copy-start.4 = (s32[16,32]{1,0:T(8,128)S(1)}, s32[16,32]{1,0:T(8,128)}, u32[]{:S(2)}) copy-start(s32[16,32]{1,0:T(8,128)} %param.5) | copy-start | bytes 6148
  4.8 50.6 %collective-permute-start = (bf16[512,2048]{1,0:T(8,128)(2,1)}, bf16[512,2048]{1,0:T(8,128)(2,1)}, u32[]{:S(2)}, u32[]{:S(2)}) collective-permute-start(bf16[512,2048]{1,0:T(8,128)(2,1)} %bitcast_multiply_fusion.1), channel_id=1, source_target_pairs={{0,64},{64,128},{128,192},{192,0},{1,65},{65,129},{129,193},{193,1... | collective-permute-start | bytes 6291464 | tf_op jit(solution)/shard_map/ppermute | solution.py:12
  9.5 5.5 %copy-start = (bf16[1024,2048]{1,0:T(8,128)(2,1)}, bf16[1024,2048]{1,0:T(8,128)(2,1)S(1)}, u32[]{:S(2)}) copy-start(bf16[1024,2048]{1,0:T(8,128)(2,1)S(1)} %bitcast_multiply_fusion) | copy-start | bytes 12582916
  15.1 2.9 %collective-permute-start.1 = (f32[2,4,32,1024]{3,2,1,0:T(8,128)S(1)}, f32[2,4,32,1024]{3,2,1,0:T(8,128)}, u32[]{:S(2)}, u32[]{:S(2)}) collective-permute-start(f32[2,4,32,1024]{3,2,1,0:T(8,128)S(1)} %dynamic-slice_bitcast_fusion.3), channel_id=1, source_target_pairs={{0,4},{4,0},{1,5},{5,1},{2,6},{6,2},{3,7},{7,3},{8,12},{12,8},{9,1... | collective-permute-start | bytes 3145736 | tf_op jit(solution)/shard_map/ppermute | solution.py:27
  19.4 9.2 %collective-permute-start.2 = (f32[2,32,1024]{2,1,0:T(8,128)S(1)}, f32[2,32,1024]{2,1,0:T(8,128)S(1)}, u32[]{:S(2)}, u32[]{:S(2)}) collective-permute-start(f32[2,32,1024]{2,1,0:T(8,128)S(1)} %get-tuple-element.29), channel_id=1, source_target_pairs={{0,1},{1,2},{2,3},{3,0},{4,5},{5,6},{6,7},{7,4},{8,9},{9,10},{10,1... | collective-permute-start | bytes 786440 | tf_op jit(solution)/shard_map/ppermute | solution.py:36
  21.0 10.7 %collective-permute-start.3 = (f32[2,32,1024]{2,1,0:T(8,128)S(1)}, f32[2,32,1024]{2,1,0:T(8,128)S(1)}, u32[]{:S(2)}, u32[]{:S(2)}) collective-permute-start(f32[2,32,1024]{2,1,0:T(8,128)S(1)} %get-tuple-element.31), channel_id=1, source_target_pairs={{0,2},{1,3},{2,0},{3,1},{4,6},{5,7},{6,4},{7,5},{8,10},{9,11},{10,... | collective-permute-start | bytes 786440 | tf_op jit(solution)/shard_map/ppermute | solution.py:36
  22.1 13.4 %collective-permute-start.4 = (f32[2,32,1024]{2,1,0:T(8,128)S(1)}, f32[2,32,1024]{2,1,0:T(8,128)S(1)}, u32[]{:S(2)}, u32[]{:S(2)}) collective-permute-start(f32[2,32,1024]{2,1,0:T(8,128)S(1)} %get-tuple-element.30), channel_id=1, source_target_pairs={{0,3},{1,0},{2,1},{3,2},{4,7},{5,4},{6,5},{7,6},{8,11},{9,8},{10,9... | collective-permute-start | bytes 786440 | tf_op jit(solution)/shard_map/ppermute | solution.py:36
  55.3 48.8 %collective-permute-start.5 = (bf16[512,2048]{1,0:T(8,128)(2,1)}, bf16[512,2048]{1,0:T(8,128)(2,1)S(1)}, u32[]{:S(2)}, u32[]{:S(2)}) collective-permute-start(bf16[512,2048]{1,0:T(8,128)(2,1)} %collective-permute-done), channel_id=1, source_target_pairs={{0,64},{64,128},{128,192},{192,0},{1,65},{65,129},{129,193},{193,1... | collective-permute-start | bytes 6291464 | tf_op jit(solution)/shard_map/ppermute | solution.py:12
  60.6 2.7 %collective-permute-start.6 = (f32[2,4,32,1024]{3,2,1,0:T(8,128)S(1)}, f32[2,4,32,1024]{3,2,1,0:T(8,128)S(1)}, u32[]{:S(2)}, u32[]{:S(2)}) collective-permute-start(f32[2,4,32,1024]{3,2,1,0:T(8,128)S(1)} %dynamic-slice_bitcast_fusion.2), channel_id=1, source_target_pairs={{0,4},{4,0},{1,5},{5,1},{2,6},{6,2},{3,7},{7,3},{8,12},{12,8},{9,1... | collective-permute-start | bytes 3145736 | tf_op jit(solution)/shard_map/ppermute | solution.py:27
  63.4 40.8 %copy-start.1 = (bf16[1024,2048]{1,0:T(8,128)(2,1)S(1)}, bf16[1024,2048]{1,0:T(8,128)(2,1)}, u32[]{:S(2)}) copy-start(bf16[1024,2048]{1,0:T(8,128)(2,1)} %copy-done) | copy-start | bytes 12582916
  63.6 9.2 %collective-permute-start.7 = (f32[2,32,1024]{2,1,0:T(8,128)S(1)}, f32[2,32,1024]{2,1,0:T(8,128)S(1)}, u32[]{:S(2)}, u32[]{:S(2)}) collective-permute-start(f32[2,32,1024]{2,1,0:T(8,128)S(1)} %get-tuple-element.26), channel_id=1, source_target_pairs={{0,1},{1,2},{2,3},{3,0},{4,5},{5,6},{6,7},{7,4},{8,9},{9,10},{10,1... | collective-permute-start | bytes 786440 | tf_op jit(solution)/shard_map/ppermute | solution.py:36
  65.2 10.7 %collective-permute-start.8 = (f32[2,32,1024]{2,1,0:T(8,128)S(1)}, f32[2,32,1024]{2,1,0:T(8,128)S(1)}, u32[]{:S(2)}, u32[]{:S(2)}) collective-permute-start(f32[2,32,1024]{2,1,0:T(8,128)S(1)} %get-tuple-element.28), channel_id=1, source_target_pairs={{0,2},{1,3},{2,0},{3,1},{4,6},{5,7},{6,4},{7,5},{8,10},{9,11},{10,... | collective-permute-start | bytes 786440 | tf_op jit(solution)/shard_map/ppermute | solution.py:36
  66.3 13.4 %collective-permute-start.9 = (f32[2,32,1024]{2,1,0:T(8,128)S(1)}, f32[2,32,1024]{2,1,0:T(8,128)S(1)}, u32[]{:S(2)}, u32[]{:S(2)}) collective-permute-start(f32[2,32,1024]{2,1,0:T(8,128)S(1)} %get-tuple-element.27), channel_id=1, source_target_pairs={{0,3},{1,0},{2,1},{3,2},{4,7},{5,4},{6,5},{7,6},{8,11},{9,8},{10,9... | collective-permute-start | bytes 786440 | tf_op jit(solution)/shard_map/ppermute | solution.py:36
  104.2 47.7 %collective-permute-start.14 = (bf16[512,2048]{1,0:T(8,128)(2,1)S(1)}, bf16[512,2048]{1,0:T(8,128)(2,1)S(1)}, u32[]{:S(2)}, u32[]{:S(2)}) collective-permute-start(bf16[512,2048]{1,0:T(8,128)(2,1)S(1)} %collective-permute-done.5), channel_id=1, source_target_pairs={{0,64},{64,128},{128,192},{192,0},{1,65},{65,129},{129,193},{193,1... | collective-permute-start | bytes 6291464 | tf_op jit(solution)/shard_map/ppermute | solution.py:12
  106.6 2.7 %collective-permute-start.10 = (f32[2,4,32,1024]{3,2,1,0:T(8,128)S(1)}, f32[2,4,32,1024]{3,2,1,0:T(8,128)S(1)}, u32[]{:S(2)}, u32[]{:S(2)}) collective-permute-start(f32[2,4,32,1024]{3,2,1,0:T(8,128)S(1)} %dynamic-slice_bitcast_fusion.1), channel_id=1, source_target_pairs={{0,4},{4,0},{1,5},{5,1},{2,6},{6,2},{3,7},{7,3},{8,12},{12,8},{9,1... | collective-permute-start | bytes 3145736 | tf_op jit(solution)/shard_map/ppermute | solution.py:27
  109.6 9.2 %collective-permute-start.11 = (f32[2,32,1024]{2,1,0:T(8,128)S(1)}, f32[2,32,1024]{2,1,0:T(8,128)S(1)}, u32[]{:S(2)}, u32[]{:S(2)}) collective-permute-start(f32[2,32,1024]{2,1,0:T(8,128)S(1)} %get-tuple-element.23), channel_id=1, source_target_pairs={{0,1},{1,2},{2,3},{3,0},{4,5},{5,6},{6,7},{7,4},{8,9},{9,10},{10,1... | collective-permute-start | bytes 786440 | tf_op jit(solution)/shard_map/ppermute | solution.py:36
  111.2 10.7 %collective-permute-start.12 = (f32[2,32,1024]{2,1,0:T(8,128)S(1)}, f32[2,32,1024]{2,1,0:T(8,128)S(1)}, u32[]{:S(2)}, u32[]{:S(2)}) collective-permute-start(f32[2,32,1024]{2,1,0:T(8,128)S(1)} %get-tuple-element.25), channel_id=1, source_target_pairs={{0,2},{1,3},{2,0},{3,1},{4,6},{5,7},{6,4},{7,5},{8,10},{9,11},{10,... | collective-permute-start | bytes 786440 | tf_op jit(solution)/shard_map/ppermute | solution.py:36
  111.9 13.7 %collective-permute-start.13 = (f32[2,32,1024]{2,1,0:T(8,128)S(1)}, f32[2,32,1024]{2,1,0:T(8,128)S(1)}, u32[]{:S(2)}, u32[]{:S(2)}) collective-permute-start(f32[2,32,1024]{2,1,0:T(8,128)S(1)} %get-tuple-element.24), channel_id=1, source_target_pairs={{0,3},{1,0},{2,1},{3,2},{4,7},{5,4},{6,5},{7,6},{8,11},{9,8},{10,9... | collective-permute-start | bytes 786440 | tf_op jit(solution)/shard_map/ppermute | solution.py:36
  155.3 3.0 %collective-permute-start.15 = (f32[2,4,32,1024]{3,2,1,0:T(8,128)}, f32[2,4,32,1024]{3,2,1,0:T(8,128)}, u32[]{:S(2)}, u32[]{:S(2)}) collective-permute-start(f32[2,4,32,1024]{3,2,1,0:T(8,128)} %dynamic-slice_bitcast_fusion), channel_id=1, source_target_pairs={{0,4},{4,0},{1,5},{5,1},{2,6},{6,2},{3,7},{7,3},{8,12},{12,8},{9,1... | collective-permute-start | bytes 3145736 | tf_op jit(solution)/shard_map/ppermute | solution.py:27
  155.5 9.1 %copy-start.2 = (f32[2,32,1024]{2,1,0:T(8,128)S(1)}, f32[2,32,1024]{2,1,0:T(8,128)}, u32[]{:S(2)}) copy-start(f32[2,32,1024]{2,1,0:T(8,128)} %fusion.13) | copy-start | bytes 786436
  155.5 9.1 %copy-start.3 = (f32[2,32,1024]{2,1,0:T(8,128)S(1)}, f32[2,32,1024]{2,1,0:T(8,128)}, u32[]{:S(2)}) copy-start(f32[2,32,1024]{2,1,0:T(8,128)} %fusion.11) | copy-start | bytes 786436
  159.7 9.2 %collective-permute-start.16 = (f32[2,32,1024]{2,1,0:T(8,128)S(1)}, f32[2,32,1024]{2,1,0:T(8,128)S(1)}, u32[]{:S(2)}, u32[]{:S(2)}) collective-permute-start(f32[2,32,1024]{2,1,0:T(8,128)S(1)} %get-tuple-element.20), channel_id=1, source_target_pairs={{0,1},{1,2},{2,3},{3,0},{4,5},{5,6},{6,7},{7,4},{8,9},{9,10},{10,1... | collective-permute-start | bytes 786440 | tf_op jit(solution)/shard_map/ppermute | solution.py:36
  161.3 10.7 %collective-permute-start.17 = (f32[2,32,1024]{2,1,0:T(8,128)S(1)}, f32[2,32,1024]{2,1,0:T(8,128)S(1)}, u32[]{:S(2)}, u32[]{:S(2)}) collective-permute-start(f32[2,32,1024]{2,1,0:T(8,128)S(1)} %get-tuple-element.22), channel_id=1, source_target_pairs={{0,2},{1,3},{2,0},{3,1},{4,6},{5,7},{6,4},{7,5},{8,10},{9,11},{10,... | collective-permute-start | bytes 786440 | tf_op jit(solution)/shard_map/ppermute | solution.py:36
  162.1 13.7 %collective-permute-start.18 = (f32[2,32,1024]{2,1,0:T(8,128)S(1)}, f32[2,32,1024]{2,1,0:T(8,128)S(1)}, u32[]{:S(2)}, u32[]{:S(2)}) collective-permute-start(f32[2,32,1024]{2,1,0:T(8,128)S(1)} %get-tuple-element.21), channel_id=1, source_target_pairs={{0,3},{1,0},{2,1},{3,2},{4,7},{5,4},{6,5},{7,6},{8,11},{9,8},{10,9... | collective-permute-start | bytes 786440 | tf_op jit(solution)/shard_map/ppermute | solution.py:36
  175.9 9.5 %collective-permute-start.19 = (f32[2,32,1024]{2,1,0:T(8,128)S(1)}, f32[2,32,1024]{2,1,0:T(8,128)S(1)}, u32[]{:S(2)}, u32[]{:S(2)}) collective-permute-start(f32[2,32,1024]{2,1,0:T(8,128)S(1)} %get-tuple-element.17), channel_id=1, source_target_pairs={{0,8},{8,16},{16,24},{24,0},{1,9},{9,17},{17,25},{25,1},{2,10},{10... | collective-permute-start | bytes 786440 | tf_op jit(solution)/shard_map/ppermute | solution.py:36
  177.6 14.0 %collective-permute-start.20 = (f32[2,32,1024]{2,1,0:T(8,128)S(1)}, f32[2,32,1024]{2,1,0:T(8,128)S(1)}, u32[]{:S(2)}, u32[]{:S(2)}) collective-permute-start(f32[2,32,1024]{2,1,0:T(8,128)S(1)} %get-tuple-element.19), channel_id=1, source_target_pairs={{0,16},{8,24},{16,0},{24,8},{1,17},{9,25},{17,1},{25,9},{2,18},{10... | collective-permute-start | bytes 786440 | tf_op jit(solution)/shard_map/ppermute | solution.py:36
  180.5 11.1 %collective-permute-start.21 = (f32[2,32,1024]{2,1,0:T(8,128)S(1)}, f32[2,32,1024]{2,1,0:T(8,128)S(1)}, u32[]{:S(2)}, u32[]{:S(2)}) collective-permute-start(f32[2,32,1024]{2,1,0:T(8,128)S(1)} %get-tuple-element.18), channel_id=1, source_target_pairs={{0,24},{8,0},{16,8},{24,16},{1,25},{9,1},{17,9},{25,17},{2,26},{10... | collective-permute-start | bytes 786440 | tf_op jit(solution)/shard_map/ppermute | solution.py:36
  191.7 9.8 %collective-permute-start.22 = (f32[32,1024]{1,0:T(8,128)S(1)}, f32[32,1024]{1,0:T(8,128)S(1)}, u32[]{:S(2)}, u32[]{:S(2)}) collective-permute-start(f32[32,1024]{1,0:T(8,128)S(1)} %dynamic-slice_bitcast_fusion.19), channel_id=1, source_target_pairs={{0,32},{32,0},{1,33},{33,1},{2,34},{34,2},{3,35},{35,3},{4,36},{36... | collective-permute-start | bytes 393224 | tf_op jit(solution)/shard_map/ppermute | solution.py:27
